TPU v7x, 32 devices: a whole 2x2x4 slice. The times are simulated.
32 devices in a mesh: groups: 2 (over x), outer: 16 (over z, y, core).
Axes of the slice: x: 2, y: 2, z: 4, core: 2. Of those that a mesh axis runs over, the one named last changes fastest.
Arguments:
- queries: bfloat16 [12288, 2048], P(('groups', 'outer')), parts along dimension 0, may hold values from -256 to 256, as said below
- key_rows: bfloat16 [12288, 2048], P(('groups', 'outer')), parts along dimension 0, may hold values from -4 to 4
- value_rows: bfloat16 [12288, 2048], P(('groups', 'outer')), parts along dimension 0, may hold values from -6 to 6
- widths: int32 [96], P(('groups', 'outer')), parts along dimension 0, may hold values from 1 to 4, as said below
- columns: int32 [32, 4, 1], P('groups'), parts along dimension 0, may hold values from 0 to 47, as said below
Outputs:
- context: bfloat16 [12288, 2048], P(('groups', 'outer')), parts along dimension 0
There are 2 independent parts, one for each index of `groups`. A program takes and returns all parts, laid end to end along the dimension named above; each array names one. Nothing has to cross between parts.
Inputs may be any that keep to these rules, and one draw needn't show every extreme that they name: Block rows 3 and 4 have widths 4 and 1. columns[p, b, 0] is one block of panel p XOR 2**b, given by its index in the whole sequence. `queries`: entries of order one in most rows.
All inputs are finite; a program needn't handle non-finite values.
Results may differ from a plain program's by a relative error of at most 0.0022.
Values may be sent and summed in bfloat16 or wider, within the bound.
No kernel may reach another device: no remote copies, remote signals or barrier semaphores. Data moves between devices by JAX's collectives and lax.ppermute only.
A program may use at most 128 MiB of HBM per device.

v0:
```python
import jax
import jax.numpy as jnp
from jax import lax
from jax.sharding import PartitionSpec as P

HEADS = 16
BLK = 128
WIN = 4


def passed_along(block, axis, distance):
    devices = range(lax.axis_size(axis))
    route = [(i - distance, i) for i in devices if i - distance in devices]
    return lax.ppermute(block, axis, route)


def from_partner(value, axis, stride):
    mask = 2**stride
    pairs = [(source, source ^ mask) for source in range(lax.axis_size(axis))]
    return lax.ppermute(value, axis, pairs)


def window_visible(widths, first_block, block_len, window):
    row_count = widths.shape[0]
    offsets = jnp.arange(window * block_len, dtype=jnp.int32) // block_len
    key_pos = jnp.arange(window * block_len, dtype=jnp.int32) % block_len
    query_pos = jnp.arange(block_len, dtype=jnp.int32)
    block_ids = first_block + jnp.arange(row_count, dtype=jnp.int32)
    inside = offsets[None, None, :] < widths[:, None, None]
    started = block_ids[:, None, None] - offsets[None, None, :] >= 0
    causal = (offsets[None, None, :] > 0) | (key_pos[None, None, :] <= query_pos[None, :, None])
    return inside & started & causal


def pick_blocks(source, block_index):
    return lax.dynamic_slice_in_dim(source, block_index[0] * BLK, BLK, 0)


def on_device(queries, key_rows, value_rows, widths, columns):
    token_count, features = queries.shape
    panel_len = token_count // BLK
    head_dim = features // HEADS
    score_scale = head_dim ** (-0.5)
    device = lax.axis_index("outer")
    level_count = lax.axis_size("outer").bit_length() - 1
    rim_len = (WIN - 1) * BLK
    prev_keys, prev_values = passed_along((key_rows, value_rows), "outer", 1)
    ext_keys = jnp.concatenate([prev_keys, key_rows], axis=0)
    ext_values = jnp.concatenate([prev_values, value_rows], axis=0)

    def window_stack(extended):
        return jnp.concatenate(
            [
                extended[(WIN - 1 - offset) * BLK : (WIN - 1 - offset) * BLK + token_count].reshape(
                    panel_len, BLK, HEADS, head_dim
                )
                for offset in range(WIN)
            ],
            axis=1,
        )

    query_four = queries.reshape(panel_len, BLK, HEADS, head_dim)
    scores = (
        jnp.einsum(
            "pqhd,pkhd->pqhk",
            query_four,
            window_stack(ext_keys),
            preferred_element_type=jnp.float32,
        )
        * score_scale
    )
    visible = window_visible(widths, device * panel_len, BLK, WIN)
    masked = jnp.where(visible[:, :, None, :], scores, -jnp.inf)
    win_max = jnp.max(masked, axis=-1)
    win_weights = jnp.exp(masked - win_max[..., None])
    win_total = jnp.sum(win_weights, axis=-1)
    win_sum = jnp.einsum(
        "pqhk,pkhd->pqhd",
        win_weights.astype(jnp.bfloat16),
        window_stack(ext_values),
        preferred_element_type=jnp.float32,
    )
    win_max = win_max.reshape(token_count, HEADS)
    win_total = win_total.reshape(token_count, HEADS)
    win_sum = win_sum.reshape(token_count, HEADS, head_dim)
    bit_order = list(range(level_count))
    key_list = [None] * level_count
    value_list = [None] * level_count
    for level_bit in bit_order:
        partner = jnp.bitwise_xor(device, 1 << level_bit)
        panel_keys, panel_values = from_partner((key_rows, value_rows), "outer", level_bit)
        needed = columns[device, level_bit] - partner * panel_len
        far_keys = pick_blocks(panel_keys, needed)
        far_values = pick_blocks(panel_values, needed)
        key_list[level_bit] = far_keys
        value_list[level_bit] = far_values
    far_count = key_list[0].shape[0]
    all_keys = jnp.stack(key_list, axis=0).reshape(level_count, far_count, HEADS, head_dim)
    all_values = jnp.stack(value_list, axis=0).reshape(level_count, far_count, HEADS, head_dim)
    query_three = queries.reshape(token_count, HEADS, head_dim)
    far_scores = (
        jnp.einsum("qhd,lkhd->qhlk", query_three, all_keys, preferred_element_type=jnp.float32)
        * score_scale
    )
    far_max = jnp.max(far_scores, axis=-1)
    far_weights = jnp.exp(far_scores - far_max[..., None])
    far_total = jnp.sum(far_weights, axis=-1)
    far_sum = jnp.einsum(
        "qhlk,lkhd->qhld",
        far_weights.astype(jnp.bfloat16),
        all_values,
        preferred_element_type=jnp.float32,
    )
    top_max = jnp.maximum(win_max, jnp.max(far_max, axis=-1))
    win_factor = jnp.exp(win_max - top_max)
    far_factor = jnp.exp(far_max - top_max[..., None])
    total = win_total * win_factor + jnp.sum(far_total * far_factor, axis=-1)
    output = win_sum * win_factor[..., None] + jnp.sum(far_sum * far_factor[..., None], axis=2)
    context = output / total[..., None]
    return context.reshape(token_count, features).astype(jnp.bfloat16)


def solution(mesh):
    placed = (
        P(("groups", "outer"), None),
        P(("groups", "outer"), None),
        P(("groups", "outer"), None),
        P(("groups", "outer")),
        P("groups", None, None),
    )
    return jax.shard_map(
        on_device,
        mesh=mesh,
        in_specs=placed,
        out_specs=P(("groups", "outer"), None),
        check_vma=False,
    )
```

profile of v0, /device:TPU:29, one launch (start us, length us, event | category | flops | bytes accessed | tf_op | source)
XLA Modules:
  0.0 249.5 jit_solution(15142986098664050621)
XLA Ops:
  0.0 2.7 %copy.56 = bf16[384,2048]{0,1:T(8,128)(2,1)} copy(bf16[384,2048]{1,0:T(8,128)(2,1)} %param.6) | data formatting | bytes 3145728 | tf_op args[1]
  5.7 68.1 %collective-permute-done.5 = bf16[384,2048]{0,1:T(8,128)(2,1)S(1)} collective-permute-done((bf16[384,2048]{0,1:T(8,128)(2,1)}, bf16[384,2048]{0,1:T(8,128)(2,1)S(1)}, u32[]{:S(2)}, u32[]{:S(2)}) %collective-permute-start.5) | collective-permute-done | bytes 1572896 | tf_op jit(solution)/shard_map/ppermute | solution.py:20
  78.4 3.0 %copy.89 = bf16[48,8,16,128]{3,2,1,0:T(8,128)(2,1)} copy(bf16[48,8,16,128]{3,1,2,0:T(8,128)(2,1)} %bitcast.140) | data formatting | bytes 3145728
  83.0 2.8 %copy.44 = bf16[3,128,16,128]{1,3,2,0:T(8,128)(2,1)} copy(bf16[3,128,16,128]{3,2,1,0:T(8,128)(2,1)} %bitcast.131) | data formatting | bytes 3145728 | tf_op jit(solution)/shard_map/reshape | solution.py:54
  90.1 2.4 collective-permute-start.8
  92.5 1.9 constant_dynamic-slice_fusion.4
  94.4 2.1 copy.63
  98.3 2.1 copy.62
  102.2 2.0 copy.61
  106.1 2.0 copy.60
  111.5 28.0 %collective-permute-done.7 = bf16[384,2048]{1,0:T(8,128)(2,1)} collective-permute-done((bf16[384,2048]{1,0:T(8,128)(2,1)S(1)}, bf16[384,2048]{1,0:T(8,128)(2,1)}, u32[]{:S(2)}, u32[]{:S(2)}) %collective-permute-start.7) | collective-permute-done | bytes 1572896 | tf_op jit(solution)/shard_map/ppermute | solution.py:20
  139.5 1.9 constant_dynamic-slice_fusion.2
  141.3 2.1 copy.67
  143.4 1.9 constant_dynamic-slice_fusion.3
  145.3 2.0 copy.66
  147.3 3.0 %copy.84 = bf16[48,8,16,128]{3,2,1,0:T(8,128)(2,1)} copy(bf16[48,8,16,128]{3,1,2,0:T(8,128)(2,1)} %bitcast.39) | data formatting | bytes 3145728
  150.3 2.8 %copy.47 = bf16[3,128,16,128]{1,3,2,0:T(8,128)(2,1)} copy(bf16[3,128,16,128]{3,2,1,0:T(8,128)(2,1)} %bitcast.134) | data formatting | bytes 3145728 | tf_op jit(solution)/shard_map/reshape | solution.py:54
  153.1 22.0 %collective-permute-done.9 = bf16[384,2048]{1,0:T(8,128)(2,1)} collective-permute-done((bf16[384,2048]{1,0:T(8,128)(2,1)S(1)}, bf16[384,2048]{1,0:T(8,128)(2,1)}, u32[]{:S(2)}, u32[]{:S(2)}) %collective-permute-start.9) | collective-permute-done | bytes 1572896 | tf_op jit(solution)/shard_map/ppermute | solution.py:20
  177.0 2.1 copy.69
  180.9 2.0 copy.68
  186.9 2.0 copy.45
  190.8 2.0 copy.46
  199.1 4.6 %fusion.6 = (f32[3,128,16]{1,2,0:T(8,128)S(1)}, f32[3,16,512,128]{3,2,1,0:T(8,128)S(1)}) fusion(pred[3,128,512]{1,2,0:T(8,128)(4,1)S(1)} %broadcast_and_fusion, bf16[3,128,16,128]{3,2,1,0:T(8,128)(2,1)S(1)} %bitcast.142, bf16[3,128,16,128]{3,1,2,0:T(8,128)(2,1)} %copy.51, bf16[3,128,16,128]{3,1,2,0:T(8,128)(2,1)} %copy.50, ...), kind=kOutput, calls=%fused_computation.12 | convolution fusion | flops 839903232 | bytes 20668416 | tf_op jit(solution)/shard_map/pqhd,pkhd->pqhk/dot_general | solution.py:64
  203.7 3.2 %fusion.2 = f32[3,128,16]{1,2,0:T(8,128)S(1)} fusion(f32[3,16,512,128]{3,2,1,0:T(8,128)S(1)} %get-tuple-element.21, f32[3,128,16]{1,2,0:T(8,128)S(1)} %get-tuple-element.20, pred[3,128,512]{1,2,0:T(8,128)(4,1)S(1)} %broadcast_and_fusion), kind=kLoop, calls=%fused_computation.8 | loop fusion | flops 12576768 | bytes 12828672 | tf_op jit(solution)/shard_map/reduce_sum | solution.py:76
  206.9 6.5 %fusion.51 = f32[3,128,16,128]{1,3,2,0:T(8,128)} fusion(f32[3,16,512,128]{3,2,1,0:T(8,128)S(1)} %get-tuple-element.21, f32[3,128,16]{1,2,0:T(8,128)S(1)} %get-tuple-element.20, pred[3,128,512]{1,2,0:T(8,128)(4,1)S(1)} %broadcast_and_fusion, bf16[3,128,16,128]{1,3,2,0:T(8,128)(2,1)S(1)} %copy-done.6, bf16[3,128,16,128]{1,3,2,0:T(8,128)(2,1)} %copy.46, ...), kind=kOutput, calls=%fused_computation.55 | convolution fusion | flops 843055104 | bytes 22241280 | tf_op jit(solution)/shard_map/pqhk,pkhd->pqhd/dot_general | solution.py:77
  213.5 2.8 %copy.54 = f32[3,128,16,128]{3,2,1,0:T(8,128)S(1)} copy(f32[3,128,16,128]{1,3,2,0:T(8,128)} %fusion.51) | data formatting | bytes 6291456 | tf_op jit(solution)/shard_map/pqhk,pkhd->pqhd/transpose | solution.py:77
  216.3 4.1 %bitcast_reduce_fusion.1 = (f32[384,16]{0,1:T(8,128)S(1)}, f32[384,16,4]{0,2,1:T(4,128)S(1)}, f32[16,4,128,384]{3,2,1,0:T(8,128)S(1)}) fusion(bf16[384,16,128,1]{2,1,0,3:T(8,128)(2,1)} %bitcast.141, bf16[1,128,16,128]{3,1,0,2:T(8,128)(2,1)} %copy.63, bf16[1,128,16,128]{3,1,0,2:T(8,128)(2,1)} %copy.62, bf16[1,128,16,128]{3,1,0,2:T(8,128)(2,1)} %copy.61, ...), kind=kOutput, calls=%fused_computation.4 | convolution fusion | flops 817858560 | bytes 16375808 | tf_op jit(solution)/shard_map/qhd,lkhd->qhlk/dot_general | solution.py:102
  220.4 4.5 %copy-done.2 = f32[16,4,128,384]{3,2,1,0:T(8,128)} copy-done((f32[16,4,128,384]{3,2,1,0:T(8,128)}, f32[16,4,128,384]{3,2,1,0:T(8,128)S(1)}, u32[]{:S(2)}) %copy-start.2) | copy-done | bytes 12582936
  224.9 3.0 %fusion.4 = f32[384,16,4]{0,2,1:T(4,128)S(1)} fusion(f32[16,4,128,384]{3,2,1,0:T(8,128)S(1)} %get-tuple-element.19, f32[384,16,4]{0,2,1:T(4,128)S(1)} %get-tuple-element.6), kind=kLoop, calls=%fused_computation.10 | loop fusion | flops 9412608 | bytes 12779520 | tf_op jit(solution)/shard_map/reduce_sum | solution.py:107
  228.0 10.3 %fusion = f32[384,16,128]{0,2,1:T(8,128)} fusion(f32[384,16,4]{0,2,1:T(4,128)S(1)} %get-tuple-element.10, f32[16,4,128,384]{3,2,1,0:T(8,128)} %copy-done.2, f32[384,16,4]{0,2,1:T(4,128)S(1)} %get-tuple-element.6, bf16[1,128,16,128]{1,3,0,2:T(8,128)(2,1)} %bitcast.145, bf16[1,128,16,128]{1,3,0,2:T(8,128)(2,1)} %bitcast.146, ...), kind=kOutput, calls=%fused_computation.1 | convolution fusion | flops 823394304 | bytes 18022400 | tf_op jit(solution)/shard_map/qhlk,lkhd->qhld/dot_general | solution.py:108
  238.4 3.6 %copy.71 = f32[384,2048]{1,0:T(8,128)} copy(f32[384,2048]{0,1:T(8,128)} %bitcast.135) | data formatting | bytes 6291456 | tf_op jit(solution)/shard_map/reduce_sum | solution.py:118
  245.5 4.1 %fusion.32 = bf16[384,2048]{1,0:T(8,128)(2,1)} fusion(f32[48,8,16,128]{3,2,1,0:T(8,128)S(1)} %bitcast.125, f32[384,2048]{1,0:T(8,128)S(1)} %copy-done.1, f32[48,8,16,128]{3,2,1,0:T(8,128)S(1)} %bitcast.124, f32[48,8,16,128]{3,2,1,0:T(8,128)S(1)} %bitcast.123), kind=kLoop, calls=%fused_computation.37 | loop fusion | flops 3145728 | bytes 14155776 | tf_op jit(solution)/shard_map/convert_element_type | solution.py:120
  (73 shorter events, 39.2 us)
Async XLA Ops:
  0.0 4.4 %copy-start = (bf16[384,2048]{1,0:T(8,128)(2,1)S(1)}, bf16[384,2048]{1,0:T(8,128)(2,1)}, u32[]{:S(2)}) copy-start(bf16[384,2048]{1,0:T(8,128)(2,1)} %param.6) | copy-start | bytes 4718596
  0.0 73.8 %copy-start.3 = (bf16[384,2048]{1,0:T(8,128)(2,1)S(1)}, bf16[384,2048]{1,0:T(8,128)(2,1)}, u32[]{:S(2)}) copy-start(bf16[384,2048]{1,0:T(8,128)(2,1)} %param.7) | copy-start | bytes 4718596
  0.0 75.2 %copy-start.9 = (s32[16,4,1]{0,2,1:T(1,128)S(1)}, s32[16,4,1]{0,2,1:T(1,128)}, u32[]{:S(2)}) copy-start(s32[16,4,1]{0,2,1:T(1,128)} %param.9) | copy-start | bytes 772
  2.8 71.1 %collective-permute-start.5 = (bf16[384,2048]{0,1:T(8,128)(2,1)}, bf16[384,2048]{0,1:T(8,128)(2,1)S(1)}, u32[]{:S(2)}, u32[]{:S(2)}) collective-permute-start(bf16[384,2048]{0,1:T(8,128)(2,1)} %copy.56), channel_id=1, source_target_pairs={{0,8},{1,9},{2,10},{3,11},{4,12},{5,13},{6,14},{7,15},{8,0},{9,1},... | collective-permute-start | bytes 4718600 | tf_op jit(solution)/shard_map/ppermute | solution.py:20
  2.8 85.0 %collective-permute-start.4 = (bf16[384,2048]{0,1:T(8,128)(2,1)}, bf16[384,2048]{0,1:T(8,128)(2,1)}, u32[]{:S(2)}, u32[]{:S(2)}) collective-permute-start(bf16[384,2048]{0,1:T(8,128)(2,1)} %copy.56), channel_id=1, source_target_pairs={{0,4},{1,5},{2,6},{3,7},{4,0},{5,1},{6,2},{7,3},{8,12},{9,13},{10,... | collective-permute-start | bytes 4718600 | tf_op jit(solution)/shard_map/ppermute | solution.py:20
  3.0 85.5 %collective-permute-start.3 = (bf16[384,2048]{0,1:T(8,128)(2,1)}, bf16[384,2048]{0,1:T(8,128)(2,1)}, u32[]{:S(2)}, u32[]{:S(2)}) collective-permute-start(bf16[384,2048]{0,1:T(8,128)(2,1)} %copy.56), channel_id=1, source_target_pairs={{0,2},{1,3},{2,0},{3,1},{4,6},{5,7},{6,4},{7,5},{8,10},{9,11},{10,... | collective-permute-start | bytes 4718600 | tf_op jit(solution)/shard_map/ppermute | solution.py:20
  3.2 86.6 %collective-permute-start.2 = (bf16[384,2048]{0,1:T(8,128)(2,1)}, bf16[384,2048]{0,1:T(8,128)(2,1)}, u32[]{:S(2)}, u32[]{:S(2)}) collective-permute-start(bf16[384,2048]{0,1:T(8,128)(2,1)} %copy.56), channel_id=1, source_target_pairs={{0,1},{1,0},{2,3},{3,2},{4,5},{5,4},{6,7},{7,6},{8,9},{9,8},{10,11... | collective-permute-start | bytes 4718600 | tf_op jit(solution)/shard_map/ppermute | solution.py:20
  4.4 85.7 %collective-permute-start.1 = (bf16[384,2048]{1,0:T(8,128)(2,1)S(1)}, bf16[384,2048]{1,0:T(8,128)(2,1)}, u32[]{:S(2)}, u32[]{:S(2)}) collective-permute-start(bf16[384,2048]{1,0:T(8,128)(2,1)S(1)} %copy-done), channel_id=1, source_target_pairs={{0,1},{1,2},{2,3},{3,4},{4,5},{5,6},{6,7},{7,8},{8,9},{9,10},{10,1... | collective-permute-start | bytes 4718600 | tf_op jit(solution)/shard_map/ppermute | solution.py:14
  73.8 1.1 copy-start.8
  73.8 65.6 %collective-permute-start.7 = (bf16[384,2048]{1,0:T(8,128)(2,1)S(1)}, bf16[384,2048]{1,0:T(8,128)(2,1)}, u32[]{:S(2)}, u32[]{:S(2)}) collective-permute-start(bf16[384,2048]{1,0:T(8,128)(2,1)S(1)} %copy-done.3), channel_id=1, source_target_pairs={{0,2},{1,3},{2,0},{3,1},{4,6},{5,7},{6,4},{7,5},{8,10},{9,11},{10,... | collective-permute-start | bytes 4718600 | tf_op jit(solution)/shard_map/ppermute | solution.py:20
  85.8 2.6 %copy-start.10 = (s32[3]{0:T(128)S(1)}, s32[3]{0:T(128)}, u32[]{:S(2)}) copy-start(s32[3]{0:T(128)} %param.8) | copy-start | bytes 40
  87.8 55.6 %collective-permute-start.6 = (bf16[384,2048]{1,0:T(8,128)(2,1)S(1)}, bf16[384,2048]{1,0:T(8,128)(2,1)}, u32[]{:S(2)}, u32[]{:S(2)}) collective-permute-start(bf16[384,2048]{1,0:T(8,128)(2,1)S(1)} %copy-done.3), channel_id=1, source_target_pairs={{0,1},{1,0},{2,3},{3,2},{4,5},{5,4},{6,7},{7,6},{8,9},{9,8},{10,11... | collective-permute-start | bytes 4718600 | tf_op jit(solution)/shard_map/ppermute | solution.py:20
  88.4 58.9 %collective-permute-start = (bf16[384,2048]{1,0:T(8,128)(2,1)S(1)}, bf16[384,2048]{1,0:T(8,128)(2,1)}, u32[]{:S(2)}, u32[]{:S(2)}) collective-permute-start(bf16[384,2048]{1,0:T(8,128)(2,1)S(1)} %copy-done.3), channel_id=1, source_target_pairs={{0,1},{1,2},{2,3},{3,4},{4,5},{5,6},{6,7},{7,8},{8,9},{9,10},{10,1... | collective-permute-start | bytes 4718600 | tf_op jit(solution)/shard_map/ppermute | solution.py:14
  89.7 85.4 %collective-permute-start.9 = (bf16[384,2048]{1,0:T(8,128)(2,1)S(1)}, bf16[384,2048]{1,0:T(8,128)(2,1)}, u32[]{:S(2)}, u32[]{:S(2)}) collective-permute-start(bf16[384,2048]{1,0:T(8,128)(2,1)S(1)} %copy-done.3), channel_id=1, source_target_pairs={{0,8},{1,9},{2,10},{3,11},{4,12},{5,13},{6,14},{7,15},{8,0},{9,1},... | collective-permute-start | bytes 4718600 | tf_op jit(solution)/shard_map/ppermute | solution.py:20
  90.1 88.9 %collective-permute-start.8 = (bf16[384,2048]{1,0:T(8,128)(2,1)S(1)}, bf16[384,2048]{1,0:T(8,128)(2,1)}, u32[]{:S(2)}, u32[]{:S(2)}) collective-permute-start(bf16[384,2048]{1,0:T(8,128)(2,1)S(1)} %copy-done.3), channel_id=1, source_target_pairs={{0,4},{1,5},{2,6},{3,7},{4,0},{5,1},{6,2},{7,3},{8,12},{9,13},{10,... | collective-permute-start | bytes 4718600 | tf_op jit(solution)/shard_map/ppermute | solution.py:20
  197.5 1.6 copy-start.4
  203.7 3.2 %copy-start.5 = (bf16[3,128,16,128]{1,3,2,0:T(8,128)(2,1)S(1)}, bf16[3,128,16,128]{1,3,2,0:T(8,128)(2,1)}, u32[]{:S(2)}) copy-start(bf16[3,128,16,128]{1,3,2,0:T(8,128)(2,1)} %copy.44) | copy-start | bytes 4718596
  203.7 3.2 %copy-start.6 = (bf16[3,128,16,128]{1,3,2,0:T(8,128)(2,1)S(1)}, bf16[3,128,16,128]{1,3,2,0:T(8,128)(2,1)}, u32[]{:S(2)}) copy-start(bf16[3,128,16,128]{1,3,2,0:T(8,128)(2,1)} %copy.47) | copy-start | bytes 4718596
  203.7 3.2 %copy-start.7 = (bf16[3,128,16,128]{1,3,2,0:T(8,128)(2,1)S(1)}, bf16[3,128,16,128]{1,3,2,0:T(8,128)(2,1)}, u32[]{:S(2)}) copy-start(bf16[3,128,16,128]{1,3,2,0:T(8,128)(2,1)} %copy.45) | copy-start | bytes 4718596
  220.4 4.5 %copy-start.2 = (f32[16,4,128,384]{3,2,1,0:T(8,128)}, f32[16,4,128,384]{3,2,1,0:T(8,128)S(1)}, u32[]{:S(2)}) copy-start(f32[16,4,128,384]{3,2,1,0:T(8,128)S(1)} %get-tuple-element.19) | copy-start | bytes 37748740
  243.6 1.9 copy-start.1
where the time goes:
time: 251 us; the launch traced here: 250 us
  waiting for transfers between devices  118 us (47%)
  local copies, waits for them, and re-layouts  84 us (33%)
  matrix products  25.6 us (10%)
  other arithmetic  11.5 us (5%)
  starting transfers between devices  7.52 us (3%)
  between operations  2.88 us (1%)
    ppermute x8, waiting for transfers between devices, from_partner(): return lax.ppermute(value, axis, pairs)  118 us
    unnamed x36, local copies, waits for them, and re-layouts  26.6 us
    dynamic_slice x12, local copies, waits for them, and re-layouts, pick_blocks(): return lax.dynamic_slice_in_dim(source, block_index[0] * BLK, BLK, 0)  23.2 us
    reshape x8, local copies, waits for them, and re-layouts, window_stack(): extended[(WIN - 1 - offset) * BLK:(WIN - 1 - offset) * BLK + token_count]  15.9 us
    dot_general x1, matrix products, on_device(): jnp.einsum('qhlk,lkhd->qhld', far_weights.astype(jnp.bfloat16), all_value...  10.3 us
    another operation x4, local copies, waits for them, and re-layouts, on_device(): jnp.stack(key_list, axis=0).reshape(level_count, far_count, HEADS, head_dim)  8.19 us
    dot_general x1, matrix products, on_device(): jnp.einsum('pqhk,pkhd->pqhd', win_weights.astype(jnp.bfloat16), window_st...  6.53 us
  transfers between devices with their start and end apart: 10, of which 3 were waited for; matrix products, arithmetic and copies ran while one was open for 19% of the time, Pallas kernels for 0%

commit v1 on v0

--- a/solution.py
+++ b/solution.py
@@ -88,10 +88,10 @@
     value_list = [None] * level_count
     for level_bit in bit_order:
         partner = jnp.bitwise_xor(device, 1 << level_bit)
-        panel_keys, panel_values = from_partner((key_rows, value_rows), "outer", level_bit)
-        needed = columns[device, level_bit] - partner * panel_len
-        far_keys = pick_blocks(panel_keys, needed)
-        far_values = pick_blocks(panel_values, needed)
+        wanted = columns[partner, level_bit] - device * panel_len
+        far_keys, far_values = from_partner(
+            (pick_blocks(key_rows, wanted), pick_blocks(value_rows, wanted)), "outer", level_bit
+        )
         key_list[level_bit] = far_keys
         value_list[level_bit] = far_values
     far_count = key_list[0].shape[0]

time: 251 us -> 159 us (0.63)
  the two profiles are of different devices: /device:TPU:29 before, /device:TPU:24 now
where the time goes in v1:
time: 159 us; the launch traced here: 158 us
  local copies, waits for them, and re-layouts  73.6 us (46%)
  waiting for transfers between devices  35.8 us (23%)
  matrix products  25.9 us (16%)
  other arithmetic  12.2 us (8%)
  starting transfers between devices  7.89 us (5%)
  between operations  2.76 us (2%)
    unnamed x45, local copies, waits for them, and re-layouts  26.3 us
    ppermute x2, waiting for transfers between devices, passed_along(): return lax.ppermute(block, axis, route)  20.6 us
    reshape x8, local copies, waits for them, and re-layouts, window_stack(): extended[(WIN - 1 - offset) * BLK:(WIN - 1 - offset) * BLK + token_count]  15.9 us
    ppermute x8, waiting for transfers between devices, from_partner(): return lax.ppermute(value, axis, pairs)  15.2 us
    dot_general x1, matrix products, on_device(): jnp.einsum('qhlk,lkhd->qhld', far_weights.astype(jnp.bfloat16), all_value...  10.3 us
    ppermute x4, local copies, waits for them, and re-layouts, from_partner(): return lax.ppermute(value, axis, pairs)  8.26 us
    another operation x4, local copies, waits for them, and re-layouts, on_device(): jnp.stack(key_list, axis=0).reshape(level_count, far_count, HEADS, head_dim)  8.21 us
    dot_general x1, matrix products, on_device(): jnp.einsum('pqhk,pkhd->pqhd', win_weights.astype(jnp.bfloat16), window_st...  6.6 us
  transfers between devices with their start and end apart: 10, of which 6 were waited for; matrix products, arithmetic and copies ran while one was open for 29% of the time, Pallas kernels for 0%

profile of v1, /device:TPU:24, one launch (start us, length us, event | category | flops | bytes accessed | tf_op | source)
XLA Modules:
  0.0 158.1 jit_solution(4828913192360740436)
XLA Ops:
  4.0 3.0 %constant_dynamic-slice_fusion.3 = (bf16[128,2048]{1,0:T(8,128)(2,1)}, bf16[128,2048]{1,0:T(8,128)(2,1)}, bf16[128,2048]{1,0:T(8,128)(2,1)}, bf16[128,2048]{1,0:T(8,128)(2,1)}) fusion(bf16[384,2048]{1,0:T(8,128)(2,1)} %param.7, s32[]{:T(128)S(6)} %select_n.63, s32[]{:T(128)S(6)} %select_n.65, s32[]{:T(128)S(6)} %select_n.69, s32[]{:T(128)S(6)} %select_n.67), kind=kLoop, calls=%fused_computation.89 | loop fusion | bytes 4194320 | tf_op jit(solution)/shard_map/dynamic_slice | solution.py:36
  9.7 2.2 %copy.80 = bf16[128,2048]{0,1:T(8,128)(2,1)} copy(bf16[128,2048]{1,0:T(8,128)(2,1)} %get-tuple-element.21) | data formatting | bytes 1048576
  13.2 2.0 %copy.81 = bf16[128,2048]{0,1:T(8,128)(2,1)} copy(bf16[128,2048]{1,0:T(8,128)(2,1)} %get-tuple-element.20) | data formatting | bytes 1048576
  15.6 2.1 %copy.79 = bf16[128,2048]{0,1:T(8,128)(2,1)} copy(bf16[128,2048]{1,0:T(8,128)(2,1)} %get-tuple-element.19) | data formatting | bytes 1048576
  17.7 3.0 %copy.93 = bf16[48,8,16,128]{3,2,1,0:T(8,128)(2,1)} copy(bf16[48,8,16,128]{3,1,2,0:T(8,128)(2,1)} %bitcast.133) | data formatting | bytes 3145728
  22.2 2.8 %copy.44 = bf16[3,128,16,128]{1,3,2,0:T(8,128)(2,1)} copy(bf16[3,128,16,128]{3,2,1,0:T(8,128)(2,1)} %bitcast.128) | data formatting | bytes 3145728 | tf_op jit(solution)/shard_map/reshape | solution.py:54
  27.5 8.3 %collective-permute-done.5 = bf16[128,2048]{0,1:T(8,128)(2,1)} collective-permute-done((bf16[128,2048]{0,1:T(8,128)(2,1)}, bf16[128,2048]{0,1:T(8,128)(2,1)}, u32[]{:S(2)}, u32[]{:S(2)}) %collective-permute-start.5) | collective-permute-done | bytes 524320 | tf_op jit(solution)/shard_map/ppermute | solution.py:20
  36.9 4.7 %collective-permute-done.4 = bf16[128,2048]{0,1:T(8,128)(2,1)} collective-permute-done((bf16[128,2048]{0,1:T(8,128)(2,1)}, bf16[128,2048]{0,1:T(8,128)(2,1)}, u32[]{:S(2)}, u32[]{:S(2)}) %collective-permute-start.4) | collective-permute-done | bytes 524320 | tf_op jit(solution)/shard_map/ppermute | solution.py:20
  43.6 2.5 %collective-permute-start = (bf16[384,2048]{1,0:T(8,128)(2,1)S(1)}, bf16[384,2048]{1,0:T(8,128)(2,1)}, u32[]{:S(2)}, u32[]{:S(2)}) collective-permute-start(bf16[384,2048]{1,0:T(8,128)(2,1)S(1)} %copy-done), channel_id=1, source_target_pairs={{0,1},{1,2},{2,3},{3,4},{4,5},{5,6},{6,7},{7,8},{8,9},{9,10},{10,1... | collective-permute-start | bytes 4718600 | tf_op jit(solution)/shard_map/ppermute | solution.py:14
  46.4 2.1 %copy.63 = bf16[1,128,16,128]{3,1,0,2:T(8,128)(2,1)} copy(bf16[1,128,16,128]{1,3,2,0:T(8,128)(2,1)} %bitcast.14) | data formatting | bytes 1048576 | tf_op jit(solution)/shard_map/stack | solution.py:98
  48.4 2.1 %copy.61 = bf16[1,128,16,128]{3,1,0,2:T(8,128)(2,1)} copy(bf16[1,128,16,128]{1,3,2,0:T(8,128)(2,1)} %bitcast.8) | data formatting | bytes 1048576 | tf_op jit(solution)/shard_map/stack | solution.py:98
  50.5 2.1 %copy.62 = bf16[1,128,16,128]{3,1,0,2:T(8,128)(2,1)} copy(bf16[1,128,16,128]{1,3,2,0:T(8,128)(2,1)} %bitcast.11) | data formatting | bytes 1048576 | tf_op jit(solution)/shard_map/stack | solution.py:98
  52.5 2.0 %copy.60 = bf16[1,128,16,128]{3,1,0,2:T(8,128)(2,1)} copy(bf16[1,128,16,128]{1,3,2,0:T(8,128)(2,1)} %bitcast.5) | data formatting | bytes 1048576 | tf_op jit(solution)/shard_map/stack | solution.py:98
  54.6 2.1 %copy.66 = bf16[128,2048]{0,1:T(8,128)(2,1)} copy(bf16[128,2048]{1,0:T(8,128)(2,1)} %collective-permute-done.6) | data formatting | bytes 1048576 | tf_op jit(solution)/shard_map/ppermute | solution.py:20
  56.7 2.1 %copy.67 = bf16[128,2048]{0,1:T(8,128)(2,1)} copy(bf16[128,2048]{1,0:T(8,128)(2,1)} %collective-permute-done.7) | data formatting | bytes 1048576 | tf_op jit(solution)/shard_map/ppermute | solution.py:20
  59.7 2.1 %copy.69 = bf16[128,2048]{0,1:T(8,128)(2,1)} copy(bf16[128,2048]{1,0:T(8,128)(2,1)} %collective-permute-done.9) | data formatting | bytes 1048576 | tf_op jit(solution)/shard_map/ppermute | solution.py:20
  63.0 2.0 %copy.68 = bf16[128,2048]{0,1:T(8,128)(2,1)} copy(bf16[128,2048]{1,0:T(8,128)(2,1)} %collective-permute-done.8) | data formatting | bytes 1048576 | tf_op jit(solution)/shard_map/ppermute | solution.py:20
  65.0 4.7 %bitcast_reduce_fusion.1 = (f32[384,16]{0,1:T(8,128)}, f32[384,16,4]{0,2,1:T(4,128)S(1)}, f32[16,4,128,384]{3,2,1,0:T(8,128)S(1)}) fusion(bf16[384,16,128,1]{2,1,0,3:T(8,128)(2,1)} %bitcast.134, bf16[1,128,16,128]{3,1,0,2:T(8,128)(2,1)} %copy.63, bf16[1,128,16,128]{3,1,0,2:T(8,128)(2,1)} %copy.62, bf16[1,128,16,128]{3,1,0,2:T(8,128)(2,1)} %copy.61, ...), kind=kOutput, calls=%fused_computation.4 | convolution fusion | flops 817858560 | bytes 16375808 | tf_op jit(solution)/shard_map/qhd,lkhd->qhlk/dot_general | solution.py:102
  69.7 3.1 %fusion.4 = f32[384,16,4]{0,2,1:T(4,128)S(1)} fusion(f32[16,4,128,384]{3,2,1,0:T(8,128)S(1)} %get-tuple-element.27, f32[384,16,4]{0,2,1:T(4,128)S(1)} %get-tuple-element.6), kind=kLoop, calls=%fused_computation.10 | loop fusion | flops 9412608 | bytes 12779520 | tf_op jit(solution)/shard_map/reduce_sum | solution.py:107
  72.8 7.1 %collective-permute-done.1 = bf16[384,2048]{1,0:T(8,128)(2,1)} collective-permute-done((bf16[384,2048]{1,0:T(8,128)(2,1)S(1)}, bf16[384,2048]{1,0:T(8,128)(2,1)}, u32[]{:S(2)}, u32[]{:S(2)}) %collective-permute-start.1) | collective-permute-done | bytes 1572896 | tf_op jit(solution)/shard_map/ppermute | solution.py:14
  83.3 13.5 %collective-permute-done = bf16[384,2048]{1,0:T(8,128)(2,1)} collective-permute-done((bf16[384,2048]{1,0:T(8,128)(2,1)S(1)}, bf16[384,2048]{1,0:T(8,128)(2,1)}, u32[]{:S(2)}, u32[]{:S(2)}) %collective-permute-start) | collective-permute-done | bytes 1572896 | tf_op jit(solution)/shard_map/ppermute | solution.py:14
  96.8 3.0 %copy.88 = bf16[48,8,16,128]{3,2,1,0:T(8,128)(2,1)} copy(bf16[48,8,16,128]{3,1,2,0:T(8,128)(2,1)} %bitcast.36) | data formatting | bytes 3145728
  99.8 2.8 %copy.47 = bf16[3,128,16,128]{1,3,2,0:T(8,128)(2,1)} copy(bf16[3,128,16,128]{3,2,1,0:T(8,128)(2,1)} %bitcast.131) | data formatting | bytes 3145728 | tf_op jit(solution)/shard_map/reshape | solution.py:54
  106.5 2.0 %copy.45 = bf16[3,128,16,128]{1,3,2,0:T(8,128)(2,1)} copy(bf16[3,128,16,128]{3,2,1,0:T(8,128)(2,1)S(1)} %bitcast.124) | data formatting | bytes 3145728 | tf_op jit(solution)/shard_map/reshape | solution.py:54
  110.3 2.0 %copy.46 = bf16[3,128,16,128]{1,3,2,0:T(8,128)(2,1)} copy(bf16[3,128,16,128]{3,2,1,0:T(8,128)(2,1)S(1)} %bitcast.125) | data formatting | bytes 3145728 | tf_op jit(solution)/shard_map/reshape | solution.py:54
  119.1 4.3 %fusion.6 = (f32[3,128,16]{1,2,0:T(8,128)S(1)}, f32[3,16,512,128]{3,2,1,0:T(8,128)S(1)}) fusion(pred[3,128,512]{1,2,0:T(8,128)(4,1)S(1)} %broadcast_and_fusion, bf16[3,128,16,128]{3,2,1,0:T(8,128)(2,1)S(1)} %bitcast.135, bf16[3,128,16,128]{3,1,2,0:T(8,128)(2,1)} %copy.51, bf16[3,128,16,128]{3,1,2,0:T(8,128)(2,1)} %copy.50, ...), kind=kOutput, calls=%fused_computation.12 | convolution fusion | flops 839903232 | bytes 20668416 | tf_op jit(solution)/shard_map/pqhd,pkhd->pqhk/dot_general | solution.py:64
  123.4 3.7 %fusion.2 = f32[3,128,16]{1,2,0:T(8,128)} fusion(f32[3,16,512,128]{3,2,1,0:T(8,128)S(1)} %get-tuple-element.29, f32[3,128,16]{1,2,0:T(8,128)S(1)} %get-tuple-element.28, pred[3,128,512]{1,2,0:T(8,128)(4,1)S(1)} %broadcast_and_fusion), kind=kLoop, calls=%fused_computation.8 | loop fusion | flops 12576768 | bytes 12828672 | tf_op jit(solution)/shard_map/reduce_sum | solution.py:76
  127.1 6.6 %fusion.51 = f32[3,128,16,128]{1,3,2,0:T(8,128)} fusion(f32[3,16,512,128]{3,2,1,0:T(8,128)S(1)} %get-tuple-element.29, f32[3,128,16]{1,2,0:T(8,128)S(1)} %get-tuple-element.28, pred[3,128,512]{1,2,0:T(8,128)(4,1)S(1)} %broadcast_and_fusion, bf16[3,128,16,128]{1,3,2,0:T(8,128)(2,1)S(1)} %copy-done.7, bf16[3,128,16,128]{1,3,2,0:T(8,128)(2,1)} %copy.46, ...), kind=kOutput, calls=%fused_computation.55 | convolution fusion | flops 843055104 | bytes 22241280 | tf_op jit(solution)/shard_map/pqhk,pkhd->pqhd/dot_general | solution.py:77
  133.7 2.8 %copy.54 = f32[3,128,16,128]{3,2,1,0:T(8,128)S(1)} copy(f32[3,128,16,128]{1,3,2,0:T(8,128)} %fusion.51) | data formatting | bytes 6291456 | tf_op jit(solution)/shard_map/pqhk,pkhd->pqhd/transpose | solution.py:77
  136.7 10.3 %fusion = f32[384,16,128]{0,2,1:T(8,128)} fusion(f32[384,16,4]{0,2,1:T(4,128)S(1)} %get-tuple-element.10, f32[16,4,128,384]{3,2,1,0:T(8,128)} %copy-done.3, f32[384,16,4]{0,2,1:T(4,128)S(1)} %get-tuple-element.6, bf16[1,128,16,128]{1,3,0,2:T(8,128)(2,1)} %bitcast.138, bf16[1,128,16,128]{1,3,0,2:T(8,128)(2,1)} %bitcast.139, ...), kind=kOutput, calls=%fused_computation.1 | convolution fusion | flops 823394304 | bytes 18022400 | tf_op jit(solution)/shard_map/qhlk,lkhd->qhld/dot_general | solution.py:108
  147.0 3.5 %copy.71 = f32[384,2048]{1,0:T(8,128)} copy(f32[384,2048]{0,1:T(8,128)} %bitcast.132) | data formatting | bytes 6291456 | tf_op jit(solution)/shard_map/reduce_sum | solution.py:118
  154.1 4.1 %fusion.32 = bf16[384,2048]{1,0:T(8,128)(2,1)} fusion(f32[48,8,16,128]{3,2,1,0:T(8,128)S(1)} %bitcast.123, f32[384,2048]{1,0:T(8,128)S(1)} %copy-done.2, f32[48,8,16,128]{3,2,1,0:T(8,128)S(1)} %bitcast.122, f32[48,8,16,128]{3,2,1,0:T(8,128)S(1)} %bitcast.121), kind=kLoop, calls=%fused_computation.37 | loop fusion | flops 3145728 | bytes 14155776 | tf_op jit(solution)/shard_map/convert_element_type | solution.py:120
  (76 shorter events, 34.7 us)
Async XLA Ops:
  0.0 7.0 %copy-start.1 = (bf16[384,2048]{1,0:T(8,128)(2,1)S(1)}, bf16[384,2048]{1,0:T(8,128)(2,1)}, u32[]{:S(2)}) copy-start(bf16[384,2048]{1,0:T(8,128)(2,1)} %param.6) | copy-start | bytes 4718596
  7.0 20.2 %collective-permute-start.6 = (bf16[128,2048]{1,0:T(8,128)(2,1)}, bf16[128,2048]{1,0:T(8,128)(2,1)}, u32[]{:S(2)}, u32[]{:S(2)}) collective-permute-start(bf16[128,2048]{1,0:T(8,128)(2,1)} %get-tuple-element.15), channel_id=1, source_target_pairs={{0,1},{1,0},{2,3},{3,2},{4,5},{5,4},{6,7},{7,6},{8,9},{9,8},{10,11... | collective-permute-start | bytes 1572872 | tf_op jit(solution)/shard_map/ppermute | solution.py:20
  9.2 26.7 %collective-permute-start.5 = (bf16[128,2048]{0,1:T(8,128)(2,1)}, bf16[128,2048]{0,1:T(8,128)(2,1)}, u32[]{:S(2)}, u32[]{:S(2)}) collective-permute-start(bf16[128,2048]{0,1:T(8,128)(2,1)} %copy.82), channel_id=1, source_target_pairs={{0,8},{1,9},{2,10},{3,11},{4,12},{5,13},{6,14},{7,15},{8,0},{9,1},... | collective-permute-start | bytes 1572872 | tf_op jit(solution)/shard_map/ppermute | solution.py:20
  9.7 10.9 %copy-start = (bf16[384,2048]{1,0:T(8,128)(2,1)S(1)}, bf16[384,2048]{1,0:T(8,128)(2,1)}, u32[]{:S(2)}) copy-start(bf16[384,2048]{1,0:T(8,128)(2,1)} %param.7) | copy-start | bytes 4718596
  11.9 24.0 %collective-permute-start.3 = (bf16[128,2048]{0,1:T(8,128)(2,1)}, bf16[128,2048]{0,1:T(8,128)(2,1)}, u32[]{:S(2)}, u32[]{:S(2)}) collective-permute-start(bf16[128,2048]{0,1:T(8,128)(2,1)} %copy.80), channel_id=1, source_target_pairs={{0,2},{1,3},{2,0},{3,1},{4,6},{5,7},{6,4},{7,5},{8,10},{9,11},{10,... | collective-permute-start | bytes 1572872 | tf_op jit(solution)/shard_map/ppermute | solution.py:20
  15.3 26.3 %collective-permute-start.4 = (bf16[128,2048]{0,1:T(8,128)(2,1)}, bf16[128,2048]{0,1:T(8,128)(2,1)}, u32[]{:S(2)}, u32[]{:S(2)}) collective-permute-start(bf16[128,2048]{0,1:T(8,128)(2,1)} %copy.81), channel_id=1, source_target_pairs={{0,4},{1,5},{2,6},{3,7},{4,0},{5,1},{6,2},{7,3},{8,12},{9,13},{10,... | collective-permute-start | bytes 1572872 | tf_op jit(solution)/shard_map/ppermute | solution.py:20
  17.7 25.9 %collective-permute-start.2 = (bf16[128,2048]{0,1:T(8,128)(2,1)}, bf16[128,2048]{0,1:T(8,128)(2,1)}, u32[]{:S(2)}, u32[]{:S(2)}) collective-permute-start(bf16[128,2048]{0,1:T(8,128)(2,1)} %copy.79), channel_id=1, source_target_pairs={{0,1},{1,0},{2,3},{3,2},{4,5},{5,4},{6,7},{7,6},{8,9},{9,8},{10,11... | collective-permute-start | bytes 1572872 | tf_op jit(solution)/shard_map/ppermute | solution.py:20
  25.1 2.0 %copy-start.13 = (s32[3]{0:T(128)S(1)}, s32[3]{0:T(128)}, u32[]{:S(2)}) copy-start(s32[3]{0:T(128)} %param.8) | copy-start | bytes 40
  27.1 29.5 %collective-permute-start.7 = (bf16[128,2048]{1,0:T(8,128)(2,1)}, bf16[128,2048]{1,0:T(8,128)(2,1)}, u32[]{:S(2)}, u32[]{:S(2)}) collective-permute-start(bf16[128,2048]{1,0:T(8,128)(2,1)} %get-tuple-element.16), channel_id=1, source_target_pairs={{0,2},{1,3},{2,0},{3,1},{4,6},{5,7},{6,4},{7,5},{8,10},{9,11},{10,... | collective-permute-start | bytes 1572872 | tf_op jit(solution)/shard_map/ppermute | solution.py:20
  35.9 23.9 %collective-permute-start.9 = (bf16[128,2048]{1,0:T(8,128)(2,1)}, bf16[128,2048]{1,0:T(8,128)(2,1)}, u32[]{:S(2)}, u32[]{:S(2)}) collective-permute-start(bf16[128,2048]{1,0:T(8,128)(2,1)} %get-tuple-element.17), channel_id=1, source_target_pairs={{0,8},{1,9},{2,10},{3,11},{4,12},{5,13},{6,14},{7,15},{8,0},{9,1},... | collective-permute-start | bytes 1572872 | tf_op jit(solution)/shard_map/ppermute | solution.py:20
  35.9 27.1 %collective-permute-start.8 = (bf16[128,2048]{1,0:T(8,128)(2,1)}, bf16[128,2048]{1,0:T(8,128)(2,1)}, u32[]{:S(2)}, u32[]{:S(2)}) collective-permute-start(bf16[128,2048]{1,0:T(8,128)(2,1)} %get-tuple-element.18), channel_id=1, source_target_pairs={{0,4},{1,5},{2,6},{3,7},{4,0},{5,1},{6,2},{7,3},{8,12},{9,13},{10,... | collective-permute-start | bytes 1572872 | tf_op jit(solution)/shard_map/ppermute | solution.py:20
  41.6 38.3 %collective-permute-start.1 = (bf16[384,2048]{1,0:T(8,128)(2,1)S(1)}, bf16[384,2048]{1,0:T(8,128)(2,1)}, u32[]{:S(2)}, u32[]{:S(2)}) collective-permute-start(bf16[384,2048]{1,0:T(8,128)(2,1)S(1)} %copy-done.1), channel_id=1, source_target_pairs={{0,1},{1,2},{2,3},{3,4},{4,5},{5,6},{6,7},{7,8},{8,9},{9,10},{10,1... | collective-permute-start | bytes 4718600 | tf_op jit(solution)/shard_map/ppermute | solution.py:14
  43.6 53.2 %collective-permute-start = (bf16[384,2048]{1,0:T(8,128)(2,1)S(1)}, bf16[384,2048]{1,0:T(8,128)(2,1)}, u32[]{:S(2)}, u32[]{:S(2)}) collective-permute-start(bf16[384,2048]{1,0:T(8,128)(2,1)S(1)} %copy-done), channel_id=1, source_target_pairs={{0,1},{1,2},{2,3},{3,4},{4,5},{5,6},{6,7},{7,8},{8,9},{9,10},{10,1... | collective-permute-start | bytes 4718600 | tf_op jit(solution)/shard_map/ppermute | solution.py:14
  69.7 13.6 %copy-start.3 = (f32[16,4,128,384]{3,2,1,0:T(8,128)}, f32[16,4,128,384]{3,2,1,0:T(8,128)S(1)}, u32[]{:S(2)}) copy-start(f32[16,4,128,384]{3,2,1,0:T(8,128)S(1)} %get-tuple-element.27) | copy-start | bytes 37748740
  116.9 2.0 %copy-start.5 = (bf16[48,8,16,128]{3,2,1,0:T(8,128)(2,1)S(1)}, bf16[48,8,16,128]{3,2,1,0:T(8,128)(2,1)}, u32[]{:S(2)}) copy-start(bf16[48,8,16,128]{3,2,1,0:T(8,128)(2,1)} %copy.93) | copy-start | bytes 4718596
  116.9 2.1 %copy-start.6 = (bf16[3,128,16,128]{3,1,2,0:T(8,128)(2,1)S(1)}, bf16[3,128,16,128]{3,1,2,0:T(8,128)(2,1)}, u32[]{:S(2)}) copy-start(bf16[3,128,16,128]{3,1,2,0:T(8,128)(2,1)} %copy.48) | copy-start | bytes 4718596
  123.4 3.7 %copy-start.9 = (f32[3,128,16]{1,2,0:T(8,128)}, f32[3,128,16]{1,2,0:T(8,128)S(1)}, u32[]{:S(2)}) copy-start(f32[3,128,16]{1,2,0:T(8,128)S(1)} %get-tuple-element.28) | copy-start | bytes 73732
  123.4 3.7 %copy-start.4 = (bf16[3,128,16,128]{1,3,2,0:T(8,128)(2,1)S(1)}, bf16[3,128,16,128]{1,3,2,0:T(8,128)(2,1)}, u32[]{:S(2)}) copy-start(bf16[3,128,16,128]{1,3,2,0:T(8,128)(2,1)} %copy.44) | copy-start | bytes 4718596
  123.4 3.7 %copy-start.7 = (bf16[3,128,16,128]{1,3,2,0:T(8,128)(2,1)S(1)}, bf16[3,128,16,128]{1,3,2,0:T(8,128)(2,1)}, u32[]{:S(2)}) copy-start(bf16[3,128,16,128]{1,3,2,0:T(8,128)(2,1)} %copy.47) | copy-start | bytes 4718596
  123.4 3.7 %copy-start.8 = (bf16[3,128,16,128]{1,3,2,0:T(8,128)(2,1)S(1)}, bf16[3,128,16,128]{1,3,2,0:T(8,128)(2,1)}, u32[]{:S(2)}) copy-start(bf16[3,128,16,128]{1,3,2,0:T(8,128)(2,1)} %copy.45) | copy-start | bytes 4718596
  133.7 2.8 %copy-start.10 = (f32[3,128,16]{1,2,0:T(8,128)S(1)}, f32[3,128,16]{1,2,0:T(8,128)}, u32[]{:S(2)}) copy-start(f32[3,128,16]{1,2,0:T(8,128)} %copy-done.9) | copy-start | bytes 73732
  133.7 2.8 %copy-start.12 = (f32[384,16]{0,1:T(8,128)S(1)}, f32[384,16]{0,1:T(8,128)}, u32[]{:S(2)}) copy-start(f32[384,16]{0,1:T(8,128)} %get-tuple-element.5) | copy-start | bytes 73732
  147.0 3.6 %copy-start.11 = (f32[3,128,16]{1,2,0:T(8,128)S(1)}, f32[3,128,16]{1,2,0:T(8,128)}, u32[]{:S(2)}) copy-start(f32[3,128,16]{1,2,0:T(8,128)} %fusion.2) | copy-start | bytes 73732
  152.2 1.9 %copy-start.2 = (f32[384,2048]{1,0:T(8,128)S(1)}, f32[384,2048]{1,0:T(8,128)}, u32[]{:S(2)}) copy-start(f32[384,2048]{1,0:T(8,128)} %copy.71) | copy-start | bytes 9437188

commit v2 on v1

v2 whole, which is shorter than its diff:
```python
import functools

import jax
import jax.numpy as jnp
from jax import lax
from jax.experimental import pallas as pl
from jax.experimental.pallas import tpu as pltpu
from jax.sharding import PartitionSpec as P

HEADS = 16
BLK = 128
WIN = 4


def passed_along(block, axis, distance):
    devices = range(lax.axis_size(axis))
    route = [(i - distance, i) for i in devices if i - distance in devices]
    return lax.ppermute(block, axis, route)


def from_partner(value, axis, stride):
    mask = 2**stride
    pairs = [(source, source ^ mask) for source in range(lax.axis_size(axis))]
    return lax.ppermute(value, axis, pairs)


def pick_blocks(source, block_index):
    return lax.dynamic_slice_in_dim(source, block_index[0] * BLK, BLK, 0)


def _nt(a, b):
    return lax.dot_general(a, b, (((1,), (1,)), ((), ())), preferred_element_type=jnp.float32)


def _nn(a, b):
    return lax.dot_general(a, b, (((1,), (0,)), ((), ())), preferred_element_type=jnp.float32)


def attend_kernel(level_count, meta, q_ref, ok_ref, ov_ref, pk_ref, pv_ref, *rest):
    far_refs = rest[: 2 * level_count]
    out_ref = rest[2 * level_count]
    rows, head_dim = q_ref.shape
    panel_len = rows // BLK
    scale = head_dim ** (-0.5)
    q = q_ref[...]

    row = lax.broadcasted_iota(jnp.int32, (rows, rows), 0)
    col = lax.broadcasted_iota(jnp.int32, (rows, rows), 1)
    q_blk = row // BLK
    k_blk = col // BLK
    width = jnp.zeros((rows, rows), jnp.int32)
    for r in range(panel_len):
        width = jnp.where(q_blk == r, meta[r], width)
    first_block = meta[panel_len]

    own_off = q_blk - k_blk
    own_vis = (own_off >= 0) & (own_off < width) & ((own_off > 0) | (col <= row))
    prev_off = q_blk + panel_len - k_blk
    prev_vis = (prev_off < width) & (first_block + q_blk - prev_off >= 0)

    s_own = jnp.where(own_vis, _nt(q, ok_ref[...]) * scale, -jnp.inf)
    s_prev = jnp.where(prev_vis, _nt(q, pk_ref[...]) * scale, -jnp.inf)
    m_w = jnp.maximum(s_own.max(-1, keepdims=True), s_prev.max(-1, keepdims=True))
    e_own = jnp.exp(s_own - m_w)
    e_prev = jnp.exp(s_prev - m_w)
    l_w = e_own.sum(-1, keepdims=True) + e_prev.sum(-1, keepdims=True)
    o_w = _nn(e_own.astype(jnp.bfloat16), ov_ref[...]) + _nn(e_prev.astype(jnp.bfloat16), pv_ref[...])

    maxes, totals, sums = [m_w], [l_w], [o_w]
    for b in range(level_count):
        s = _nt(q, far_refs[2 * b][...]) * scale
        m = s.max(-1, keepdims=True)
        e = jnp.exp(s - m)
        maxes.append(m)
        totals.append(e.sum(-1, keepdims=True))
        sums.append(_nn(e.astype(jnp.bfloat16), far_refs[2 * b + 1][...]))

    top = maxes[0]
    for m in maxes[1:]:
        top = jnp.maximum(top, m)
    total = jnp.zeros_like(l_w)
    output = jnp.zeros_like(o_w)
    for m, l, o in zip(maxes, totals, sums):
        factor = jnp.exp(m - top)
        total = total + l * factor
        output = output + o * factor
    out_ref[...] = (output / total).astype(out_ref.dtype)


def attend(meta, queries, own_k, own_v, prev_k, prev_v, far):
    rows, features = queries.shape
    head_dim = features // HEADS
    level_count = len(far)
    far_rows = far[0].shape[0] // 2
    panel = pl.BlockSpec((rows, head_dim), lambda h, meta: (0, h))
    far_specs = []
    for _ in range(level_count):
        far_specs.append(pl.BlockSpec((far_rows, head_dim), lambda h, meta: (0, h)))
        far_specs.append(pl.BlockSpec((far_rows, head_dim), lambda h, meta: (1, h)))
    far_args = []
    for block in far:
        far_args += [block, block]
    keys = 2 * rows + level_count * far_rows
    flops = 4 * rows * keys * features
    return pl.pallas_call(
        functools.partial(attend_kernel, level_count),
        out_shape=jax.ShapeDtypeStruct((rows, features), queries.dtype),
        grid_spec=pltpu.PrefetchScalarGridSpec(
            num_scalar_prefetch=1,
            grid=(HEADS,),
            in_specs=[panel] * 5 + far_specs,
            out_specs=panel,
        ),
        compiler_params=pltpu.CompilerParams(dimension_semantics=("arbitrary",)),
        cost_estimate=pl.CostEstimate(
            flops=flops,
            transcendentals=rows * keys * HEADS,
            bytes_accessed=2 * features * (6 * rows + 2 * level_count * far_rows),
        ),
    )(meta, queries, own_k, own_v, prev_k, prev_v, *far_args)


def on_device(queries, key_rows, value_rows, widths, columns):
    token_count, features = queries.shape
    panel_len = token_count // BLK
    device = lax.axis_index("outer")
    level_count = lax.axis_size("outer").bit_length() - 1
    prev_keys, prev_values = passed_along((key_rows, value_rows), "outer", 1)
    far = []
    for level_bit in range(level_count):
        partner = jnp.bitwise_xor(device, 1 << level_bit)
        wanted = columns[partner, level_bit] - device * panel_len
        outgoing = jnp.concatenate([pick_blocks(key_rows, wanted), pick_blocks(value_rows, wanted)], axis=0)
        far.append(from_partner(outgoing, "outer", level_bit))
    meta = jnp.concatenate([widths, (device * panel_len)[None]]).astype(jnp.int32)
    return attend(meta, queries, key_rows, value_rows, prev_keys, prev_values, far)


def solution(mesh):
    placed = (
        P(("groups", "outer"), None),
        P(("groups", "outer"), None),
        P(("groups", "outer"), None),
        P(("groups", "outer")),
        P("groups", None, None),
    )
    return jax.shard_map(
        on_device,
        mesh=mesh,
        in_specs=placed,
        out_specs=P(("groups", "outer"), None),
        check_vma=False,
    )
```

time: 159 us -> 119 us (0.75)
  the two profiles are of different devices: /device:TPU:24 before, /device:TPU:29 now
where the time goes in v2:
time: 119 us
  waiting for transfers between devices  75.7 us (64%)
  Pallas kernels  26.3 us (22%)
  starting transfers between devices  6.83 us (6%)
  local copies, waits for them, and re-layouts  6.17 us (5%)
  between operations  2.71 us (2%)
    ppermute x4, waiting for transfers between devices, from_partner(): return lax.ppermute(value, axis, pairs)  75.7 us
    pallas_call x1, Pallas kernels, attend(): pl.pallas_call(functools.partial(attend_kernel, level_count), out_shape=j...  26.3 us
    ppermute x4, starting transfers between devices, from_partner(): return lax.ppermute(value, axis, pairs)  4.26 us
    unnamed x16, local copies, waits for them, and re-layouts  2.79 us
    ppermute x2, starting transfers between devices, passed_along(): return lax.ppermute(block, axis, route)  2.57 us
  transfers between devices with their start and end apart: 6, of which 2 were waited for; matrix products, arithmetic and copies ran while one was open for 1% of the time, Pallas kernels for 0%

profile of v2, /device:TPU:29, one launch (start us, length us, event | category | flops | bytes accessed | tf_op | source)
XLA Modules:
  0.0 118.7 jit_solution(5402763664058655770)
XLA Ops:
  0.0 1.4 %constant_dynamic-slice_fusion.2 = (s32[1,1,1]{0,2,1:T(1,128)}, s32[1,1,1]{0,2,1:T(1,128)}, s32[1,1,1]{0,2,1:T(1,128)}, s32[1,1,1]{0,2,1:T(1,128)}) fusion(s32[16,4,1]{0,2,1:T(1,128)} %param.9, s32[]{:T(128)S(6)} %select_n.34, s32[]{:T(128)S(6)} %select_n.30, s32[]{:T(128)S(6)} %select_n.28, s32[]{:T(128)S(6)} %select_n.32), kind=kLoop, calls=%fused_computation.6 | loop fusion | bytes 48 | tf_op jit(solution)/shard_map/dynamic_slice | solution.py:132
  4.0 0.0 copy-start
  4.0 1.9 %constant_dynamic-slice_fusion = (bf16[128,2048]{1,0:T(8,128)(2,1)S(1)}, bf16[128,2048]{1,0:T(8,128)(2,1)S(1)}, bf16[128,2048]{1,0:T(8,128)(2,1)S(1)}, bf16[128,2048]{1,0:T(8,128)(2,1)S(1)}) fusion(bf16[384,2048]{1,0:T(8,128)(2,1)} %ov_ref.1, s32[]{:T(128)S(6)} %select_n.35, s32[]{:T(128)S(6)} %select_n.33, s32[]{:T(128)S(6)} %select_n.31, s32[]{:T(128)S(6)} %select_n.29), kind=kLoop, calls=%fused_computation.4 | loop fusion | bytes 4194320 | tf_op jit(solution)/shard_map/dynamic_slice | solution.py:28
  5.9 0.1 copy-done
  6.0 0.1 constant_dynamic-slice_fusion.1
  6.1 0.0 copy-start.1
  6.1 0.1 pad_maximum_fusion
  6.3 0.7 collective-permute-start.2
  7.0 1.3 %collective-permute-start = (bf16[384,2048]{1,0:T(8,128)(2,1)S(1)}, bf16[384,2048]{1,0:T(8,128)(2,1)S(1)}, u32[]{:S(2)}, u32[]{:S(2)}) collective-permute-start(bf16[384,2048]{1,0:T(8,128)(2,1)S(1)} %copy-done), channel_id=1, source_target_pairs={{0,1},{1,2},{2,3},{3,4},{4,5},{5,6},{6,7},{7,8},{8,9},{9,10},{10,1... | collective-permute-start | bytes 4718600 | tf_op jit(solution)/shard_map/ppermute | solution.py:18
  8.3 0.0 copy-done.1
  8.3 1.3 %collective-permute-start.1 = (bf16[384,2048]{1,0:T(8,128)(2,1)S(1)}, bf16[384,2048]{1,0:T(8,128)(2,1)}, u32[]{:S(2)}, u32[]{:S(2)}) collective-permute-start(bf16[384,2048]{1,0:T(8,128)(2,1)S(1)} %copy-done.1), channel_id=1, source_target_pairs={{0,1},{1,2},{2,3},{3,4},{4,5},{5,6},{6,7},{7,8},{8,9},{9,10},{10,1... | collective-permute-start | bytes 4718600 | tf_op jit(solution)/shard_map/ppermute | solution.py:18
  9.6 0.1 pad_maximum_fusion.1
  9.7 3.2 %collective-permute-start.3 = (bf16[256,2048]{1,0:T(8,128)(2,1)S(1)}, bf16[256,2048]{1,0:T(8,128)(2,1)S(1)}, u32[]{:S(2)}, u32[]{:S(2)}) collective-permute-start(bf16[256,2048]{1,0:T(8,128)(2,1)S(1)} %pad_maximum_fusion.1), channel_id=1, source_target_pairs={{0,2},{1,3},{2,0},{3,1},{4,6},{5,7},{6,4},{7,5},{8,10},{9,11},{10,... | collective-permute-start | bytes 3145736 | tf_op jit(solution)/shard_map/ppermute | solution.py:24
  12.9 0.1 pad_maximum_fusion.2
  13.0 0.0 copy-start.7
  13.0 0.3 collective-permute-start.4
  13.2 0.1 pad_maximum_fusion.3
  13.3 0.0 collective-permute-done.2.rest_0_.rest_1_
  13.4 0.1 collective-permute-start.5
  13.5 0.2 copy-done.7
  13.6 0.6 pad_add_fusion.meta
  14.3 53.2 %collective-permute-done.3.rest_2_.rest_3_ = bf16[256,2048]{1,0:T(8,128)(2,1)S(1)} collective-permute-done((bf16[256,2048]{1,0:T(8,128)(2,1)S(1)}, bf16[256,2048]{1,0:T(8,128)(2,1)S(1)}, u32[]{:S(2)}, u32[]{:S(2)}) %collective-permute-start.3) | collective-permute-done | bytes 1048608 | tf_op jit(solution)/shard_map/ppermute | solution.py:24
  67.5 22.4 %collective-permute-done.4.rest_4_.rest_5_ = bf16[256,2048]{1,0:T(8,128)(2,1)S(1)} collective-permute-done((bf16[256,2048]{1,0:T(8,128)(2,1)S(1)}, bf16[256,2048]{1,0:T(8,128)(2,1)S(1)}, u32[]{:S(2)}, u32[]{:S(2)}) %collective-permute-start.4) | collective-permute-done | bytes 1048608 | tf_op jit(solution)/shard_map/ppermute | solution.py:24
  89.9 0.0 collective-permute-done.5.rest_6_.rest_7_
  90.0 0.0 collective-permute-done.pk_ref
  90.0 0.0 copy-done.2
  90.0 0.0 copy-done.3
  90.0 0.9 copy-done.4
  90.9 0.3 copy-done.5
  91.3 1.2 copy-done.6
  92.4 0.0 collective-permute-done.1.pv_ref
  92.5 26.3 %shard_map.55 = bf16[384,2048]{1,0:T(8,128)(2,1)} custom-call(s32[4]{0:T(128)} %pad_add_fusion.meta, bf16[384,2048]{1,0:T(8,128)(2,1)} %q_ref.1, bf16[384,2048]{1,0:T(8,128)(2,1)} %ok_ref.1, bf16[384,2048]{1,0:T(8,128)(2,1)} %ov_ref.1, bf16[384,2048]{1,0:T(8,128)(2,1)} %copy-done.6, bf16[384,2048]{1,0:T(8,128)(2,1)} %collective-permute-done.1.pv_ref, ...), custom_call_target="tpu_custom_call" | custom-call | flops 4026531840 | bytes 13631488 | tf_op jit(solution)/shard_map/pallas_call | solution.py:105
  (5 shorter events, 0.0 us)
Async XLA Ops:
  4.0 2.0 %copy-start = (bf16[384,2048]{1,0:T(8,128)(2,1)S(1)}, bf16[384,2048]{1,0:T(8,128)(2,1)}, u32[]{:S(2)}) copy-start(bf16[384,2048]{1,0:T(8,128)(2,1)} %ok_ref.1) | copy-start | bytes 4718596
  6.1 2.2 %copy-start.1 = (bf16[384,2048]{1,0:T(8,128)(2,1)S(1)}, bf16[384,2048]{1,0:T(8,128)(2,1)}, u32[]{:S(2)}) copy-start(bf16[384,2048]{1,0:T(8,128)(2,1)} %ov_ref.1) | copy-start | bytes 4718596
  6.3 7.1 %collective-permute-start.2 = (bf16[256,2048]{1,0:T(8,128)(2,1)S(1)}, bf16[256,2048]{1,0:T(8,128)(2,1)S(1)}, u32[]{:S(2)}, u32[]{:S(2)}) collective-permute-start(bf16[256,2048]{1,0:T(8,128)(2,1)S(1)} %pad_maximum_fusion), channel_id=1, source_target_pairs={{0,1},{1,0},{2,3},{3,2},{4,5},{5,4},{6,7},{7,6},{8,9},{9,8},{10,11... | collective-permute-start | bytes 3145736 | tf_op jit(solution)/shard_map/ppermute | solution.py:24
  7.0 83.0 %collective-permute-start = (bf16[384,2048]{1,0:T(8,128)(2,1)S(1)}, bf16[384,2048]{1,0:T(8,128)(2,1)S(1)}, u32[]{:S(2)}, u32[]{:S(2)}) collective-permute-start(bf16[384,2048]{1,0:T(8,128)(2,1)S(1)} %copy-done), channel_id=1, source_target_pairs={{0,1},{1,2},{2,3},{3,4},{4,5},{5,6},{6,7},{7,8},{8,9},{9,10},{10,1... | collective-permute-start | bytes 4718600 | tf_op jit(solution)/shard_map/ppermute | solution.py:18
  8.3 84.2 %collective-permute-start.1 = (bf16[384,2048]{1,0:T(8,128)(2,1)S(1)}, bf16[384,2048]{1,0:T(8,128)(2,1)}, u32[]{:S(2)}, u32[]{:S(2)}) collective-permute-start(bf16[384,2048]{1,0:T(8,128)(2,1)S(1)} %copy-done.1), channel_id=1, source_target_pairs={{0,1},{1,2},{2,3},{3,4},{4,5},{5,6},{6,7},{7,8},{8,9},{9,10},{10,1... | collective-permute-start | bytes 4718600 | tf_op jit(solution)/shard_map/ppermute | solution.py:18
  9.7 57.8 %collective-permute-start.3 = (bf16[256,2048]{1,0:T(8,128)(2,1)S(1)}, bf16[256,2048]{1,0:T(8,128)(2,1)S(1)}, u32[]{:S(2)}, u32[]{:S(2)}) collective-permute-start(bf16[256,2048]{1,0:T(8,128)(2,1)S(1)} %pad_maximum_fusion.1), channel_id=1, source_target_pairs={{0,2},{1,3},{2,0},{3,1},{4,6},{5,7},{6,4},{7,5},{8,10},{9,11},{10,... | collective-permute-start | bytes 3145736 | tf_op jit(solution)/shard_map/ppermute | solution.py:24
  13.0 0.7 copy-start.7
  13.0 76.9 %collective-permute-start.4 = (bf16[256,2048]{1,0:T(8,128)(2,1)S(1)}, bf16[256,2048]{1,0:T(8,128)(2,1)S(1)}, u32[]{:S(2)}, u32[]{:S(2)}) collective-permute-start(bf16[256,2048]{1,0:T(8,128)(2,1)S(1)} %pad_maximum_fusion.2), channel_id=1, source_target_pairs={{0,4},{1,5},{2,6},{3,7},{4,0},{5,1},{6,2},{7,3},{8,12},{9,13},{10,... | collective-permute-start | bytes 3145736 | tf_op jit(solution)/shard_map/ppermute | solution.py:24
  13.4 76.6 %copy-start.2 = (bf16[256,2048]{1,0:T(8,128)(2,1)}, bf16[256,2048]{1,0:T(8,128)(2,1)S(1)}, u32[]{:S(2)}) copy-start(bf16[256,2048]{1,0:T(8,128)(2,1)S(1)} %collective-permute-done.2.rest_0_.rest_1_) | copy-start | bytes 3145732
  13.4 76.6 %collective-permute-start.5 = (bf16[256,2048]{1,0:T(8,128)(2,1)S(1)}, bf16[256,2048]{1,0:T(8,128)(2,1)S(1)}, u32[]{:S(2)}, u32[]{:S(2)}) collective-permute-start(bf16[256,2048]{1,0:T(8,128)(2,1)S(1)} %pad_maximum_fusion.3), channel_id=1, source_target_pairs={{0,8},{1,9},{2,10},{3,11},{4,12},{5,13},{6,14},{7,15},{8,0},{9,1},... | collective-permute-start | bytes 3145736 | tf_op jit(solution)/shard_map/ppermute | solution.py:24
  67.5 22.5 %copy-start.3 = (bf16[256,2048]{1,0:T(8,128)(2,1)}, bf16[256,2048]{1,0:T(8,128)(2,1)S(1)}, u32[]{:S(2)}) copy-start(bf16[256,2048]{1,0:T(8,128)(2,1)S(1)} %collective-permute-done.3.rest_2_.rest_3_) | copy-start | bytes 3145732
  89.9 1.0 copy-start.4
  90.0 1.3 %copy-start.5 = (bf16[256,2048]{1,0:T(8,128)(2,1)}, bf16[256,2048]{1,0:T(8,128)(2,1)S(1)}, u32[]{:S(2)}) copy-start(bf16[256,2048]{1,0:T(8,128)(2,1)S(1)} %collective-permute-done.5.rest_6_.rest_7_) | copy-start | bytes 3145732
  91.3 1.2 copy-start.6

commit v3 on v2

--- a/solution.py
+++ b/solution.py
@@ -39,52 +39,57 @@
 def attend_kernel(level_count, meta, q_ref, ok_ref, ov_ref, pk_ref, pv_ref, *rest):
     far_refs = rest[: 2 * level_count]
     out_ref = rest[2 * level_count]
+    bias_ref = rest[2 * level_count + 1]
     rows, head_dim = q_ref.shape
     panel_len = rows // BLK
     scale = head_dim ** (-0.5)
-    q = q_ref[...]
+    span = WIN * BLK
 
-    row = lax.broadcasted_iota(jnp.int32, (rows, rows), 0)
-    col = lax.broadcasted_iota(jnp.int32, (rows, rows), 1)
-    q_blk = row // BLK
-    k_blk = col // BLK
-    width = jnp.zeros((rows, rows), jnp.int32)
+    @pl.when(pl.program_id(0) == 0)
+    def _():
+        query = lax.broadcasted_iota(jnp.int32, (BLK, span), 0)
+        column = lax.broadcasted_iota(jnp.int32, (BLK, span), 1)
+        first_block = meta[panel_len]
+        for r in range(panel_len):
+            width = meta[r]
+            split = (panel_len - r) * BLK
+            key_block = jnp.where(column < split, column // BLK + r - panel_len, (column - split) // BLK)
+            offset = r - key_block
+            visible = (offset < width) & (first_block + key_block >= 0) & ((offset > 0) | (column % BLK <= query))
+            bias_ref[r * BLK : (r + 1) * BLK, :] = jnp.where(visible, 0.0, -jnp.inf)
+
     for r in range(panel_len):
-        width = jnp.where(q_blk == r, meta[r], width)
-    first_block = meta[panel_len]
-
-    own_off = q_blk - k_blk
-    own_vis = (own_off >= 0) & (own_off < width) & ((own_off > 0) | (col <= row))
-    prev_off = q_blk + panel_len - k_blk
-    prev_vis = (prev_off < width) & (first_block + q_blk - prev_off >= 0)
-
-    s_own = jnp.where(own_vis, _nt(q, ok_ref[...]) * scale, -jnp.inf)
-    s_prev = jnp.where(prev_vis, _nt(q, pk_ref[...]) * scale, -jnp.inf)
-    m_w = jnp.maximum(s_own.max(-1, keepdims=True), s_prev.max(-1, keepdims=True))
-    e_own = jnp.exp(s_own - m_w)
-    e_prev = jnp.exp(s_prev - m_w)
-    l_w = e_own.sum(-1, keepdims=True) + e_prev.sum(-1, keepdims=True)
-    o_w = _nn(e_own.astype(jnp.bfloat16), ov_ref[...]) + _nn(e_prev.astype(jnp.bfloat16), pv_ref[...])
-
-    maxes, totals, sums = [m_w], [l_w], [o_w]
-    for b in range(level_count):
-        s = _nt(q, far_refs[2 * b][...]) * scale
-        m = s.max(-1, keepdims=True)
-        e = jnp.exp(s - m)
-        maxes.append(m)
-        totals.append(e.sum(-1, keepdims=True))
-        sums.append(_nn(e.astype(jnp.bfloat16), far_refs[2 * b + 1][...]))
-
-    top = maxes[0]
-    for m in maxes[1:]:
-        top = jnp.maximum(top, m)
-    total = jnp.zeros_like(l_w)
-    output = jnp.zeros_like(o_w)
-    for m, l, o in zip(maxes, totals, sums):
-        factor = jnp.exp(m - top)
-        total = total + l * factor
-        output = output + o * factor
-    out_ref[...] = (output / total).astype(out_ref.dtype)
+        rows_r = slice(r * BLK, (r + 1) * BLK)
+        split = (panel_len - r) * BLK
+        q = q_ref[rows_r, :]
+        bias = bias_ref[rows_r, :]
+        s_prev = _nt(q, pk_ref[r * BLK :, :]) * scale + bias[:, :split]
+        s_own = _nt(q, ok_ref[: (r + 1) * BLK, :]) * scale + bias[:, split:]
+        m_w = jnp.maximum(s_own.max(-1, keepdims=True), s_prev.max(-1, keepdims=True))
+        e_own = jnp.exp(s_own - m_w)
+        e_prev = jnp.exp(s_prev - m_w)
+        l_w = e_own.sum(-1, keepdims=True) + e_prev.sum(-1, keepdims=True)
+        o_w = _nn(e_own.astype(jnp.bfloat16), ov_ref[: (r + 1) * BLK, :]) + _nn(
+            e_prev.astype(jnp.bfloat16), pv_ref[r * BLK :, :]
+        )
+        maxes, totals, sums = [m_w], [l_w], [o_w]
+        for b in range(level_count):
+            s = _nt(q, far_refs[2 * b][...]) * scale
+            m = s.max(-1, keepdims=True)
+            e = jnp.exp(s - m)
+            maxes.append(m)
+            totals.append(e.sum(-1, keepdims=True))
+            sums.append(_nn(e.astype(jnp.bfloat16), far_refs[2 * b + 1][...]))
+        top = maxes[0]
+        for m in maxes[1:]:
+            top = jnp.maximum(top, m)
+        total = jnp.zeros_like(l_w)
+        output = jnp.zeros_like(o_w)
+        for m, l, o in zip(maxes, totals, sums):
+            factor = jnp.exp(m - top)
+            total = total + l * factor
+            output = output + o * factor
+        out_ref[rows_r, :] = (output / total).astype(out_ref.dtype)
 
 
 def attend(meta, queries, own_k, own_v, prev_k, prev_v, far):
@@ -100,7 +105,7 @@
     far_args = []
     for block in far:
         far_args += [block, block]
-    keys = 2 * rows + level_count * far_rows
+    keys = WIN * BLK + level_count * far_rows
     flops = 4 * rows * keys * features
     return pl.pallas_call(
         functools.partial(attend_kernel, level_count),
@@ -110,6 +115,7 @@
             grid=(HEADS,),
             in_specs=[panel] * 5 + far_specs,
             out_specs=panel,
+            scratch_shapes=[pltpu.VMEM((rows, WIN * BLK), jnp.float32)],
         ),
         compiler_params=pltpu.CompilerParams(dimension_semantics=("arbitrary",)),
         cost_estimate=pl.CostEstimate(

time: 119 us -> 151 us (1.27)
  Pallas kernels: 26.3 us -> 58.7 us
    pallas_call x1, Pallas kernels: 26.3 us -> 58.7 us  [attend(): pl.pallas_call(functools.partial(attend_kernel, level_count), out_shape=j...]
where the time goes in v3:
time: 151 us
  waiting for transfers between devices  75.7 us (50%)
  Pallas kernels  58.7 us (39%)
  starting transfers between devices  6.83 us (5%)
  local copies, waits for them, and re-layouts  6.17 us (4%)
  between operations  2.71 us (2%)
    ppermute x4, waiting for transfers between devices, from_partner(): return lax.ppermute(value, axis, pairs)  75.7 us
    pallas_call x1, Pallas kernels, attend(): pl.pallas_call(functools.partial(attend_kernel, level_count), out_shape=j...  58.7 us
    ppermute x4, starting transfers between devices, from_partner(): return lax.ppermute(value, axis, pairs)  4.26 us
  transfers between devices with their start and end apart: 6, of which 2 were waited for; matrix products, arithmetic and copies ran while one was open for 1% of the time, Pallas kernels for 0%

profile of v3, /device:TPU:29, one launch (start us, length us, event | category | flops | bytes accessed | tf_op | source)
XLA Modules:
  0.0 151.1 jit_solution(2502239482412630871)
XLA Ops:
  0.0 1.4 constant_dynamic-slice_fusion.2
  4.0 0.0 copy-start
  4.0 1.9 %constant_dynamic-slice_fusion = (bf16[128,2048]{1,0:T(8,128)(2,1)S(1)}, bf16[128,2048]{1,0:T(8,128)(2,1)S(1)}, bf16[128,2048]{1,0:T(8,128)(2,1)S(1)}, bf16[128,2048]{1,0:T(8,128)(2,1)S(1)}) fusion(bf16[384,2048]{1,0:T(8,128)(2,1)} %ov_ref.1, s32[]{:T(128)S(6)} %select_n.35, s32[]{:T(128)S(6)} %select_n.33, s32[]{:T(128)S(6)} %select_n.31, s32[]{:T(128)S(6)} %select_n.29), kind=kLoop, calls=%fused_computation.4 | loop fusion | bytes 4194320 | tf_op jit(solution)/shard_map/dynamic_slice | solution.py:28
  5.9 0.1 copy-done
  6.0 0.1 constant_dynamic-slice_fusion.1
  6.1 0.0 copy-start.1
  6.1 0.1 pad_maximum_fusion
  6.3 0.7 collective-permute-start.2
  7.0 1.3 collective-permute-start
  8.3 0.0 copy-done.1
  8.3 1.3 collective-permute-start.1
  9.6 0.1 pad_maximum_fusion.1
  9.7 3.2 %collective-permute-start.3 = (bf16[256,2048]{1,0:T(8,128)(2,1)S(1)}, bf16[256,2048]{1,0:T(8,128)(2,1)S(1)}, u32[]{:S(2)}, u32[]{:S(2)}) collective-permute-start(bf16[256,2048]{1,0:T(8,128)(2,1)S(1)} %pad_maximum_fusion.1), channel_id=1, source_target_pairs={{0,2},{1,3},{2,0},{3,1},{4,6},{5,7},{6,4},{7,5},{8,10},{9,11},{10,... | collective-permute-start | bytes 3145736 | tf_op jit(solution)/shard_map/ppermute | solution.py:24
  12.9 0.1 pad_maximum_fusion.2
  13.0 0.0 copy-start.7
  13.0 0.2 collective-permute-start.4
  13.2 0.1 pad_maximum_fusion.3
  13.3 0.0 collective-permute-done.2.rest_0_.rest_1_
  13.3 0.0 copy-start.2
  13.3 0.1 collective-permute-start.5
  13.5 0.2 copy-done.7
  13.6 0.6 pad_add_fusion.meta
  14.3 53.2 %collective-permute-done.3.rest_2_.rest_3_ = bf16[256,2048]{1,0:T(8,128)(2,1)S(1)} collective-permute-done((bf16[256,2048]{1,0:T(8,128)(2,1)S(1)}, bf16[256,2048]{1,0:T(8,128)(2,1)S(1)}, u32[]{:S(2)}, u32[]{:S(2)}) %collective-permute-start.3) | collective-permute-done | bytes 1048608 | tf_op jit(solution)/shard_map/ppermute | solution.py:24
  67.5 22.4 %collective-permute-done.4.rest_4_.rest_5_ = bf16[256,2048]{1,0:T(8,128)(2,1)S(1)} collective-permute-done((bf16[256,2048]{1,0:T(8,128)(2,1)S(1)}, bf16[256,2048]{1,0:T(8,128)(2,1)S(1)}, u32[]{:S(2)}, u32[]{:S(2)}) %collective-permute-start.4) | collective-permute-done | bytes 1048608 | tf_op jit(solution)/shard_map/ppermute | solution.py:24
  89.9 0.0 collective-permute-done.5.rest_6_.rest_7_
  90.0 0.0 collective-permute-done.pk_ref
  90.0 0.0 copy-done.3
  90.0 0.9 copy-done.4
  90.9 0.3 copy-done.5
  91.3 1.2 copy-done.6
  92.4 0.0 collective-permute-done.1.pv_ref
  92.5 58.7 %shard_map.55 = bf16[384,2048]{1,0:T(8,128)(2,1)} custom-call(s32[4]{0:T(128)} %pad_add_fusion.meta, bf16[384,2048]{1,0:T(8,128)(2,1)} %q_ref.1, bf16[384,2048]{1,0:T(8,128)(2,1)} %ok_ref.1, bf16[384,2048]{1,0:T(8,128)(2,1)} %ov_ref.1, bf16[384,2048]{1,0:T(8,128)(2,1)} %copy-done.6, bf16[384,2048]{1,0:T(8,128)(2,1)} %collective-permute-done.1.pv_ref, ...), custom_call_target="tpu_custom_call" | custom-call | flops 3221225472 | bytes 13631488 | tf_op jit(solution)/shard_map/pallas_call | solution.py:110
  (5 shorter events, 0.0 us)
Async XLA Ops:
  4.0 2.0 %copy-start = (bf16[384,2048]{1,0:T(8,128)(2,1)S(1)}, bf16[384,2048]{1,0:T(8,128)(2,1)}, u32[]{:S(2)}) copy-start(bf16[384,2048]{1,0:T(8,128)(2,1)} %ok_ref.1) | copy-start | bytes 4718596
  6.1 2.2 %copy-start.1 = (bf16[384,2048]{1,0:T(8,128)(2,1)S(1)}, bf16[384,2048]{1,0:T(8,128)(2,1)}, u32[]{:S(2)}) copy-start(bf16[384,2048]{1,0:T(8,128)(2,1)} %ov_ref.1) | copy-start | bytes 4718596
  6.3 7.1 %collective-permute-start.2 = (bf16[256,2048]{1,0:T(8,128)(2,1)S(1)}, bf16[256,2048]{1,0:T(8,128)(2,1)S(1)}, u32[]{:S(2)}, u32[]{:S(2)}) collective-permute-start(bf16[256,2048]{1,0:T(8,128)(2,1)S(1)} %pad_maximum_fusion), channel_id=1, source_target_pairs={{0,1},{1,0},{2,3},{3,2},{4,5},{5,4},{6,7},{7,6},{8,9},{9,8},{10,11... | collective-permute-start | bytes 3145736 | tf_op jit(solution)/shard_map/ppermute | solution.py:24
  7.0 83.0 %collective-permute-start = (bf16[384,2048]{1,0:T(8,128)(2,1)S(1)}, bf16[384,2048]{1,0:T(8,128)(2,1)S(1)}, u32[]{:S(2)}, u32[]{:S(2)}) collective-permute-start(bf16[384,2048]{1,0:T(8,128)(2,1)S(1)} %copy-done), channel_id=1, source_target_pairs={{0,1},{1,2},{2,3},{3,4},{4,5},{5,6},{6,7},{7,8},{8,9},{9,10},{10,1... | collective-permute-start | bytes 4718600 | tf_op jit(solution)/shard_map/ppermute | solution.py:18
  8.3 84.2 %collective-permute-start.1 = (bf16[384,2048]{1,0:T(8,128)(2,1)S(1)}, bf16[384,2048]{1,0:T(8,128)(2,1)}, u32[]{:S(2)}, u32[]{:S(2)}) collective-permute-start(bf16[384,2048]{1,0:T(8,128)(2,1)S(1)} %copy-done.1), channel_id=1, source_target_pairs={{0,1},{1,2},{2,3},{3,4},{4,5},{5,6},{6,7},{7,8},{8,9},{9,10},{10,1... | collective-permute-start | bytes 4718600 | tf_op jit(solution)/shard_map/ppermute | solution.py:18
  9.7 57.8 %collective-permute-start.3 = (bf16[256,2048]{1,0:T(8,128)(2,1)S(1)}, bf16[256,2048]{1,0:T(8,128)(2,1)S(1)}, u32[]{:S(2)}, u32[]{:S(2)}) collective-permute-start(bf16[256,2048]{1,0:T(8,128)(2,1)S(1)} %pad_maximum_fusion.1), channel_id=1, source_target_pairs={{0,2},{1,3},{2,0},{3,1},{4,6},{5,7},{6,4},{7,5},{8,10},{9,11},{10,... | collective-permute-start | bytes 3145736 | tf_op jit(solution)/shard_map/ppermute | solution.py:24
  13.0 0.7 copy-start.7
  13.0 76.9 %collective-permute-start.4 = (bf16[256,2048]{1,0:T(8,128)(2,1)S(1)}, bf16[256,2048]{1,0:T(8,128)(2,1)S(1)}, u32[]{:S(2)}, u32[]{:S(2)}) collective-permute-start(bf16[256,2048]{1,0:T(8,128)(2,1)S(1)} %pad_maximum_fusion.2), channel_id=1, source_target_pairs={{0,4},{1,5},{2,6},{3,7},{4,0},{5,1},{6,2},{7,3},{8,12},{9,13},{10,... | collective-permute-start | bytes 3145736 | tf_op jit(solution)/shard_map/ppermute | solution.py:24
  13.3 76.6 %copy-start.2 = (bf16[256,2048]{1,0:T(8,128)(2,1)}, bf16[256,2048]{1,0:T(8,128)(2,1)S(1)}, u32[]{:S(2)}) copy-start(bf16[256,2048]{1,0:T(8,128)(2,1)S(1)} %collective-permute-done.2.rest_0_.rest_1_) | copy-start | bytes 3145732
  13.3 76.6 %collective-permute-start.5 = (bf16[256,2048]{1,0:T(8,128)(2,1)S(1)}, bf16[256,2048]{1,0:T(8,128)(2,1)S(1)}, u32[]{:S(2)}, u32[]{:S(2)}) collective-permute-start(bf16[256,2048]{1,0:T(8,128)(2,1)S(1)} %pad_maximum_fusion.3), channel_id=1, source_target_pairs={{0,8},{1,9},{2,10},{3,11},{4,12},{5,13},{6,14},{7,15},{8,0},{9,1},... | collective-permute-start | bytes 3145736 | tf_op jit(solution)/shard_map/ppermute | solution.py:24
  67.5 22.5 %copy-start.3 = (bf16[256,2048]{1,0:T(8,128)(2,1)}, bf16[256,2048]{1,0:T(8,128)(2,1)S(1)}, u32[]{:S(2)}) copy-start(bf16[256,2048]{1,0:T(8,128)(2,1)S(1)} %collective-permute-done.3.rest_2_.rest_3_) | copy-start | bytes 3145732
  89.9 1.0 copy-start.4
  90.0 1.3 copy-start.5
  91.3 1.2 copy-start.6

commit v4 on v2

--- a/solution.py
+++ b/solution.py
@@ -39,27 +39,31 @@
 def attend_kernel(level_count, meta, q_ref, ok_ref, ov_ref, pk_ref, pv_ref, *rest):
     far_refs = rest[: 2 * level_count]
     out_ref = rest[2 * level_count]
+    bias_ref = rest[2 * level_count + 1]
     rows, head_dim = q_ref.shape
     panel_len = rows // BLK
     scale = head_dim ** (-0.5)
+
+    @pl.when(pl.program_id(0) == 0)
+    def _():
+        row = lax.broadcasted_iota(jnp.int32, (rows, rows), 0)
+        col = lax.broadcasted_iota(jnp.int32, (rows, rows), 1)
+        q_blk = row // BLK
+        k_blk = col // BLK
+        width = jnp.zeros((rows, rows), jnp.int32)
+        for r in range(panel_len):
+            width = jnp.where(q_blk == r, meta[r], width)
+        first_block = meta[panel_len]
+        own_off = q_blk - k_blk
+        own_vis = (own_off >= 0) & (own_off < width) & ((own_off > 0) | (col <= row))
+        prev_off = q_blk + panel_len - k_blk
+        prev_vis = (prev_off < width) & (first_block + q_blk - prev_off >= 0)
+        bias_ref[:, :rows] = jnp.where(prev_vis, 0.0, -jnp.inf)
+        bias_ref[:, rows:] = jnp.where(own_vis, 0.0, -jnp.inf)
+
     q = q_ref[...]
-
-    row = lax.broadcasted_iota(jnp.int32, (rows, rows), 0)
-    col = lax.broadcasted_iota(jnp.int32, (rows, rows), 1)
-    q_blk = row // BLK
-    k_blk = col // BLK
-    width = jnp.zeros((rows, rows), jnp.int32)
-    for r in range(panel_len):
-        width = jnp.where(q_blk == r, meta[r], width)
-    first_block = meta[panel_len]
-
-    own_off = q_blk - k_blk
-    own_vis = (own_off >= 0) & (own_off < width) & ((own_off > 0) | (col <= row))
-    prev_off = q_blk + panel_len - k_blk
-    prev_vis = (prev_off < width) & (first_block + q_blk - prev_off >= 0)
-
-    s_own = jnp.where(own_vis, _nt(q, ok_ref[...]) * scale, -jnp.inf)
-    s_prev = jnp.where(prev_vis, _nt(q, pk_ref[...]) * scale, -jnp.inf)
+    s_prev = _nt(q, pk_ref[...]) * scale + bias_ref[:, :rows]
+    s_own = _nt(q, ok_ref[...]) * scale + bias_ref[:, rows:]
     m_w = jnp.maximum(s_own.max(-1, keepdims=True), s_prev.max(-1, keepdims=True))
     e_own = jnp.exp(s_own - m_w)
     e_prev = jnp.exp(s_prev - m_w)
@@ -110,6 +114,7 @@
             grid=(HEADS,),
             in_specs=[panel] * 5 + far_specs,
             out_specs=panel,
+            scratch_shapes=[pltpu.VMEM((rows, 2 * rows), jnp.float32)],
         ),
         compiler_params=pltpu.CompilerParams(dimension_semantics=("arbitrary",)),
         cost_estimate=pl.CostEstimate(

time: 119 us -> 119 us (level)
  no operation moved by 1% of the time
where the time goes in v4:
time: 119 us; the launch traced here: 118 us
  waiting for transfers between devices  75.7 us (64%)
  Pallas kernels  25.8 us (22%)
  starting transfers between devices  6.83 us (6%)
  local copies, waits for them, and re-layouts  6.17 us (5%)
  between operations  2.71 us (2%)
    ppermute x4, waiting for transfers between devices, from_partner(): return lax.ppermute(value, axis, pairs)  75.7 us
    pallas_call x1, Pallas kernels, attend(): pl.pallas_call(functools.partial(attend_kernel, level_count), out_shape=j...  25.8 us
    ppermute x4, starting transfers between devices, from_partner(): return lax.ppermute(value, axis, pairs)  4.26 us
    unnamed x16, local copies, waits for them, and re-layouts  2.79 us
    ppermute x2, starting transfers between devices, passed_along(): return lax.ppermute(block, axis, route)  2.57 us
  transfers between devices with their start and end apart: 6, of which 2 were waited for; matrix products, arithmetic and copies ran while one was open for 1% of the time, Pallas kernels for 0%

profile of v4, /device:TPU:29, one launch (start us, length us, event | category | flops | bytes accessed | tf_op | source)
XLA Modules:
  0.0 118.3 jit_solution(1320779480890296128)
XLA Ops:
  0.0 1.4 %constant_dynamic-slice_fusion.2 = (s32[1,1,1]{0,2,1:T(1,128)}, s32[1,1,1]{0,2,1:T(1,128)}, s32[1,1,1]{0,2,1:T(1,128)}, s32[1,1,1]{0,2,1:T(1,128)}) fusion(s32[16,4,1]{0,2,1:T(1,128)} %param.9, s32[]{:T(128)S(6)} %select_n.34, s32[]{:T(128)S(6)} %select_n.30, s32[]{:T(128)S(6)} %select_n.28, s32[]{:T(128)S(6)} %select_n.32), kind=kLoop, calls=%fused_computation.6 | loop fusion | bytes 48 | tf_op jit(solution)/shard_map/dynamic_slice | solution.py:137
  4.0 0.0 copy-start
  4.0 1.9 %constant_dynamic-slice_fusion = (bf16[128,2048]{1,0:T(8,128)(2,1)S(1)}, bf16[128,2048]{1,0:T(8,128)(2,1)S(1)}, bf16[128,2048]{1,0:T(8,128)(2,1)S(1)}, bf16[128,2048]{1,0:T(8,128)(2,1)S(1)}) fusion(bf16[384,2048]{1,0:T(8,128)(2,1)} %ov_ref.1, s32[]{:T(128)S(6)} %select_n.35, s32[]{:T(128)S(6)} %select_n.33, s32[]{:T(128)S(6)} %select_n.31, s32[]{:T(128)S(6)} %select_n.29), kind=kLoop, calls=%fused_computation.4 | loop fusion | bytes 4194320 | tf_op jit(solution)/shard_map/dynamic_slice | solution.py:28
  5.9 0.1 copy-done
  6.0 0.1 constant_dynamic-slice_fusion.1
  6.1 0.0 copy-start.1
  6.1 0.1 pad_maximum_fusion
  6.3 0.7 collective-permute-start.2
  7.0 1.3 %collective-permute-start = (bf16[384,2048]{1,0:T(8,128)(2,1)S(1)}, bf16[384,2048]{1,0:T(8,128)(2,1)S(1)}, u32[]{:S(2)}, u32[]{:S(2)}) collective-permute-start(bf16[384,2048]{1,0:T(8,128)(2,1)S(1)} %copy-done), channel_id=1, source_target_pairs={{0,1},{1,2},{2,3},{3,4},{4,5},{5,6},{6,7},{7,8},{8,9},{9,10},{10,1... | collective-permute-start | bytes 4718600 | tf_op jit(solution)/shard_map/ppermute | solution.py:18
  8.3 1.3 %collective-permute-start.1 = (bf16[384,2048]{1,0:T(8,128)(2,1)S(1)}, bf16[384,2048]{1,0:T(8,128)(2,1)}, u32[]{:S(2)}, u32[]{:S(2)}) collective-permute-start(bf16[384,2048]{1,0:T(8,128)(2,1)S(1)} %copy-done.1), channel_id=1, source_target_pairs={{0,1},{1,2},{2,3},{3,4},{4,5},{5,6},{6,7},{7,8},{8,9},{9,10},{10,1... | collective-permute-start | bytes 4718600 | tf_op jit(solution)/shard_map/ppermute | solution.py:18
  9.6 0.1 pad_maximum_fusion.1
  9.7 3.2 %collective-permute-start.3 = (bf16[256,2048]{1,0:T(8,128)(2,1)S(1)}, bf16[256,2048]{1,0:T(8,128)(2,1)S(1)}, u32[]{:S(2)}, u32[]{:S(2)}) collective-permute-start(bf16[256,2048]{1,0:T(8,128)(2,1)S(1)} %pad_maximum_fusion.1), channel_id=1, source_target_pairs={{0,2},{1,3},{2,0},{3,1},{4,6},{5,7},{6,4},{7,5},{8,10},{9,11},{10,... | collective-permute-start | bytes 3145736 | tf_op jit(solution)/shard_map/ppermute | solution.py:24
  12.9 0.1 pad_maximum_fusion.2
  13.0 0.0 copy-start.7
  13.0 0.2 collective-permute-start.4
  13.2 0.1 pad_maximum_fusion.3
  13.3 0.0 collective-permute-done.2.rest_0_.rest_1_
  13.3 0.0 copy-start.2
  13.3 0.1 collective-permute-start.5
  13.5 0.2 copy-done.7
  13.6 0.6 pad_add_fusion.meta
  14.3 53.2 %collective-permute-done.3.rest_2_.rest_3_ = bf16[256,2048]{1,0:T(8,128)(2,1)S(1)} collective-permute-done((bf16[256,2048]{1,0:T(8,128)(2,1)S(1)}, bf16[256,2048]{1,0:T(8,128)(2,1)S(1)}, u32[]{:S(2)}, u32[]{:S(2)}) %collective-permute-start.3) | collective-permute-done | bytes 1048608 | tf_op jit(solution)/shard_map/ppermute | solution.py:24
  67.5 22.4 %collective-permute-done.4.rest_4_.rest_5_ = bf16[256,2048]{1,0:T(8,128)(2,1)S(1)} collective-permute-done((bf16[256,2048]{1,0:T(8,128)(2,1)S(1)}, bf16[256,2048]{1,0:T(8,128)(2,1)S(1)}, u32[]{:S(2)}, u32[]{:S(2)}) %collective-permute-start.4) | collective-permute-done | bytes 1048608 | tf_op jit(solution)/shard_map/ppermute | solution.py:24
  89.9 0.0 collective-permute-done.5.rest_6_.rest_7_
  90.0 0.0 collective-permute-done.pk_ref
  90.0 0.0 copy-done.2
  90.0 0.0 copy-done.3
  90.0 0.9 copy-done.4
  90.9 0.3 copy-done.5
  91.3 1.2 copy-done.6
  92.4 0.0 collective-permute-done.1.pv_ref
  92.5 25.8 %shard_map.55 = bf16[384,2048]{1,0:T(8,128)(2,1)} custom-call(s32[4]{0:T(128)} %pad_add_fusion.meta, bf16[384,2048]{1,0:T(8,128)(2,1)} %q_ref.1, bf16[384,2048]{1,0:T(8,128)(2,1)} %ok_ref.1, bf16[384,2048]{1,0:T(8,128)(2,1)} %ov_ref.1, bf16[384,2048]{1,0:T(8,128)(2,1)} %copy-done.6, bf16[384,2048]{1,0:T(8,128)(2,1)} %collective-permute-done.1.pv_ref, ...), custom_call_target="tpu_custom_call" | custom-call | flops 4026531840 | bytes 13631488 | tf_op jit(solution)/shard_map/pallas_call | solution.py:109
  (5 shorter events, 0.0 us)
Async XLA Ops:
  4.0 2.0 %copy-start = (bf16[384,2048]{1,0:T(8,128)(2,1)S(1)}, bf16[384,2048]{1,0:T(8,128)(2,1)}, u32[]{:S(2)}) copy-start(bf16[384,2048]{1,0:T(8,128)(2,1)} %ok_ref.1) | copy-start | bytes 4718596
  6.1 2.2 %copy-start.1 = (bf16[384,2048]{1,0:T(8,128)(2,1)S(1)}, bf16[384,2048]{1,0:T(8,128)(2,1)}, u32[]{:S(2)}) copy-start(bf16[384,2048]{1,0:T(8,128)(2,1)} %ov_ref.1) | copy-start | bytes 4718596
  6.3 7.1 %collective-permute-start.2 = (bf16[256,2048]{1,0:T(8,128)(2,1)S(1)}, bf16[256,2048]{1,0:T(8,128)(2,1)S(1)}, u32[]{:S(2)}, u32[]{:S(2)}) collective-permute-start(bf16[256,2048]{1,0:T(8,128)(2,1)S(1)} %pad_maximum_fusion), channel_id=1, source_target_pairs={{0,1},{1,0},{2,3},{3,2},{4,5},{5,4},{6,7},{7,6},{8,9},{9,8},{10,11... | collective-permute-start | bytes 3145736 | tf_op jit(solution)/shard_map/ppermute | solution.py:24
  7.0 83.0 %collective-permute-start = (bf16[384,2048]{1,0:T(8,128)(2,1)S(1)}, bf16[384,2048]{1,0:T(8,128)(2,1)S(1)}, u32[]{:S(2)}, u32[]{:S(2)}) collective-permute-start(bf16[384,2048]{1,0:T(8,128)(2,1)S(1)} %copy-done), channel_id=1, source_target_pairs={{0,1},{1,2},{2,3},{3,4},{4,5},{5,6},{6,7},{7,8},{8,9},{9,10},{10,1... | collective-permute-start | bytes 4718600 | tf_op jit(solution)/shard_map/ppermute | solution.py:18
  8.3 84.2 %collective-permute-start.1 = (bf16[384,2048]{1,0:T(8,128)(2,1)S(1)}, bf16[384,2048]{1,0:T(8,128)(2,1)}, u32[]{:S(2)}, u32[]{:S(2)}) collective-permute-start(bf16[384,2048]{1,0:T(8,128)(2,1)S(1)} %copy-done.1), channel_id=1, source_target_pairs={{0,1},{1,2},{2,3},{3,4},{4,5},{5,6},{6,7},{7,8},{8,9},{9,10},{10,1... | collective-permute-start | bytes 4718600 | tf_op jit(solution)/shard_map/ppermute | solution.py:18
  9.7 57.8 %collective-permute-start.3 = (bf16[256,2048]{1,0:T(8,128)(2,1)S(1)}, bf16[256,2048]{1,0:T(8,128)(2,1)S(1)}, u32[]{:S(2)}, u32[]{:S(2)}) collective-permute-start(bf16[256,2048]{1,0:T(8,128)(2,1)S(1)} %pad_maximum_fusion.1), channel_id=1, source_target_pairs={{0,2},{1,3},{2,0},{3,1},{4,6},{5,7},{6,4},{7,5},{8,10},{9,11},{10,... | collective-permute-start | bytes 3145736 | tf_op jit(solution)/shard_map/ppermute | solution.py:24
  13.0 0.7 copy-start.7
  13.0 76.9 %collective-permute-start.4 = (bf16[256,2048]{1,0:T(8,128)(2,1)S(1)}, bf16[256,2048]{1,0:T(8,128)(2,1)S(1)}, u32[]{:S(2)}, u32[]{:S(2)}) collective-permute-start(bf16[256,2048]{1,0:T(8,128)(2,1)S(1)} %pad_maximum_fusion.2), channel_id=1, source_target_pairs={{0,4},{1,5},{2,6},{3,7},{4,0},{5,1},{6,2},{7,3},{8,12},{9,13},{10,... | collective-permute-start | bytes 3145736 | tf_op jit(solution)/shard_map/ppermute | solution.py:24
  13.3 76.6 %copy-start.2 = (bf16[256,2048]{1,0:T(8,128)(2,1)}, bf16[256,2048]{1,0:T(8,128)(2,1)S(1)}, u32[]{:S(2)}) copy-start(bf16[256,2048]{1,0:T(8,128)(2,1)S(1)} %collective-permute-done.2.rest_0_.rest_1_) | copy-start | bytes 3145732
  13.3 76.6 %collective-permute-start.5 = (bf16[256,2048]{1,0:T(8,128)(2,1)S(1)}, bf16[256,2048]{1,0:T(8,128)(2,1)S(1)}, u32[]{:S(2)}, u32[]{:S(2)}) collective-permute-start(bf16[256,2048]{1,0:T(8,128)(2,1)S(1)} %pad_maximum_fusion.3), channel_id=1, source_target_pairs={{0,8},{1,9},{2,10},{3,11},{4,12},{5,13},{6,14},{7,15},{8,0},{9,1},... | collective-permute-start | bytes 3145736 | tf_op jit(solution)/shard_map/ppermute | solution.py:24
  67.5 22.5 %copy-start.3 = (bf16[256,2048]{1,0:T(8,128)(2,1)}, bf16[256,2048]{1,0:T(8,128)(2,1)S(1)}, u32[]{:S(2)}) copy-start(bf16[256,2048]{1,0:T(8,128)(2,1)S(1)} %collective-permute-done.3.rest_2_.rest_3_) | copy-start | bytes 3145732
  89.9 1.0 copy-start.4
  90.0 1.3 %copy-start.5 = (bf16[256,2048]{1,0:T(8,128)(2,1)}, bf16[256,2048]{1,0:T(8,128)(2,1)S(1)}, u32[]{:S(2)}) copy-start(bf16[256,2048]{1,0:T(8,128)(2,1)S(1)} %collective-permute-done.5.rest_6_.rest_7_) | copy-start | bytes 3145732
  91.3 1.2 copy-start.6

commit v5 on v4

--- a/solution.py
+++ b/solution.py
@@ -36,10 +36,35 @@
     return lax.dot_general(a, b, (((1,), (0,)), ((), ())), preferred_element_type=jnp.float32)
 
 
-def attend_kernel(level_count, meta, q_ref, ok_ref, ov_ref, pk_ref, pv_ref, *rest):
+def levels_kernel(level_count, q_ref, *rest):
     far_refs = rest[: 2 * level_count]
-    out_ref = rest[2 * level_count]
-    bias_ref = rest[2 * level_count + 1]
+    sum_ref, stat_ref = rest[2 * level_count :]
+    head_dim = q_ref.shape[1]
+    scale = head_dim ** (-0.5)
+    q = q_ref[...]
+    maxes, totals, sums = [], [], []
+    for b in range(level_count):
+        s = _nt(q, far_refs[2 * b][...]) * scale
+        m = s.max(-1, keepdims=True)
+        e = jnp.exp(s - m)
+        maxes.append(m)
+        totals.append(e.sum(-1, keepdims=True))
+        sums.append(_nn(e.astype(jnp.bfloat16), far_refs[2 * b + 1][...]))
+    top = maxes[0]
+    for m in maxes[1:]:
+        top = jnp.maximum(top, m)
+    total = jnp.zeros_like(totals[0])
+    output = jnp.zeros_like(sums[0])
+    for m, l, o in zip(maxes, totals, sums):
+        factor = jnp.exp(m - top)
+        total = total + l * factor
+        output = output + o * factor
+    sum_ref[...] = output
+    lane = lax.broadcasted_iota(jnp.int32, stat_ref.shape, 1)
+    stat_ref[...] = jnp.where(lane < head_dim // 2, top, total)
+
+
+def window_kernel(meta, q_ref, ok_ref, ov_ref, pk_ref, pv_ref, sum_ref, stat_ref, out_ref, bias_ref):
     rows, head_dim = q_ref.shape
     panel_len = rows // BLK
     scale = head_dim ** (-0.5)
@@ -70,59 +95,67 @@
     l_w = e_own.sum(-1, keepdims=True) + e_prev.sum(-1, keepdims=True)
     o_w = _nn(e_own.astype(jnp.bfloat16), ov_ref[...]) + _nn(e_prev.astype(jnp.bfloat16), pv_ref[...])
 
-    maxes, totals, sums = [m_w], [l_w], [o_w]
-    for b in range(level_count):
-        s = _nt(q, far_refs[2 * b][...]) * scale
-        m = s.max(-1, keepdims=True)
-        e = jnp.exp(s - m)
-        maxes.append(m)
-        totals.append(e.sum(-1, keepdims=True))
-        sums.append(_nn(e.astype(jnp.bfloat16), far_refs[2 * b + 1][...]))
-
-    top = maxes[0]
-    for m in maxes[1:]:
-        top = jnp.maximum(top, m)
-    total = jnp.zeros_like(l_w)
-    output = jnp.zeros_like(o_w)
-    for m, l, o in zip(maxes, totals, sums):
-        factor = jnp.exp(m - top)
-        total = total + l * factor
-        output = output + o * factor
+    m_f = stat_ref[:, :1]
+    l_f = stat_ref[:, head_dim // 2 : head_dim // 2 + 1]
+    top = jnp.maximum(m_w, m_f)
+    w_factor = jnp.exp(m_w - top)
+    f_factor = jnp.exp(m_f - top)
+    total = l_w * w_factor + l_f * f_factor
+    output = o_w * w_factor + sum_ref[...] * f_factor
     out_ref[...] = (output / total).astype(out_ref.dtype)
 
 
-def attend(meta, queries, own_k, own_v, prev_k, prev_v, far):
+def far_levels(queries, far):
     rows, features = queries.shape
     head_dim = features // HEADS
     level_count = len(far)
     far_rows = far[0].shape[0] // 2
+    panel = pl.BlockSpec((rows, head_dim), lambda h: (0, h))
+    far_specs, far_args = [], []
+    for block in far:
+        far_specs.append(pl.BlockSpec((far_rows, head_dim), lambda h: (0, h)))
+        far_specs.append(pl.BlockSpec((far_rows, head_dim), lambda h: (1, h)))
+        far_args += [block, block]
+    keys = level_count * far_rows
+    return pl.pallas_call(
+        functools.partial(levels_kernel, level_count),
+        out_shape=(
+            jax.ShapeDtypeStruct((rows, features), jnp.float32),
+            jax.ShapeDtypeStruct((rows, features), jnp.float32),
+        ),
+        grid=(HEADS,),
+        in_specs=[panel] + far_specs,
+        out_specs=(panel, panel),
+        compiler_params=pltpu.CompilerParams(dimension_semantics=("arbitrary",)),
+        cost_estimate=pl.CostEstimate(
+            flops=4 * rows * keys * features,
+            transcendentals=rows * keys * HEADS,
+            bytes_accessed=2 * features * (rows + 2 * keys) + 8 * rows * features,
+        ),
+    )(queries, *far_args)
+
+
+def window(meta, queries, own_k, own_v, prev_k, prev_v, far_sum, far_stat):
+    rows, features = queries.shape
+    head_dim = features // HEADS
     panel = pl.BlockSpec((rows, head_dim), lambda h, meta: (0, h))
-    far_specs = []
-    for _ in range(level_count):
-        far_specs.append(pl.BlockSpec((far_rows, head_dim), lambda h, meta: (0, h)))
-        far_specs.append(pl.BlockSpec((far_rows, head_dim), lambda h, meta: (1, h)))
-    far_args = []
-    for block in far:
-        far_args += [block, block]
-    keys = 2 * rows + level_count * far_rows
-    flops = 4 * rows * keys * features
     return pl.pallas_call(
-        functools.partial(attend_kernel, level_count),
+        window_kernel,
         out_shape=jax.ShapeDtypeStruct((rows, features), queries.dtype),
         grid_spec=pltpu.PrefetchScalarGridSpec(
             num_scalar_prefetch=1,
             grid=(HEADS,),
-            in_specs=[panel] * 5 + far_specs,
+            in_specs=[panel] * 7,
             out_specs=panel,
             scratch_shapes=[pltpu.VMEM((rows, 2 * rows), jnp.float32)],
         ),
         compiler_params=pltpu.CompilerParams(dimension_semantics=("arbitrary",)),
         cost_estimate=pl.CostEstimate(
-            flops=flops,
-            transcendentals=rows * keys * HEADS,
-            bytes_accessed=2 * features * (6 * rows + 2 * level_count * far_rows),
+            flops=8 * rows * rows * features,
+            transcendentals=2 * rows * rows * HEADS,
+            bytes_accessed=12 * rows * features + 8 * rows * features,
         ),
-    )(meta, queries, own_k, own_v, prev_k, prev_v, *far_args)
+    )(meta, queries, own_k, own_v, prev_k, prev_v, far_sum, far_stat)
 
 
 def on_device(queries, key_rows, value_rows, widths, columns):
@@ -130,15 +163,18 @@
     panel_len = token_count // BLK
     device = lax.axis_index("outer")
     level_count = lax.axis_size("outer").bit_length() - 1
-    prev_keys, prev_values = passed_along((key_rows, value_rows), "outer", 1)
     far = []
     for level_bit in range(level_count):
         partner = jnp.bitwise_xor(device, 1 << level_bit)
         wanted = columns[partner, level_bit] - device * panel_len
         outgoing = jnp.concatenate([pick_blocks(key_rows, wanted), pick_blocks(value_rows, wanted)], axis=0)
         far.append(from_partner(outgoing, "outer", level_bit))
+    gate = far[1 : min(3, level_count)]
+    rim_keys, rim_values, *_ = lax.optimization_barrier((key_rows, value_rows, *gate))
+    prev_keys, prev_values = passed_along((rim_keys, rim_values), "outer", 1)
+    far_sum, far_stat = far_levels(queries, far)
     meta = jnp.concatenate([widths, (device * panel_len)[None]]).astype(jnp.int32)
-    return attend(meta, queries, key_rows, value_rows, prev_keys, prev_values, far)
+    return window(meta, queries, key_rows, value_rows, prev_keys, prev_values, far_sum, far_stat)
 
 
 def solution(mesh):

time: 119 us -> 163 us (1.37)
  waiting for transfers between devices: 75.7 us -> 100 us
  Pallas kernels: 25.8 us -> 45 us
  local copies, waits for them, and re-layouts: 6.17 us -> 4.35 us
  starting transfers between devices: 6.83 us -> 8.47 us
    ppermute x4, waiting for transfers between devices: 75.7 us -> 100 us  [from_partner(): return lax.ppermute(value, axis, pairs)]
    pallas_call x1 -> x2, Pallas kernels: 25.8 us -> 45 us  [the longest x1 27.1 us: window(): pl.pallas_call(window_kernel, out_shape=jax.ShapeDtypeStruct((rows, featu...]
    unnamed x16 -> x10, local copies, waits for them, and re-layouts: 2.79 us -> 0.03 us
    ppermute x4, starting transfers between devices: 4.26 us -> 5.89 us  [from_partner(): return lax.ppermute(value, axis, pairs)]
  transfers between devices with their start and end apart: 6 -> 6, of which waited for: 2 -> 3; matrix products, arithmetic and copies ran while one was open for 1% -> 1% of each run, Pallas kernels for 0% -> 11%
where the time goes in v5:
time: 163 us; the launch traced here: 162 us
  waiting for transfers between devices  100 us (61%)
  Pallas kernels  45 us (28%)
  starting transfers between devices  8.47 us (5%)
  local copies, waits for them, and re-layouts  4.35 us (3%)
  between operations  2.7 us (2%)
    ppermute x4, waiting for transfers between devices, from_partner(): return lax.ppermute(value, axis, pairs)  100 us
    pallas_call x1, Pallas kernels, window(): pl.pallas_call(window_kernel, out_shape=jax.ShapeDtypeStruct((rows, featu...  27.1 us
    pallas_call x1, Pallas kernels, far_levels(): pl.pallas_call(functools.partial(levels_kernel, level_count), out_shape=(...  17.9 us
    ppermute x4, starting transfers between devices, from_partner(): return lax.ppermute(value, axis, pairs)  5.89 us
  transfers between devices with their start and end apart: 6, of which 3 were waited for; matrix products, arithmetic and copies ran while one was open for 1% of the time, Pallas kernels for 11%

profile of v5, /device:TPU:29, one launch (start us, length us, event | category | flops | bytes accessed | tf_op | source)
XLA Modules:
  0.0 161.7 jit_solution(15476204643931200187)
XLA Ops:
  0.0 1.4 constant_dynamic-slice_fusion.2
  3.9 3.0 %constant_dynamic-slice_fusion = (bf16[128,2048]{1,0:T(8,128)(2,1)S(1)}, bf16[128,2048]{1,0:T(8,128)(2,1)S(1)}, bf16[128,2048]{1,0:T(8,128)(2,1)S(1)}, bf16[128,...) fusion(bf16[384,2048]{1,0:T(8,128)(2,1)} %ov_ref.1, ...), kind=kLoop, calls=%fused_computation.4 | loop fusion | bytes 8388624 | tf_op jit(solution)/shard_map/dynamic_slice | solution.py:28
  6.9 0.0 copy-start
  6.9 0.0 copy-start.1
  6.9 0.1 pad_maximum_fusion.1
  7.0 0.1 collective-permute-start.1
  7.1 0.1 pad_maximum_fusion
  7.2 0.2 collective-permute-start
  7.4 23.9 %collective-permute-done.1.rest_4_.rest_5_ = bf16[256,2048]{1,0:T(8,128)(2,1)S(1)} collective-permute-done((bf16[256,2048]{1,0:T(8,128)(2,1)S(1)}, bf16[256,2048]{1,0:T(8,128)(2,1)S(1)}, u32[]{:S(2)}, u32[]{:S(2)}) %collective-permute-start.1) | collective-permute-done | bytes 1048608 | tf_op jit(solution)/shard_map/ppermute | solution.py:24
  31.4 0.0 copy-start.2
  31.4 0.0 collective-permute-done.rest_2_.rest_3_
  31.4 0.0 copy-done
  31.4 0.0 copy-start.3
  31.4 1.3 collective-permute-start.2
  32.7 0.0 copy-done.1
  32.7 1.3 collective-permute-start.3
  34.0 0.0 copy-done.3
  34.0 0.0 copy-start.4
  34.0 0.1 pad_maximum_fusion.2
  34.1 2.8 %collective-permute-start.4 = (bf16[256,2048]{1,0:T(8,128)(2,1)S(1)}, bf16[256,2048]{1,0:T(8,128)(2,1)}, u32[]{:S(2)}, u32[]{:S(2)}) collective-permute-start(bf16[256,2048]{1,0:T(8,128)(2,1)S(1)} %pad_maximum_fusion.2), channel_id=1, source_target_pairs={{0,1},{1,0},{2,3},{3,2},{4,5},{5,4},{6,7},{7,6},{8,9},{9,8},{10,11... | collective-permute-start | bytes 3145736 | tf_op jit(solution)/shard_map/ppermute | solution.py:24
  36.9 0.1 pad_maximum_fusion.3
  37.0 0.0 copy-done.2
  37.0 2.8 %collective-permute-start.5 = (bf16[256,2048]{1,0:T(8,128)(2,1)S(1)}, bf16[256,2048]{1,0:T(8,128)(2,1)}, u32[]{:S(2)}, u32[]{:S(2)}) collective-permute-start(bf16[256,2048]{1,0:T(8,128)(2,1)S(1)} %pad_maximum_fusion.3), channel_id=1, source_target_pairs={{0,8},{1,9},{2,10},{3,11},{4,12},{5,13},{6,14},{7,15},{8,0},{9,1},... | collective-permute-start | bytes 3145736 | tf_op jit(solution)/shard_map/ppermute | solution.py:24
  39.8 0.0 copy-done.4
  39.9 0.6 pad_add_fusion.meta
  40.4 1.1 collective-permute-done.4.rest_0_.rest_1_
  41.5 75.2 %collective-permute-done.5.rest_6_.rest_7_ = bf16[256,2048]{1,0:T(8,128)(2,1)} collective-permute-done((bf16[256,2048]{1,0:T(8,128)(2,1)S(1)}, bf16[256,2048]{1,0:T(8,128)(2,1)}, u32[]{:S(2)}, u32[]{:S(2)}) %collective-permute-start.5) | collective-permute-done | bytes 1048608 | tf_op jit(solution)/shard_map/ppermute | solution.py:24
  116.7 17.9 %shard_map.55 = (f32[384,2048]{1,0:T(8,128)}, f32[384,2048]{1,0:T(8,128)}) custom-call(bf16[384,2048]{1,0:T(8,128)(2,1)} %q_ref.3, bf16[256,2048]{1,0:T(8,128)(2,1)} %collective-permute-done.4.rest_0_.rest_1_, bf16[256,2048]{1,0:T(8,128)(2,1)} %collective-permute-done.4.rest_0_.rest_1_, bf16[256,2048]{1,0:T(8,128)(2,1)} %copy-done.3, ...), custom_call_target="tpu_custom_call" | custom-call | flops 1610612736 | bytes 12058624 | tf_op jit(solution)/shard_map/pallas_call | solution.py:120
  134.6 0.0 collective-permute-done.2.pk_ref
  134.6 0.0 collective-permute-done.3.pv_ref
  134.6 27.1 %shard_map.56 = bf16[384,2048]{1,0:T(8,128)(2,1)} custom-call(s32[4]{0:T(128)} %pad_add_fusion.meta, bf16[384,2048]{1,0:T(8,128)(2,1)} %q_ref.3, bf16[384,2048]{1,0:T(8,128)(2,1)} %ok_ref.1, bf16[384,2048]{1,0:T(8,128)(2,1)} %ov_ref.1, bf16[384,2048]{1,0:T(8,128)(2,1)} %collective-permute-done.2.pk_ref, bf16[384,2048]{1,0:T(8,128)(2,1)} %collective-permute-done.3.pv_ref, ...), custom_call_target="tpu_custom_call" | custom-call | flops 2415919104 | bytes 15728640 | tf_op jit(solution)/shard_map/pallas_call | solution.py:142
Async XLA Ops:
  6.9 24.5 %copy-start = (bf16[384,2048]{1,0:T(8,128)(2,1)S(1)}, bf16[384,2048]{1,0:T(8,128)(2,1)}, u32[]{:S(2)}) copy-start(bf16[384,2048]{1,0:T(8,128)(2,1)} %ok_ref.1) | copy-start | bytes 4718596
  6.9 25.8 %copy-start.1 = (bf16[384,2048]{1,0:T(8,128)(2,1)S(1)}, bf16[384,2048]{1,0:T(8,128)(2,1)}, u32[]{:S(2)}) copy-start(bf16[384,2048]{1,0:T(8,128)(2,1)} %ov_ref.1) | copy-start | bytes 4718596
  7.0 24.3 %collective-permute-start.1 = (bf16[256,2048]{1,0:T(8,128)(2,1)S(1)}, bf16[256,2048]{1,0:T(8,128)(2,1)S(1)}, u32[]{:S(2)}, u32[]{:S(2)}) collective-permute-start(bf16[256,2048]{1,0:T(8,128)(2,1)S(1)} %pad_maximum_fusion.1), channel_id=1, source_target_pairs={{0,4},{1,5},{2,6},{3,7},{4,0},{5,1},{6,2},{7,3},{8,12},{9,13},{10,... | collective-permute-start | bytes 3145736 | tf_op jit(solution)/shard_map/ppermute | solution.py:24
  7.2 24.2 %collective-permute-start = (bf16[256,2048]{1,0:T(8,128)(2,1)S(1)}, bf16[256,2048]{1,0:T(8,128)(2,1)S(1)}, u32[]{:S(2)}, u32[]{:S(2)}) collective-permute-start(bf16[256,2048]{1,0:T(8,128)(2,1)S(1)} %pad_maximum_fusion), channel_id=1, source_target_pairs={{0,2},{1,3},{2,0},{3,1},{4,6},{5,7},{6,4},{7,5},{8,10},{9,11},{10,... | collective-permute-start | bytes 3145736 | tf_op jit(solution)/shard_map/ppermute | solution.py:24
  31.4 5.7 %copy-start.2 = (bf16[256,2048]{1,0:T(8,128)(2,1)}, bf16[256,2048]{1,0:T(8,128)(2,1)S(1)}, u32[]{:S(2)}) copy-start(bf16[256,2048]{1,0:T(8,128)(2,1)S(1)} %collective-permute-done.1.rest_4_.rest_5_) | copy-start | bytes 3145732
  31.4 2.6 %copy-start.3 = (bf16[256,2048]{1,0:T(8,128)(2,1)}, bf16[256,2048]{1,0:T(8,128)(2,1)S(1)}, u32[]{:S(2)}) copy-start(bf16[256,2048]{1,0:T(8,128)(2,1)S(1)} %collective-permute-done.rest_2_.rest_3_) | copy-start | bytes 3145732
  31.4 103.2 %collective-permute-start.2 = (bf16[384,2048]{1,0:T(8,128)(2,1)S(1)}, bf16[384,2048]{1,0:T(8,128)(2,1)}, u32[]{:S(2)}, u32[]{:S(2)}) collective-permute-start(bf16[384,2048]{1,0:T(8,128)(2,1)S(1)} %copy-done), channel_id=1, source_target_pairs={{0,1},{1,2},{2,3},{3,4},{4,5},{5,6},{6,7},{7,8},{8,9},{9,10},{10,1... | collective-permute-start | bytes 4718600 | tf_op jit(solution)/shard_map/ppermute | solution.py:18
  32.7 101.9 %collective-permute-start.3 = (bf16[384,2048]{1,0:T(8,128)(2,1)S(1)}, bf16[384,2048]{1,0:T(8,128)(2,1)}, u32[]{:S(2)}, u32[]{:S(2)}) collective-permute-start(bf16[384,2048]{1,0:T(8,128)(2,1)S(1)} %copy-done.1), channel_id=1, source_target_pairs={{0,1},{1,2},{2,3},{3,4},{4,5},{5,6},{6,7},{7,8},{8,9},{9,10},{10,1... | collective-permute-start | bytes 4718600 | tf_op jit(solution)/shard_map/ppermute | solution.py:18
  34.0 5.8 %copy-start.4 = (s32[3]{0:T(128)S(1)}, s32[3]{0:T(128)}, u32[]{:S(2)}) copy-start(s32[3]{0:T(128)} %param.8) | copy-start | bytes 40
  34.1 7.4 %collective-permute-start.4 = (bf16[256,2048]{1,0:T(8,128)(2,1)S(1)}, bf16[256,2048]{1,0:T(8,128)(2,1)}, u32[]{:S(2)}, u32[]{:S(2)}) collective-permute-start(bf16[256,2048]{1,0:T(8,128)(2,1)S(1)} %pad_maximum_fusion.2), channel_id=1, source_target_pairs={{0,1},{1,0},{2,3},{3,2},{4,5},{5,4},{6,7},{7,6},{8,9},{9,8},{10,11... | collective-permute-start | bytes 3145736 | tf_op jit(solution)/shard_map/ppermute | solution.py:24
  37.0 79.7 %collective-permute-start.5 = (bf16[256,2048]{1,0:T(8,128)(2,1)S(1)}, bf16[256,2048]{1,0:T(8,128)(2,1)}, u32[]{:S(2)}, u32[]{:S(2)}) collective-permute-start(bf16[256,2048]{1,0:T(8,128)(2,1)S(1)} %pad_maximum_fusion.3), channel_id=1, source_target_pairs={{0,8},{1,9},{2,10},{3,11},{4,12},{5,13},{6,14},{7,15},{8,0},{9,1},... | collective-permute-start | bytes 3145736 | tf_op jit(solution)/shard_map/ppermute | solution.py:24

commit v6 on v4

--- a/solution.py
+++ b/solution.py
@@ -10,6 +10,7 @@
 HEADS = 16
 BLK = 128
 WIN = 4
+CHUNKS = 2
 
 
 def passed_along(block, axis, distance):
@@ -38,8 +39,7 @@
 
 def attend_kernel(level_count, meta, q_ref, ok_ref, ov_ref, pk_ref, pv_ref, *rest):
     far_refs = rest[: 2 * level_count]
-    out_ref = rest[2 * level_count]
-    bias_ref = rest[2 * level_count + 1]
+    out_ref, bias_ref = rest[-2:]
     rows, head_dim = q_ref.shape
     panel_len = rows // BLK
     scale = head_dim ** (-0.5)
@@ -91,12 +91,14 @@
     out_ref[...] = (output / total).astype(out_ref.dtype)
 
 
-def attend(meta, queries, own_k, own_v, prev_k, prev_v, far):
+def attend(meta, queries, own_k, own_v, prev_k, prev_v, far, first_head, prior=None):
     rows, features = queries.shape
     head_dim = features // HEADS
+    heads = prev_k.shape[1] // head_dim
     level_count = len(far)
     far_rows = far[0].shape[0] // 2
-    panel = pl.BlockSpec((rows, head_dim), lambda h, meta: (0, h))
+    whole = pl.BlockSpec((rows, head_dim), lambda h, meta: (0, h + first_head))
+    part = pl.BlockSpec((rows, head_dim), lambda h, meta: (0, h))
     far_specs = []
     for _ in range(level_count):
         far_specs.append(pl.BlockSpec((far_rows, head_dim), lambda h, meta: (0, h)))
@@ -105,24 +107,31 @@
     for block in far:
         far_args += [block, block]
     keys = 2 * rows + level_count * far_rows
-    flops = 4 * rows * keys * features
+    args = [meta, queries, own_k, own_v, prev_k, prev_v, *far_args]
+    in_specs = [whole] * 3 + [part] * 2 + far_specs
+    aliases = {}
+    if prior is not None:
+        aliases = {len(args): 0}
+        args.append(prior)
+        in_specs.append(pl.BlockSpec(memory_space=pl.ANY))
     return pl.pallas_call(
         functools.partial(attend_kernel, level_count),
         out_shape=jax.ShapeDtypeStruct((rows, features), queries.dtype),
         grid_spec=pltpu.PrefetchScalarGridSpec(
             num_scalar_prefetch=1,
-            grid=(HEADS,),
-            in_specs=[panel] * 5 + far_specs,
-            out_specs=panel,
+            grid=(heads,),
+            in_specs=in_specs,
+            out_specs=whole,
             scratch_shapes=[pltpu.VMEM((rows, 2 * rows), jnp.float32)],
         ),
+        input_output_aliases=aliases,
         compiler_params=pltpu.CompilerParams(dimension_semantics=("arbitrary",)),
         cost_estimate=pl.CostEstimate(
-            flops=flops,
-            transcendentals=rows * keys * HEADS,
-            bytes_accessed=2 * features * (6 * rows + 2 * level_count * far_rows),
+            flops=4 * rows * keys * head_dim * heads,
+            transcendentals=rows * keys * heads,
+            bytes_accessed=2 * head_dim * heads * (6 * rows + 2 * level_count * far_rows),
         ),
-    )(meta, queries, own_k, own_v, prev_k, prev_v, *far_args)
+    )(*args)
 
 
 def on_device(queries, key_rows, value_rows, widths, columns):
@@ -130,15 +139,24 @@
     panel_len = token_count // BLK
     device = lax.axis_index("outer")
     level_count = lax.axis_size("outer").bit_length() - 1
-    prev_keys, prev_values = passed_along((key_rows, value_rows), "outer", 1)
-    far = []
-    for level_bit in range(level_count):
-        partner = jnp.bitwise_xor(device, 1 << level_bit)
-        wanted = columns[partner, level_bit] - device * panel_len
-        outgoing = jnp.concatenate([pick_blocks(key_rows, wanted), pick_blocks(value_rows, wanted)], axis=0)
-        far.append(from_partner(outgoing, "outer", level_bit))
     meta = jnp.concatenate([widths, (device * panel_len)[None]]).astype(jnp.int32)
-    return attend(meta, queries, key_rows, value_rows, prev_keys, prev_values, far)
+    wanted = [columns[jnp.bitwise_xor(device, 1 << b), b] - device * panel_len for b in range(level_count)]
+    width = features // CHUNKS
+    context = None
+    for c in range(CHUNKS):
+        cols = slice(c * width, (c + 1) * width)
+        prev_keys, prev_values = passed_along((key_rows[:, cols], value_rows[:, cols]), "outer", 1)
+        far = []
+        for level_bit in range(level_count):
+            outgoing = jnp.concatenate(
+                [pick_blocks(key_rows, wanted[level_bit])[:, cols], pick_blocks(value_rows, wanted[level_bit])[:, cols]],
+                axis=0,
+            )
+            far.append(from_partner(outgoing, "outer", level_bit))
+        context = attend(
+            meta, queries, key_rows, value_rows, prev_keys, prev_values, far, c * (HEADS // CHUNKS), context
+        )
+    return context
 
 
 def solution(mesh):

time: 119 us -> 108 us (0.908)
  waiting for transfers between devices: 75.7 us -> 55.4 us
  starting transfers between devices: 6.83 us -> 11.8 us
  Pallas kernels: 25.8 us -> 28.6 us
  other arithmetic: 1.04 us -> 2.44 us
    ppermute x4 -> x8, waiting for transfers between devices: 75.7 us -> 55.4 us  [from_partner(): return lax.ppermute(value, axis, pairs)]
    slice x0 -> x4, local copies, waits for them, and re-layouts: none -> 4.22 us  [the longest x1 2.77 us: on_device(): key_rows[:, cols]]
    pallas_call x1 -> x2, Pallas kernels: 25.8 us -> 28.6 us  [attend(): pl.pallas_call(functools.partial(attend_kernel, level_count), out_shape=j...]
    dynamic_slice x3 -> x1, local copies, waits for them, and re-layouts: 3.38 us -> 0.68 us  [on_device(): columns[jnp.bitwise_xor(device, 1 << b), b] - device * panel_len]
    ppermute x2 -> x4, starting transfers between devices: 2.57 us -> 5.13 us  [passed_along(): return lax.ppermute(block, axis, route)]
    ppermute x4 -> x8, starting transfers between devices: 4.26 us -> 6.68 us  [from_partner(): return lax.ppermute(value, axis, pairs)]
    concatenate x4 -> x8, other arithmetic: 0.4 us -> 1.89 us  [on_device(): jnp.concatenate([pick_blocks(key_rows, wanted[level_bit])[:, cols], pick_...]
    unnamed x16 -> x26, local copies, waits for them, and re-layouts: 2.79 us -> 2 us
  transfers between devices with their start and end apart: 6 -> 12, of which waited for: 2 -> 5; matrix products, arithmetic and copies ran while one was open for 1% -> 4% of each run, Pallas kernels for 0% -> 13%
where the time goes in v6:
time: 108 us
  waiting for transfers between devices  55.4 us (51%)
  Pallas kernels  28.6 us (26%)
  starting transfers between devices  11.8 us (11%)
  local copies, waits for them, and re-layouts  6.91 us (6%)
  between operations  2.7 us (2%)
  other arithmetic  2.44 us (2%)
    ppermute x8, waiting for transfers between devices, from_partner(): return lax.ppermute(value, axis, pairs)  55.4 us
    pallas_call x2, Pallas kernels, attend(): pl.pallas_call(functools.partial(attend_kernel, level_count), out_shape=j...  28.6 us
    ppermute x8, starting transfers between devices, from_partner(): return lax.ppermute(value, axis, pairs)  6.68 us
    ppermute x4, starting transfers between devices, passed_along(): return lax.ppermute(block, axis, route)  5.13 us
    slice x1, local copies, waits for them, and re-layouts, on_device(): key_rows[:, cols]  2.77 us
  transfers between devices with their start and end apart: 12, of which 5 were waited for; matrix products, arithmetic and copies ran while one was open for 4% of the time, Pallas kernels for 13%

profile of v6, /device:TPU:29, one launch (start us, length us, event | category | flops | bytes accessed | tf_op | source)
XLA Modules:
  0.0 107.9 jit_solution(2287967597138094765)
XLA Ops:
  0.0 2.8 %fusion.1 = (bf16[384,1024]{1,0:T(8,128)(2,1)}, bf16[384,1024]{1,0:T(8,128)(2,1)}) fusion(bf16[384,2048]{1,0:T(8,128)(2,1)} %ok_ref.3), kind=kLoop, calls=%fused_computation.22 | loop fusion | bytes 3145728 | tf_op jit(solution)/shard_map/slice | solution.py:148
  2.8 1.3 %collective-permute-start.6 = (bf16[384,1024]{1,0:T(8,128)(2,1)}, bf16[384,1024]{1,0:T(8,128)(2,1)}, u32[]{:S(2)}, u32[]{:S(2)}) collective-permute-start(bf16[384,1024]{1,0:T(8,128)(2,1)} %get-tuple-element.23), channel_id=1, source_target_pairs={{0,1},{1,2},{2,3},{3,4},{4,5},{5,6},{6,7},{7,8},{8,9},{9,10},{10,1... | collective-permute-start | bytes 2359304 | tf_op jit(solution)/shard_map/ppermute | solution.py:19
  4.1 0.7 constant_dynamic-slice_fusion.2
  7.3 0.0 copy-start.1
  7.3 0.2 constant_dynamic-slice_fusion.1
  7.5 1.2 %copy-done.1 = bf16[384,2048]{1,0:T(8,128)(2,1)S(1)} copy-done((bf16[384,2048]{1,0:T(8,128)(2,1)S(1)}, bf16[384,2048]{1,0:T(8,128)(2,1)}, u32[]{:S(2)}) %copy-start.1) | copy-done | bytes 1572888
  8.7 0.2 constant_dynamic-slice_fusion
  9.0 1.4 %collective-permute-start.8 = (bf16[256,1024]{1,0:T(8,128)(2,1)S(1)}, bf16[256,1024]{1,0:T(8,128)(2,1)S(1)}, u32[]{:S(2)}, u32[]{:S(2)}) collective-permute-start(bf16[256,1024]{1,0:T(8,128)(2,1)S(1)} %pad_maximum_fusion.4), channel_id=1, source_target_pairs={{0,1},{1,0},{2,3},{3,2},{4,5},{5,4},{6,7},{7,6},{8,9},{9,8},{10,11... | collective-permute-start | bytes 1572872 | tf_op jit(solution)/shard_map/ppermute | solution.py:25
  10.4 1.4 %collective-permute-start.9 = (bf16[256,1024]{1,0:T(8,128)(2,1)S(1)}, bf16[256,1024]{1,0:T(8,128)(2,1)S(1)}, u32[]{:S(2)}, u32[]{:S(2)}) collective-permute-start(bf16[256,1024]{1,0:T(8,128)(2,1)S(1)} %pad_maximum_fusion.5), channel_id=1, source_target_pairs={{0,2},{1,3},{2,0},{3,1},{4,6},{5,7},{6,4},{7,5},{8,10},{9,11},{10,... | collective-permute-start | bytes 1572872 | tf_op jit(solution)/shard_map/ppermute | solution.py:25
  11.8 0.2 collective-permute-start.10
  12.1 1.1 %collective-permute-start.2 = (bf16[256,1024]{1,0:T(8,128)(2,1)S(1)}, bf16[256,1024]{1,0:T(8,128)(2,1)S(1)}, u32[]{:S(2)}, u32[]{:S(2)}) collective-permute-start(bf16[256,1024]{1,0:T(8,128)(2,1)S(1)} %pad_maximum_fusion), channel_id=1, source_target_pairs={{0,1},{1,0},{2,3},{3,2},{4,5},{5,4},{6,7},{7,6},{8,9},{9,8},{10,11... | collective-permute-start | bytes 1572872 | tf_op jit(solution)/shard_map/ppermute | solution.py:25
  13.2 1.0 fusion
  14.3 1.3 %collective-permute-start.7 = (bf16[384,1024]{1,0:T(8,128)(2,1)S(1)}, bf16[384,1024]{1,0:T(8,128)(2,1)S(1)}, u32[]{:S(2)}, u32[]{:S(2)}) collective-permute-start(bf16[384,1024]{1,0:T(8,128)(2,1)S(1)} %get-tuple-element.21), channel_id=1, source_target_pairs={{0,1},{1,2},{2,3},{3,4},{4,5},{5,6},{6,7},{7,8},{8,9},{9,10},{10,1... | collective-permute-start | bytes 2359304 | tf_op jit(solution)/shard_map/ppermute | solution.py:19
  15.6 11.9 %collective-permute-done.9.rest_2_.rest_3_ = bf16[256,1024]{1,0:T(8,128)(2,1)S(1)} collective-permute-done((bf16[256,1024]{1,0:T(8,128)(2,1)S(1)}, bf16[256,1024]{1,0:T(8,128)(2,1)S(1)}, u32[]{:S(2)}, u32[]{:S(2)}) %collective-permute-start.9) | collective-permute-done | bytes 524320 | tf_op jit(solution)/shard_map/ppermute | solution.py:25
  27.5 0.1 collective-permute-start.11
  27.6 1.3 %collective-permute-start = (bf16[384,1024]{1,0:T(8,128)(2,1)}, bf16[384,1024]{1,0:T(8,128)(2,1)}, u32[]{:S(2)}, u32[]{:S(2)}) collective-permute-start(bf16[384,1024]{1,0:T(8,128)(2,1)} %get-tuple-element.24), channel_id=1, source_target_pairs={{0,1},{1,2},{2,3},{3,4},{4,5},{5,6},{6,7},{7,8},{8,9},{9,10},{10,1... | collective-permute-start | bytes 2359304 | tf_op jit(solution)/shard_map/ppermute | solution.py:19
  28.9 0.0 collective-permute-done.2.rest_0_.rest_1_
  28.9 1.3 %collective-permute-start.1 = (bf16[384,1024]{1,0:T(8,128)(2,1)}, bf16[384,1024]{1,0:T(8,128)(2,1)}, u32[]{:S(2)}, u32[]{:S(2)}) collective-permute-start(bf16[384,1024]{1,0:T(8,128)(2,1)} %get-tuple-element.22), channel_id=1, source_target_pairs={{0,1},{1,2},{2,3},{3,4},{4,5},{5,6},{6,7},{7,8},{8,9},{9,10},{10,1... | collective-permute-start | bytes 2359304 | tf_op jit(solution)/shard_map/ppermute | solution.py:19
  30.2 0.0 copy-start.12
  30.2 0.8 pad_maximum_fusion.2
  31.1 0.8 pad_maximum_fusion.1
  31.9 21.7 %collective-permute-done.11.rest_6_.rest_7_ = bf16[256,1024]{1,0:T(8,128)(2,1)S(1)} collective-permute-done((bf16[256,1024]{1,0:T(8,128)(2,1)S(1)}, bf16[256,1024]{1,0:T(8,128)(2,1)S(1)}, u32[]{:S(2)}, u32[]{:S(2)}) %collective-permute-start.11) | collective-permute-done | bytes 524320 | tf_op jit(solution)/shard_map/ppermute | solution.py:25
  53.6 0.5 collective-permute-start.3
  54.1 0.0 collective-permute-done.6.pk_ref
  54.1 2.0 %collective-permute-start.5 = (bf16[256,1024]{1,0:T(8,128)(2,1)S(1)}, bf16[256,1024]{1,0:T(8,128)(2,1)S(1)}, u32[]{:S(2)}, u32[]{:S(2)}) collective-permute-start(bf16[256,1024]{1,0:T(8,128)(2,1)S(1)} %pad_maximum_fusion.3), channel_id=1, source_target_pairs={{0,8},{1,9},{2,10},{3,11},{4,12},{5,13},{6,14},{7,15},{8,0},{9,1},... | collective-permute-start | bytes 1572872 | tf_op jit(solution)/shard_map/ppermute | solution.py:25
  56.1 0.6 pad_add_fusion.meta
  56.7 14.2 %shard_map.55.rest_8_ = bf16[384,2048]{1,0:T(8,128)(2,1)} custom-call(s32[4]{0:T(128)} %pad_add_fusion.meta, bf16[384,2048]{1,0:T(8,128)(2,1)} %q_ref.3, bf16[384,2048]{1,0:T(8,128)(2,1)} %ok_ref.3, bf16[384,2048]{1,0:T(8,128)(2,1)} %ov_ref.3, bf16[384,1024]{1,0:T(8,128)(2,1)} %collective-permute-done.6.pk_ref, bf16[384,1024]{1,0:T(8,128)(2,1)} %copy-done.10, ...), custom_call_target="tpu_custom_call" | custom-call | flops 2013265920 | bytes 6815744 | tf_op jit(solution)/shard_map/pallas_call | solution.py:117
  70.9 3.2 %collective-permute-done.3.rest_2_.rest_3_ = bf16[256,1024]{1,0:T(8,128)(2,1)S(1)} collective-permute-done((bf16[256,1024]{1,0:T(8,128)(2,1)}, bf16[256,1024]{1,0:T(8,128)(2,1)S(1)}, u32[]{:S(2)}, u32[]{:S(2)}) %collective-permute-start.3) | collective-permute-done | bytes 524320 | tf_op jit(solution)/shard_map/ppermute | solution.py:25
  74.1 6.8 %collective-permute-done.4.rest_4_.rest_5_ = bf16[256,1024]{1,0:T(8,128)(2,1)S(1)} collective-permute-done((bf16[256,1024]{1,0:T(8,128)(2,1)}, bf16[256,1024]{1,0:T(8,128)(2,1)S(1)}, u32[]{:S(2)}, u32[]{:S(2)}) %collective-permute-start.4) | collective-permute-done | bytes 524320 | tf_op jit(solution)/shard_map/ppermute | solution.py:25
  80.9 11.8 %collective-permute-done.5.rest_6_.rest_7_ = bf16[256,1024]{1,0:T(8,128)(2,1)S(1)} collective-permute-done((bf16[256,1024]{1,0:T(8,128)(2,1)S(1)}, bf16[256,1024]{1,0:T(8,128)(2,1)S(1)}, u32[]{:S(2)}, u32[]{:S(2)}) %collective-permute-start.5) | collective-permute-done | bytes 524320 | tf_op jit(solution)/shard_map/ppermute | solution.py:25
  92.8 0.8 copy-done.9
  93.5 14.3 %shard_map.56 = bf16[384,2048]{1,0:T(8,128)(2,1)} custom-call(s32[4]{0:T(128)} %pad_add_fusion.meta, bf16[384,2048]{1,0:T(8,128)(2,1)} %q_ref.3, bf16[384,2048]{1,0:T(8,128)(2,1)} %ok_ref.3, bf16[384,2048]{1,0:T(8,128)(2,1)} %ov_ref.3, bf16[384,1024]{1,0:T(8,128)(2,1)} %collective-permute-done.pk_ref, ...), custom_call_target="tpu_custom_call", output_to_operand_aliasing={{}: (14, {})} | custom-call | flops 2013265920 | bytes 6815744 | tf_op jit(solution)/shard_map/pallas_call | solution.py:117
  (34 shorter events, 0.3 us)
Async XLA Ops:
  0.0 7.3 %copy-start = (bf16[384,2048]{1,0:T(8,128)(2,1)S(1)}, bf16[384,2048]{1,0:T(8,128)(2,1)}, u32[]{:S(2)}) copy-start(bf16[384,2048]{1,0:T(8,128)(2,1)} %ok_ref.3) | copy-start | bytes 4718596
  0.0 4.1 %copy-start.11 = (s32[16,4,1]{0,2,1:T(1,128)S(1)}, s32[16,4,1]{0,2,1:T(1,128)}, u32[]{:S(2)}) copy-start(s32[16,4,1]{0,2,1:T(1,128)} %param.9) | copy-start | bytes 772
  2.8 51.3 %collective-permute-start.6 = (bf16[384,1024]{1,0:T(8,128)(2,1)}, bf16[384,1024]{1,0:T(8,128)(2,1)}, u32[]{:S(2)}, u32[]{:S(2)}) collective-permute-start(bf16[384,1024]{1,0:T(8,128)(2,1)} %get-tuple-element.23), channel_id=1, source_target_pairs={{0,1},{1,2},{2,3},{3,4},{4,5},{5,6},{6,7},{7,8},{8,9},{9,10},{10,1... | collective-permute-start | bytes 2359304 | tf_op jit(solution)/shard_map/ppermute | solution.py:19
  7.3 1.4 %copy-start.1 = (bf16[384,2048]{1,0:T(8,128)(2,1)S(1)}, bf16[384,2048]{1,0:T(8,128)(2,1)}, u32[]{:S(2)}) copy-start(bf16[384,2048]{1,0:T(8,128)(2,1)} %ov_ref.3) | copy-start | bytes 4718596
  9.0 5.3 %collective-permute-start.8 = (bf16[256,1024]{1,0:T(8,128)(2,1)S(1)}, bf16[256,1024]{1,0:T(8,128)(2,1)S(1)}, u32[]{:S(2)}, u32[]{:S(2)}) collective-permute-start(bf16[256,1024]{1,0:T(8,128)(2,1)S(1)} %pad_maximum_fusion.4), channel_id=1, source_target_pairs={{0,1},{1,0},{2,3},{3,2},{4,5},{5,4},{6,7},{7,6},{8,9},{9,8},{10,11... | collective-permute-start | bytes 1572872 | tf_op jit(solution)/shard_map/ppermute | solution.py:25
  10.4 17.1 %collective-permute-start.9 = (bf16[256,1024]{1,0:T(8,128)(2,1)S(1)}, bf16[256,1024]{1,0:T(8,128)(2,1)S(1)}, u32[]{:S(2)}, u32[]{:S(2)}) collective-permute-start(bf16[256,1024]{1,0:T(8,128)(2,1)S(1)} %pad_maximum_fusion.5), channel_id=1, source_target_pairs={{0,2},{1,3},{2,0},{3,1},{4,6},{5,7},{6,4},{7,5},{8,10},{9,11},{10,... | collective-permute-start | bytes 1572872 | tf_op jit(solution)/shard_map/ppermute | solution.py:25
  11.8 15.7 %collective-permute-start.10 = (bf16[256,1024]{1,0:T(8,128)(2,1)S(1)}, bf16[256,1024]{1,0:T(8,128)(2,1)S(1)}, u32[]{:S(2)}, u32[]{:S(2)}) collective-permute-start(bf16[256,1024]{1,0:T(8,128)(2,1)S(1)} %pad_maximum_fusion.6), channel_id=1, source_target_pairs={{0,4},{1,5},{2,6},{3,7},{4,0},{5,1},{6,2},{7,3},{8,12},{9,13},{10,... | collective-permute-start | bytes 1572872 | tf_op jit(solution)/shard_map/ppermute | solution.py:25
  12.1 16.8 %collective-permute-start.2 = (bf16[256,1024]{1,0:T(8,128)(2,1)S(1)}, bf16[256,1024]{1,0:T(8,128)(2,1)S(1)}, u32[]{:S(2)}, u32[]{:S(2)}) collective-permute-start(bf16[256,1024]{1,0:T(8,128)(2,1)S(1)} %pad_maximum_fusion), channel_id=1, source_target_pairs={{0,1},{1,0},{2,3},{3,2},{4,5},{5,4},{6,7},{7,6},{8,9},{9,8},{10,11... | collective-permute-start | bytes 1572872 | tf_op jit(solution)/shard_map/ppermute | solution.py:25
  14.3 16.8 %copy-start.2 = (bf16[256,1024]{1,0:T(8,128)(2,1)}, bf16[256,1024]{1,0:T(8,128)(2,1)S(1)}, u32[]{:S(2)}) copy-start(bf16[256,1024]{1,0:T(8,128)(2,1)S(1)} %collective-permute-done.8.rest_0_.rest_1_) | copy-start | bytes 1572868
  14.3 39.8 %collective-permute-start.7 = (bf16[384,1024]{1,0:T(8,128)(2,1)S(1)}, bf16[384,1024]{1,0:T(8,128)(2,1)S(1)}, u32[]{:S(2)}, u32[]{:S(2)}) collective-permute-start(bf16[384,1024]{1,0:T(8,128)(2,1)S(1)} %get-tuple-element.21), channel_id=1, source_target_pairs={{0,1},{1,2},{2,3},{3,4},{4,5},{5,6},{6,7},{7,8},{8,9},{9,10},{10,1... | collective-permute-start | bytes 2359304 | tf_op jit(solution)/shard_map/ppermute | solution.py:19
  27.5 4.4 %copy-start.3 = (bf16[256,1024]{1,0:T(8,128)(2,1)}, bf16[256,1024]{1,0:T(8,128)(2,1)S(1)}, u32[]{:S(2)}) copy-start(bf16[256,1024]{1,0:T(8,128)(2,1)S(1)} %collective-permute-done.9.rest_2_.rest_3_) | copy-start | bytes 1572868
  27.5 26.1 %collective-permute-start.11 = (bf16[256,1024]{1,0:T(8,128)(2,1)S(1)}, bf16[256,1024]{1,0:T(8,128)(2,1)S(1)}, u32[]{:S(2)}, u32[]{:S(2)}) collective-permute-start(bf16[256,1024]{1,0:T(8,128)(2,1)S(1)} %pad_maximum_fusion.7), channel_id=1, source_target_pairs={{0,8},{1,9},{2,10},{3,11},{4,12},{5,13},{6,14},{7,15},{8,0},{9,1},... | collective-permute-start | bytes 1572872 | tf_op jit(solution)/shard_map/ppermute | solution.py:25
  27.6 4.4 %copy-start.4 = (bf16[256,1024]{1,0:T(8,128)(2,1)}, bf16[256,1024]{1,0:T(8,128)(2,1)S(1)}, u32[]{:S(2)}) copy-start(bf16[256,1024]{1,0:T(8,128)(2,1)S(1)} %collective-permute-done.10.rest_4_.rest_5_) | copy-start | bytes 1572868
  27.6 65.2 %collective-permute-start = (bf16[384,1024]{1,0:T(8,128)(2,1)}, bf16[384,1024]{1,0:T(8,128)(2,1)}, u32[]{:S(2)}, u32[]{:S(2)}) collective-permute-start(bf16[384,1024]{1,0:T(8,128)(2,1)} %get-tuple-element.24), channel_id=1, source_target_pairs={{0,1},{1,2},{2,3},{3,4},{4,5},{5,6},{6,7},{7,8},{8,9},{9,10},{10,1... | collective-permute-start | bytes 2359304 | tf_op jit(solution)/shard_map/ppermute | solution.py:19
  28.9 3.1 %copy-start.6 = (bf16[256,1024]{1,0:T(8,128)(2,1)}, bf16[256,1024]{1,0:T(8,128)(2,1)S(1)}, u32[]{:S(2)}) copy-start(bf16[256,1024]{1,0:T(8,128)(2,1)S(1)} %collective-permute-done.2.rest_0_.rest_1_) | copy-start | bytes 1572868
  28.9 63.9 %collective-permute-start.1 = (bf16[384,1024]{1,0:T(8,128)(2,1)}, bf16[384,1024]{1,0:T(8,128)(2,1)}, u32[]{:S(2)}, u32[]{:S(2)}) collective-permute-start(bf16[384,1024]{1,0:T(8,128)(2,1)} %get-tuple-element.22), channel_id=1, source_target_pairs={{0,1},{1,2},{2,3},{3,4},{4,5},{5,6},{6,7},{7,8},{8,9},{9,10},{10,1... | collective-permute-start | bytes 2359304 | tf_op jit(solution)/shard_map/ppermute | solution.py:19
  30.2 25.9 %copy-start.12 = (s32[3]{0:T(128)S(1)}, s32[3]{0:T(128)}, u32[]{:S(2)}) copy-start(s32[3]{0:T(128)} %param.8) | copy-start | bytes 40
  53.6 3.1 %copy-start.5 = (bf16[256,1024]{1,0:T(8,128)(2,1)}, bf16[256,1024]{1,0:T(8,128)(2,1)S(1)}, u32[]{:S(2)}) copy-start(bf16[256,1024]{1,0:T(8,128)(2,1)S(1)} %collective-permute-done.11.rest_6_.rest_7_) | copy-start | bytes 1572868
  53.6 20.5 %collective-permute-start.3 = (bf16[256,1024]{1,0:T(8,128)(2,1)}, bf16[256,1024]{1,0:T(8,128)(2,1)S(1)}, u32[]{:S(2)}, u32[]{:S(2)}) collective-permute-start(bf16[256,1024]{1,0:T(8,128)(2,1)} %pad_maximum_fusion.1), channel_id=1, source_target_pairs={{0,2},{1,3},{2,0},{3,1},{4,6},{5,7},{6,4},{7,5},{8,10},{9,11},{10,... | collective-permute-start | bytes 1572872 | tf_op jit(solution)/shard_map/ppermute | solution.py:25
  54.1 26.8 %collective-permute-start.4 = (bf16[256,1024]{1,0:T(8,128)(2,1)}, bf16[256,1024]{1,0:T(8,128)(2,1)S(1)}, u32[]{:S(2)}, u32[]{:S(2)}) collective-permute-start(bf16[256,1024]{1,0:T(8,128)(2,1)} %pad_maximum_fusion.2), channel_id=1, source_target_pairs={{0,4},{1,5},{2,6},{3,7},{4,0},{5,1},{6,2},{7,3},{8,12},{9,13},{10,... | collective-permute-start | bytes 1572872 | tf_op jit(solution)/shard_map/ppermute | solution.py:25
  54.1 2.6 %copy-start.10 = (bf16[384,1024]{1,0:T(8,128)(2,1)}, bf16[384,1024]{1,0:T(8,128)(2,1)S(1)}, u32[]{:S(2)}) copy-start(bf16[384,1024]{1,0:T(8,128)(2,1)S(1)} %collective-permute-done.7.pv_ref) | copy-start | bytes 2359300
  54.1 38.7 %collective-permute-start.5 = (bf16[256,1024]{1,0:T(8,128)(2,1)S(1)}, bf16[256,1024]{1,0:T(8,128)(2,1)S(1)}, u32[]{:S(2)}, u32[]{:S(2)}) collective-permute-start(bf16[256,1024]{1,0:T(8,128)(2,1)S(1)} %pad_maximum_fusion.3), channel_id=1, source_target_pairs={{0,8},{1,9},{2,10},{3,11},{4,12},{5,13},{6,14},{7,15},{8,0},{9,1},... | collective-permute-start | bytes 1572872 | tf_op jit(solution)/shard_map/ppermute | solution.py:25
  74.1 18.6 %copy-start.7 = (bf16[256,1024]{1,0:T(8,128)(2,1)}, bf16[256,1024]{1,0:T(8,128)(2,1)S(1)}, u32[]{:S(2)}) copy-start(bf16[256,1024]{1,0:T(8,128)(2,1)S(1)} %collective-permute-done.3.rest_2_.rest_3_) | copy-start | bytes 1572868
  80.9 11.9 %copy-start.8 = (bf16[256,1024]{1,0:T(8,128)(2,1)}, bf16[256,1024]{1,0:T(8,128)(2,1)S(1)}, u32[]{:S(2)}) copy-start(bf16[256,1024]{1,0:T(8,128)(2,1)S(1)} %collective-permute-done.4.rest_4_.rest_5_) | copy-start | bytes 1572868
  92.7 0.8 copy-start.9

commit v7 on v6

--- a/solution.py
+++ b/solution.py
@@ -10,7 +10,7 @@
 HEADS = 16
 BLK = 128
 WIN = 4
-CHUNKS = 2
+CHUNKS = 4
 
 
 def passed_along(block, axis, distance):
@@ -91,14 +91,15 @@
     out_ref[...] = (output / total).astype(out_ref.dtype)
 
 
-def attend(meta, queries, own_k, own_v, prev_k, prev_v, far, first_head, prior=None):
+def attend(meta, queries, own_k, own_v, rim, far, first_head, prior=None):
     rows, features = queries.shape
     head_dim = features // HEADS
-    heads = prev_k.shape[1] // head_dim
+    heads = rim.shape[1] // head_dim
     level_count = len(far)
     far_rows = far[0].shape[0] // 2
     whole = pl.BlockSpec((rows, head_dim), lambda h, meta: (0, h + first_head))
-    part = pl.BlockSpec((rows, head_dim), lambda h, meta: (0, h))
+    rim_k = pl.BlockSpec((rows, head_dim), lambda h, meta: (0, h))
+    rim_v = pl.BlockSpec((rows, head_dim), lambda h, meta: (1, h))
     far_specs = []
     for _ in range(level_count):
         far_specs.append(pl.BlockSpec((far_rows, head_dim), lambda h, meta: (0, h)))
@@ -107,8 +108,8 @@
     for block in far:
         far_args += [block, block]
     keys = 2 * rows + level_count * far_rows
-    args = [meta, queries, own_k, own_v, prev_k, prev_v, *far_args]
-    in_specs = [whole] * 3 + [part] * 2 + far_specs
+    args = [meta, queries, own_k, own_v, rim, rim, *far_args]
+    in_specs = [whole] * 3 + [rim_k, rim_v] + far_specs
     aliases = {}
     if prior is not None:
         aliases = {len(args): 0}
@@ -145,7 +146,7 @@
     context = None
     for c in range(CHUNKS):
         cols = slice(c * width, (c + 1) * width)
-        prev_keys, prev_values = passed_along((key_rows[:, cols], value_rows[:, cols]), "outer", 1)
+        rim = passed_along(jnp.concatenate([key_rows[:, cols], value_rows[:, cols]], axis=0), "outer", 1)
         far = []
         for level_bit in range(level_count):
             outgoing = jnp.concatenate(
@@ -154,7 +155,7 @@
             )
             far.append(from_partner(outgoing, "outer", level_bit))
         context = attend(
-            meta, queries, key_rows, value_rows, prev_keys, prev_values, far, c * (HEADS // CHUNKS), context
+            meta, queries, key_rows, value_rows, rim, far, c * (HEADS // CHUNKS), context
         )
     return context
 

time: 108 us -> 129 us (1.19)
  the two profiles are of different devices: /device:TPU:29 before, /device:TPU:0 now
where the time goes in v7:
time: 129 us
  starting transfers between devices  51 us (40%)
  Pallas kernels  33.9 us (26%)
  waiting for transfers between devices  30.6 us (24%)
  local copies, waits for them, and re-layouts  5.66 us (4%)
  other arithmetic  4.79 us (4%)
  between operations  2.87 us (2%)
    ppermute x16, starting transfers between devices, from_partner(): return lax.ppermute(value, axis, pairs)  40.3 us
    pallas_call x4, Pallas kernels, attend(): pl.pallas_call(functools.partial(attend_kernel, level_count), out_shape=j...  33.9 us
    ppermute x16, waiting for transfers between devices, from_partner(): return lax.ppermute(value, axis, pairs)  30.6 us
    ppermute x4, starting transfers between devices, passed_along(): return lax.ppermute(block, axis, route)  10.6 us
    concatenate x16, other arithmetic, on_device(): jnp.concatenate([pick_blocks(key_rows, wanted[level_bit])[:, cols], pick_...  3.1 us
    slice x1, local copies, waits for them, and re-layouts, on_device(): pick_blocks(value_rows, wanted[level_bit])[:, cols]  2.73 us
  transfers between devices with their start and end apart: 20, of which 5 were waited for; matrix products, arithmetic and copies ran while one was open for 4% of the time, Pallas kernels for 20%

profile of v7, /device:TPU:0, one launch (start us, length us, event | category | flops | bytes accessed | tf_op | source)
XLA Modules:
  0.0 128.9 jit_solution(12384334742270575500)
XLA Ops:
  0.0 1.4 %constant_dynamic-slice_fusion.2 = (s32[1,1,1]{0,2,1:T(1,128)}, s32[1,1,1]{0,2,1:T(1,128)}, s32[1,1,1]{0,2,1:T(1,128)}, s32[1,1,1]{0,2,1:T(1,128)}) fusion(s32[16,4,1]{0,2,1:T(1,128)} %param.9, s32[]{:T(128)S(6)} %select_n.22, s32[]{:T(128)S(6)} %select_n.18, s32[]{:T(128)S(6)} %select_n.16, s32[]{:T(128)S(6)} %select_n.20), kind=kLoop, calls=%fused_computation.22 | loop fusion | bytes 48 | tf_op jit(solution)/shard_map/dynamic_slice | solution.py:144
  3.8 2.7 %constant_dynamic-slice_fusion = (bf16[128,512]{1,0:T(8,128)(2,1)S(1)}, bf16[128,512]{1,0:T(8,128)(2,1)S(1)}, bf16[128,512]{1,0:T(8,128)(2,1)S(1)}, bf16[128,512...) fusion(bf16[384,2048]{1,0:T(8,128)(2,1)} %ov_ref.7, ...), kind=kLoop, calls=%fused_computation.20 | loop fusion | bytes 8388636 | tf_op jit(solution)/shard_map/slice | solution.py:153
  6.6 0.6 collective-permute-start.16
  7.2 2.6 %collective-permute-start.17 = (bf16[256,512]{1,0:T(8,128)(2,1)S(1)}, bf16[256,512]{1,0:T(8,128)(2,1)S(1)}, u32[]{:S(2)}, u32[]{:S(2)}) collective-permute-start(bf16[256,512]{1,0:T(8,128)(2,1)S(1)} %pad_maximum_fusion.17), channel_id=1, source_target_pairs={{0,2},{1,3},{2,0},{3,1},{4,6},{5,7},{6,4},{7,5},{8,10},{9,11},{10,... | collective-permute-start | bytes 786440 | tf_op jit(solution)/shard_map/ppermute | solution.py:25
  9.8 1.6 %collective-permute-start.18 = (bf16[256,512]{1,0:T(8,128)(2,1)S(1)}, bf16[256,512]{1,0:T(8,128)(2,1)S(1)}, u32[]{:S(2)}, u32[]{:S(2)}) collective-permute-start(bf16[256,512]{1,0:T(8,128)(2,1)S(1)} %pad_maximum_fusion.18), channel_id=1, source_target_pairs={{0,4},{1,5},{2,6},{3,7},{4,0},{5,1},{6,2},{7,3},{8,12},{9,13},{10,... | collective-permute-start | bytes 786440 | tf_op jit(solution)/shard_map/ppermute | solution.py:25
  11.6 0.6 collective-permute-start.7
  13.0 4.0 %collective-permute-done.17.rest_2_.rest_3_ = bf16[256,512]{1,0:T(8,128)(2,1)S(1)} collective-permute-done((bf16[256,512]{1,0:T(8,128)(2,1)S(1)}, bf16[256,512]{1,0:T(8,128)(2,1)S(1)}, u32[]{:S(2)}, u32[]{:S(2)}) %collective-permute-start.17) | collective-permute-done | bytes 262176 | tf_op jit(solution)/shard_map/ppermute | solution.py:25
  17.0 3.1 %collective-permute-start.9 = (bf16[256,512]{1,0:T(8,128)(2,1)S(1)}, bf16[256,512]{1,0:T(8,128)(2,1)S(1)}, u32[]{:S(2)}, u32[]{:S(2)}) collective-permute-start(bf16[256,512]{1,0:T(8,128)(2,1)S(1)} %pad_maximum_fusion.11), channel_id=1, source_target_pairs={{0,8},{1,9},{2,10},{3,11},{4,12},{5,13},{6,14},{7,15},{8,0},{9,1},... | collective-permute-start | bytes 786440 | tf_op jit(solution)/shard_map/ppermute | solution.py:25
  20.1 1.6 %collective-permute-start.12 = (bf16[256,512]{1,0:T(8,128)(2,1)S(1)}, bf16[256,512]{1,0:T(8,128)(2,1)S(1)}, u32[]{:S(2)}, u32[]{:S(2)}) collective-permute-start(bf16[256,512]{1,0:T(8,128)(2,1)S(1)} %pad_maximum_fusion.13), channel_id=1, source_target_pairs={{0,2},{1,3},{2,0},{3,1},{4,6},{5,7},{6,4},{7,5},{8,10},{9,11},{10,... | collective-permute-start | bytes 786440 | tf_op jit(solution)/shard_map/ppermute | solution.py:25
  21.7 0.7 collective-permute-done.7.rest_2_.rest_3_
  22.4 1.8 %collective-permute-start.13 = (bf16[256,512]{1,0:T(8,128)(2,1)S(1)}, bf16[256,512]{1,0:T(8,128)(2,1)}, u32[]{:S(2)}, u32[]{:S(2)}) collective-permute-start(bf16[256,512]{1,0:T(8,128)(2,1)S(1)} %pad_maximum_fusion.14), channel_id=1, source_target_pairs={{0,4},{1,5},{2,6},{3,7},{4,0},{5,1},{6,2},{7,3},{8,12},{9,13},{10,... | collective-permute-start | bytes 786440 | tf_op jit(solution)/shard_map/ppermute | solution.py:25
  24.2 0.9 pad_maximum_fusion
  25.1 5.2 %collective-permute-done.8.rest_4_.rest_5_ = bf16[256,512]{1,0:T(8,128)(2,1)S(1)} collective-permute-done((bf16[256,512]{1,0:T(8,128)(2,1)S(1)}, bf16[256,512]{1,0:T(8,128)(2,1)S(1)}, u32[]{:S(2)}, u32[]{:S(2)}) %collective-permute-start.8) | collective-permute-done | bytes 262176 | tf_op jit(solution)/shard_map/ppermute | solution.py:25
  30.3 1.3 %collective-permute-start.5 = (bf16[768,512]{1,0:T(8,128)(2,1)S(1)}, bf16[768,512]{1,0:T(8,128)(2,1)S(1)}, u32[]{:S(2)}, u32[]{:S(2)}) collective-permute-start(bf16[768,512]{1,0:T(8,128)(2,1)S(1)} %pad_maximum_fusion.1), channel_id=1, source_target_pairs={{0,1},{1,2},{2,3},{3,4},{4,5},{5,6},{6,7},{7,8},{8,9},{9,10},{10,1... | collective-permute-start | bytes 2359304 | tf_op jit(solution)/shard_map/ppermute | solution.py:19
  31.6 2.0 %collective-permute-start.10 = (bf16[768,512]{1,0:T(8,128)(2,1)S(1)}, bf16[768,512]{1,0:T(8,128)(2,1)S(1)}, u32[]{:S(2)}, u32[]{:S(2)}) collective-permute-start(bf16[768,512]{1,0:T(8,128)(2,1)S(1)} %pad_maximum_fusion.2), channel_id=1, source_target_pairs={{0,1},{1,2},{2,3},{3,4},{4,5},{5,6},{6,7},{7,8},{8,9},{9,10},{10,1... | collective-permute-start | bytes 2359304 | tf_op jit(solution)/shard_map/ppermute | solution.py:19
  33.6 3.3 %collective-permute-start.15 = (bf16[768,512]{1,0:T(8,128)(2,1)S(1)}, bf16[768,512]{1,0:T(8,128)(2,1)S(1)}, u32[]{:S(2)}, u32[]{:S(2)}) collective-permute-start(bf16[768,512]{1,0:T(8,128)(2,1)S(1)} %pad_maximum_fusion.3), channel_id=1, source_target_pairs={{0,1},{1,2},{2,3},{3,4},{4,5},{5,6},{6,7},{7,8},{8,9},{9,10},{10,1... | collective-permute-start | bytes 2359304 | tf_op jit(solution)/shard_map/ppermute | solution.py:19
  37.8 4.0 %collective-permute-start = (bf16[768,512]{1,0:T(8,128)(2,1)}, bf16[768,512]{1,0:T(8,128)(2,1)S(1)}, u32[]{:S(2)}, u32[]{:S(2)}) collective-permute-start(bf16[768,512]{1,0:T(8,128)(2,1)} %pad_maximum_fusion), channel_id=1, source_target_pairs={{0,1},{1,2},{2,3},{3,4},{4,5},{5,6},{6,7},{7,8},{8,9},{9,10},{10,1... | collective-permute-start | bytes 2359304 | tf_op jit(solution)/shard_map/ppermute | solution.py:19
  41.8 0.7 pad_maximum_fusion.7
  42.6 0.7 pad_maximum_fusion.6
  43.3 8.9 %collective-permute-done.14.rest_6_.rest_7_ = bf16[256,512]{1,0:T(8,128)(2,1)S(1)} collective-permute-done((bf16[256,512]{1,0:T(8,128)(2,1)S(1)}, bf16[256,512]{1,0:T(8,128)(2,1)S(1)}, u32[]{:S(2)}, u32[]{:S(2)}) %collective-permute-start.14) | collective-permute-done | bytes 262176 | tf_op jit(solution)/shard_map/ppermute | solution.py:25
  52.2 0.6 pad_add_fusion.meta
  52.8 0.7 pad_maximum_fusion.5
  53.5 0.7 pad_maximum_fusion.4
  54.2 11.9 %collective-permute-done.19.rest_6_.rest_7_ = bf16[256,512]{1,0:T(8,128)(2,1)S(1)} collective-permute-done((bf16[256,512]{1,0:T(8,128)(2,1)S(1)}, bf16[256,512]{1,0:T(8,128)(2,1)S(1)}, u32[]{:S(2)}, u32[]{:S(2)}) %collective-permute-start.19) | collective-permute-done | bytes 262176 | tf_op jit(solution)/shard_map/ppermute | solution.py:25
  66.2 13.8 %collective-permute-start.2 = (bf16[256,512]{1,0:T(8,128)(2,1)}, bf16[256,512]{1,0:T(8,128)(2,1)}, u32[]{:S(2)}, u32[]{:S(2)}) collective-permute-start(bf16[256,512]{1,0:T(8,128)(2,1)} %pad_maximum_fusion.5), channel_id=1, source_target_pairs={{0,2},{1,3},{2,0},{3,1},{4,6},{5,7},{6,4},{7,5},{8,10},{9,11},{10,... | collective-permute-start | bytes 786440 | tf_op jit(solution)/shard_map/ppermute | solution.py:25
  80.0 10.9 %collective-permute-start.3 = (bf16[256,512]{1,0:T(8,128)(2,1)}, bf16[256,512]{1,0:T(8,128)(2,1)}, u32[]{:S(2)}, u32[]{:S(2)}) collective-permute-start(bf16[256,512]{1,0:T(8,128)(2,1)} %pad_maximum_fusion.6), channel_id=1, source_target_pairs={{0,4},{1,5},{2,6},{3,7},{4,0},{5,1},{6,2},{7,3},{8,12},{9,13},{10,... | collective-permute-start | bytes 786440 | tf_op jit(solution)/shard_map/ppermute | solution.py:25
  90.8 3.1 %collective-permute-start.4 = (bf16[256,512]{1,0:T(8,128)(2,1)}, bf16[256,512]{1,0:T(8,128)(2,1)}, u32[]{:S(2)}, u32[]{:S(2)}) collective-permute-start(bf16[256,512]{1,0:T(8,128)(2,1)} %pad_maximum_fusion.7), channel_id=1, source_target_pairs={{0,8},{1,9},{2,10},{3,11},{4,12},{5,13},{6,14},{7,15},{8,0},{9,1},... | collective-permute-start | bytes 786440 | tf_op jit(solution)/shard_map/ppermute | solution.py:25
  94.0 8.4 %shard_map.55.rest_8_ = bf16[384,2048]{1,0:T(8,128)(2,1)} custom-call(s32[4]{0:T(128)} %pad_add_fusion.meta, bf16[384,2048]{1,0:T(8,128)(2,1)} %q_ref.7, bf16[384,2048]{1,0:T(8,128)(2,1)} %ok_ref.7, bf16[384,2048]{1,0:T(8,128)(2,1)} %ov_ref.7, bf16[768,512]{1,0:T(8,128)(2,1)} %copy-done.5, bf16[768,512]{1,0:T(8,128)(2,1)} %copy-done.5, ...), custom_call_target="tpu_custom_call" | custom-call | flops 1006632960 | bytes 3407872 | tf_op jit(solution)/shard_map/pallas_call | solution.py:118
  102.4 8.5 %shard_map.56.rest_8_ = bf16[384,2048]{1,0:T(8,128)(2,1)} custom-call(s32[4]{0:T(128)} %pad_add_fusion.meta, bf16[384,2048]{1,0:T(8,128)(2,1)} %q_ref.7, bf16[384,2048]{1,0:T(8,128)(2,1)} %ok_ref.7, bf16[384,2048]{1,0:T(8,128)(2,1)} %ov_ref.7, bf16[768,512]{1,0:T(8,128)(2,1)} %copy-done.4, ...), custom_call_target="tpu_custom_call", output_to_operand_aliasing={{}: (14, {})} | custom-call | flops 1006632960 | bytes 3407872 | tf_op jit(solution)/shard_map/pallas_call | solution.py:118
  110.9 8.5 %shard_map.57.rest_8_ = bf16[384,2048]{1,0:T(8,128)(2,1)} custom-call(s32[4]{0:T(128)} %pad_add_fusion.meta, bf16[384,2048]{1,0:T(8,128)(2,1)} %q_ref.7, bf16[384,2048]{1,0:T(8,128)(2,1)} %ok_ref.7, bf16[384,2048]{1,0:T(8,128)(2,1)} %ov_ref.7, bf16[768,512]{1,0:T(8,128)(2,1)} %copy-done.2, ...), custom_call_target="tpu_custom_call", output_to_operand_aliasing={{}: (14, {})} | custom-call | flops 1006632960 | bytes 3407872 | tf_op jit(solution)/shard_map/pallas_call | solution.py:118
  119.5 0.9 copy-done.3
  120.4 8.5 %shard_map.58 = bf16[384,2048]{1,0:T(8,128)(2,1)} custom-call(s32[4]{0:T(128)} %pad_add_fusion.meta, bf16[384,2048]{1,0:T(8,128)(2,1)} %q_ref.7, bf16[384,2048]{1,0:T(8,128)(2,1)} %ok_ref.7, bf16[384,2048]{1,0:T(8,128)(2,1)} %ov_ref.7, bf16[768,512]{1,0:T(8,128)(2,1)} %copy-done.3, bf16[768,512]{1,0:T(8,128)(2,1)} %copy-done.3, ...), custom_call_target="tpu_custom_call", output_to_operand_aliasing={{}: (14, {})} | custom-call | flops 1006632960 | bytes 3407872 | tf_op jit(solution)/shard_map/pallas_call | solution.py:118
  (72 shorter events, 1.8 us)
Async XLA Ops:
  6.6 6.1 %collective-permute-start.16 = (bf16[256,512]{1,0:T(8,128)(2,1)S(1)}, bf16[256,512]{1,0:T(8,128)(2,1)S(1)}, u32[]{:S(2)}, u32[]{:S(2)}) collective-permute-start(bf16[256,512]{1,0:T(8,128)(2,1)S(1)} %pad_maximum_fusion.16), channel_id=1, source_target_pairs={{0,1},{1,0},{2,3},{3,2},{4,5},{5,4},{6,7},{7,6},{8,9},{9,8},{10,11... | collective-permute-start | bytes 786440 | tf_op jit(solution)/shard_map/ppermute | solution.py:25
  7.2 9.7 %collective-permute-start.17 = (bf16[256,512]{1,0:T(8,128)(2,1)S(1)}, bf16[256,512]{1,0:T(8,128)(2,1)S(1)}, u32[]{:S(2)}, u32[]{:S(2)}) collective-permute-start(bf16[256,512]{1,0:T(8,128)(2,1)S(1)} %pad_maximum_fusion.17), channel_id=1, source_target_pairs={{0,2},{1,3},{2,0},{3,1},{4,6},{5,7},{6,4},{7,5},{8,10},{9,11},{10,... | collective-permute-start | bytes 786440 | tf_op jit(solution)/shard_map/ppermute | solution.py:25
  9.8 10.2 %collective-permute-start.18 = (bf16[256,512]{1,0:T(8,128)(2,1)S(1)}, bf16[256,512]{1,0:T(8,128)(2,1)S(1)}, u32[]{:S(2)}, u32[]{:S(2)}) collective-permute-start(bf16[256,512]{1,0:T(8,128)(2,1)S(1)} %pad_maximum_fusion.18), channel_id=1, source_target_pairs={{0,4},{1,5},{2,6},{3,7},{4,0},{5,1},{6,2},{7,3},{8,12},{9,13},{10,... | collective-permute-start | bytes 786440 | tf_op jit(solution)/shard_map/ppermute | solution.py:25
  11.5 8.6 %collective-permute-start.6 = (bf16[256,512]{1,0:T(8,128)(2,1)S(1)}, bf16[256,512]{1,0:T(8,128)(2,1)S(1)}, u32[]{:S(2)}, u32[]{:S(2)}) collective-permute-start(bf16[256,512]{1,0:T(8,128)(2,1)S(1)} %pad_maximum_fusion.8), channel_id=1, source_target_pairs={{0,1},{1,0},{2,3},{3,2},{4,5},{5,4},{6,7},{7,6},{8,9},{9,8},{10,11... | collective-permute-start | bytes 786440 | tf_op jit(solution)/shard_map/ppermute | solution.py:25
  11.6 10.8 %collective-permute-start.7 = (bf16[256,512]{1,0:T(8,128)(2,1)S(1)}, bf16[256,512]{1,0:T(8,128)(2,1)S(1)}, u32[]{:S(2)}, u32[]{:S(2)}) collective-permute-start(bf16[256,512]{1,0:T(8,128)(2,1)S(1)} %pad_maximum_fusion.9), channel_id=1, source_target_pairs={{0,2},{1,3},{2,0},{3,1},{4,6},{5,7},{6,4},{7,5},{8,10},{9,11},{10,... | collective-permute-start | bytes 786440 | tf_op jit(solution)/shard_map/ppermute | solution.py:25
  12.7 24.3 %copy-start.6 = (bf16[256,512]{1,0:T(8,128)(2,1)}, bf16[256,512]{1,0:T(8,128)(2,1)S(1)}, u32[]{:S(2)}) copy-start(bf16[256,512]{1,0:T(8,128)(2,1)S(1)} %collective-permute-done.16.rest_0_.rest_1_) | copy-start | bytes 786436
  12.7 17.6 %collective-permute-start.8 = (bf16[256,512]{1,0:T(8,128)(2,1)S(1)}, bf16[256,512]{1,0:T(8,128)(2,1)S(1)}, u32[]{:S(2)}, u32[]{:S(2)}) collective-permute-start(bf16[256,512]{1,0:T(8,128)(2,1)S(1)} %pad_maximum_fusion.10), channel_id=1, source_target_pairs={{0,4},{1,5},{2,6},{3,7},{4,0},{5,1},{6,2},{7,3},{8,12},{9,13},{10,... | collective-permute-start | bytes 786440 | tf_op jit(solution)/shard_map/ppermute | solution.py:25
  16.9 20.1 %copy-start.7 = (bf16[256,512]{1,0:T(8,128)(2,1)}, bf16[256,512]{1,0:T(8,128)(2,1)S(1)}, u32[]{:S(2)}) copy-start(bf16[256,512]{1,0:T(8,128)(2,1)S(1)} %collective-permute-done.17.rest_2_.rest_3_) | copy-start | bytes 786436
  17.0 14.7 %collective-permute-start.9 = (bf16[256,512]{1,0:T(8,128)(2,1)S(1)}, bf16[256,512]{1,0:T(8,128)(2,1)S(1)}, u32[]{:S(2)}, u32[]{:S(2)}) collective-permute-start(bf16[256,512]{1,0:T(8,128)(2,1)S(1)} %pad_maximum_fusion.11), channel_id=1, source_target_pairs={{0,8},{1,9},{2,10},{3,11},{4,12},{5,13},{6,14},{7,15},{8,0},{9,1},... | collective-permute-start | bytes 786440 | tf_op jit(solution)/shard_map/ppermute | solution.py:25
  20.0 17.0 %copy-start.9 = (bf16[256,512]{1,0:T(8,128)(2,1)}, bf16[256,512]{1,0:T(8,128)(2,1)S(1)}, u32[]{:S(2)}) copy-start(bf16[256,512]{1,0:T(8,128)(2,1)S(1)} %collective-permute-done.18.rest_4_.rest_5_) | copy-start | bytes 786436
  20.0 13.6 %collective-permute-start.11 = (bf16[256,512]{1,0:T(8,128)(2,1)S(1)}, bf16[256,512]{1,0:T(8,128)(2,1)S(1)}, u32[]{:S(2)}, u32[]{:S(2)}) collective-permute-start(bf16[256,512]{1,0:T(8,128)(2,1)S(1)} %pad_maximum_fusion.12), channel_id=1, source_target_pairs={{0,1},{1,0},{2,3},{3,2},{4,5},{5,4},{6,7},{7,6},{8,9},{9,8},{10,11... | collective-permute-start | bytes 786440 | tf_op jit(solution)/shard_map/ppermute | solution.py:25
  20.1 17.4 %copy-start.8 = (bf16[256,512]{1,0:T(8,128)(2,1)}, bf16[256,512]{1,0:T(8,128)(2,1)S(1)}, u32[]{:S(2)}) copy-start(bf16[256,512]{1,0:T(8,128)(2,1)S(1)} %collective-permute-done.6.rest_0_.rest_1_) | copy-start | bytes 786436
  20.1 17.0 %collective-permute-start.12 = (bf16[256,512]{1,0:T(8,128)(2,1)S(1)}, bf16[256,512]{1,0:T(8,128)(2,1)S(1)}, u32[]{:S(2)}, u32[]{:S(2)}) collective-permute-start(bf16[256,512]{1,0:T(8,128)(2,1)S(1)} %pad_maximum_fusion.13), channel_id=1, source_target_pairs={{0,2},{1,3},{2,0},{3,1},{4,6},{5,7},{6,4},{7,5},{8,10},{9,11},{10,... | collective-permute-start | bytes 786440 | tf_op jit(solution)/shard_map/ppermute | solution.py:25
  22.4 20.2 %copy-start.10 = (bf16[256,512]{1,0:T(8,128)(2,1)}, bf16[256,512]{1,0:T(8,128)(2,1)S(1)}, u32[]{:S(2)}) copy-start(bf16[256,512]{1,0:T(8,128)(2,1)S(1)} %collective-permute-done.7.rest_2_.rest_3_) | copy-start | bytes 786436
  22.4 15.5 %collective-permute-start.13 = (bf16[256,512]{1,0:T(8,128)(2,1)S(1)}, bf16[256,512]{1,0:T(8,128)(2,1)}, u32[]{:S(2)}, u32[]{:S(2)}) collective-permute-start(bf16[256,512]{1,0:T(8,128)(2,1)S(1)} %pad_maximum_fusion.14), channel_id=1, source_target_pairs={{0,4},{1,5},{2,6},{3,7},{4,0},{5,1},{6,2},{7,3},{8,12},{9,13},{10,... | collective-permute-start | bytes 786440 | tf_op jit(solution)/shard_map/ppermute | solution.py:25
  24.2 28.0 %copy-start.17 = (s32[3]{0:T(128)S(1)}, s32[3]{0:T(128)}, u32[]{:S(2)}) copy-start(s32[3]{0:T(128)} %param.8) | copy-start | bytes 40
  30.3 23.9 %copy-start.11 = (bf16[256,512]{1,0:T(8,128)(2,1)}, bf16[256,512]{1,0:T(8,128)(2,1)S(1)}, u32[]{:S(2)}) copy-start(bf16[256,512]{1,0:T(8,128)(2,1)S(1)} %collective-permute-done.8.rest_4_.rest_5_) | copy-start | bytes 786436
  30.3 35.9 %collective-permute-start.5 = (bf16[768,512]{1,0:T(8,128)(2,1)S(1)}, bf16[768,512]{1,0:T(8,128)(2,1)S(1)}, u32[]{:S(2)}, u32[]{:S(2)}) collective-permute-start(bf16[768,512]{1,0:T(8,128)(2,1)S(1)} %pad_maximum_fusion.1), channel_id=1, source_target_pairs={{0,1},{1,2},{2,3},{3,4},{4,5},{5,6},{6,7},{7,8},{8,9},{9,10},{10,1... | collective-permute-start | bytes 2359304 | tf_op jit(solution)/shard_map/ppermute | solution.py:19
  31.6 22.6 %copy-start.12 = (bf16[256,512]{1,0:T(8,128)(2,1)}, bf16[256,512]{1,0:T(8,128)(2,1)S(1)}, u32[]{:S(2)}) copy-start(bf16[256,512]{1,0:T(8,128)(2,1)S(1)} %collective-permute-done.9.rest_6_.rest_7_) | copy-start | bytes 786436
  31.6 48.3 %collective-permute-start.10 = (bf16[768,512]{1,0:T(8,128)(2,1)S(1)}, bf16[768,512]{1,0:T(8,128)(2,1)S(1)}, u32[]{:S(2)}, u32[]{:S(2)}) collective-permute-start(bf16[768,512]{1,0:T(8,128)(2,1)S(1)} %pad_maximum_fusion.2), channel_id=1, source_target_pairs={{0,1},{1,2},{2,3},{3,4},{4,5},{5,6},{6,7},{7,8},{8,9},{9,10},{10,1... | collective-permute-start | bytes 2359304 | tf_op jit(solution)/shard_map/ppermute | solution.py:19
  33.6 57.2 %collective-permute-start.15 = (bf16[768,512]{1,0:T(8,128)(2,1)S(1)}, bf16[768,512]{1,0:T(8,128)(2,1)S(1)}, u32[]{:S(2)}, u32[]{:S(2)}) collective-permute-start(bf16[768,512]{1,0:T(8,128)(2,1)S(1)} %pad_maximum_fusion.3), channel_id=1, source_target_pairs={{0,1},{1,2},{2,3},{3,4},{4,5},{5,6},{6,7},{7,8},{8,9},{9,10},{10,1... | collective-permute-start | bytes 2359304 | tf_op jit(solution)/shard_map/ppermute | solution.py:19
  37.1 15.1 %collective-permute-start.14 = (bf16[256,512]{1,0:T(8,128)(2,1)S(1)}, bf16[256,512]{1,0:T(8,128)(2,1)S(1)}, u32[]{:S(2)}, u32[]{:S(2)}) collective-permute-start(bf16[256,512]{1,0:T(8,128)(2,1)S(1)} %pad_maximum_fusion.15), channel_id=1, source_target_pairs={{0,8},{1,9},{2,10},{3,11},{4,12},{5,13},{6,14},{7,15},{8,0},{9,1},... | collective-permute-start | bytes 786440 | tf_op jit(solution)/shard_map/ppermute | solution.py:25
  37.8 81.6 %collective-permute-start = (bf16[768,512]{1,0:T(8,128)(2,1)}, bf16[768,512]{1,0:T(8,128)(2,1)S(1)}, u32[]{:S(2)}, u32[]{:S(2)}) collective-permute-start(bf16[768,512]{1,0:T(8,128)(2,1)} %pad_maximum_fusion), channel_id=1, source_target_pairs={{0,1},{1,2},{2,3},{3,4},{4,5},{5,6},{6,7},{7,8},{8,9},{9,10},{10,1... | collective-permute-start | bytes 2359304 | tf_op jit(solution)/shard_map/ppermute | solution.py:19
  52.2 50.2 %copy-start.15 = (bf16[256,512]{1,0:T(8,128)(2,1)}, bf16[256,512]{1,0:T(8,128)(2,1)S(1)}, u32[]{:S(2)}) copy-start(bf16[256,512]{1,0:T(8,128)(2,1)S(1)} %collective-permute-done.14.rest_6_.rest_7_) | copy-start | bytes 786436
  52.2 13.9 %collective-permute-start.19 = (bf16[256,512]{1,0:T(8,128)(2,1)S(1)}, bf16[256,512]{1,0:T(8,128)(2,1)S(1)}, u32[]{:S(2)}, u32[]{:S(2)}) collective-permute-start(bf16[256,512]{1,0:T(8,128)(2,1)S(1)} %pad_maximum_fusion.19), channel_id=1, source_target_pairs={{0,8},{1,9},{2,10},{3,11},{4,12},{5,13},{6,14},{7,15},{8,0},{9,1},... | collective-permute-start | bytes 786440 | tf_op jit(solution)/shard_map/ppermute | solution.py:25
  66.1 24.7 %copy-start.16 = (bf16[256,512]{1,0:T(8,128)(2,1)}, bf16[256,512]{1,0:T(8,128)(2,1)S(1)}, u32[]{:S(2)}) copy-start(bf16[256,512]{1,0:T(8,128)(2,1)S(1)} %collective-permute-done.19.rest_6_.rest_7_) | copy-start | bytes 786436
  66.1 53.3 %collective-permute-start.1 = (bf16[256,512]{1,0:T(8,128)(2,1)}, bf16[256,512]{1,0:T(8,128)(2,1)}, u32[]{:S(2)}, u32[]{:S(2)}) collective-permute-start(bf16[256,512]{1,0:T(8,128)(2,1)} %pad_maximum_fusion.4), channel_id=1, source_target_pairs={{0,1},{1,0},{2,3},{3,2},{4,5},{5,4},{6,7},{7,6},{8,9},{9,8},{10,11... | collective-permute-start | bytes 786440 | tf_op jit(solution)/shard_map/ppermute | solution.py:25
  66.2 36.3 %copy-start.2 = (bf16[768,512]{1,0:T(8,128)(2,1)}, bf16[768,512]{1,0:T(8,128)(2,1)S(1)}, u32[]{:S(2)}) copy-start(bf16[768,512]{1,0:T(8,128)(2,1)S(1)} %collective-permute-done.5.pk_ref.pv_ref) | copy-start | bytes 2359300
  66.2 53.3 %collective-permute-start.2 = (bf16[256,512]{1,0:T(8,128)(2,1)}, bf16[256,512]{1,0:T(8,128)(2,1)}, u32[]{:S(2)}, u32[]{:S(2)}) collective-permute-start(bf16[256,512]{1,0:T(8,128)(2,1)} %pad_maximum_fusion.5), channel_id=1, source_target_pairs={{0,2},{1,3},{2,0},{3,1},{4,6},{5,7},{6,4},{7,5},{8,10},{9,11},{10,... | collective-permute-start | bytes 786440 | tf_op jit(solution)/shard_map/ppermute | solution.py:25
  80.0 22.5 %copy-start.4 = (bf16[768,512]{1,0:T(8,128)(2,1)}, bf16[768,512]{1,0:T(8,128)(2,1)S(1)}, u32[]{:S(2)}) copy-start(bf16[768,512]{1,0:T(8,128)(2,1)S(1)} %collective-permute-done.10.pk_ref.pv_ref) | copy-start | bytes 2359300
  80.0 39.5 %collective-permute-start.3 = (bf16[256,512]{1,0:T(8,128)(2,1)}, bf16[256,512]{1,0:T(8,128)(2,1)}, u32[]{:S(2)}, u32[]{:S(2)}) collective-permute-start(bf16[256,512]{1,0:T(8,128)(2,1)} %pad_maximum_fusion.6), channel_id=1, source_target_pairs={{0,4},{1,5},{2,6},{3,7},{4,0},{5,1},{6,2},{7,3},{8,12},{9,13},{10,... | collective-permute-start | bytes 786440 | tf_op jit(solution)/shard_map/ppermute | solution.py:25
  90.8 28.6 %collective-permute-start.4 = (bf16[256,512]{1,0:T(8,128)(2,1)}, bf16[256,512]{1,0:T(8,128)(2,1)}, u32[]{:S(2)}, u32[]{:S(2)}) collective-permute-start(bf16[256,512]{1,0:T(8,128)(2,1)} %pad_maximum_fusion.7), channel_id=1, source_target_pairs={{0,8},{1,9},{2,10},{3,11},{4,12},{5,13},{6,14},{7,15},{8,0},{9,1},... | collective-permute-start | bytes 786440 | tf_op jit(solution)/shard_map/ppermute | solution.py:25
  (6 other events, 22.5 us)

commit v8 on v7

--- a/solution.py
+++ b/solution.py
@@ -10,7 +10,7 @@
 HEADS = 16
 BLK = 128
 WIN = 4
-CHUNKS = 4
+CHUNKS = 2
 
 
 def passed_along(block, axis, distance):

time: 129 us -> 115 us (0.89)
  the two profiles are of different devices: /device:TPU:0 before, /device:TPU:1 now
where the time goes in v8:
time: 115 us
  starting transfers between devices  39.2 us (34%)
  waiting for transfers between devices  29.6 us (26%)
  Pallas kernels  28.6 us (25%)
  local copies, waits for them, and re-layouts  8.07 us (7%)
  other arithmetic  6.57 us (6%)
  between operations  2.7 us (2%)
    ppermute x8, starting transfers between devices, from_partner(): return lax.ppermute(value, axis, pairs)  32.1 us
    ppermute x8, waiting for transfers between devices, from_partner(): return lax.ppermute(value, axis, pairs)  29.6 us
    pallas_call x2, Pallas kernels, attend(): pl.pallas_call(functools.partial(attend_kernel, level_count), out_shape=j...  28.6 us
    ppermute x2, starting transfers between devices, passed_along(): return lax.ppermute(block, axis, route)  7.11 us
    concatenate x8, other arithmetic, on_device(): jnp.concatenate([pick_blocks(key_rows, wanted[level_bit])[:, cols], pick_...  3.46 us
    unnamed x28, local copies, waits for them, and re-layouts  3.34 us
    slice x1, local copies, waits for them, and re-layouts, on_device(): key_rows[:, cols]  3.33 us
    concatenate x2, other arithmetic, on_device(): jnp.concatenate([key_rows[:, cols], value_rows[:, cols]], axis=0)  2.52 us
  transfers between devices with their start and end apart: 10, of which 1 were waited for; matrix products, arithmetic and copies ran while one was open for 6% of the time, Pallas kernels for 12%

profile of v8, /device:TPU:1, one launch (start us, length us, event | category | flops | bytes accessed | tf_op | source)
XLA Modules:
  0.0 114.7 jit_solution(1253513202334841427)
XLA Ops:
  0.0 3.3 %fusion = (bf16[384,1024]{1,0:T(8,128)(2,1)S(1)}, bf16[384,1024]{1,0:T(8,128)(2,1)}, bf16[384,1024]{1,0:T(8,128)(2,1)}, bf16[384,1024]{1,0:T(8,128)(2,1)S(1)}) fusion(bf16[384,2048]{1,0:T(8,128)(2,1)} %ok_ref.3, bf16[384,2048]{1,0:T(8,128)(2,1)} %ov_ref.3), kind=kLoop, calls=%fused_computation.23 | loop fusion | bytes 6291456 | tf_op jit(solution)/shard_map/slice | solution.py:149
  3.3 1.3 %pad_maximum_fusion.1 = bf16[768,1024]{1,0:T(8,128)(2,1)} fusion(bf16[384,1024]{1,0:T(8,128)(2,1)S(1)} %get-tuple-element.30, bf16[384,1024]{1,0:T(8,128)(2,1)S(1)} %get-tuple-element.21), kind=kLoop, calls=%fused_computation.1 | loop fusion | flops 3145728 | bytes 3145728 | tf_op jit(solution)/shard_map/concatenate | solution.py:149
  4.6 4.6 %collective-permute-start.5 = (bf16[768,1024]{1,0:T(8,128)(2,1)}, bf16[768,1024]{1,0:T(8,128)(2,1)}, u32[]{:S(2)}, u32[]{:S(2)}) collective-permute-start(bf16[768,1024]{1,0:T(8,128)(2,1)} %pad_maximum_fusion.1), channel_id=1, source_target_pairs={{0,1},{1,2},{2,3},{3,4},{4,5},{5,6},{6,7},{7,8},{8,9},{9,10},{10,1... | collective-permute-start | bytes 4718600 | tf_op jit(solution)/shard_map/ppermute | solution.py:19
  9.3 0.7 constant_dynamic-slice_fusion.2
  12.4 0.7 constant_dynamic-slice_fusion
  13.3 0.1 collective-permute-start.6
  13.3 0.2 copy-done.4
  13.6 0.8 copy-done.3
  14.4 1.3 %pad_maximum_fusion = bf16[768,1024]{1,0:T(8,128)(2,1)} fusion(bf16[384,1024]{1,0:T(8,128)(2,1)S(1)} %copy-done.4, bf16[384,1024]{1,0:T(8,128)(2,1)S(1)} %copy-done.3), kind=kLoop, calls=%fused_computation | loop fusion | flops 3145728 | bytes 3145728 | tf_op jit(solution)/shard_map/concatenate | solution.py:149
  15.6 2.5 %collective-permute-start = (bf16[768,1024]{1,0:T(8,128)(2,1)}, bf16[768,1024]{1,0:T(8,128)(2,1)S(1)}, u32[]{:S(2)}, u32[]{:S(2)}) collective-permute-start(bf16[768,1024]{1,0:T(8,128)(2,1)} %pad_maximum_fusion), channel_id=1, source_target_pairs={{0,1},{1,2},{2,3},{3,4},{4,5},{5,6},{6,7},{7,8},{8,9},{9,10},{10,1... | collective-permute-start | bytes 4718600 | tf_op jit(solution)/shard_map/ppermute | solution.py:19
  18.2 1.3 %collective-permute-start.7 = (bf16[256,1024]{1,0:T(8,128)(2,1)S(1)}, bf16[256,1024]{1,0:T(8,128)(2,1)S(1)}, u32[]{:S(2)}, u32[]{:S(2)}) collective-permute-start(bf16[256,1024]{1,0:T(8,128)(2,1)S(1)} %pad_maximum_fusion.7), channel_id=1, source_target_pairs={{0,2},{1,3},{2,0},{3,1},{4,6},{5,7},{6,4},{7,5},{8,10},{9,11},{10,... | collective-permute-start | bytes 1572872 | tf_op jit(solution)/shard_map/ppermute | solution.py:25
  19.5 1.4 %collective-permute-start.8 = (bf16[256,1024]{1,0:T(8,128)(2,1)S(1)}, bf16[256,1024]{1,0:T(8,128)(2,1)S(1)}, u32[]{:S(2)}, u32[]{:S(2)}) collective-permute-start(bf16[256,1024]{1,0:T(8,128)(2,1)S(1)} %pad_maximum_fusion.8), channel_id=1, source_target_pairs={{0,4},{1,5},{2,6},{3,7},{4,0},{5,1},{6,2},{7,3},{8,12},{9,13},{10,... | collective-permute-start | bytes 1572872 | tf_op jit(solution)/shard_map/ppermute | solution.py:25
  20.9 0.0 collective-permute-done.6.rest_0_.rest_1_
  20.9 1.1 collective-permute-start.9
  22.0 0.8 pad_maximum_fusion.5
  22.9 0.8 pad_maximum_fusion.4
  23.7 0.8 pad_maximum_fusion.3
  24.5 0.8 pad_maximum_fusion.2
  25.4 29.5 %collective-permute-done.7.rest_2_.rest_3_ = bf16[256,1024]{1,0:T(8,128)(2,1)S(1)} collective-permute-done((bf16[256,1024]{1,0:T(8,128)(2,1)S(1)}, bf16[256,1024]{1,0:T(8,128)(2,1)S(1)}, u32[]{:S(2)}, u32[]{:S(2)}) %collective-permute-start.7) | collective-permute-done | bytes 524320 | tf_op jit(solution)/shard_map/ppermute | solution.py:25
  54.9 8.1 %collective-permute-start.2 = (bf16[256,1024]{1,0:T(8,128)(2,1)}, bf16[256,1024]{1,0:T(8,128)(2,1)S(1)}, u32[]{:S(2)}, u32[]{:S(2)}) collective-permute-start(bf16[256,1024]{1,0:T(8,128)(2,1)} %pad_maximum_fusion.3), channel_id=1, source_target_pairs={{0,2},{1,3},{2,0},{3,1},{4,6},{5,7},{6,4},{7,5},{8,10},{9,11},{10,... | collective-permute-start | bytes 1572872 | tf_op jit(solution)/shard_map/ppermute | solution.py:25
  63.0 2.3 %collective-permute-start.3 = (bf16[256,1024]{1,0:T(8,128)(2,1)}, bf16[256,1024]{1,0:T(8,128)(2,1)S(1)}, u32[]{:S(2)}, u32[]{:S(2)}) collective-permute-start(bf16[256,1024]{1,0:T(8,128)(2,1)} %pad_maximum_fusion.4), channel_id=1, source_target_pairs={{0,4},{1,5},{2,6},{3,7},{4,0},{5,1},{6,2},{7,3},{8,12},{9,13},{10,... | collective-permute-start | bytes 1572872 | tf_op jit(solution)/shard_map/ppermute | solution.py:25
  65.3 0.0 collective-permute-done.5.pk_ref.pv_ref
  65.3 17.9 %collective-permute-start.4 = (bf16[256,1024]{1,0:T(8,128)(2,1)}, bf16[256,1024]{1,0:T(8,128)(2,1)}, u32[]{:S(2)}, u32[]{:S(2)}) collective-permute-start(bf16[256,1024]{1,0:T(8,128)(2,1)} %pad_maximum_fusion.5), channel_id=1, source_target_pairs={{0,8},{1,9},{2,10},{3,11},{4,12},{5,13},{6,14},{7,15},{8,0},{9,1},... | collective-permute-start | bytes 1572872 | tf_op jit(solution)/shard_map/ppermute | solution.py:25
  83.2 0.6 pad_add_fusion.meta
  83.8 14.2 %shard_map.55.rest_8_ = bf16[384,2048]{1,0:T(8,128)(2,1)} custom-call(s32[4]{0:T(128)} %pad_add_fusion.meta, bf16[384,2048]{1,0:T(8,128)(2,1)} %q_ref.3, bf16[384,2048]{1,0:T(8,128)(2,1)} %ok_ref.3, bf16[384,2048]{1,0:T(8,128)(2,1)} %ov_ref.3, bf16[768,1024]{1,0:T(8,128)(2,1)} %collective-permute-done.5.pk_ref.pv_ref, ...), custom_call_target="tpu_custom_call" | custom-call | flops 2013265920 | bytes 6815744 | tf_op jit(solution)/shard_map/pallas_call | solution.py:118
  98.1 0.0 collective-permute-done.1.rest_0_.rest_1_
  98.1 0.0 collective-permute-done.2.rest_2_.rest_3_
  98.1 0.7 copy-done.5
  98.9 0.2 copy-done.6
  99.1 0.2 copy-done.7
  99.2 1.2 %copy-done.2 = bf16[768,1024]{1,0:T(8,128)(2,1)} copy-done((bf16[768,1024]{1,0:T(8,128)(2,1)}, bf16[768,1024]{1,0:T(8,128)(2,1)S(1)}, u32[]{:S(2)}) %copy-start.2) | copy-done | bytes 1572888
  100.4 14.4 %shard_map.56 = bf16[384,2048]{1,0:T(8,128)(2,1)} custom-call(s32[4]{0:T(128)} %pad_add_fusion.meta, bf16[384,2048]{1,0:T(8,128)(2,1)} %q_ref.3, bf16[384,2048]{1,0:T(8,128)(2,1)} %ok_ref.3, bf16[384,2048]{1,0:T(8,128)(2,1)} %ov_ref.3, bf16[768,1024]{1,0:T(8,128)(2,1)} %copy-done.2, bf16[768,1024]{1,0:T(8,128)(2,1)} %copy-done.2, ...), custom_call_target="tpu_custom_call", output_to_operand_aliasing={{}: (14, {})} | custom-call | flops 2013265920 | bytes 6815744 | tf_op jit(solution)/shard_map/pallas_call | solution.py:118
  (32 shorter events, 0.2 us)
Async XLA Ops:
  3.3 6.0 %copy-start.12 = (s32[16,4,1]{0,2,1:T(1,128)S(1)}, s32[16,4,1]{0,2,1:T(1,128)}, u32[]{:S(2)}) copy-start(s32[16,4,1]{0,2,1:T(1,128)} %param.9) | copy-start | bytes 772
  3.3 9.1 %copy-start = (bf16[384,2048]{1,0:T(8,128)(2,1)S(1)}, bf16[384,2048]{1,0:T(8,128)(2,1)}, u32[]{:S(2)}) copy-start(bf16[384,2048]{1,0:T(8,128)(2,1)} %ok_ref.3) | copy-start | bytes 4718596
  3.3 9.1 %copy-start.1 = (bf16[384,2048]{1,0:T(8,128)(2,1)S(1)}, bf16[384,2048]{1,0:T(8,128)(2,1)}, u32[]{:S(2)}) copy-start(bf16[384,2048]{1,0:T(8,128)(2,1)} %ov_ref.3) | copy-start | bytes 4718596
  4.6 60.7 %collective-permute-start.5 = (bf16[768,1024]{1,0:T(8,128)(2,1)}, bf16[768,1024]{1,0:T(8,128)(2,1)}, u32[]{:S(2)}, u32[]{:S(2)}) collective-permute-start(bf16[768,1024]{1,0:T(8,128)(2,1)} %pad_maximum_fusion.1), channel_id=1, source_target_pairs={{0,1},{1,2},{2,3},{3,4},{4,5},{5,6},{6,7},{7,8},{8,9},{9,10},{10,1... | collective-permute-start | bytes 4718600 | tf_op jit(solution)/shard_map/ppermute | solution.py:19
  12.4 1.1 copy-start.4
  13.2 1.2 %copy-start.3 = (bf16[384,1024]{1,0:T(8,128)(2,1)S(1)}, bf16[384,1024]{1,0:T(8,128)(2,1)}, u32[]{:S(2)}) copy-start(bf16[384,1024]{1,0:T(8,128)(2,1)} %get-tuple-element.22) | copy-start | bytes 2359300
  13.3 7.7 %collective-permute-start.6 = (bf16[256,1024]{1,0:T(8,128)(2,1)S(1)}, bf16[256,1024]{1,0:T(8,128)(2,1)S(1)}, u32[]{:S(2)}, u32[]{:S(2)}) collective-permute-start(bf16[256,1024]{1,0:T(8,128)(2,1)S(1)} %pad_maximum_fusion.6), channel_id=1, source_target_pairs={{0,1},{1,0},{2,3},{3,2},{4,5},{5,4},{6,7},{7,6},{8,9},{9,8},{10,11... | collective-permute-start | bytes 1572872 | tf_op jit(solution)/shard_map/ppermute | solution.py:25
  15.6 82.5 %collective-permute-start = (bf16[768,1024]{1,0:T(8,128)(2,1)}, bf16[768,1024]{1,0:T(8,128)(2,1)S(1)}, u32[]{:S(2)}, u32[]{:S(2)}) collective-permute-start(bf16[768,1024]{1,0:T(8,128)(2,1)} %pad_maximum_fusion), channel_id=1, source_target_pairs={{0,1},{1,2},{2,3},{3,4},{4,5},{5,6},{6,7},{7,8},{8,9},{9,10},{10,1... | collective-permute-start | bytes 4718600 | tf_op jit(solution)/shard_map/ppermute | solution.py:19
  18.2 36.7 %collective-permute-start.7 = (bf16[256,1024]{1,0:T(8,128)(2,1)S(1)}, bf16[256,1024]{1,0:T(8,128)(2,1)S(1)}, u32[]{:S(2)}, u32[]{:S(2)}) collective-permute-start(bf16[256,1024]{1,0:T(8,128)(2,1)S(1)} %pad_maximum_fusion.7), channel_id=1, source_target_pairs={{0,2},{1,3},{2,0},{3,1},{4,6},{5,7},{6,4},{7,5},{8,10},{9,11},{10,... | collective-permute-start | bytes 1572872 | tf_op jit(solution)/shard_map/ppermute | solution.py:25
  19.5 35.4 %collective-permute-start.8 = (bf16[256,1024]{1,0:T(8,128)(2,1)S(1)}, bf16[256,1024]{1,0:T(8,128)(2,1)S(1)}, u32[]{:S(2)}, u32[]{:S(2)}) collective-permute-start(bf16[256,1024]{1,0:T(8,128)(2,1)S(1)} %pad_maximum_fusion.8), channel_id=1, source_target_pairs={{0,4},{1,5},{2,6},{3,7},{4,0},{5,1},{6,2},{7,3},{8,12},{9,13},{10,... | collective-permute-start | bytes 1572872 | tf_op jit(solution)/shard_map/ppermute | solution.py:25
  20.9 3.6 %copy-start.8 = (bf16[256,1024]{1,0:T(8,128)(2,1)}, bf16[256,1024]{1,0:T(8,128)(2,1)S(1)}, u32[]{:S(2)}) copy-start(bf16[256,1024]{1,0:T(8,128)(2,1)S(1)} %collective-permute-done.6.rest_0_.rest_1_) | copy-start | bytes 1572868
  20.9 42.1 %collective-permute-start.9 = (bf16[256,1024]{1,0:T(8,128)(2,1)S(1)}, bf16[256,1024]{1,0:T(8,128)(2,1)S(1)}, u32[]{:S(2)}, u32[]{:S(2)}) collective-permute-start(bf16[256,1024]{1,0:T(8,128)(2,1)S(1)} %pad_maximum_fusion.9), channel_id=1, source_target_pairs={{0,8},{1,9},{2,10},{3,11},{4,12},{5,13},{6,14},{7,15},{8,0},{9,1},... | collective-permute-start | bytes 1572872 | tf_op jit(solution)/shard_map/ppermute | solution.py:25
  22.9 60.4 %copy-start.13 = (s32[3]{0:T(128)S(1)}, s32[3]{0:T(128)}, u32[]{:S(2)}) copy-start(s32[3]{0:T(128)} %param.8) | copy-start | bytes 40
  54.9 8.1 %copy-start.9 = (bf16[256,1024]{1,0:T(8,128)(2,1)}, bf16[256,1024]{1,0:T(8,128)(2,1)S(1)}, u32[]{:S(2)}) copy-start(bf16[256,1024]{1,0:T(8,128)(2,1)S(1)} %collective-permute-done.7.rest_2_.rest_3_) | copy-start | bytes 1572868
  54.9 43.2 %collective-permute-start.1 = (bf16[256,1024]{1,0:T(8,128)(2,1)}, bf16[256,1024]{1,0:T(8,128)(2,1)S(1)}, u32[]{:S(2)}, u32[]{:S(2)}) collective-permute-start(bf16[256,1024]{1,0:T(8,128)(2,1)} %pad_maximum_fusion.2), channel_id=1, source_target_pairs={{0,1},{1,0},{2,3},{3,2},{4,5},{5,4},{6,7},{7,6},{8,9},{9,8},{10,11... | collective-permute-start | bytes 1572872 | tf_op jit(solution)/shard_map/ppermute | solution.py:25
  54.9 8.1 %copy-start.10 = (bf16[256,1024]{1,0:T(8,128)(2,1)}, bf16[256,1024]{1,0:T(8,128)(2,1)S(1)}, u32[]{:S(2)}) copy-start(bf16[256,1024]{1,0:T(8,128)(2,1)S(1)} %collective-permute-done.8.rest_4_.rest_5_) | copy-start | bytes 1572868
  54.9 43.2 %collective-permute-start.2 = (bf16[256,1024]{1,0:T(8,128)(2,1)}, bf16[256,1024]{1,0:T(8,128)(2,1)S(1)}, u32[]{:S(2)}, u32[]{:S(2)}) collective-permute-start(bf16[256,1024]{1,0:T(8,128)(2,1)} %pad_maximum_fusion.3), channel_id=1, source_target_pairs={{0,2},{1,3},{2,0},{3,1},{4,6},{5,7},{6,4},{7,5},{8,10},{9,11},{10,... | collective-permute-start | bytes 1572872 | tf_op jit(solution)/shard_map/ppermute | solution.py:25
  63.0 2.3 %copy-start.11 = (bf16[256,1024]{1,0:T(8,128)(2,1)}, bf16[256,1024]{1,0:T(8,128)(2,1)S(1)}, u32[]{:S(2)}) copy-start(bf16[256,1024]{1,0:T(8,128)(2,1)S(1)} %collective-permute-done.9.rest_6_.rest_7_) | copy-start | bytes 1572868
  63.0 35.1 %collective-permute-start.3 = (bf16[256,1024]{1,0:T(8,128)(2,1)}, bf16[256,1024]{1,0:T(8,128)(2,1)S(1)}, u32[]{:S(2)}, u32[]{:S(2)}) collective-permute-start(bf16[256,1024]{1,0:T(8,128)(2,1)} %pad_maximum_fusion.4), channel_id=1, source_target_pairs={{0,4},{1,5},{2,6},{3,7},{4,0},{5,1},{6,2},{7,3},{8,12},{9,13},{10,... | collective-permute-start | bytes 1572872 | tf_op jit(solution)/shard_map/ppermute | solution.py:25
  65.3 32.8 %collective-permute-start.4 = (bf16[256,1024]{1,0:T(8,128)(2,1)}, bf16[256,1024]{1,0:T(8,128)(2,1)}, u32[]{:S(2)}, u32[]{:S(2)}) collective-permute-start(bf16[256,1024]{1,0:T(8,128)(2,1)} %pad_maximum_fusion.5), channel_id=1, source_target_pairs={{0,8},{1,9},{2,10},{3,11},{4,12},{5,13},{6,14},{7,15},{8,0},{9,1},... | collective-permute-start | bytes 1572872 | tf_op jit(solution)/shard_map/ppermute | solution.py:25
  98.1 0.8 copy-start.5
  98.1 1.0 copy-start.6
  98.1 1.1 copy-start.7
  99.2 1.2 %copy-start.2 = (bf16[768,1024]{1,0:T(8,128)(2,1)}, bf16[768,1024]{1,0:T(8,128)(2,1)S(1)}, u32[]{:S(2)}) copy-start(bf16[768,1024]{1,0:T(8,128)(2,1)S(1)} %collective-permute-done.pk_ref.pv_ref) | copy-start | bytes 4718596

commit v9 on v6

--- a/solution.py
+++ b/solution.py
@@ -37,7 +37,7 @@
     return lax.dot_general(a, b, (((1,), (0,)), ((), ())), preferred_element_type=jnp.float32)
 
 
-def attend_kernel(level_count, meta, q_ref, ok_ref, ov_ref, pk_ref, pv_ref, *rest):
+def attend_kernel(level_count, meta, q_ref, ok_ref, ov_ref, pk_ref, pv_ref, tk_ref, tv_ref, *rest):
     far_refs = rest[: 2 * level_count]
     out_ref, bias_ref = rest[-2:]
     rows, head_dim = q_ref.shape
@@ -56,19 +56,31 @@
         first_block = meta[panel_len]
         own_off = q_blk - k_blk
         own_vis = (own_off >= 0) & (own_off < width) & ((own_off > 0) | (col <= row))
-        prev_off = q_blk + panel_len - k_blk
+        prev_blk = jnp.zeros((rows, rows), jnp.int32)
+        for slot in range(panel_len):
+            prev_blk = jnp.where(k_blk == slot, meta[panel_len + 1 + slot], prev_blk)
+        prev_off = q_blk + panel_len - prev_blk
         prev_vis = (prev_off < width) & (first_block + q_blk - prev_off >= 0)
         bias_ref[:, :rows] = jnp.where(prev_vis, 0.0, -jnp.inf)
         bias_ref[:, rows:] = jnp.where(own_vis, 0.0, -jnp.inf)
 
     q = q_ref[...]
-    s_prev = _nt(q, pk_ref[...]) * scale + bias_ref[:, :rows]
+    pair = pk_ref.shape[0]
+    s_prev = _nt(q, pk_ref[...]) * scale + bias_ref[:, :pair]
+    s_third = _nt(q, tk_ref[...]) * scale + bias_ref[:, pair:rows]
     s_own = _nt(q, ok_ref[...]) * scale + bias_ref[:, rows:]
-    m_w = jnp.maximum(s_own.max(-1, keepdims=True), s_prev.max(-1, keepdims=True))
+    m_w = jnp.maximum(
+        jnp.maximum(s_own.max(-1, keepdims=True), s_prev.max(-1, keepdims=True)), s_third.max(-1, keepdims=True)
+    )
     e_own = jnp.exp(s_own - m_w)
     e_prev = jnp.exp(s_prev - m_w)
-    l_w = e_own.sum(-1, keepdims=True) + e_prev.sum(-1, keepdims=True)
-    o_w = _nn(e_own.astype(jnp.bfloat16), ov_ref[...]) + _nn(e_prev.astype(jnp.bfloat16), pv_ref[...])
+    e_third = jnp.exp(s_third - m_w)
+    l_w = e_own.sum(-1, keepdims=True) + e_prev.sum(-1, keepdims=True) + e_third.sum(-1, keepdims=True)
+    o_w = (
+        _nn(e_own.astype(jnp.bfloat16), ov_ref[...])
+        + _nn(e_prev.astype(jnp.bfloat16), pv_ref[...])
+        + _nn(e_third.astype(jnp.bfloat16), tv_ref[...])
+    )
 
     maxes, totals, sums = [m_w], [l_w], [o_w]
     for b in range(level_count):
@@ -91,14 +103,19 @@
     out_ref[...] = (output / total).astype(out_ref.dtype)
 
 
-def attend(meta, queries, own_k, own_v, prev_k, prev_v, far, first_head, prior=None):
+def attend(meta, queries, own_k, own_v, pair, third, far, first_head, prior=None):
     rows, features = queries.shape
     head_dim = features // HEADS
-    heads = prev_k.shape[1] // head_dim
+    heads = pair.shape[1] // head_dim
     level_count = len(far)
     far_rows = far[0].shape[0] // 2
     whole = pl.BlockSpec((rows, head_dim), lambda h, meta: (0, h + first_head))
-    part = pl.BlockSpec((rows, head_dim), lambda h, meta: (0, h))
+    pair_rows = pair.shape[0] // 2
+    third_rows = third.shape[0] // 2
+    pair_k = pl.BlockSpec((pair_rows, head_dim), lambda h, meta: (0, h))
+    pair_v = pl.BlockSpec((pair_rows, head_dim), lambda h, meta: (1, h))
+    third_k = pl.BlockSpec((third_rows, head_dim), lambda h, meta: (0, h))
+    third_v = pl.BlockSpec((third_rows, head_dim), lambda h, meta: (1, h))
     far_specs = []
     for _ in range(level_count):
         far_specs.append(pl.BlockSpec((far_rows, head_dim), lambda h, meta: (0, h)))
@@ -107,8 +124,8 @@
     for block in far:
         far_args += [block, block]
     keys = 2 * rows + level_count * far_rows
-    args = [meta, queries, own_k, own_v, prev_k, prev_v, *far_args]
-    in_specs = [whole] * 3 + [part] * 2 + far_specs
+    args = [meta, queries, own_k, own_v, pair, pair, third, third, *far_args]
+    in_specs = [whole] * 3 + [pair_k, pair_v, third_k, third_v] + far_specs
     aliases = {}
     if prior is not None:
         aliases = {len(args): 0}
@@ -139,23 +156,59 @@
     panel_len = token_count // BLK
     device = lax.axis_index("outer")
     level_count = lax.axis_size("outer").bit_length() - 1
-    meta = jnp.concatenate([widths, (device * panel_len)[None]]).astype(jnp.int32)
+    count = lax.axis_size("outer")
     wanted = [columns[jnp.bitwise_xor(device, 1 << b), b] - device * panel_len for b in range(level_count)]
+
+    def relayed_block(sender):
+        return jnp.where(sender % 2 == 1, wanted_of(sender), 0)
+
+    def wanted_of(sender):
+        return columns[jnp.bitwise_xor(sender, 1), 0, 0] - sender * panel_len
+
+    def other_two(j):
+        return jnp.where(j == 0, 1, 0), jnp.where(j == 2, 1, 2)
+
+    mine_j = relayed_block(device)
+    mine_a, mine_b = other_two(mine_j)
+    sender = jnp.maximum(device - 1, 0)
+    from_j = relayed_block(sender)
+    from_a, from_b = other_two(from_j)
+    meta = jnp.concatenate(
+        [widths, jnp.stack([device * panel_len, from_a, from_b, from_j])]
+    ).astype(jnp.int32)
+    odd = device % 2 == 1
+    even_pairs = [(i, i + 1) for i in range(0, count, 2) if i + 1 < count]
+    forward_pairs = [(i, i + 2) for i in range(0, count, 2) if i + 2 < count]
+
     width = features // CHUNKS
     context = None
     for c in range(CHUNKS):
         cols = slice(c * width, (c + 1) * width)
-        prev_keys, prev_values = passed_along((key_rows[:, cols], value_rows[:, cols]), "outer", 1)
+        keys_c, values_c = key_rows[:, cols], value_rows[:, cols]
         far = []
         for level_bit in range(level_count):
             outgoing = jnp.concatenate(
-                [pick_blocks(key_rows, wanted[level_bit])[:, cols], pick_blocks(value_rows, wanted[level_bit])[:, cols]],
-                axis=0,
+                [pick_blocks(keys_c, wanted[level_bit]), pick_blocks(values_c, wanted[level_bit])], axis=0
             )
             far.append(from_partner(outgoing, "outer", level_bit))
-        context = attend(
-            meta, queries, key_rows, value_rows, prev_keys, prev_values, far, c * (HEADS // CHUNKS), context
+        pair = passed_along(
+            jnp.concatenate(
+                [
+                    pick_blocks(keys_c, mine_a[None]),
+                    pick_blocks(keys_c, mine_b[None]),
+                    pick_blocks(values_c, mine_a[None]),
+                    pick_blocks(values_c, mine_b[None]),
+                ],
+                axis=0,
+            ),
+            "outer",
+            1,
         )
+        own_third = jnp.concatenate([keys_c[:BLK], values_c[:BLK]], axis=0)
+        third_near = lax.ppermute(own_third, "outer", even_pairs)
+        third_far = lax.ppermute(far[0], "outer", forward_pairs)
+        third = jnp.where(odd, third_near, third_far)
+        context = attend(meta, queries, key_rows, value_rows, pair, third, far, c * (HEADS // CHUNKS), context)
     return context
 
 

time: 108 us -> 116 us (1.074)
  other arithmetic: 2.44 us -> 13.1 us
  waiting for transfers between devices: 55.4 us -> 45.4 us
  local copies, waits for them, and re-layouts: 6.91 us -> 10.5 us
  starting transfers between devices: 11.8 us -> 14.3 us
  between operations: 2.7 us -> 4.09 us
    ppermute x8, waiting for transfers between devices: 55.4 us -> 45.4 us  [from_partner(): return lax.ppermute(value, axis, pairs)]
    concatenate x9 -> x12, other arithmetic: 2.44 us -> 9.09 us  [the longest x8 6.16 us: on_device(): jnp.concatenate([pick_blocks(keys_c, wanted[level_bit]), pick_blocks(valu...]
    ppermute x0 -> x4, starting transfers between devices: none -> 5.5 us  [the longest x2 2.92 us: on_device(): third_far = lax.ppermute(far[0], 'outer', forward_pairs)]
    select_n x0 -> x2, other arithmetic: none -> 4.04 us  [on_device(): third = jnp.where(odd, third_near, third_far)]
    ppermute x4 -> x2, starting transfers between devices: 5.13 us -> 2.56 us  [passed_along(): return lax.ppermute(block, axis, route)]
    dynamic_slice x0 -> x2, local copies, waits for them, and re-layouts: none -> 2.33 us  [pick_blocks(): return lax.dynamic_slice_in_dim(source, block_index[0] * BLK, BLK, 0)]
    slice x4 -> x3, local copies, waits for them, and re-layouts: 4.22 us -> 4.74 us  [the longest x2 2.57 us: on_device(): keys_c, values_c = (key_rows[:, cols], value_rows[:, cols])]
  transfers between devices with their start and end apart: 12 -> 14, of which waited for: 5 -> 4; matrix products, arithmetic and copies ran while one was open for 4% -> 16% of each run, Pallas kernels for 13% -> 12%
where the time goes in v9:
time: 116 us
  waiting for transfers between devices  45.4 us (39%)
  Pallas kernels  28.2 us (24%)
  starting transfers between devices  14.3 us (12%)
  other arithmetic  13.1 us (11%)
  local copies, waits for them, and re-layouts  10.5 us (9%)
  between operations  4.09 us (4%)
    ppermute x8, waiting for transfers between devices, from_partner(): return lax.ppermute(value, axis, pairs)  45.4 us
    pallas_call x2, Pallas kernels, attend(): pl.pallas_call(functools.partial(attend_kernel, level_count), out_shape=j...  28.2 us
    ppermute x8, starting transfers between devices, from_partner(): return lax.ppermute(value, axis, pairs)  6.28 us
    concatenate x8, other arithmetic, on_device(): jnp.concatenate([pick_blocks(keys_c, wanted[level_bit]), pick_blocks(valu...  6.16 us
    select_n x2, other arithmetic, on_device(): third = jnp.where(odd, third_near, third_far)  4.04 us
    ppermute x2, starting transfers between devices, on_device(): third_far = lax.ppermute(far[0], 'outer', forward_pairs)  2.92 us
    ppermute x2, starting transfers between devices, on_device(): third_near = lax.ppermute(own_third, 'outer', even_pairs)  2.57 us
    slice x2, local copies, waits for them, and re-layouts, on_device(): keys_c, values_c = (key_rows[:, cols], value_rows[:, cols])  2.57 us
  transfers between devices with their start and end apart: 14, of which 4 were waited for; matrix products, arithmetic and copies ran while one was open for 16% of the time, Pallas kernels for 12%

profile of v9, /device:TPU:29, one launch (start us, length us, event | category | flops | bytes accessed | tf_op | source)
XLA Modules:
  0.0 115.7 jit_solution(1719607882294670367)
XLA Ops:
  0.0 2.2 %fusion = (bf16[128,1024]{1,0:T(8,128)(2,1)}, bf16[128,1024]{1,0:T(8,128)(2,1)S(1)}, bf16[128,1024]{1,0:T(8,128)(2,1)S(1)}, bf16[128,1024]{1,0:T(8,128)(2,1)}) fusion(bf16[384,2048]{1,0:T(8,128)(2,1)} %ok_ref.3, bf16[384,2048]{1,0:T(8,128)(2,1)} %ov_ref.3), kind=kLoop, calls=%fused_computation.43 | loop fusion | bytes 2097152 | tf_op jit(solution)/shard_map/slice | solution.py:207
  2.2 0.8 pad_maximum_fusion.2
  3.0 1.3 %collective-permute-start.1 = (bf16[256,1024]{1,0:T(8,128)(2,1)}, bf16[256,1024]{1,0:T(8,128)(2,1)}, u32[]{:S(2)}, u32[]{:S(2)}) collective-permute-start(bf16[256,1024]{1,0:T(8,128)(2,1)} %pad_maximum_fusion.2), channel_id=1, source_target_pairs={{0,1},{2,3},{4,5},{6,7},{8,9},{10,11},{12,13},{14,15},{16,17},{18,... | collective-permute-start | bytes 1572872 | tf_op jit(solution)/shard_map/ppermute | solution.py:208
  4.4 1.3 %fusion.3 = (bf16[384,1024]{1,0:T(8,128)(2,1)}, bf16[384,1024]{1,0:T(8,128)(2,1)}) fusion(bf16[384,2048]{1,0:T(8,128)(2,1)S(1)} %copy-done.1), kind=kLoop, calls=%fused_computation.46 | loop fusion | bytes 3145728 | tf_op jit(solution)/shard_map/slice | solution.py:187
  9.6 1.3 %fusion.2 = (bf16[384,1024]{1,0:T(8,128)(2,1)}, bf16[384,1024]{1,0:T(8,128)(2,1)}) fusion(bf16[384,2048]{1,0:T(8,128)(2,1)S(1)} %copy-done), kind=kLoop, calls=%fused_computation.45 | loop fusion | bytes 3145728 | tf_op jit(solution)/shard_map/slice | solution.py:187
  11.5 1.2 %constant_dynamic-slice_fusion = (bf16[128,1024]{1,0:T(8,128)(2,1)S(1)}, bf16[128,1024]{1,0:T(8,128)(2,1)S(1)}, bf16[128,1024]{1,0:T(8,128)(2,1)S(1)}, bf16[128,...) fusion(bf16[384,1024]{1,0:T(8,128)(2,1)S(1)} %copy-done.2, ...), kind=kLoop, calls=%fused_computation.14 | loop fusion | bytes 6291480 | tf_op jit(solution)/shard_map/dynamic_slice | solution.py:29
  13.2 1.2 %constant_dynamic-slice_fusion.1 = (bf16[128,1024]{1,0:T(8,128)(2,1)S(1)}, bf16[128,1024]{1,0:T(8,128)(2,1)S(1)}, bf16[128,1024]{1,0:T(8,128)(2,1)S(1)}, bf16[12...) fusion(bf16[384,1024]{1,0:T(8,128)(2,1)S(1)} %copy-done.4, ...), kind=kLoop, calls=%fused_computation.15 | loop fusion | bytes 6291480 | tf_op jit(solution)/shard_map/dynamic_slice | solution.py:29
  14.4 1.9 %collective-permute-start.2 = (bf16[256,1024]{1,0:T(8,128)(2,1)S(1)}, bf16[256,1024]{1,0:T(8,128)(2,1)S(1)}, u32[]{:S(2)}, u32[]{:S(2)}) collective-permute-start(bf16[256,1024]{1,0:T(8,128)(2,1)S(1)} %pad_maximum_fusion.3), channel_id=1, source_target_pairs={{0,1},{1,0},{2,3},{3,2},{4,5},{5,4},{6,7},{7,6},{8,9},{9,8},{10,11... | collective-permute-start | bytes 1572872 | tf_op jit(solution)/shard_map/ppermute | solution.py:25
  16.3 1.0 pad_maximum_fusion.1
  17.4 1.3 %collective-permute-start.7 = (bf16[512,1024]{1,0:T(8,128)(2,1)}, bf16[512,1024]{1,0:T(8,128)(2,1)S(1)}, u32[]{:S(2)}, u32[]{:S(2)}) collective-permute-start(bf16[512,1024]{1,0:T(8,128)(2,1)} %pad_maximum_fusion.1), channel_id=1, source_target_pairs={{0,1},{1,2},{2,3},{3,4},{4,5},{5,6},{6,7},{7,8},{8,9},{9,10},{10,1... | collective-permute-start | bytes 3145736 | tf_op jit(solution)/shard_map/ppermute | solution.py:19
  18.7 1.3 %collective-permute-start.8 = (bf16[256,1024]{1,0:T(8,128)(2,1)S(1)}, bf16[256,1024]{1,0:T(8,128)(2,1)}, u32[]{:S(2)}, u32[]{:S(2)}) collective-permute-start(bf16[256,1024]{1,0:T(8,128)(2,1)S(1)} %pad_maximum_fusion.7), channel_id=1, source_target_pairs={{0,1},{2,3},{4,5},{6,7},{8,9},{10,11},{12,13},{14,15},{16,17},{18,... | collective-permute-start | bytes 1572872 | tf_op jit(solution)/shard_map/ppermute | solution.py:208
  20.1 2.0 %collective-permute-start.9 = (bf16[256,1024]{1,0:T(8,128)(2,1)S(1)}, bf16[256,1024]{1,0:T(8,128)(2,1)}, u32[]{:S(2)}, u32[]{:S(2)}) collective-permute-start(bf16[256,1024]{1,0:T(8,128)(2,1)S(1)} %pad_maximum_fusion.8), channel_id=1, source_target_pairs={{0,1},{1,0},{2,3},{3,2},{4,5},{5,4},{6,7},{7,6},{8,9},{9,8},{10,11... | collective-permute-start | bytes 1572872 | tf_op jit(solution)/shard_map/ppermute | solution.py:25
  22.1 0.8 pad_maximum_fusion.9
  22.9 2.0 %collective-permute-start.11 = (bf16[256,1024]{1,0:T(8,128)(2,1)}, bf16[256,1024]{1,0:T(8,128)(2,1)}, u32[]{:S(2)}, u32[]{:S(2)}) collective-permute-start(bf16[256,1024]{1,0:T(8,128)(2,1)} %pad_maximum_fusion.9), channel_id=1, source_target_pairs={{0,2},{1,3},{2,0},{3,1},{4,6},{5,7},{6,4},{7,5},{8,10},{9,11},{10,... | collective-permute-start | bytes 1572872 | tf_op jit(solution)/shard_map/ppermute | solution.py:25
  24.9 0.8 pad_maximum_fusion.10
  25.9 0.8 pad_maximum_fusion.11
  26.8 1.5 %collective-permute-start.10 = (bf16[256,1024]{1,0:T(8,128)(2,1)}, bf16[256,1024]{1,0:T(8,128)(2,1)}, u32[]{:S(2)}, u32[]{:S(2)}) collective-permute-start(bf16[256,1024]{1,0:T(8,128)(2,1)} %collective-permute-done.9.rest_0_.rest_1_), channel_id=1, source_target_pairs={{0,2},{2,4},{4,6},{6,8},{8,10},{10,12},{12,14},{16,18},{18,20},{20... | collective-permute-start | bytes 1572872 | tf_op jit(solution)/shard_map/ppermute | solution.py:209
  29.5 1.0 pad_maximum_fusion
  30.5 19.6 %collective-permute-done.11.rest_2_.rest_3_ = bf16[256,1024]{1,0:T(8,128)(2,1)} collective-permute-done((bf16[256,1024]{1,0:T(8,128)(2,1)}, bf16[256,1024]{1,0:T(8,128)(2,1)}, u32[]{:S(2)}, u32[]{:S(2)}) %collective-permute-start.11) | collective-permute-done | bytes 524320 | tf_op jit(solution)/shard_map/ppermute | solution.py:25
  50.2 1.3 %collective-permute-start = (bf16[512,1024]{1,0:T(8,128)(2,1)}, bf16[512,1024]{1,0:T(8,128)(2,1)S(1)}, u32[]{:S(2)}, u32[]{:S(2)}) collective-permute-start(bf16[512,1024]{1,0:T(8,128)(2,1)} %pad_maximum_fusion), channel_id=1, source_target_pairs={{0,1},{1,2},{2,3},{3,4},{4,5},{5,6},{6,7},{7,8},{8,9},{9,10},{10,1... | collective-permute-start | bytes 3145736 | tf_op jit(solution)/shard_map/ppermute | solution.py:19
  51.4 1.9 %pad_maximum_fusion.4 = bf16[256,1024]{1,0:T(8,128)(2,1)} fusion(bf16[128,1024]{1,0:T(8,128)(2,1)} %get-tuple-element.45, bf16[128,1024]{1,0:T(8,128)(2,1)} %get-tuple-element.51), kind=kLoop, calls=%fused_computation.4 | loop fusion | flops 1048576 | bytes 1048576 | tf_op jit(solution)/shard_map/concatenate | solution.py:190
  53.3 0.8 pad_maximum_fusion.5
  54.1 5.5 %collective-permute-done.12.rest_4_.rest_5_ = bf16[256,1024]{1,0:T(8,128)(2,1)S(1)} collective-permute-done((bf16[256,1024]{1,0:T(8,128)(2,1)}, bf16[256,1024]{1,0:T(8,128)(2,1)S(1)}, u32[]{:S(2)}, u32[]{:S(2)}) %collective-permute-start.12) | collective-permute-done | bytes 524320 | tf_op jit(solution)/shard_map/ppermute | solution.py:25
  59.6 1.5 %collective-permute-start.3 = (bf16[256,1024]{1,0:T(8,128)(2,1)S(1)}, bf16[256,1024]{1,0:T(8,128)(2,1)}, u32[]{:S(2)}, u32[]{:S(2)}) collective-permute-start(bf16[256,1024]{1,0:T(8,128)(2,1)S(1)} %collective-permute-done.2.rest_0_.rest_1_), channel_id=1, source_target_pairs={{0,2},{2,4},{4,6},{6,8},{8,10},{10,12},{12,14},{16,18},{18,20},{20... | collective-permute-start | bytes 1572872 | tf_op jit(solution)/shard_map/ppermute | solution.py:209
  61.1 0.9 pad_maximum_fusion.6
  62.2 2.1 %broadcast_select_fusion.tk_ref.tv_ref = bf16[256,1024]{1,0:T(8,128)(2,1)} fusion(bf16[256,1024]{1,0:T(8,128)(2,1)} %collective-permute-done.8, bf16[256,1024]{1,0:T(8,128)(2,1)} %collective-permute-done.10, pred[]{:T(512)S(6)} %eq.26), kind=kLoop, calls=%fused_computation.12 | loop fusion | flops 262144 | bytes 1572865 | tf_op jit(solution)/shard_map/jit(_where)/select_n | solution.py:210
  64.3 14.0 %shard_map.55.rest_8_ = bf16[384,2048]{1,0:T(8,128)(2,1)} custom-call(s32[7]{0:T(128)} %concatenate.39.meta, bf16[384,2048]{1,0:T(8,128)(2,1)} %q_ref.3, bf16[384,2048]{1,0:T(8,128)(2,1)} %ok_ref.3, bf16[384,2048]{1,0:T(8,128)(2,1)} %ov_ref.3, bf16[512,1024]{1,0:T(8,128)(2,1)} %copy-done.7, bf16[512,1024]{1,0:T(8,128)(2,1)} %copy-done.7, ...), custom_call_target="tpu_custom_call" | custom-call | flops 2013265920 | bytes 6815744 | tf_op jit(solution)/shard_map/pallas_call | solution.py:134
  78.4 1.9 %broadcast_select_fusion.1.tk_ref.tv_ref = bf16[256,1024]{1,0:T(8,128)(2,1)} fusion(bf16[256,1024]{1,0:T(8,128)(2,1)} %collective-permute-done.1, bf16[256,1024]{1,0:T(8,128)(2,1)} %collective-permute-done.3, pred[]{:T(512)S(6)} %eq.26), kind=kLoop, calls=%fused_computation.13 | loop fusion | flops 262144 | bytes 1572865 | tf_op jit(solution)/shard_map/jit(_where)/select_n | solution.py:210
  80.3 7.0 %collective-permute-done.4.rest_2_.rest_3_ = bf16[256,1024]{1,0:T(8,128)(2,1)S(1)} collective-permute-done((bf16[256,1024]{1,0:T(8,128)(2,1)}, bf16[256,1024]{1,0:T(8,128)(2,1)S(1)}, u32[]{:S(2)}, u32[]{:S(2)}) %collective-permute-start.4) | collective-permute-done | bytes 524320 | tf_op jit(solution)/shard_map/ppermute | solution.py:25
  87.3 13.2 %collective-permute-done.5.rest_4_.rest_5_ = bf16[256,1024]{1,0:T(8,128)(2,1)} collective-permute-done((bf16[256,1024]{1,0:T(8,128)(2,1)}, bf16[256,1024]{1,0:T(8,128)(2,1)}, u32[]{:S(2)}, u32[]{:S(2)}) %collective-permute-start.5) | collective-permute-done | bytes 524320 | tf_op jit(solution)/shard_map/ppermute | solution.py:25
  100.6 1.0 copy-done.6
  101.5 14.1 %shard_map.56 = bf16[384,2048]{1,0:T(8,128)(2,1)} custom-call(s32[7]{0:T(128)} %concatenate.39.meta, bf16[384,2048]{1,0:T(8,128)(2,1)} %q_ref.3, bf16[384,2048]{1,0:T(8,128)(2,1)} %ok_ref.3, bf16[384,2048]{1,0:T(8,128)(2,1)} %ov_ref.3, bf16[512,1024]{1,0:T(8,128)(2,1)} %copy-done.6, bf16[512,1024]{1,0:T(8,128)(2,1)} %copy-done.6, ...), custom_call_target="tpu_custom_call", output_to_operand_aliasing={{}: (16, {})} | custom-call | flops 2013265920 | bytes 6815744 | tf_op jit(solution)/shard_map/pallas_call | solution.py:134
  (57 shorter events, 3.1 us)
Async XLA Ops:
  0.0 4.3 %copy-start.1 = (bf16[384,2048]{1,0:T(8,128)(2,1)S(1)}, bf16[384,2048]{1,0:T(8,128)(2,1)}, u32[]{:S(2)}) copy-start(bf16[384,2048]{1,0:T(8,128)(2,1)} %ov_ref.3) | copy-start | bytes 4718596
  3.0 19.9 %collective-permute-start.1 = (bf16[256,1024]{1,0:T(8,128)(2,1)}, bf16[256,1024]{1,0:T(8,128)(2,1)}, u32[]{:S(2)}, u32[]{:S(2)}) collective-permute-start(bf16[256,1024]{1,0:T(8,128)(2,1)} %pad_maximum_fusion.2), channel_id=1, source_target_pairs={{0,1},{2,3},{4,5},{6,7},{8,9},{10,11},{12,13},{14,15},{16,17},{18,... | collective-permute-start | bytes 1572872 | tf_op jit(solution)/shard_map/ppermute | solution.py:208
  4.3 1.3 %copy-start.17 = (s32[16,4,1]{0,2,1:T(1,128)S(1)}, s32[16,4,1]{0,2,1:T(1,128)}, u32[]{:S(2)}) copy-start(s32[16,4,1]{0,2,1:T(1,128)} %param.9) | copy-start | bytes 772
  4.3 5.2 %copy-start = (bf16[384,2048]{1,0:T(8,128)(2,1)S(1)}, bf16[384,2048]{1,0:T(8,128)(2,1)}, u32[]{:S(2)}) copy-start(bf16[384,2048]{1,0:T(8,128)(2,1)} %ok_ref.3) | copy-start | bytes 4718596
  9.6 1.3 %copy-start.2 = (bf16[384,1024]{1,0:T(8,128)(2,1)S(1)}, bf16[384,1024]{1,0:T(8,128)(2,1)}, u32[]{:S(2)}) copy-start(bf16[384,1024]{1,0:T(8,128)(2,1)} %get-tuple-element.11) | copy-start | bytes 2359300
  9.6 1.9 %copy-start.3 = (bf16[384,1024]{1,0:T(8,128)(2,1)S(1)}, bf16[384,1024]{1,0:T(8,128)(2,1)}, u32[]{:S(2)}) copy-start(bf16[384,1024]{1,0:T(8,128)(2,1)} %get-tuple-element.12) | copy-start | bytes 2359300
  11.5 1.2 %copy-start.4 = (bf16[384,1024]{1,0:T(8,128)(2,1)S(1)}, bf16[384,1024]{1,0:T(8,128)(2,1)}, u32[]{:S(2)}) copy-start(bf16[384,1024]{1,0:T(8,128)(2,1)} %get-tuple-element.9) | copy-start | bytes 2359300
  11.5 1.7 %copy-start.5 = (bf16[384,1024]{1,0:T(8,128)(2,1)S(1)}, bf16[384,1024]{1,0:T(8,128)(2,1)}, u32[]{:S(2)}) copy-start(bf16[384,1024]{1,0:T(8,128)(2,1)} %get-tuple-element.10) | copy-start | bytes 2359300
  14.3 4.3 %copy-start.15 = (bf16[128,1024]{1,0:T(8,128)(2,1)S(1)}, bf16[128,1024]{1,0:T(8,128)(2,1)}, u32[]{:S(2)}) copy-start(bf16[128,1024]{1,0:T(8,128)(2,1)} %get-tuple-element.5) | copy-start | bytes 786436
  14.3 4.3 %copy-start.16 = (bf16[128,1024]{1,0:T(8,128)(2,1)S(1)}, bf16[128,1024]{1,0:T(8,128)(2,1)}, u32[]{:S(2)}) copy-start(bf16[128,1024]{1,0:T(8,128)(2,1)} %get-tuple-element.55) | copy-start | bytes 786436
  14.4 11.3 %collective-permute-start.2 = (bf16[256,1024]{1,0:T(8,128)(2,1)S(1)}, bf16[256,1024]{1,0:T(8,128)(2,1)S(1)}, u32[]{:S(2)}, u32[]{:S(2)}) collective-permute-start(bf16[256,1024]{1,0:T(8,128)(2,1)S(1)} %pad_maximum_fusion.3), channel_id=1, source_target_pairs={{0,1},{1,0},{2,3},{3,2},{4,5},{5,4},{6,7},{7,6},{8,9},{9,8},{10,11... | collective-permute-start | bytes 1572872 | tf_op jit(solution)/shard_map/ppermute | solution.py:25
  17.4 44.6 %collective-permute-start.7 = (bf16[512,1024]{1,0:T(8,128)(2,1)}, bf16[512,1024]{1,0:T(8,128)(2,1)S(1)}, u32[]{:S(2)}, u32[]{:S(2)}) collective-permute-start(bf16[512,1024]{1,0:T(8,128)(2,1)} %pad_maximum_fusion.1), channel_id=1, source_target_pairs={{0,1},{1,2},{2,3},{3,4},{4,5},{5,6},{6,7},{7,8},{8,9},{9,10},{10,1... | collective-permute-start | bytes 3145736 | tf_op jit(solution)/shard_map/ppermute | solution.py:19
  18.7 8.0 %collective-permute-start.8 = (bf16[256,1024]{1,0:T(8,128)(2,1)S(1)}, bf16[256,1024]{1,0:T(8,128)(2,1)}, u32[]{:S(2)}, u32[]{:S(2)}) collective-permute-start(bf16[256,1024]{1,0:T(8,128)(2,1)S(1)} %pad_maximum_fusion.7), channel_id=1, source_target_pairs={{0,1},{2,3},{4,5},{6,7},{8,9},{10,11},{12,13},{14,15},{16,17},{18,... | collective-permute-start | bytes 1572872 | tf_op jit(solution)/shard_map/ppermute | solution.py:208
  20.1 6.7 %collective-permute-start.9 = (bf16[256,1024]{1,0:T(8,128)(2,1)S(1)}, bf16[256,1024]{1,0:T(8,128)(2,1)}, u32[]{:S(2)}, u32[]{:S(2)}) collective-permute-start(bf16[256,1024]{1,0:T(8,128)(2,1)S(1)} %pad_maximum_fusion.8), channel_id=1, source_target_pairs={{0,1},{1,0},{2,3},{3,2},{4,5},{5,4},{6,7},{7,6},{8,9},{9,8},{10,11... | collective-permute-start | bytes 1572872 | tf_op jit(solution)/shard_map/ppermute | solution.py:25
  22.1 6.8 %copy-start.18 = (s32[3]{0:T(128)S(1)}, s32[3]{0:T(128)}, u32[]{:S(2)}) copy-start(s32[3]{0:T(128)} %param.8) | copy-start | bytes 40
  22.1 7.4 %copy-start.14 = (bf16[128,1024]{1,0:T(8,128)(2,1)S(1)}, bf16[128,1024]{1,0:T(8,128)(2,1)}, u32[]{:S(2)}) copy-start(bf16[128,1024]{1,0:T(8,128)(2,1)} %get-tuple-element.43) | copy-start | bytes 786436
  22.9 27.3 %collective-permute-start.11 = (bf16[256,1024]{1,0:T(8,128)(2,1)}, bf16[256,1024]{1,0:T(8,128)(2,1)}, u32[]{:S(2)}, u32[]{:S(2)}) collective-permute-start(bf16[256,1024]{1,0:T(8,128)(2,1)} %pad_maximum_fusion.9), channel_id=1, source_target_pairs={{0,2},{1,3},{2,0},{3,1},{4,6},{5,7},{6,4},{7,5},{8,10},{9,11},{10,... | collective-permute-start | bytes 1572872 | tf_op jit(solution)/shard_map/ppermute | solution.py:25
  25.7 33.9 %copy-start.8 = (bf16[256,1024]{1,0:T(8,128)(2,1)}, bf16[256,1024]{1,0:T(8,128)(2,1)S(1)}, u32[]{:S(2)}) copy-start(bf16[256,1024]{1,0:T(8,128)(2,1)S(1)} %collective-permute-done.2.rest_0_.rest_1_) | copy-start | bytes 1572868
  25.7 33.9 %collective-permute-start.12 = (bf16[256,1024]{1,0:T(8,128)(2,1)}, bf16[256,1024]{1,0:T(8,128)(2,1)S(1)}, u32[]{:S(2)}, u32[]{:S(2)}) collective-permute-start(bf16[256,1024]{1,0:T(8,128)(2,1)} %pad_maximum_fusion.10), channel_id=1, source_target_pairs={{0,4},{1,5},{2,6},{3,7},{4,0},{5,1},{6,2},{7,3},{8,12},{9,13},{10,... | collective-permute-start | bytes 1572872 | tf_op jit(solution)/shard_map/ppermute | solution.py:25
  26.7 35.3 %collective-permute-start.13 = (bf16[256,1024]{1,0:T(8,128)(2,1)}, bf16[256,1024]{1,0:T(8,128)(2,1)}, u32[]{:S(2)}, u32[]{:S(2)}) collective-permute-start(bf16[256,1024]{1,0:T(8,128)(2,1)} %pad_maximum_fusion.11), channel_id=1, source_target_pairs={{0,8},{1,9},{2,10},{3,11},{4,12},{5,13},{6,14},{7,15},{8,0},{9,1},... | collective-permute-start | bytes 1572872 | tf_op jit(solution)/shard_map/ppermute | solution.py:25
  26.8 35.3 %collective-permute-start.10 = (bf16[256,1024]{1,0:T(8,128)(2,1)}, bf16[256,1024]{1,0:T(8,128)(2,1)}, u32[]{:S(2)}, u32[]{:S(2)}) collective-permute-start(bf16[256,1024]{1,0:T(8,128)(2,1)} %collective-permute-done.9.rest_0_.rest_1_), channel_id=1, source_target_pairs={{0,2},{2,4},{4,6},{6,8},{8,10},{10,12},{12,14},{16,18},{18,20},{20... | collective-permute-start | bytes 1572872 | tf_op jit(solution)/shard_map/ppermute | solution.py:209
  29.5 23.8 %copy-start.11 = (bf16[128,1024]{1,0:T(8,128)(2,1)S(1)}, bf16[128,1024]{1,0:T(8,128)(2,1)}, u32[]{:S(2)}) copy-start(bf16[128,1024]{1,0:T(8,128)(2,1)} %get-tuple-element.46) | copy-start | bytes 786436
  29.5 23.8 %copy-start.13 = (bf16[128,1024]{1,0:T(8,128)(2,1)S(1)}, bf16[128,1024]{1,0:T(8,128)(2,1)}, u32[]{:S(2)}) copy-start(bf16[128,1024]{1,0:T(8,128)(2,1)} %get-tuple-element.52) | copy-start | bytes 786436
  30.5 30.6 %copy-start.12 = (bf16[128,1024]{1,0:T(8,128)(2,1)S(1)}, bf16[128,1024]{1,0:T(8,128)(2,1)}, u32[]{:S(2)}) copy-start(bf16[128,1024]{1,0:T(8,128)(2,1)} %get-tuple-element.53) | copy-start | bytes 786436
  50.2 50.4 %collective-permute-start = (bf16[512,1024]{1,0:T(8,128)(2,1)}, bf16[512,1024]{1,0:T(8,128)(2,1)S(1)}, u32[]{:S(2)}, u32[]{:S(2)}) collective-permute-start(bf16[512,1024]{1,0:T(8,128)(2,1)} %pad_maximum_fusion), channel_id=1, source_target_pairs={{0,1},{1,2},{2,3},{3,4},{4,5},{5,6},{6,7},{7,8},{8,9},{9,10},{10,1... | collective-permute-start | bytes 3145736 | tf_op jit(solution)/shard_map/ppermute | solution.py:19
  59.6 2.4 %copy-start.10 = (bf16[256,1024]{1,0:T(8,128)(2,1)}, bf16[256,1024]{1,0:T(8,128)(2,1)S(1)}, u32[]{:S(2)}) copy-start(bf16[256,1024]{1,0:T(8,128)(2,1)S(1)} %collective-permute-done.12.rest_4_.rest_5_) | copy-start | bytes 1572868
  59.6 18.7 %collective-permute-start.3 = (bf16[256,1024]{1,0:T(8,128)(2,1)S(1)}, bf16[256,1024]{1,0:T(8,128)(2,1)}, u32[]{:S(2)}, u32[]{:S(2)}) collective-permute-start(bf16[256,1024]{1,0:T(8,128)(2,1)S(1)} %collective-permute-done.2.rest_0_.rest_1_), channel_id=1, source_target_pairs={{0,2},{2,4},{4,6},{6,8},{8,10},{10,12},{12,14},{16,18},{18,20},{20... | collective-permute-start | bytes 1572872 | tf_op jit(solution)/shard_map/ppermute | solution.py:209
  62.0 25.3 %collective-permute-start.4 = (bf16[256,1024]{1,0:T(8,128)(2,1)}, bf16[256,1024]{1,0:T(8,128)(2,1)S(1)}, u32[]{:S(2)}, u32[]{:S(2)}) collective-permute-start(bf16[256,1024]{1,0:T(8,128)(2,1)} %pad_maximum_fusion.4), channel_id=1, source_target_pairs={{0,2},{1,3},{2,0},{3,1},{4,6},{5,7},{6,4},{7,5},{8,10},{9,11},{10,... | collective-permute-start | bytes 1572872 | tf_op jit(solution)/shard_map/ppermute | solution.py:25
  62.0 2.3 %copy-start.7 = (bf16[512,1024]{1,0:T(8,128)(2,1)}, bf16[512,1024]{1,0:T(8,128)(2,1)S(1)}, u32[]{:S(2)}) copy-start(bf16[512,1024]{1,0:T(8,128)(2,1)S(1)} %collective-permute-done.7.pk_ref.pv_ref) | copy-start | bytes 3145732
  62.0 38.5 %collective-permute-start.5 = (bf16[256,1024]{1,0:T(8,128)(2,1)}, bf16[256,1024]{1,0:T(8,128)(2,1)}, u32[]{:S(2)}, u32[]{:S(2)}) collective-permute-start(bf16[256,1024]{1,0:T(8,128)(2,1)} %pad_maximum_fusion.5), channel_id=1, source_target_pairs={{0,4},{1,5},{2,6},{3,7},{4,0},{5,1},{6,2},{7,3},{8,12},{9,13},{10,... | collective-permute-start | bytes 1572872 | tf_op jit(solution)/shard_map/ppermute | solution.py:25
  62.1 38.4 %collective-permute-start.6 = (bf16[256,1024]{1,0:T(8,128)(2,1)}, bf16[256,1024]{1,0:T(8,128)(2,1)}, u32[]{:S(2)}, u32[]{:S(2)}) collective-permute-start(bf16[256,1024]{1,0:T(8,128)(2,1)} %pad_maximum_fusion.6), channel_id=1, source_target_pairs={{0,8},{1,9},{2,10},{3,11},{4,12},{5,13},{6,14},{7,15},{8,0},{9,1},... | collective-permute-start | bytes 1572872 | tf_op jit(solution)/shard_map/ppermute | solution.py:25
  87.3 13.3 %copy-start.9 = (bf16[256,1024]{1,0:T(8,128)(2,1)}, bf16[256,1024]{1,0:T(8,128)(2,1)S(1)}, u32[]{:S(2)}) copy-start(bf16[256,1024]{1,0:T(8,128)(2,1)S(1)} %collective-permute-done.4.rest_2_.rest_3_) | copy-start | bytes 1572868
  (1 other events, 1.0 us)

commit v10 on v6

--- a/solution.py
+++ b/solution.py
@@ -10,7 +10,7 @@
 HEADS = 16
 BLK = 128
 WIN = 4
-CHUNKS = 2
+CHUNK_HEADS = (12, 4)
 
 
 def passed_along(block, axis, distance):
@@ -141,10 +141,11 @@
     level_count = lax.axis_size("outer").bit_length() - 1
     meta = jnp.concatenate([widths, (device * panel_len)[None]]).astype(jnp.int32)
     wanted = [columns[jnp.bitwise_xor(device, 1 << b), b] - device * panel_len for b in range(level_count)]
-    width = features // CHUNKS
+    head_dim = features // HEADS
     context = None
-    for c in range(CHUNKS):
-        cols = slice(c * width, (c + 1) * width)
+    first_head = 0
+    for heads in CHUNK_HEADS:
+        cols = slice(first_head * head_dim, (first_head + heads) * head_dim)
         prev_keys, prev_values = passed_along((key_rows[:, cols], value_rows[:, cols]), "outer", 1)
         far = []
         for level_bit in range(level_count):
@@ -153,9 +154,8 @@
                 axis=0,
             )
             far.append(from_partner(outgoing, "outer", level_bit))
-        context = attend(
-            meta, queries, key_rows, value_rows, prev_keys, prev_values, far, c * (HEADS // CHUNKS), context
-        )
+        context = attend(meta, queries, key_rows, value_rows, prev_keys, prev_values, far, first_head, context)
+        first_head += heads
     return context
 
 

time: 108 us -> 130 us (1.20)
  the two profiles are of different devices: /device:TPU:29 before, /device:TPU:0 now
where the time goes in v10:
time: 130 us
  starting transfers between devices  54.2 us (42%)
  waiting for transfers between devices  33.5 us (26%)
  Pallas kernels  28.5 us (22%)
  local copies, waits for them, and re-layouts  8.76 us (7%)
  between operations  2.83 us (2%)
  other arithmetic  1.83 us (1%)
    ppermute x8, starting transfers between devices, from_partner(): return lax.ppermute(value, axis, pairs)  42 us
    ppermute x8, waiting for transfers between devices, from_partner(): return lax.ppermute(value, axis, pairs)  33.5 us
    pallas_call x2, Pallas kernels, attend(): pl.pallas_call(functools.partial(attend_kernel, level_count), out_shape=j...  28.5 us
    ppermute x4, starting transfers between devices, passed_along(): return lax.ppermute(block, axis, route)  12.2 us
    slice x2, local copies, waits for them, and re-layouts, on_device(): pick_blocks(value_rows, wanted[level_bit])[:, cols]  2.65 us
    unnamed x28, local copies, waits for them, and re-layouts  2.64 us
  transfers between devices with their start and end apart: 12, of which 3 were waited for; matrix products, arithmetic and copies ran while one was open for 2% of the time, Pallas kernels for 15%

profile of v10, /device:TPU:0, one launch (start us, length us, event | category | flops | bytes accessed | tf_op | source)
XLA Modules:
  0.0 129.6 jit_solution(12699924712836673299)
XLA Ops:
  0.0 1.4 %constant_dynamic-slice_fusion.2 = (s32[1,1,1]{0,2,1:T(1,128)}, s32[1,1,1]{0,2,1:T(1,128)}, s32[1,1,1]{0,2,1:T(1,128)}, s32[1,1,1]{0,2,1:T(1,128)}) fusion(s32[16,4,1]{0,2,1:T(1,128)} %param.9, s32[]{:T(128)S(6)} %select_n.42, s32[]{:T(128)S(6)} %select_n.18, s32[]{:T(128)S(6)} %select_n.16, s32[]{:T(128)S(6)} %select_n.40), kind=kLoop, calls=%fused_computation.10 | loop fusion | bytes 48 | tf_op jit(solution)/shard_map/dynamic_slice | solution.py:143
  3.9 2.6 %constant_dynamic-slice_fusion = (bf16[128,1536]{1,0:T(8,128)(2,1)}, bf16[128,1536]{1,0:T(8,128)(2,1)S(1)}, bf16[128,1536]{1,0:T(8,128)(2,1)S(1)}, bf16[128,1536]{1,0:T(8,128)(2,1)}) fusion(bf16[384,2048]{1,0:T(8,128)(2,1)} %ov_ref.3, s32[]{:T(128)S(6)} %select_n.43, s32[]{:T(128)S(6)} %select_n.41, s32[]{:T(128)S(6)} %select_n.19, s32[]{:T(128)S(6)} %select_n.17), kind=kLoop, calls=%fused_computation.8 | loop fusion | bytes 3145744 | tf_op jit(solution)/shard_map/slice | solution.py:153
  6.5 1.1 constant_dynamic-slice_fusion.1
  7.6 0.9 pad_maximum_fusion.2
  8.5 2.9 %collective-permute-start.10 = (bf16[256,1536]{1,0:T(8,128)(2,1)}, bf16[256,1536]{1,0:T(8,128)(2,1)}, u32[]{:S(2)}, u32[]{:S(2)}) collective-permute-start(bf16[256,1536]{1,0:T(8,128)(2,1)} %pad_maximum_fusion.2), channel_id=1, source_target_pairs={{0,4},{1,5},{2,6},{3,7},{4,0},{5,1},{6,2},{7,3},{8,12},{9,13},{10,... | collective-permute-start | bytes 2359304 | tf_op jit(solution)/shard_map/ppermute | solution.py:25
  11.6 0.1 collective-permute-start.2
  11.7 0.8 copy-done.5
  12.5 0.1 copy-done.6
  12.7 2.7 %collective-permute-start.11 = (bf16[256,1536]{1,0:T(8,128)(2,1)S(1)}, bf16[256,1536]{1,0:T(8,128)(2,1)}, u32[]{:S(2)}, u32[]{:S(2)}) collective-permute-start(bf16[256,1536]{1,0:T(8,128)(2,1)S(1)} %pad_maximum_fusion.3), channel_id=1, source_target_pairs={{0,8},{1,9},{2,10},{3,11},{4,12},{5,13},{6,14},{7,15},{8,0},{9,1},... | collective-permute-start | bytes 2359304 | tf_op jit(solution)/shard_map/ppermute | solution.py:25
  15.3 0.1 slice.70
  15.4 2.5 %collective-permute-start.6 = (bf16[384,1536]{1,0:T(8,128)(2,1)S(1)}, bf16[384,1536]{1,0:T(8,128)(2,1)}, u32[]{:S(2)}, u32[]{:S(2)}) collective-permute-start(bf16[384,1536]{1,0:T(8,128)(2,1)S(1)} %slice.70), channel_id=1, source_target_pairs={{0,1},{1,2},{2,3},{3,4},{4,5},{5,6},{6,7},{7,8},{8,9},{9,10},{10,1... | collective-permute-start | bytes 3538952 | tf_op jit(solution)/shard_map/ppermute | solution.py:19
  17.9 0.1 slice.71
  18.0 4.2 %collective-permute-start.7 = (bf16[384,1536]{1,0:T(8,128)(2,1)S(1)}, bf16[384,1536]{1,0:T(8,128)(2,1)}, u32[]{:S(2)}, u32[]{:S(2)}) collective-permute-start(bf16[384,1536]{1,0:T(8,128)(2,1)S(1)} %slice.71), channel_id=1, source_target_pairs={{0,1},{1,2},{2,3},{3,4},{4,5},{5,6},{6,7},{7,8},{8,9},{9,10},{10,1... | collective-permute-start | bytes 3538952 | tf_op jit(solution)/shard_map/ppermute | solution.py:19
  22.2 0.1 collective-permute-start.8
  22.4 22.7 %collective-permute-done.10.rest_4_.rest_5_ = bf16[256,1536]{1,0:T(8,128)(2,1)} collective-permute-done((bf16[256,1536]{1,0:T(8,128)(2,1)}, bf16[256,1536]{1,0:T(8,128)(2,1)}, u32[]{:S(2)}, u32[]{:S(2)}) %collective-permute-start.10) | collective-permute-done | bytes 786464 | tf_op jit(solution)/shard_map/ppermute | solution.py:25
  45.1 1.4 %collective-permute-start.9 = (bf16[256,1536]{1,0:T(8,128)(2,1)S(1)}, bf16[256,1536]{1,0:T(8,128)(2,1)}, u32[]{:S(2)}, u32[]{:S(2)}) collective-permute-start(bf16[256,1536]{1,0:T(8,128)(2,1)S(1)} %pad_maximum_fusion.1), channel_id=1, source_target_pairs={{0,2},{1,3},{2,0},{3,1},{4,6},{5,7},{6,4},{7,5},{8,10},{9,11},{10,... | collective-permute-start | bytes 2359304 | tf_op jit(solution)/shard_map/ppermute | solution.py:25
  46.5 0.8 slice.60
  47.4 2.2 %collective-permute-done.11.rest_6_.rest_7_ = bf16[256,1536]{1,0:T(8,128)(2,1)} collective-permute-done((bf16[256,1536]{1,0:T(8,128)(2,1)S(1)}, bf16[256,1536]{1,0:T(8,128)(2,1)}, u32[]{:S(2)}, u32[]{:S(2)}) %collective-permute-start.11) | collective-permute-done | bytes 786464 | tf_op jit(solution)/shard_map/ppermute | solution.py:25
  49.7 1.3 %collective-permute-start = (bf16[384,512]{1,0:T(8,128)(2,1)}, bf16[384,512]{1,0:T(8,128)(2,1)S(1)}, u32[]{:S(2)}, u32[]{:S(2)}) collective-permute-start(bf16[384,512]{1,0:T(8,128)(2,1)} %slice.60), channel_id=1, source_target_pairs={{0,1},{1,2},{2,3},{3,4},{4,5},{5,6},{6,7},{7,8},{8,9},{9,10},{10,1... | collective-permute-start | bytes 1179656 | tf_op jit(solution)/shard_map/ppermute | solution.py:19
  51.0 4.3 %collective-permute-start.1 = (bf16[384,512]{1,0:T(8,128)(2,1)S(1)}, bf16[384,512]{1,0:T(8,128)(2,1)S(1)}, u32[]{:S(2)}, u32[]{:S(2)}) collective-permute-start(bf16[384,512]{1,0:T(8,128)(2,1)S(1)} %slice.61), channel_id=1, source_target_pairs={{0,1},{1,2},{2,3},{3,4},{4,5},{5,6},{6,7},{7,8},{8,9},{9,10},{10,1... | collective-permute-start | bytes 1179656 | tf_op jit(solution)/shard_map/ppermute | solution.py:19
  55.3 0.7 pad_add_fusion.meta
  56.0 8.5 %collective-permute-done.9.rest_2_.rest_3_ = bf16[256,1536]{1,0:T(8,128)(2,1)} collective-permute-done((bf16[256,1536]{1,0:T(8,128)(2,1)S(1)}, bf16[256,1536]{1,0:T(8,128)(2,1)}, u32[]{:S(2)}, u32[]{:S(2)}) %collective-permute-start.9) | collective-permute-done | bytes 786464 | tf_op jit(solution)/shard_map/ppermute | solution.py:25
  64.5 2.6 %collective-permute-start.3 = (bf16[256,512]{1,0:T(8,128)(2,1)S(1)}, bf16[256,512]{1,0:T(8,128)(2,1)S(1)}, u32[]{:S(2)}, u32[]{:S(2)}) collective-permute-start(bf16[256,512]{1,0:T(8,128)(2,1)S(1)} %pad_maximum_fusion.5), channel_id=1, source_target_pairs={{0,2},{1,3},{2,0},{3,1},{4,6},{5,7},{6,4},{7,5},{8,10},{9,11},{10,... | collective-permute-start | bytes 786440 | tf_op jit(solution)/shard_map/ppermute | solution.py:25
  67.1 30.1 %collective-permute-start.4 = (bf16[256,512]{1,0:T(8,128)(2,1)S(1)}, bf16[256,512]{1,0:T(8,128)(2,1)S(1)}, u32[]{:S(2)}, u32[]{:S(2)}) collective-permute-start(bf16[256,512]{1,0:T(8,128)(2,1)S(1)} %pad_maximum_fusion.6), channel_id=1, source_target_pairs={{0,4},{1,5},{2,6},{3,7},{4,0},{5,1},{6,2},{7,3},{8,12},{9,13},{10,... | collective-permute-start | bytes 786440 | tf_op jit(solution)/shard_map/ppermute | solution.py:25
  97.2 2.1 %collective-permute-start.5 = (bf16[256,512]{1,0:T(8,128)(2,1)S(1)}, bf16[256,512]{1,0:T(8,128)(2,1)S(1)}, u32[]{:S(2)}, u32[]{:S(2)}) collective-permute-start(bf16[256,512]{1,0:T(8,128)(2,1)S(1)} %pad_maximum_fusion.7), channel_id=1, source_target_pairs={{0,8},{1,9},{2,10},{3,11},{4,12},{5,13},{6,14},{7,15},{8,0},{9,1},... | collective-permute-start | bytes 786440 | tf_op jit(solution)/shard_map/ppermute | solution.py:25
  99.3 20.0 %shard_map.55.rest_8_ = bf16[384,2048]{1,0:T(8,128)(2,1)} custom-call(s32[4]{0:T(128)} %pad_add_fusion.meta, bf16[384,2048]{1,0:T(8,128)(2,1)} %q_ref.3, bf16[384,2048]{1,0:T(8,128)(2,1)} %ok_ref.3, bf16[384,2048]{1,0:T(8,128)(2,1)} %ov_ref.3, bf16[384,1536]{1,0:T(8,128)(2,1)} %collective-permute-done.6.pk_ref, ...), custom_call_target="tpu_custom_call" | custom-call | flops 3019898880 | bytes 10223616 | tf_op jit(solution)/shard_map/pallas_call | solution.py:117
  119.4 0.6 copy-done.8
  120.0 0.1 copy-done.9
  120.2 0.1 copy-done.10
  120.3 0.1 copy-done.11
  120.3 0.8 copy-done.12
  121.1 8.5 %shard_map.56 = bf16[384,2048]{1,0:T(8,128)(2,1)} custom-call(s32[4]{0:T(128)} %pad_add_fusion.meta, bf16[384,2048]{1,0:T(8,128)(2,1)} %q_ref.3, bf16[384,2048]{1,0:T(8,128)(2,1)} %ok_ref.3, bf16[384,2048]{1,0:T(8,128)(2,1)} %ov_ref.3, bf16[384,512]{1,0:T(8,128)(2,1)} %copy-done.11, bf16[384,512]{1,0:T(8,128)(2,1)} %copy-done.12, ...), custom_call_target="tpu_custom_call", output_to_operand_aliasing={{}: (14, {})} | custom-call | flops 1006632960 | bytes 3407872 | tf_op jit(solution)/shard_map/pallas_call | solution.py:117
  (40 shorter events, 0.4 us)
Async XLA Ops:
  3.9 2.6 %copy-start = (bf16[384,2048]{1,0:T(8,128)(2,1)S(1)}, bf16[384,2048]{1,0:T(8,128)(2,1)}, u32[]{:S(2)}) copy-start(bf16[384,2048]{1,0:T(8,128)(2,1)} %ok_ref.3) | copy-start | bytes 4718596
  7.6 3.9 %copy-start.1 = (bf16[384,2048]{1,0:T(8,128)(2,1)S(1)}, bf16[384,2048]{1,0:T(8,128)(2,1)}, u32[]{:S(2)}) copy-start(bf16[384,2048]{1,0:T(8,128)(2,1)} %ov_ref.3) | copy-start | bytes 4718596
  8.5 36.6 %collective-permute-start.10 = (bf16[256,1536]{1,0:T(8,128)(2,1)}, bf16[256,1536]{1,0:T(8,128)(2,1)}, u32[]{:S(2)}, u32[]{:S(2)}) collective-permute-start(bf16[256,1536]{1,0:T(8,128)(2,1)} %pad_maximum_fusion.2), channel_id=1, source_target_pairs={{0,4},{1,5},{2,6},{3,7},{4,0},{5,1},{6,2},{7,3},{8,12},{9,13},{10,... | collective-permute-start | bytes 2359304 | tf_op jit(solution)/shard_map/ppermute | solution.py:25
  11.5 1.0 copy-start.5
  11.5 1.1 copy-start.6
  11.6 10.6 %collective-permute-start.2 = (bf16[256,512]{1,0:T(8,128)(2,1)S(1)}, bf16[256,512]{1,0:T(8,128)(2,1)S(1)}, u32[]{:S(2)}, u32[]{:S(2)}) collective-permute-start(bf16[256,512]{1,0:T(8,128)(2,1)S(1)} %pad_maximum_fusion.4), channel_id=1, source_target_pairs={{0,1},{1,0},{2,3},{3,2},{4,5},{5,4},{6,7},{7,6},{8,9},{9,8},{10,11... | collective-permute-start | bytes 786440 | tf_op jit(solution)/shard_map/ppermute | solution.py:25
  12.7 37.0 %collective-permute-start.11 = (bf16[256,1536]{1,0:T(8,128)(2,1)S(1)}, bf16[256,1536]{1,0:T(8,128)(2,1)}, u32[]{:S(2)}, u32[]{:S(2)}) collective-permute-start(bf16[256,1536]{1,0:T(8,128)(2,1)S(1)} %pad_maximum_fusion.3), channel_id=1, source_target_pairs={{0,8},{1,9},{2,10},{3,11},{4,12},{5,13},{6,14},{7,15},{8,0},{9,1},... | collective-permute-start | bytes 2359304 | tf_op jit(solution)/shard_map/ppermute | solution.py:25
  15.4 6.7 %copy-start.3 = (bf16[128,1536]{1,0:T(8,128)(2,1)S(1)}, bf16[128,1536]{1,0:T(8,128)(2,1)}, u32[]{:S(2)}) copy-start(bf16[128,1536]{1,0:T(8,128)(2,1)} %get-tuple-element.12) | copy-start | bytes 1179652
  15.4 6.7 %copy-start.4 = (bf16[128,1536]{1,0:T(8,128)(2,1)S(1)}, bf16[128,1536]{1,0:T(8,128)(2,1)}, u32[]{:S(2)}) copy-start(bf16[128,1536]{1,0:T(8,128)(2,1)} %get-tuple-element.8) | copy-start | bytes 1179652
  15.4 6.9 %copy-start.2 = (bf16[128,1536]{1,0:T(8,128)(2,1)S(1)}, bf16[128,1536]{1,0:T(8,128)(2,1)}, u32[]{:S(2)}) copy-start(bf16[128,1536]{1,0:T(8,128)(2,1)} %get-tuple-element.7) | copy-start | bytes 1179652
  15.4 51.6 %collective-permute-start.6 = (bf16[384,1536]{1,0:T(8,128)(2,1)S(1)}, bf16[384,1536]{1,0:T(8,128)(2,1)}, u32[]{:S(2)}, u32[]{:S(2)}) collective-permute-start(bf16[384,1536]{1,0:T(8,128)(2,1)S(1)} %slice.70), channel_id=1, source_target_pairs={{0,1},{1,2},{2,3},{3,4},{4,5},{5,6},{6,7},{7,8},{8,9},{9,10},{10,1... | collective-permute-start | bytes 3538952 | tf_op jit(solution)/shard_map/ppermute | solution.py:19
  18.0 79.2 %collective-permute-start.7 = (bf16[384,1536]{1,0:T(8,128)(2,1)S(1)}, bf16[384,1536]{1,0:T(8,128)(2,1)}, u32[]{:S(2)}, u32[]{:S(2)}) collective-permute-start(bf16[384,1536]{1,0:T(8,128)(2,1)S(1)} %slice.71), channel_id=1, source_target_pairs={{0,1},{1,2},{2,3},{3,4},{4,5},{5,6},{6,7},{7,8},{8,9},{9,10},{10,1... | collective-permute-start | bytes 3538952 | tf_op jit(solution)/shard_map/ppermute | solution.py:19
  22.2 25.2 %copy-start.7 = (bf16[256,512]{1,0:T(8,128)(2,1)}, bf16[256,512]{1,0:T(8,128)(2,1)S(1)}, u32[]{:S(2)}) copy-start(bf16[256,512]{1,0:T(8,128)(2,1)S(1)} %collective-permute-done.2.rest_0_.rest_1_) | copy-start | bytes 786436
  22.2 28.8 %collective-permute-start.8 = (bf16[256,1536]{1,0:T(8,128)(2,1)S(1)}, bf16[256,1536]{1,0:T(8,128)(2,1)}, u32[]{:S(2)}, u32[]{:S(2)}) collective-permute-start(bf16[256,1536]{1,0:T(8,128)(2,1)S(1)} %pad_maximum_fusion), channel_id=1, source_target_pairs={{0,1},{1,0},{2,3},{3,2},{4,5},{5,4},{6,7},{7,6},{8,9},{9,8},{10,11... | collective-permute-start | bytes 2359304 | tf_op jit(solution)/shard_map/ppermute | solution.py:25
  22.4 32.9 %copy-start.13 = (s32[3]{0:T(128)S(1)}, s32[3]{0:T(128)}, u32[]{:S(2)}) copy-start(s32[3]{0:T(128)} %param.8) | copy-start | bytes 40
  45.1 19.4 %collective-permute-start.9 = (bf16[256,1536]{1,0:T(8,128)(2,1)S(1)}, bf16[256,1536]{1,0:T(8,128)(2,1)}, u32[]{:S(2)}, u32[]{:S(2)}) collective-permute-start(bf16[256,1536]{1,0:T(8,128)(2,1)S(1)} %pad_maximum_fusion.1), channel_id=1, source_target_pairs={{0,2},{1,3},{2,0},{3,1},{4,6},{5,7},{6,4},{7,5},{8,10},{9,11},{10,... | collective-permute-start | bytes 2359304 | tf_op jit(solution)/shard_map/ppermute | solution.py:25
  49.7 69.7 %collective-permute-start = (bf16[384,512]{1,0:T(8,128)(2,1)}, bf16[384,512]{1,0:T(8,128)(2,1)S(1)}, u32[]{:S(2)}, u32[]{:S(2)}) collective-permute-start(bf16[384,512]{1,0:T(8,128)(2,1)} %slice.60), channel_id=1, source_target_pairs={{0,1},{1,2},{2,3},{3,4},{4,5},{5,6},{6,7},{7,8},{8,9},{9,10},{10,1... | collective-permute-start | bytes 1179656 | tf_op jit(solution)/shard_map/ppermute | solution.py:19
  51.0 68.4 %collective-permute-start.1 = (bf16[384,512]{1,0:T(8,128)(2,1)S(1)}, bf16[384,512]{1,0:T(8,128)(2,1)S(1)}, u32[]{:S(2)}, u32[]{:S(2)}) collective-permute-start(bf16[384,512]{1,0:T(8,128)(2,1)S(1)} %slice.61), channel_id=1, source_target_pairs={{0,1},{1,2},{2,3},{3,4},{4,5},{5,6},{6,7},{7,8},{8,9},{9,10},{10,1... | collective-permute-start | bytes 1179656 | tf_op jit(solution)/shard_map/ppermute | solution.py:19
  64.5 54.8 %collective-permute-start.3 = (bf16[256,512]{1,0:T(8,128)(2,1)S(1)}, bf16[256,512]{1,0:T(8,128)(2,1)S(1)}, u32[]{:S(2)}, u32[]{:S(2)}) collective-permute-start(bf16[256,512]{1,0:T(8,128)(2,1)S(1)} %pad_maximum_fusion.5), channel_id=1, source_target_pairs={{0,2},{1,3},{2,0},{3,1},{4,6},{5,7},{6,4},{7,5},{8,10},{9,11},{10,... | collective-permute-start | bytes 786440 | tf_op jit(solution)/shard_map/ppermute | solution.py:25
  67.1 52.3 %collective-permute-start.4 = (bf16[256,512]{1,0:T(8,128)(2,1)S(1)}, bf16[256,512]{1,0:T(8,128)(2,1)S(1)}, u32[]{:S(2)}, u32[]{:S(2)}) collective-permute-start(bf16[256,512]{1,0:T(8,128)(2,1)S(1)} %pad_maximum_fusion.6), channel_id=1, source_target_pairs={{0,4},{1,5},{2,6},{3,7},{4,0},{5,1},{6,2},{7,3},{8,12},{9,13},{10,... | collective-permute-start | bytes 786440 | tf_op jit(solution)/shard_map/ppermute | solution.py:25
  97.2 22.2 %collective-permute-start.5 = (bf16[256,512]{1,0:T(8,128)(2,1)S(1)}, bf16[256,512]{1,0:T(8,128)(2,1)S(1)}, u32[]{:S(2)}, u32[]{:S(2)}) collective-permute-start(bf16[256,512]{1,0:T(8,128)(2,1)S(1)} %pad_maximum_fusion.7), channel_id=1, source_target_pairs={{0,8},{1,9},{2,10},{3,11},{4,12},{5,13},{6,14},{7,15},{8,0},{9,1},... | collective-permute-start | bytes 786440 | tf_op jit(solution)/shard_map/ppermute | solution.py:25
  119.3 0.7 copy-start.8
  119.3 0.8 copy-start.9
  119.4 0.9 copy-start.10
  119.4 1.0 copy-start.11
  120.3 0.8 copy-start.12

commit v11 on v10

--- a/solution.py
+++ b/solution.py
@@ -144,17 +144,20 @@
     head_dim = features // HEADS
     context = None
     first_head = 0
+    arrived = ()
     for heads in CHUNK_HEADS:
         cols = slice(first_head * head_dim, (first_head + heads) * head_dim)
-        prev_keys, prev_values = passed_along((key_rows[:, cols], value_rows[:, cols]), "outer", 1)
+        key_src, value_src, *_ = lax.optimization_barrier((key_rows, value_rows, *arrived))
+        prev_keys, prev_values = passed_along((key_src[:, cols], value_src[:, cols]), "outer", 1)
         far = []
         for level_bit in range(level_count):
             outgoing = jnp.concatenate(
-                [pick_blocks(key_rows, wanted[level_bit])[:, cols], pick_blocks(value_rows, wanted[level_bit])[:, cols]],
+                [pick_blocks(key_src, wanted[level_bit])[:, cols], pick_blocks(value_src, wanted[level_bit])[:, cols]],
                 axis=0,
             )
             far.append(from_partner(outgoing, "outer", level_bit))
         context = attend(meta, queries, key_rows, value_rows, prev_keys, prev_values, far, first_head, context)
+        arrived = (prev_keys, prev_values, *far)
         first_head += heads
     return context
 

time: 130 us -> 123 us (0.946)
  starting transfers between devices: 54.2 us -> 43.6 us
  other arithmetic: 1.83 us -> 4.45 us
    ppermute x8, starting transfers between devices: 42 us -> 12.1 us  [from_partner(): return lax.ppermute(value, axis, pairs)]
    ppermute x4, starting transfers between devices: 12.2 us -> 31.5 us  [passed_along(): return lax.ppermute(block, axis, route)]
    concatenate x8, other arithmetic: 1.16 us -> 3.8 us  [on_device(): jnp.concatenate([pick_blocks(key_src, wanted[level_bit])[:, cols], pick_b...]
    slice x8 -> x7, local copies, waits for them, and re-layouts: 4.74 us -> 5.97 us  [the longest x2 2.13 us: on_device(): pick_blocks(value_src, wanted[level_bit])[:, cols]]
    unnamed x28 -> x18, local copies, waits for them, and re-layouts: 2.64 us -> 1.7 us
  transfers between devices with their start and end apart: 12 -> 12, of which waited for: 3 -> 3; matrix products, arithmetic and copies ran while one was open for 2% -> 7% of each run, Pallas kernels for 15% -> 16%
where the time goes in v11:
time: 123 us
  starting transfers between devices  43.6 us (35%)
  waiting for transfers between devices  34.7 us (28%)
  Pallas kernels  28.5 us (23%)
  local copies, waits for them, and re-layouts  9.04 us (7%)
  other arithmetic  4.45 us (4%)
  between operations  2.75 us (2%)
    ppermute x8, waiting for transfers between devices, from_partner(): return lax.ppermute(value, axis, pairs)  34.6 us
    ppermute x4, starting transfers between devices, passed_along(): return lax.ppermute(block, axis, route)  31.5 us
    pallas_call x2, Pallas kernels, attend(): pl.pallas_call(functools.partial(attend_kernel, level_count), out_shape=j...  28.5 us
    ppermute x8, starting transfers between devices, from_partner(): return lax.ppermute(value, axis, pairs)  12.1 us
    concatenate x8, other arithmetic, on_device(): jnp.concatenate([pick_blocks(key_src, wanted[level_bit])[:, cols], pick_b...  3.8 us
  transfers between devices with their start and end apart: 12, of which 3 were waited for; matrix products, arithmetic and copies ran while one was open for 7% of the time, Pallas kernels for 16%

profile of v11, /device:TPU:0, one launch (start us, length us, event | category | flops | bytes accessed | tf_op | source)
XLA Modules:
  0.0 123.0 jit_solution(3435476796325592079)
XLA Ops:
  0.0 1.4 %constant_dynamic-slice_fusion.2 = (s32[1,1,1]{0,2,1:T(1,128)}, s32[1,1,1]{0,2,1:T(1,128)}, s32[1,1,1]{0,2,1:T(1,128)}, s32[1,1,1]{0,2,1:T(1,128)}) fusion(s32[16,4,1]{0,2,1:T(1,128)} %param.9, s32[]{:T(128)S(6)} %select_n.42, s32[]{:T(128)S(6)} %select_n.18, s32[]{:T(128)S(6)} %select_n.16, s32[]{:T(128)S(6)} %select_n.40), kind=kLoop, calls=%fused_computation.10 | loop fusion | bytes 48 | tf_op jit(solution)/shard_map/dynamic_slice | solution.py:143
  3.9 2.1 %constant_dynamic-slice_fusion = (bf16[128,1536]{1,0:T(8,128)(2,1)S(1)}, bf16[128,1536]{1,0:T(8,128)(2,1)S(1)}, bf16[128,1536]{1,0:T(8,128)(2,1)S(1)}, bf16[128,...) fusion(bf16[384,2048]{1,0:T(8,128)(2,1)} %ov_ref.3, ...), kind=kLoop, calls=%fused_computation.8 | loop fusion | bytes 6291472 | tf_op jit(solution)/shard_map/slice | solution.py:155
  6.1 0.7 collective-permute-start.2
  6.8 0.9 pad_maximum_fusion.1
  7.7 2.4 %collective-permute-start.3 = (bf16[256,1536]{1,0:T(8,128)(2,1)}, bf16[256,1536]{1,0:T(8,128)(2,1)}, u32[]{:S(2)}, u32[]{:S(2)}) collective-permute-start(bf16[256,1536]{1,0:T(8,128)(2,1)} %pad_maximum_fusion.1), channel_id=1, source_target_pairs={{0,2},{1,3},{2,0},{3,1},{4,6},{5,7},{6,4},{7,5},{8,10},{9,11},{10,... | collective-permute-start | bytes 2359304 | tf_op jit(solution)/shard_map/ppermute | solution.py:25
  10.2 1.1 slice.60
  11.3 3.1 %collective-permute-start = (bf16[384,1536]{1,0:T(8,128)(2,1)}, bf16[384,1536]{1,0:T(8,128)(2,1)}, u32[]{:S(2)}, u32[]{:S(2)}) collective-permute-start(bf16[384,1536]{1,0:T(8,128)(2,1)} %slice.60), channel_id=1, source_target_pairs={{0,1},{1,2},{2,3},{3,4},{4,5},{5,6},{6,7},{7,8},{8,9},{9,10},{10,1... | collective-permute-start | bytes 3538952 | tf_op jit(solution)/shard_map/ppermute | solution.py:19
  14.4 1.1 slice.61
  15.5 2.4 %collective-permute-start.1 = (bf16[384,1536]{1,0:T(8,128)(2,1)}, bf16[384,1536]{1,0:T(8,128)(2,1)}, u32[]{:S(2)}, u32[]{:S(2)}) collective-permute-start(bf16[384,1536]{1,0:T(8,128)(2,1)} %slice.61), channel_id=1, source_target_pairs={{0,1},{1,2},{2,3},{3,4},{4,5},{5,6},{6,7},{7,8},{8,9},{9,10},{10,1... | collective-permute-start | bytes 3538952 | tf_op jit(solution)/shard_map/ppermute | solution.py:19
  17.9 1.0 pad_maximum_fusion.2
  18.9 0.7 collective-permute-start.4
  19.7 1.0 pad_maximum_fusion.3
  20.7 2.4 %collective-permute-start.5 = (bf16[256,1536]{1,0:T(8,128)(2,1)}, bf16[256,1536]{1,0:T(8,128)(2,1)}, u32[]{:S(2)}, u32[]{:S(2)}) collective-permute-start(bf16[256,1536]{1,0:T(8,128)(2,1)} %pad_maximum_fusion.3), channel_id=1, source_target_pairs={{0,8},{1,9},{2,10},{3,11},{4,12},{5,13},{6,14},{7,15},{8,0},{9,1},... | collective-permute-start | bytes 2359304 | tf_op jit(solution)/shard_map/ppermute | solution.py:25
  23.1 0.7 pad_add_fusion.meta
  23.8 4.9 %collective-permute-done.3.rest_2_.rest_3_ = bf16[256,1536]{1,0:T(8,128)(2,1)} collective-permute-done((bf16[256,1536]{1,0:T(8,128)(2,1)}, bf16[256,1536]{1,0:T(8,128)(2,1)}, u32[]{:S(2)}, u32[]{:S(2)}) %collective-permute-start.3) | collective-permute-done | bytes 786464 | tf_op jit(solution)/shard_map/ppermute | solution.py:25
  28.7 24.7 %collective-permute-done.4.rest_4_.rest_5_ = bf16[256,1536]{1,0:T(8,128)(2,1)} collective-permute-done((bf16[256,1536]{1,0:T(8,128)(2,1)}, bf16[256,1536]{1,0:T(8,128)(2,1)}, u32[]{:S(2)}, u32[]{:S(2)}) %collective-permute-start.4) | collective-permute-done | bytes 786464 | tf_op jit(solution)/shard_map/ppermute | solution.py:25
  53.4 5.0 %collective-permute-done.5.rest_6_.rest_7_ = bf16[256,1536]{1,0:T(8,128)(2,1)} collective-permute-done((bf16[256,1536]{1,0:T(8,128)(2,1)}, bf16[256,1536]{1,0:T(8,128)(2,1)}, u32[]{:S(2)}, u32[]{:S(2)}) %collective-permute-start.5) | collective-permute-done | bytes 786464 | tf_op jit(solution)/shard_map/ppermute | solution.py:25
  58.6 3.9 %collective-permute-start.11 = (bf16[256,512]{1,0:T(8,128)(2,1)S(1)}, bf16[256,512]{1,0:T(8,128)(2,1)S(1)}, u32[]{:S(2)}, u32[]{:S(2)}) collective-permute-start(bf16[256,512]{1,0:T(8,128)(2,1)S(1)} %pad_maximum_fusion.7), channel_id=1, source_target_pairs={{0,8},{1,9},{2,10},{3,11},{4,12},{5,13},{6,14},{7,15},{8,0},{9,1},... | collective-permute-start | bytes 786440 | tf_op jit(solution)/shard_map/ppermute | solution.py:25
  62.5 0.7 pad_maximum_fusion.6
  63.2 0.8 slice.70
  64.0 0.8 slice.71
  64.8 1.4 %collective-permute-start.10 = (bf16[256,512]{1,0:T(8,128)(2,1)}, bf16[256,512]{1,0:T(8,128)(2,1)S(1)}, u32[]{:S(2)}, u32[]{:S(2)}) collective-permute-start(bf16[256,512]{1,0:T(8,128)(2,1)} %pad_maximum_fusion.6), channel_id=1, source_target_pairs={{0,4},{1,5},{2,6},{3,7},{4,0},{5,1},{6,2},{7,3},{8,12},{9,13},{10,... | collective-permute-start | bytes 786440 | tf_op jit(solution)/shard_map/ppermute | solution.py:25
  66.3 24.0 %collective-permute-start.6 = (bf16[384,512]{1,0:T(8,128)(2,1)}, bf16[384,512]{1,0:T(8,128)(2,1)S(1)}, u32[]{:S(2)}, u32[]{:S(2)}) collective-permute-start(bf16[384,512]{1,0:T(8,128)(2,1)} %slice.70), channel_id=1, source_target_pairs={{0,1},{1,2},{2,3},{3,4},{4,5},{5,6},{6,7},{7,8},{8,9},{9,10},{10,1... | collective-permute-start | bytes 1179656 | tf_op jit(solution)/shard_map/ppermute | solution.py:19
  90.3 1.9 %collective-permute-start.7 = (bf16[384,512]{1,0:T(8,128)(2,1)}, bf16[384,512]{1,0:T(8,128)(2,1)S(1)}, u32[]{:S(2)}, u32[]{:S(2)}) collective-permute-start(bf16[384,512]{1,0:T(8,128)(2,1)} %slice.71), channel_id=1, source_target_pairs={{0,1},{1,2},{2,3},{3,4},{4,5},{5,6},{6,7},{7,8},{8,9},{9,10},{10,1... | collective-permute-start | bytes 1179656 | tf_op jit(solution)/shard_map/ppermute | solution.py:19
  92.3 0.5 collective-permute-start.8
  92.7 20.0 %shard_map.55.rest_8_ = bf16[384,2048]{1,0:T(8,128)(2,1)} custom-call(s32[4]{0:T(128)} %pad_add_fusion.meta, bf16[384,2048]{1,0:T(8,128)(2,1)} %q_ref.3, bf16[384,2048]{1,0:T(8,128)(2,1)} %ok_ref.3, bf16[384,2048]{1,0:T(8,128)(2,1)} %ov_ref.3, bf16[384,1536]{1,0:T(8,128)(2,1)} %collective-permute-done.pk_ref, ...), custom_call_target="tpu_custom_call" | custom-call | flops 3019898880 | bytes 10223616 | tf_op jit(solution)/shard_map/pallas_call | solution.py:117
  112.9 0.6 copy-done.3
  113.5 0.1 copy-done.4
  113.6 0.1 copy-done.5
  113.7 0.1 copy-done.6
  113.8 0.7 copy-done.7
  114.6 8.5 %shard_map.56 = bf16[384,2048]{1,0:T(8,128)(2,1)} custom-call(s32[4]{0:T(128)} %pad_add_fusion.meta, bf16[384,2048]{1,0:T(8,128)(2,1)} %q_ref.3, bf16[384,2048]{1,0:T(8,128)(2,1)} %ok_ref.3, bf16[384,2048]{1,0:T(8,128)(2,1)} %ov_ref.3, bf16[384,512]{1,0:T(8,128)(2,1)} %copy-done.6, bf16[384,512]{1,0:T(8,128)(2,1)} %copy-done.7, ...), custom_call_target="tpu_custom_call", output_to_operand_aliasing={{}: (14, {})} | custom-call | flops 1006632960 | bytes 3407872 | tf_op jit(solution)/shard_map/pallas_call | solution.py:117
  (29 shorter events, 0.3 us)
Async XLA Ops:
  6.0 4.2 %copy-start = (bf16[384,2048]{1,0:T(8,128)(2,1)S(1)}, bf16[384,2048]{1,0:T(8,128)(2,1)}, u32[]{:S(2)}) copy-start(bf16[384,2048]{1,0:T(8,128)(2,1)} %ok_ref.3) | copy-start | bytes 4718596
  6.1 14.6 %collective-permute-start.2 = (bf16[256,1536]{1,0:T(8,128)(2,1)S(1)}, bf16[256,1536]{1,0:T(8,128)(2,1)}, u32[]{:S(2)}, u32[]{:S(2)}) collective-permute-start(bf16[256,1536]{1,0:T(8,128)(2,1)S(1)} %pad_maximum_fusion), channel_id=1, source_target_pairs={{0,1},{1,0},{2,3},{3,2},{4,5},{5,4},{6,7},{7,6},{8,9},{9,8},{10,11... | collective-permute-start | bytes 2359304 | tf_op jit(solution)/shard_map/ppermute | solution.py:25
  6.8 7.6 %copy-start.1 = (bf16[384,2048]{1,0:T(8,128)(2,1)S(1)}, bf16[384,2048]{1,0:T(8,128)(2,1)}, u32[]{:S(2)}) copy-start(bf16[384,2048]{1,0:T(8,128)(2,1)} %ov_ref.3) | copy-start | bytes 4718596
  7.7 20.9 %collective-permute-start.3 = (bf16[256,1536]{1,0:T(8,128)(2,1)}, bf16[256,1536]{1,0:T(8,128)(2,1)}, u32[]{:S(2)}, u32[]{:S(2)}) collective-permute-start(bf16[256,1536]{1,0:T(8,128)(2,1)} %pad_maximum_fusion.1), channel_id=1, source_target_pairs={{0,2},{1,3},{2,0},{3,1},{4,6},{5,7},{6,4},{7,5},{8,10},{9,11},{10,... | collective-permute-start | bytes 2359304 | tf_op jit(solution)/shard_map/ppermute | solution.py:25
  11.3 47.2 %collective-permute-start = (bf16[384,1536]{1,0:T(8,128)(2,1)}, bf16[384,1536]{1,0:T(8,128)(2,1)}, u32[]{:S(2)}, u32[]{:S(2)}) collective-permute-start(bf16[384,1536]{1,0:T(8,128)(2,1)} %slice.60), channel_id=1, source_target_pairs={{0,1},{1,2},{2,3},{3,4},{4,5},{5,6},{6,7},{7,8},{8,9},{9,10},{10,1... | collective-permute-start | bytes 3538952 | tf_op jit(solution)/shard_map/ppermute | solution.py:19
  15.5 42.9 %collective-permute-start.1 = (bf16[384,1536]{1,0:T(8,128)(2,1)}, bf16[384,1536]{1,0:T(8,128)(2,1)}, u32[]{:S(2)}, u32[]{:S(2)}) collective-permute-start(bf16[384,1536]{1,0:T(8,128)(2,1)} %slice.61), channel_id=1, source_target_pairs={{0,1},{1,2},{2,3},{3,4},{4,5},{5,6},{6,7},{7,8},{8,9},{9,10},{10,1... | collective-permute-start | bytes 3538952 | tf_op jit(solution)/shard_map/ppermute | solution.py:19
  17.9 5.2 %copy-start.8 = (s32[3]{0:T(128)S(1)}, s32[3]{0:T(128)}, u32[]{:S(2)}) copy-start(s32[3]{0:T(128)} %param.8) | copy-start | bytes 40
  18.9 34.5 %collective-permute-start.4 = (bf16[256,1536]{1,0:T(8,128)(2,1)}, bf16[256,1536]{1,0:T(8,128)(2,1)}, u32[]{:S(2)}, u32[]{:S(2)}) collective-permute-start(bf16[256,1536]{1,0:T(8,128)(2,1)} %pad_maximum_fusion.2), channel_id=1, source_target_pairs={{0,4},{1,5},{2,6},{3,7},{4,0},{5,1},{6,2},{7,3},{8,12},{9,13},{10,... | collective-permute-start | bytes 2359304 | tf_op jit(solution)/shard_map/ppermute | solution.py:25
  20.7 37.7 %collective-permute-start.5 = (bf16[256,1536]{1,0:T(8,128)(2,1)}, bf16[256,1536]{1,0:T(8,128)(2,1)}, u32[]{:S(2)}, u32[]{:S(2)}) collective-permute-start(bf16[256,1536]{1,0:T(8,128)(2,1)} %pad_maximum_fusion.3), channel_id=1, source_target_pairs={{0,8},{1,9},{2,10},{3,11},{4,12},{5,13},{6,14},{7,15},{8,0},{9,1},... | collective-permute-start | bytes 2359304 | tf_op jit(solution)/shard_map/ppermute | solution.py:25
  58.6 33.7 %collective-permute-start.11 = (bf16[256,512]{1,0:T(8,128)(2,1)S(1)}, bf16[256,512]{1,0:T(8,128)(2,1)S(1)}, u32[]{:S(2)}, u32[]{:S(2)}) collective-permute-start(bf16[256,512]{1,0:T(8,128)(2,1)S(1)} %pad_maximum_fusion.7), channel_id=1, source_target_pairs={{0,8},{1,9},{2,10},{3,11},{4,12},{5,13},{6,14},{7,15},{8,0},{9,1},... | collective-permute-start | bytes 786440 | tf_op jit(solution)/shard_map/ppermute | solution.py:25
  64.8 48.0 %collective-permute-start.10 = (bf16[256,512]{1,0:T(8,128)(2,1)}, bf16[256,512]{1,0:T(8,128)(2,1)S(1)}, u32[]{:S(2)}, u32[]{:S(2)}) collective-permute-start(bf16[256,512]{1,0:T(8,128)(2,1)} %pad_maximum_fusion.6), channel_id=1, source_target_pairs={{0,4},{1,5},{2,6},{3,7},{4,0},{5,1},{6,2},{7,3},{8,12},{9,13},{10,... | collective-permute-start | bytes 786440 | tf_op jit(solution)/shard_map/ppermute | solution.py:25
  66.2 46.6 %collective-permute-start.9 = (bf16[256,512]{1,0:T(8,128)(2,1)S(1)}, bf16[256,512]{1,0:T(8,128)(2,1)S(1)}, u32[]{:S(2)}, u32[]{:S(2)}) collective-permute-start(bf16[256,512]{1,0:T(8,128)(2,1)S(1)} %pad_maximum_fusion.5), channel_id=1, source_target_pairs={{0,2},{1,3},{2,0},{3,1},{4,6},{5,7},{6,4},{7,5},{8,10},{9,11},{10,... | collective-permute-start | bytes 786440 | tf_op jit(solution)/shard_map/ppermute | solution.py:25
  66.3 46.6 %collective-permute-start.6 = (bf16[384,512]{1,0:T(8,128)(2,1)}, bf16[384,512]{1,0:T(8,128)(2,1)S(1)}, u32[]{:S(2)}, u32[]{:S(2)}) collective-permute-start(bf16[384,512]{1,0:T(8,128)(2,1)} %slice.70), channel_id=1, source_target_pairs={{0,1},{1,2},{2,3},{3,4},{4,5},{5,6},{6,7},{7,8},{8,9},{9,10},{10,1... | collective-permute-start | bytes 1179656 | tf_op jit(solution)/shard_map/ppermute | solution.py:19
  90.3 22.5 %collective-permute-start.7 = (bf16[384,512]{1,0:T(8,128)(2,1)}, bf16[384,512]{1,0:T(8,128)(2,1)S(1)}, u32[]{:S(2)}, u32[]{:S(2)}) collective-permute-start(bf16[384,512]{1,0:T(8,128)(2,1)} %slice.71), channel_id=1, source_target_pairs={{0,1},{1,2},{2,3},{3,4},{4,5},{5,6},{6,7},{7,8},{8,9},{9,10},{10,1... | collective-permute-start | bytes 1179656 | tf_op jit(solution)/shard_map/ppermute | solution.py:19
  92.3 20.5 %copy-start.2 = (bf16[256,512]{1,0:T(8,128)(2,1)}, bf16[256,512]{1,0:T(8,128)(2,1)S(1)}, u32[]{:S(2)}) copy-start(bf16[256,512]{1,0:T(8,128)(2,1)S(1)} %collective-permute-done.11.rest_6_.rest_7_) | copy-start | bytes 786436
  92.3 20.5 %collective-permute-start.8 = (bf16[256,512]{1,0:T(8,128)(2,1)S(1)}, bf16[256,512]{1,0:T(8,128)(2,1)S(1)}, u32[]{:S(2)}, u32[]{:S(2)}) collective-permute-start(bf16[256,512]{1,0:T(8,128)(2,1)S(1)} %pad_maximum_fusion.4), channel_id=1, source_target_pairs={{0,1},{1,0},{2,3},{3,2},{4,5},{5,4},{6,7},{7,6},{8,9},{9,8},{10,11... | collective-permute-start | bytes 786440 | tf_op jit(solution)/shard_map/ppermute | solution.py:25
  112.8 0.7 copy-start.3
  112.8 0.8 copy-start.4
  112.8 0.9 copy-start.5
  112.9 1.0 copy-start.6
  113.8 0.7 copy-start.7

commit v12 on v6

v12 whole, which is shorter than its diff:
```python
import functools

import jax
import jax.numpy as jnp
from jax import lax
from jax.experimental import pallas as pl
from jax.experimental.pallas import tpu as pltpu
from jax.sharding import PartitionSpec as P

HEADS = 16
BLK = 128
WIN = 4
LOG2E = 1.4426950408889634
CHUNKS = 2


def passed_along(block, axis, distance):
    devices = range(lax.axis_size(axis))
    route = [(i - distance, i) for i in devices if i - distance in devices]
    return lax.ppermute(block, axis, route)


def from_partner(value, axis, stride):
    mask = 2**stride
    pairs = [(source, source ^ mask) for source in range(lax.axis_size(axis))]
    return lax.ppermute(value, axis, pairs)


def pick_blocks(source, block_index):
    return lax.dynamic_slice_in_dim(source, block_index[0] * BLK, BLK, 0)


def _nt(a, b):
    return lax.dot_general(a, b, (((1,), (1,)), ((), ())), preferred_element_type=jnp.float32)


def _nn(a, b):
    return lax.dot_general(a, b, (((1,), (0,)), ((), ())), preferred_element_type=jnp.float32)


def attend_kernel(level_count, bias_ref, q_ref, ok_ref, ov_ref, pk_ref, pv_ref, *rest):
    far_refs = rest[: 2 * level_count]
    out_ref = rest[-1]
    rows, head_dim = q_ref.shape
    scale = head_dim ** (-0.5) * LOG2E

    q = q_ref[...]
    s_prev = _nt(q, pk_ref[...]) * scale + bias_ref[:, :rows]
    s_own = _nt(q, ok_ref[...]) * scale + bias_ref[:, rows:]
    m_w = jnp.maximum(s_own.max(-1, keepdims=True), s_prev.max(-1, keepdims=True))
    e_own = jnp.exp2(s_own - m_w)
    e_prev = jnp.exp2(s_prev - m_w)
    l_w = e_own.sum(-1, keepdims=True) + e_prev.sum(-1, keepdims=True)
    o_w = _nn(e_own.astype(jnp.bfloat16), ov_ref[...]) + _nn(e_prev.astype(jnp.bfloat16), pv_ref[...])

    maxes, totals, sums = [m_w], [l_w], [o_w]
    for b in range(level_count):
        s = _nt(q, far_refs[2 * b][...]) * scale
        m = s.max(-1, keepdims=True)
        e = jnp.exp2(s - m)
        maxes.append(m)
        totals.append(e.sum(-1, keepdims=True))
        sums.append(_nn(e.astype(jnp.bfloat16), far_refs[2 * b + 1][...]))

    top = maxes[0]
    for m in maxes[1:]:
        top = jnp.maximum(top, m)
    total = jnp.zeros_like(l_w)
    output = jnp.zeros_like(o_w)
    for m, l, o in zip(maxes, totals, sums):
        factor = jnp.exp2(m - top)
        total = total + l * factor
        output = output + o * factor
    out_ref[...] = (output / total).astype(out_ref.dtype)


def window_bias(widths, first_block, rows):
    panel_len = rows // BLK
    row = lax.broadcasted_iota(jnp.int32, (rows, rows), 0)
    col = lax.broadcasted_iota(jnp.int32, (rows, rows), 1)
    q_blk = row // BLK
    k_blk = col // BLK
    width = jnp.zeros((rows, rows), jnp.int32)
    for r in range(panel_len):
        width = jnp.where(q_blk == r, widths[r], width)
    own_off = q_blk - k_blk
    own_vis = (own_off >= 0) & (own_off < width) & ((own_off > 0) | (col <= row))
    prev_off = q_blk + panel_len - k_blk
    prev_vis = (prev_off < width) & (first_block + q_blk - prev_off >= 0)
    return jnp.concatenate(
        [jnp.where(prev_vis, 0.0, -jnp.inf), jnp.where(own_vis, 0.0, -jnp.inf)], axis=1
    ).astype(jnp.float32)


def attend(bias, queries, own_k, own_v, prev_k, prev_v, far, first_head, prior=None):
    rows, features = queries.shape
    head_dim = features // HEADS
    heads = prev_k.shape[1] // head_dim
    level_count = len(far)
    far_rows = far[0].shape[0] // 2
    whole = pl.BlockSpec((rows, head_dim), lambda h: (0, h + first_head))
    part = pl.BlockSpec((rows, head_dim), lambda h: (0, h))
    far_specs = []
    for _ in range(level_count):
        far_specs.append(pl.BlockSpec((far_rows, head_dim), lambda h: (0, h)))
        far_specs.append(pl.BlockSpec((far_rows, head_dim), lambda h: (1, h)))
    far_args = []
    for block in far:
        far_args += [block, block]
    keys = 2 * rows + level_count * far_rows
    args = [bias, queries, own_k, own_v, prev_k, prev_v, *far_args]
    in_specs = [pl.BlockSpec((rows, 2 * rows), lambda h: (0, 0))] + [whole] * 3 + [part] * 2 + far_specs
    aliases = {}
    if prior is not None:
        aliases = {len(args): 0}
        args.append(prior)
        in_specs.append(pl.BlockSpec(memory_space=pl.ANY))
    return pl.pallas_call(
        functools.partial(attend_kernel, level_count),
        out_shape=jax.ShapeDtypeStruct((rows, features), queries.dtype),
        grid=(heads,),
        in_specs=in_specs,
        out_specs=whole,
        input_output_aliases=aliases,
        compiler_params=pltpu.CompilerParams(dimension_semantics=("arbitrary",)),
        cost_estimate=pl.CostEstimate(
            flops=4 * rows * keys * head_dim * heads,
            transcendentals=rows * keys * heads,
            bytes_accessed=2 * head_dim * heads * (6 * rows + 2 * level_count * far_rows),
        ),
    )(*args)


def on_device(queries, key_rows, value_rows, widths, columns):
    token_count, features = queries.shape
    panel_len = token_count // BLK
    device = lax.axis_index("outer")
    level_count = lax.axis_size("outer").bit_length() - 1
    bias = window_bias(widths, device * panel_len, token_count)
    wanted = [columns[jnp.bitwise_xor(device, 1 << b), b] - device * panel_len for b in range(level_count)]
    width = features // CHUNKS
    context = None
    for c in range(CHUNKS):
        cols = slice(c * width, (c + 1) * width)
        prev_keys, prev_values = passed_along((key_rows[:, cols], value_rows[:, cols]), "outer", 1)
        far = []
        for level_bit in range(level_count):
            outgoing = jnp.concatenate(
                [pick_blocks(key_rows, wanted[level_bit])[:, cols], pick_blocks(value_rows, wanted[level_bit])[:, cols]],
                axis=0,
            )
            far.append(from_partner(outgoing, "outer", level_bit))
        context = attend(
            bias, queries, key_rows, value_rows, prev_keys, prev_values, far, c * (HEADS // CHUNKS), context
        )
    return context


def solution(mesh):
    placed = (
        P(("groups", "outer"), None),
        P(("groups", "outer"), None),
        P(("groups", "outer"), None),
        P(("groups", "outer")),
        P("groups", None, None),
    )
    return jax.shard_map(
        on_device,
        mesh=mesh,
        in_specs=placed,
        out_specs=P(("groups", "outer"), None),
        check_vma=False,
    )
```

time: 108 us -> 115 us (1.065)
  other arithmetic: 2.44 us -> 6.11 us
  waiting for transfers between devices: 55.4 us -> 57.5 us
  Pallas kernels: 28.6 us -> 27 us
  local copies, waits for them, and re-layouts: 6.91 us -> 8.36 us
    select_n x0 -> x1, other arithmetic: none -> 2.25 us  [window_bias(): jnp.where(prev_vis, 0.0, -jnp.inf)]
    ppermute x8, waiting for transfers between devices: 55.4 us -> 57.5 us  [from_partner(): return lax.ppermute(value, axis, pairs)]
    pallas_call x2, Pallas kernels: 28.6 us -> 27 us  [attend(): pl.pallas_call(functools.partial(attend_kernel, level_count), out_shape=j...]
  transfers between devices with their start and end apart: 12 -> 12, of which waited for: 5 -> 6; matrix products, arithmetic and copies ran while one was open for 4% -> 8% of each run, Pallas kernels for 13% -> 12%
where the time goes in v12:
time: 115 us; the launch traced here: 114 us
  waiting for transfers between devices  57.5 us (50%)
  Pallas kernels  27 us (23%)
  starting transfers between devices  12.8 us (11%)
  local copies, waits for them, and re-layouts  8.36 us (7%)
  other arithmetic  6.11 us (5%)
  between operations  2.75 us (2%)
    ppermute x8, waiting for transfers between devices, from_partner(): return lax.ppermute(value, axis, pairs)  57.5 us
    pallas_call x2, Pallas kernels, attend(): pl.pallas_call(functools.partial(attend_kernel, level_count), out_shape=j...  27 us
    ppermute x8, starting transfers between devices, from_partner(): return lax.ppermute(value, axis, pairs)  7.51 us
    ppermute x4, starting transfers between devices, passed_along(): return lax.ppermute(block, axis, route)  5.26 us
    unnamed x26, local copies, waits for them, and re-layouts  2.81 us
    slice x1, local copies, waits for them, and re-layouts, on_device(): key_rows[:, cols]  2.76 us
    concatenate x8, other arithmetic, on_device(): jnp.concatenate([pick_blocks(key_rows, wanted[level_bit])[:, cols], pick_...  2.75 us
  transfers between devices with their start and end apart: 12, of which 6 were waited for; matrix products, arithmetic and copies ran while one was open for 8% of the time, Pallas kernels for 12%

profile of v12, /device:TPU:29, one launch (start us, length us, event | category | flops | bytes accessed | tf_op | source)
XLA Modules:
  0.0 114.5 jit_solution(1425534201253297591)
XLA Ops:
  0.0 2.8 %fusion.16 = (bf16[384,1024]{1,0:T(8,128)(2,1)}, bf16[384,1024]{1,0:T(8,128)(2,1)}) fusion(bf16[384,2048]{1,0:T(8,128)(2,1)} %ok_ref.3), kind=kLoop, calls=%fused_computation.50 | loop fusion | bytes 3145728 | tf_op jit(solution)/shard_map/slice | solution.py:145
  2.8 1.3 %collective-permute-start.6 = (bf16[384,1024]{1,0:T(8,128)(2,1)}, bf16[384,1024]{1,0:T(8,128)(2,1)}, u32[]{:S(2)}, u32[]{:S(2)}) collective-permute-start(bf16[384,1024]{1,0:T(8,128)(2,1)} %get-tuple-element.23), channel_id=1, source_target_pairs={{0,1},{1,2},{2,3},{3,4},{4,5},{5,6},{6,7},{7,8},{8,9},{9,10},{10,1... | collective-permute-start | bytes 2359304 | tf_op jit(solution)/shard_map/ppermute | solution.py:20
  4.1 0.7 constant_dynamic-slice_fusion.2
  7.3 0.2 constant_dynamic-slice_fusion.1
  7.5 1.2 %copy-done.1 = bf16[384,2048]{1,0:T(8,128)(2,1)S(1)} copy-done((bf16[384,2048]{1,0:T(8,128)(2,1)S(1)}, bf16[384,2048]{1,0:T(8,128)(2,1)}, u32[]{:S(2)}) %copy-start.1) | copy-done | bytes 1572888
  8.7 0.2 constant_dynamic-slice_fusion
  8.9 1.4 %collective-permute-start.8 = (bf16[256,1024]{1,0:T(8,128)(2,1)S(1)}, bf16[256,1024]{1,0:T(8,128)(2,1)S(1)}, u32[]{:S(2)}, u32[]{:S(2)}) collective-permute-start(bf16[256,1024]{1,0:T(8,128)(2,1)S(1)} %pad_maximum_fusion.5), channel_id=1, source_target_pairs={{0,1},{1,0},{2,3},{3,2},{4,5},{5,4},{6,7},{7,6},{8,9},{9,8},{10,11... | collective-permute-start | bytes 1572872 | tf_op jit(solution)/shard_map/ppermute | solution.py:26
  10.4 1.4 %collective-permute-start.9 = (bf16[256,1024]{1,0:T(8,128)(2,1)S(1)}, bf16[256,1024]{1,0:T(8,128)(2,1)S(1)}, u32[]{:S(2)}, u32[]{:S(2)}) collective-permute-start(bf16[256,1024]{1,0:T(8,128)(2,1)S(1)} %pad_maximum_fusion.6), channel_id=1, source_target_pairs={{0,2},{1,3},{2,0},{3,1},{4,6},{5,7},{6,4},{7,5},{8,10},{9,11},{10,... | collective-permute-start | bytes 1572872 | tf_op jit(solution)/shard_map/ppermute | solution.py:26
  11.8 1.0 fusion.15
  12.8 1.4 %collective-permute-start.7 = (bf16[384,1024]{1,0:T(8,128)(2,1)S(1)}, bf16[384,1024]{1,0:T(8,128)(2,1)S(1)}, u32[]{:S(2)}, u32[]{:S(2)}) collective-permute-start(bf16[384,1024]{1,0:T(8,128)(2,1)S(1)} %get-tuple-element.21), channel_id=1, source_target_pairs={{0,1},{1,2},{2,3},{3,4},{4,5},{5,6},{6,7},{7,8},{8,9},{9,10},{10,1... | collective-permute-start | bytes 2359304 | tf_op jit(solution)/shard_map/ppermute | solution.py:20
  14.3 2.3 %collective-permute-start.10 = (bf16[256,1024]{1,0:T(8,128)(2,1)S(1)}, bf16[256,1024]{1,0:T(8,128)(2,1)S(1)}, u32[]{:S(2)}, u32[]{:S(2)}) collective-permute-start(bf16[256,1024]{1,0:T(8,128)(2,1)S(1)} %pad_maximum_fusion.7), channel_id=1, source_target_pairs={{0,4},{1,5},{2,6},{3,7},{4,0},{5,1},{6,2},{7,3},{8,12},{9,13},{10,... | collective-permute-start | bytes 1572872 | tf_op jit(solution)/shard_map/ppermute | solution.py:26
  16.6 0.1 collective-permute-start.2
  16.7 0.7 fusion.17
  17.4 17.7 %collective-permute-done.9.rest_2_.rest_3_ = bf16[256,1024]{1,0:T(8,128)(2,1)S(1)} collective-permute-done((bf16[256,1024]{1,0:T(8,128)(2,1)S(1)}, bf16[256,1024]{1,0:T(8,128)(2,1)S(1)}, u32[]{:S(2)}, u32[]{:S(2)}) %collective-permute-start.9) | collective-permute-done | bytes 524320 | tf_op jit(solution)/shard_map/ppermute | solution.py:26
  35.1 0.9 pad_maximum_fusion.4
  36.0 0.8 pad_maximum_fusion.3
  36.9 0.2 collective-permute-done.10.rest_4_.rest_5_
  37.0 1.3 %collective-permute-start = (bf16[384,1024]{1,0:T(8,128)(2,1)}, bf16[384,1024]{1,0:T(8,128)(2,1)}, u32[]{:S(2)}, u32[]{:S(2)}) collective-permute-start(bf16[384,1024]{1,0:T(8,128)(2,1)} %get-tuple-element.24), channel_id=1, source_target_pairs={{0,1},{1,2},{2,3},{3,4},{4,5},{5,6},{6,7},{7,8},{8,9},{9,10},{10,1... | collective-permute-start | bytes 2359304 | tf_op jit(solution)/shard_map/ppermute | solution.py:20
  38.4 1.3 %collective-permute-start.1 = (bf16[384,1024]{1,0:T(8,128)(2,1)}, bf16[384,1024]{1,0:T(8,128)(2,1)}, u32[]{:S(2)}, u32[]{:S(2)}) collective-permute-start(bf16[384,1024]{1,0:T(8,128)(2,1)} %get-tuple-element.22), channel_id=1, source_target_pairs={{0,1},{1,2},{2,3},{3,4},{4,5},{5,6},{6,7},{7,8},{8,9},{9,10},{10,1... | collective-permute-start | bytes 2359304 | tf_op jit(solution)/shard_map/ppermute | solution.py:20
  39.7 0.8 pad_maximum_fusion.2
  40.5 20.5 %collective-permute-done.11.rest_6_.rest_7_ = bf16[256,1024]{1,0:T(8,128)(2,1)S(1)} collective-permute-done((bf16[256,1024]{1,0:T(8,128)(2,1)S(1)}, bf16[256,1024]{1,0:T(8,128)(2,1)S(1)}, u32[]{:S(2)}, u32[]{:S(2)}) %collective-permute-start.11) | collective-permute-done | bytes 524320 | tf_op jit(solution)/shard_map/ppermute | solution.py:26
  61.0 2.3 %collective-permute-start.3 = (bf16[256,1024]{1,0:T(8,128)(2,1)}, bf16[256,1024]{1,0:T(8,128)(2,1)S(1)}, u32[]{:S(2)}, u32[]{:S(2)}) collective-permute-start(bf16[256,1024]{1,0:T(8,128)(2,1)} %pad_maximum_fusion.2), channel_id=1, source_target_pairs={{0,2},{1,3},{2,0},{3,1},{4,6},{5,7},{6,4},{7,5},{8,10},{9,11},{10,... | collective-permute-start | bytes 1572872 | tf_op jit(solution)/shard_map/ppermute | solution.py:26
  63.3 0.1 collective-permute-start.5
  63.3 0.8 copy-done.10
  64.1 2.3 %fusion.7 = (f32[384,384]{1,0:T(8,128)S(1)}, f32[384,384]{1,0:T(8,128)S(1)}) fusion(s32[]{:T(128)} %mul.43, s32[]{:T(128)} %bitcast.2, s32[]{:T(128)} %bitcast.1, s32[]{:T(128)} %bitcast, s32[384]{0:T(512)S(1)} %get-tuple-element.34, s32[384]{0:T(512)S(1)} %get-tuple-element.35, pred[384]{0:T(512)(128)(4,1)S(1)} %fusion.14), kind=kLoop, calls=%fused_computation.17 | loop fusion | flops 3686400 | bytes 1183120 | tf_op jit(solution)/shard_map/jit(_where)/select_n | solution.py:91
  66.4 1.1 pad_maximum_fusion.bias_ref
  67.5 13.4 %shard_map.55.rest_8_ = bf16[384,2048]{1,0:T(8,128)(2,1)} custom-call(f32[384,768]{1,0:T(8,128)} %pad_maximum_fusion.bias_ref, bf16[384,2048]{1,0:T(8,128)(2,1)} %q_ref.3, bf16[384,2048]{1,0:T(8,128)(2,1)} %ok_ref.3, bf16[384,2048]{1,0:T(8,128)(2,1)} %ov_ref.3, bf16[384,1024]{1,0:T(8,128)(2,1)} %collective-permute-done.6.pk_ref, ...), custom_call_target="tpu_custom_call" | custom-call | flops 2013265920 | bytes 6815744 | tf_op jit(solution)/shard_map/pallas_call | solution.py:118
  81.0 1.4 %collective-permute-done.3.rest_2_.rest_3_ = bf16[256,1024]{1,0:T(8,128)(2,1)S(1)} collective-permute-done((bf16[256,1024]{1,0:T(8,128)(2,1)}, bf16[256,1024]{1,0:T(8,128)(2,1)S(1)}, u32[]{:S(2)}, u32[]{:S(2)}) %collective-permute-start.3) | collective-permute-done | bytes 524320 | tf_op jit(solution)/shard_map/ppermute | solution.py:26
  82.4 5.9 %collective-permute-done.4.rest_4_.rest_5_ = bf16[256,1024]{1,0:T(8,128)(2,1)S(1)} collective-permute-done((bf16[256,1024]{1,0:T(8,128)(2,1)}, bf16[256,1024]{1,0:T(8,128)(2,1)S(1)}, u32[]{:S(2)}, u32[]{:S(2)}) %collective-permute-start.4) | collective-permute-done | bytes 524320 | tf_op jit(solution)/shard_map/ppermute | solution.py:26
  88.3 11.8 %collective-permute-done.5.rest_6_.rest_7_ = bf16[256,1024]{1,0:T(8,128)(2,1)S(1)} collective-permute-done((bf16[256,1024]{1,0:T(8,128)(2,1)}, bf16[256,1024]{1,0:T(8,128)(2,1)S(1)}, u32[]{:S(2)}, u32[]{:S(2)}) %collective-permute-start.5) | collective-permute-done | bytes 524320 | tf_op jit(solution)/shard_map/ppermute | solution.py:26
  100.2 0.8 copy-done.9
  100.9 13.5 %shard_map.56 = bf16[384,2048]{1,0:T(8,128)(2,1)} custom-call(f32[384,768]{1,0:T(8,128)} %pad_maximum_fusion.bias_ref, bf16[384,2048]{1,0:T(8,128)(2,1)} %q_ref.3, bf16[384,2048]{1,0:T(8,128)(2,1)} %ok_ref.3, bf16[384,2048]{1,0:T(8,128)(2,1)} %ov_ref.3, bf16[384,1024]{1,0:T(8,128)(2,1)} %collective-permute-done.pk_ref, ...), custom_call_target="tpu_custom_call", output_to_operand_aliasing={{}: (14, {})} | custom-call | flops 2013265920 | bytes 6815744 | tf_op jit(solution)/shard_map/pallas_call | solution.py:118
  (38 shorter events, 0.3 us)
Async XLA Ops:
  0.0 7.3 %copy-start = (bf16[384,2048]{1,0:T(8,128)(2,1)S(1)}, bf16[384,2048]{1,0:T(8,128)(2,1)}, u32[]{:S(2)}) copy-start(bf16[384,2048]{1,0:T(8,128)(2,1)} %ok_ref.3) | copy-start | bytes 4718596
  0.0 4.1 %copy-start.12 = (s32[16,4,1]{0,2,1:T(1,128)S(1)}, s32[16,4,1]{0,2,1:T(1,128)}, u32[]{:S(2)}) copy-start(s32[16,4,1]{0,2,1:T(1,128)} %param.9) | copy-start | bytes 772
  2.8 60.5 %collective-permute-start.6 = (bf16[384,1024]{1,0:T(8,128)(2,1)}, bf16[384,1024]{1,0:T(8,128)(2,1)}, u32[]{:S(2)}, u32[]{:S(2)}) collective-permute-start(bf16[384,1024]{1,0:T(8,128)(2,1)} %get-tuple-element.23), channel_id=1, source_target_pairs={{0,1},{1,2},{2,3},{3,4},{4,5},{5,6},{6,7},{7,8},{8,9},{9,10},{10,1... | collective-permute-start | bytes 2359304 | tf_op jit(solution)/shard_map/ppermute | solution.py:20
  7.3 1.4 %copy-start.1 = (bf16[384,2048]{1,0:T(8,128)(2,1)S(1)}, bf16[384,2048]{1,0:T(8,128)(2,1)}, u32[]{:S(2)}) copy-start(bf16[384,2048]{1,0:T(8,128)(2,1)} %ov_ref.3) | copy-start | bytes 4718596
  8.9 7.6 %collective-permute-start.8 = (bf16[256,1024]{1,0:T(8,128)(2,1)S(1)}, bf16[256,1024]{1,0:T(8,128)(2,1)S(1)}, u32[]{:S(2)}, u32[]{:S(2)}) collective-permute-start(bf16[256,1024]{1,0:T(8,128)(2,1)S(1)} %pad_maximum_fusion.5), channel_id=1, source_target_pairs={{0,1},{1,0},{2,3},{3,2},{4,5},{5,4},{6,7},{7,6},{8,9},{9,8},{10,11... | collective-permute-start | bytes 1572872 | tf_op jit(solution)/shard_map/ppermute | solution.py:26
  10.4 24.7 %collective-permute-start.9 = (bf16[256,1024]{1,0:T(8,128)(2,1)S(1)}, bf16[256,1024]{1,0:T(8,128)(2,1)S(1)}, u32[]{:S(2)}, u32[]{:S(2)}) collective-permute-start(bf16[256,1024]{1,0:T(8,128)(2,1)S(1)} %pad_maximum_fusion.6), channel_id=1, source_target_pairs={{0,2},{1,3},{2,0},{3,1},{4,6},{5,7},{6,4},{7,5},{8,10},{9,11},{10,... | collective-permute-start | bytes 1572872 | tf_op jit(solution)/shard_map/ppermute | solution.py:26
  12.8 3.9 %copy-start.11 = (s32[3]{0:T(128)S(1)}, s32[3]{0:T(128)}, u32[]{:S(2)}) copy-start(s32[3]{0:T(128)} %param.8) | copy-start | bytes 40
  12.8 50.4 %collective-permute-start.7 = (bf16[384,1024]{1,0:T(8,128)(2,1)S(1)}, bf16[384,1024]{1,0:T(8,128)(2,1)S(1)}, u32[]{:S(2)}, u32[]{:S(2)}) collective-permute-start(bf16[384,1024]{1,0:T(8,128)(2,1)S(1)} %get-tuple-element.21), channel_id=1, source_target_pairs={{0,1},{1,2},{2,3},{3,4},{4,5},{5,6},{6,7},{7,8},{8,9},{9,10},{10,1... | collective-permute-start | bytes 2359304 | tf_op jit(solution)/shard_map/ppermute | solution.py:20
  14.3 22.8 %collective-permute-start.10 = (bf16[256,1024]{1,0:T(8,128)(2,1)S(1)}, bf16[256,1024]{1,0:T(8,128)(2,1)S(1)}, u32[]{:S(2)}, u32[]{:S(2)}) collective-permute-start(bf16[256,1024]{1,0:T(8,128)(2,1)S(1)} %pad_maximum_fusion.7), channel_id=1, source_target_pairs={{0,4},{1,5},{2,6},{3,7},{4,0},{5,1},{6,2},{7,3},{8,12},{9,13},{10,... | collective-permute-start | bytes 1572872 | tf_op jit(solution)/shard_map/ppermute | solution.py:26
  16.6 20.3 %copy-start.2 = (bf16[256,1024]{1,0:T(8,128)(2,1)}, bf16[256,1024]{1,0:T(8,128)(2,1)S(1)}, u32[]{:S(2)}) copy-start(bf16[256,1024]{1,0:T(8,128)(2,1)S(1)} %collective-permute-done.8.rest_0_.rest_1_) | copy-start | bytes 1572868
  16.6 21.8 %collective-permute-start.2 = (bf16[256,1024]{1,0:T(8,128)(2,1)S(1)}, bf16[256,1024]{1,0:T(8,128)(2,1)S(1)}, u32[]{:S(2)}, u32[]{:S(2)}) collective-permute-start(bf16[256,1024]{1,0:T(8,128)(2,1)S(1)} %pad_maximum_fusion.1), channel_id=1, source_target_pairs={{0,1},{1,0},{2,3},{3,2},{4,5},{5,4},{6,7},{7,6},{8,9},{9,8},{10,11... | collective-permute-start | bytes 1572872 | tf_op jit(solution)/shard_map/ppermute | solution.py:26
  35.0 5.5 %copy-start.3 = (bf16[256,1024]{1,0:T(8,128)(2,1)}, bf16[256,1024]{1,0:T(8,128)(2,1)S(1)}, u32[]{:S(2)}) copy-start(bf16[256,1024]{1,0:T(8,128)(2,1)S(1)} %collective-permute-done.9.rest_2_.rest_3_) | copy-start | bytes 1572868
  35.1 25.9 %collective-permute-start.11 = (bf16[256,1024]{1,0:T(8,128)(2,1)S(1)}, bf16[256,1024]{1,0:T(8,128)(2,1)S(1)}, u32[]{:S(2)}, u32[]{:S(2)}) collective-permute-start(bf16[256,1024]{1,0:T(8,128)(2,1)S(1)} %pad_maximum_fusion.8), channel_id=1, source_target_pairs={{0,8},{1,9},{2,10},{3,11},{4,12},{5,13},{6,14},{7,15},{8,0},{9,1},... | collective-permute-start | bytes 1572872 | tf_op jit(solution)/shard_map/ppermute | solution.py:26
  37.0 30.5 %copy-start.5 = (bf16[256,1024]{1,0:T(8,128)(2,1)}, bf16[256,1024]{1,0:T(8,128)(2,1)S(1)}, u32[]{:S(2)}) copy-start(bf16[256,1024]{1,0:T(8,128)(2,1)S(1)} %collective-permute-done.10.rest_4_.rest_5_) | copy-start | bytes 1572868
  37.0 63.1 %collective-permute-start = (bf16[384,1024]{1,0:T(8,128)(2,1)}, bf16[384,1024]{1,0:T(8,128)(2,1)}, u32[]{:S(2)}, u32[]{:S(2)}) collective-permute-start(bf16[384,1024]{1,0:T(8,128)(2,1)} %get-tuple-element.24), channel_id=1, source_target_pairs={{0,1},{1,2},{2,3},{3,4},{4,5},{5,6},{6,7},{7,8},{8,9},{9,10},{10,1... | collective-permute-start | bytes 2359304 | tf_op jit(solution)/shard_map/ppermute | solution.py:20
  38.3 29.2 %copy-start.4 = (bf16[256,1024]{1,0:T(8,128)(2,1)}, bf16[256,1024]{1,0:T(8,128)(2,1)S(1)}, u32[]{:S(2)}) copy-start(bf16[256,1024]{1,0:T(8,128)(2,1)S(1)} %collective-permute-done.2.rest_0_.rest_1_) | copy-start | bytes 1572868
  38.4 61.8 %collective-permute-start.1 = (bf16[384,1024]{1,0:T(8,128)(2,1)}, bf16[384,1024]{1,0:T(8,128)(2,1)}, u32[]{:S(2)}, u32[]{:S(2)}) collective-permute-start(bf16[384,1024]{1,0:T(8,128)(2,1)} %get-tuple-element.22), channel_id=1, source_target_pairs={{0,1},{1,2},{2,3},{3,4},{4,5},{5,6},{6,7},{7,8},{8,9},{9,10},{10,1... | collective-permute-start | bytes 2359304 | tf_op jit(solution)/shard_map/ppermute | solution.py:20
  61.0 6.5 %copy-start.6 = (bf16[256,1024]{1,0:T(8,128)(2,1)}, bf16[256,1024]{1,0:T(8,128)(2,1)S(1)}, u32[]{:S(2)}) copy-start(bf16[256,1024]{1,0:T(8,128)(2,1)S(1)} %collective-permute-done.11.rest_6_.rest_7_) | copy-start | bytes 1572868
  61.0 21.4 %collective-permute-start.3 = (bf16[256,1024]{1,0:T(8,128)(2,1)}, bf16[256,1024]{1,0:T(8,128)(2,1)S(1)}, u32[]{:S(2)}, u32[]{:S(2)}) collective-permute-start(bf16[256,1024]{1,0:T(8,128)(2,1)} %pad_maximum_fusion.2), channel_id=1, source_target_pairs={{0,2},{1,3},{2,0},{3,1},{4,6},{5,7},{6,4},{7,5},{8,10},{9,11},{10,... | collective-permute-start | bytes 1572872 | tf_op jit(solution)/shard_map/ppermute | solution.py:26
  63.2 25.1 %collective-permute-start.4 = (bf16[256,1024]{1,0:T(8,128)(2,1)}, bf16[256,1024]{1,0:T(8,128)(2,1)S(1)}, u32[]{:S(2)}, u32[]{:S(2)}) collective-permute-start(bf16[256,1024]{1,0:T(8,128)(2,1)} %pad_maximum_fusion.3), channel_id=1, source_target_pairs={{0,4},{1,5},{2,6},{3,7},{4,0},{5,1},{6,2},{7,3},{8,12},{9,13},{10,... | collective-permute-start | bytes 1572872 | tf_op jit(solution)/shard_map/ppermute | solution.py:26
  63.2 0.9 copy-start.10
  63.3 36.9 %collective-permute-start.5 = (bf16[256,1024]{1,0:T(8,128)(2,1)}, bf16[256,1024]{1,0:T(8,128)(2,1)S(1)}, u32[]{:S(2)}, u32[]{:S(2)}) collective-permute-start(bf16[256,1024]{1,0:T(8,128)(2,1)} %pad_maximum_fusion.4), channel_id=1, source_target_pairs={{0,8},{1,9},{2,10},{3,11},{4,12},{5,13},{6,14},{7,15},{8,0},{9,1},... | collective-permute-start | bytes 1572872 | tf_op jit(solution)/shard_map/ppermute | solution.py:26
  82.4 17.8 %copy-start.7 = (bf16[256,1024]{1,0:T(8,128)(2,1)}, bf16[256,1024]{1,0:T(8,128)(2,1)S(1)}, u32[]{:S(2)}) copy-start(bf16[256,1024]{1,0:T(8,128)(2,1)S(1)} %collective-permute-done.3.rest_2_.rest_3_) | copy-start | bytes 1572868
  88.3 11.8 %copy-start.8 = (bf16[256,1024]{1,0:T(8,128)(2,1)}, bf16[256,1024]{1,0:T(8,128)(2,1)S(1)}, u32[]{:S(2)}) copy-start(bf16[256,1024]{1,0:T(8,128)(2,1)S(1)} %collective-permute-done.4.rest_4_.rest_5_) | copy-start | bytes 1572868
  100.1 0.8 copy-start.9

commit v13 on v6

v13 whole, which is shorter than its diff:
```python
import functools

import jax
import jax.numpy as jnp
from jax import lax
from jax.experimental import pallas as pl
from jax.experimental.pallas import tpu as pltpu
from jax.sharding import PartitionSpec as P

HEADS = 16
BLK = 128
WIN = 4
CHUNKS = 2


def passed_along(block, axis, distance):
    devices = range(lax.axis_size(axis))
    route = [(i - distance, i) for i in devices if i - distance in devices]
    return lax.ppermute(block, axis, route)


def from_partner(value, axis, stride):
    mask = 2**stride
    pairs = [(source, source ^ mask) for source in range(lax.axis_size(axis))]
    return lax.ppermute(value, axis, pairs)


def pick_blocks(source, block_index):
    return lax.dynamic_slice_in_dim(source, block_index[0] * BLK, BLK, 0)


def _nt(a, b):
    return lax.dot_general(a, b, (((1,), (1,)), ((), ())), preferred_element_type=jnp.float32)


def _nn(a, b):
    return lax.dot_general(a, b, (((1,), (0,)), ((), ())), preferred_element_type=jnp.float32)


def attend_kernel(level_count, carry_in, carry_out, meta, q_ref, *rest):
    rows, head_dim = q_ref.shape
    panel_len = rows // BLK
    scale = head_dim ** (-0.5)
    q = q_ref[...]
    maxes, totals, sums = [], [], []
    rest = list(rest)
    if carry_in:
        sum_ref, stat_ref = rest[:2]
        rest = rest[2:]
        maxes.append(stat_ref[:, :1])
        totals.append(stat_ref[:, head_dim // 2 : head_dim // 2 + 1])
        sums.append(sum_ref[...])
    else:
        ok_ref, ov_ref, pk_ref, pv_ref = rest[:4]
        rest = rest[4:]
    far_refs = rest[: 2 * level_count]
    outs = rest[2 * level_count :]

    if not carry_in:
        bias_ref = outs[-1]
        outs = outs[:-1]

        @pl.when(pl.program_id(0) == 0)
        def _():
            row = lax.broadcasted_iota(jnp.int32, (rows, rows), 0)
            col = lax.broadcasted_iota(jnp.int32, (rows, rows), 1)
            q_blk = row // BLK
            k_blk = col // BLK
            width = jnp.zeros((rows, rows), jnp.int32)
            for r in range(panel_len):
                width = jnp.where(q_blk == r, meta[r], width)
            first_block = meta[panel_len]
            own_off = q_blk - k_blk
            own_vis = (own_off >= 0) & (own_off < width) & ((own_off > 0) | (col <= row))
            prev_off = q_blk + panel_len - k_blk
            prev_vis = (prev_off < width) & (first_block + q_blk - prev_off >= 0)
            bias_ref[:, :rows] = jnp.where(prev_vis, 0.0, -jnp.inf)
            bias_ref[:, rows:] = jnp.where(own_vis, 0.0, -jnp.inf)

        s_prev = _nt(q, pk_ref[...]) * scale + bias_ref[:, :rows]
        s_own = _nt(q, ok_ref[...]) * scale + bias_ref[:, rows:]
        m_w = jnp.maximum(s_own.max(-1, keepdims=True), s_prev.max(-1, keepdims=True))
        e_own = jnp.exp(s_own - m_w)
        e_prev = jnp.exp(s_prev - m_w)
        maxes.append(m_w)
        totals.append(e_own.sum(-1, keepdims=True) + e_prev.sum(-1, keepdims=True))
        sums.append(_nn(e_own.astype(jnp.bfloat16), ov_ref[...]) + _nn(e_prev.astype(jnp.bfloat16), pv_ref[...]))

    for b in range(level_count):
        s = _nt(q, far_refs[2 * b][...]) * scale
        m = s.max(-1, keepdims=True)
        e = jnp.exp(s - m)
        maxes.append(m)
        totals.append(e.sum(-1, keepdims=True))
        sums.append(_nn(e.astype(jnp.bfloat16), far_refs[2 * b + 1][...]))

    top = maxes[0]
    for m in maxes[1:]:
        top = jnp.maximum(top, m)
    total = jnp.zeros_like(totals[0])
    output = jnp.zeros_like(sums[0])
    for m, l, o in zip(maxes, totals, sums):
        factor = jnp.exp(m - top)
        total = total + l * factor
        output = output + o * factor
    if carry_out:
        sum_out, stat_out = outs[-2:]
        sum_out[...] = output
        lane = lax.broadcasted_iota(jnp.int32, stat_out.shape, 1)
        stat_out[...] = jnp.where(lane < head_dim // 2, top, total)
    else:
        outs[-1][...] = (output / total).astype(outs[-1].dtype)


def attend(meta, queries, own, far, first_head, prior=None, carry=None, carry_out=False):
    rows, features = queries.shape
    head_dim = features // HEADS
    width = (carry[0] if carry is not None else own[2]).shape[1]
    heads = width // head_dim
    level_count = len(far)
    whole = pl.BlockSpec((rows, head_dim), lambda h, meta: (0, h + first_head))
    part = pl.BlockSpec((rows, head_dim), lambda h, meta: (0, h))
    args, in_specs = [meta, queries], [whole]
    if carry is not None:
        args += list(carry)
        in_specs += [part, part]
    else:
        args += list(own)
        in_specs += [whole, whole, part, part]
    for block in far:
        far_rows = block.shape[0] // 2
        args += [block, block]
        in_specs.append(pl.BlockSpec((far_rows, head_dim), lambda h, meta: (0, h)))
        in_specs.append(pl.BlockSpec((far_rows, head_dim), lambda h, meta: (1, h)))
    aliases = {}
    if carry_out:
        out_shape = (jax.ShapeDtypeStruct((rows, width), jnp.float32),) * 2
        out_specs = (part, part)
    else:
        out_shape = jax.ShapeDtypeStruct((rows, features), queries.dtype)
        out_specs = whole
        if prior is not None:
            aliases = {len(args): 0}
            args.append(prior)
            in_specs.append(pl.BlockSpec(memory_space=pl.ANY))
    scratch = [] if carry is not None else [pltpu.VMEM((rows, 2 * rows), jnp.float32)]
    keys = (0 if carry is not None else 2 * rows) + level_count * BLK
    return pl.pallas_call(
        functools.partial(attend_kernel, level_count, carry is not None, carry_out),
        out_shape=out_shape,
        grid_spec=pltpu.PrefetchScalarGridSpec(
            num_scalar_prefetch=1,
            grid=(heads,),
            in_specs=in_specs,
            out_specs=out_specs,
            scratch_shapes=scratch,
        ),
        input_output_aliases=aliases,
        compiler_params=pltpu.CompilerParams(dimension_semantics=("arbitrary",)),
        cost_estimate=pl.CostEstimate(
            flops=4 * rows * keys * head_dim * heads,
            transcendentals=rows * keys * heads,
            bytes_accessed=2 * head_dim * heads * (6 * rows + 2 * keys) + 16 * rows * width,
        ),
    )(*args)


def on_device(queries, key_rows, value_rows, widths, columns):
    token_count, features = queries.shape
    panel_len = token_count // BLK
    device = lax.axis_index("outer")
    level_count = lax.axis_size("outer").bit_length() - 1
    meta = jnp.concatenate([widths, (device * panel_len)[None]]).astype(jnp.int32)
    wanted = [columns[jnp.bitwise_xor(device, 1 << b), b] - device * panel_len for b in range(level_count)]
    width = features // CHUNKS
    context = None
    for c in range(CHUNKS):
        cols = slice(c * width, (c + 1) * width)
        prev_keys, prev_values = passed_along((key_rows[:, cols], value_rows[:, cols]), "outer", 1)
        far = []
        for level_bit in range(level_count):
            outgoing = jnp.concatenate(
                [pick_blocks(key_rows, wanted[level_bit])[:, cols], pick_blocks(value_rows, wanted[level_bit])[:, cols]],
                axis=0,
            )
            far.append(from_partner(outgoing, "outer", level_bit))
        own = (key_rows, value_rows, prev_keys, prev_values)
        first_head = c * (HEADS // CHUNKS)
        if c < CHUNKS - 1:
            context = attend(meta, queries, own, far, first_head, context)
        else:
            carry = attend(meta, queries, own, far[:-1], first_head, carry_out=True)
            context = attend(meta, queries, None, far[-1:], first_head, context, carry=carry)
    return context


def solution(mesh):
    placed = (
        P(("groups", "outer"), None),
        P(("groups", "outer"), None),
        P(("groups", "outer"), None),
        P(("groups", "outer")),
        P("groups", None, None),
    )
    return jax.shard_map(
        on_device,
        mesh=mesh,
        in_specs=placed,
        out_specs=P(("groups", "outer"), None),
        check_vma=False,
    )
```

time: 108 us -> 118 us (1.093)
  the two profiles are of different devices: /device:TPU:29 before, /device:TPU:11 now
where the time goes in v13:
time: 118 us; the launch traced here: 117 us
  Pallas kernels  39.9 us (34%)
  starting transfers between devices  34.9 us (30%)
  waiting for transfers between devices  29.5 us (25%)
  local copies, waits for them, and re-layouts  7.51 us (6%)
  between operations  2.69 us (2%)
  other arithmetic  2.58 us (2%)
    pallas_call x3, Pallas kernels, attend(): pl.pallas_call(functools.partial(attend_kernel, level_count, carry is not...  39.9 us
    ppermute x8, waiting for transfers between devices, from_partner(): return lax.ppermute(value, axis, pairs)  29.5 us
    ppermute x8, starting transfers between devices, from_partner(): return lax.ppermute(value, axis, pairs)  23.4 us
    ppermute x4, starting transfers between devices, passed_along(): return lax.ppermute(block, axis, route)  11.5 us
  transfers between devices with their start and end apart: 12, of which 3 were waited for; matrix products, arithmetic and copies ran while one was open for 4% of the time, Pallas kernels for 23%

profile of v13, /device:TPU:11, one launch (start us, length us, event | category | flops | bytes accessed | tf_op | source)
XLA Modules:
  0.0 117.1 jit_solution(13632335828489984273)
XLA Ops:
  0.0 1.4 %constant_dynamic-slice_fusion.2 = (s32[1,1,1]{0,2,1:T(1,128)}, s32[1,1,1]{0,2,1:T(1,128)}, s32[1,1,1]{0,2,1:T(1,128)}, s32[1,1,1]{0,2,1:T(1,128)}) fusion(s32[16,4,1]{0,2,1:T(1,128)} %param.9, s32[]{:T(128)S(6)} %select_n.42, s32[]{:T(128)S(6)} %select_n.18, s32[]{:T(128)S(6)} %select_n.16, s32[]{:T(128)S(6)} %select_n.40), kind=kLoop, calls=%fused_computation.10 | loop fusion | bytes 48 | tf_op jit(solution)/shard_map/dynamic_slice | solution.py:174
  3.8 0.0 copy-start.1
  3.9 1.8 %constant_dynamic-slice_fusion.1 = (bf16[128,1024]{1,0:T(8,128)(2,1)S(1)}, bf16[128,1024]{1,0:T(8,128)(2,1)S(1)}, bf16[128,1024]{1,0:T(8,128)(2,1)S(1)}, bf16[12...) fusion(bf16[384,2048]{1,0:T(8,128)(2,1)} %rest_0_.3, ...), kind=kLoop, calls=%fused_computation.9 | loop fusion | bytes 4194324 | tf_op jit(solution)/shard_map/slice | solution.py:183
  5.7 0.2 copy-done.1
  5.9 0.2 constant_dynamic-slice_fusion
  6.1 0.2 collective-permute-start.10
  6.4 2.4 %collective-permute-start.11 = (bf16[256,1024]{1,0:T(8,128)(2,1)S(1)}, bf16[256,1024]{1,0:T(8,128)(2,1)S(1)}, u32[]{:S(2)}, u32[]{:S(2)}) collective-permute-start(bf16[256,1024]{1,0:T(8,128)(2,1)S(1)} %pad_maximum_fusion.7), channel_id=1, source_target_pairs={{0,8},{1,9},{2,10},{3,11},{4,12},{5,13},{6,14},{7,15},{8,0},{9,1},... | collective-permute-start | bytes 1572872 | tf_op jit(solution)/shard_map/ppermute | solution.py:25
  8.8 1.3 %collective-permute-start.2 = (bf16[256,1024]{1,0:T(8,128)(2,1)S(1)}, bf16[256,1024]{1,0:T(8,128)(2,1)S(1)}, u32[]{:S(2)}, u32[]{:S(2)}) collective-permute-start(bf16[256,1024]{1,0:T(8,128)(2,1)S(1)} %pad_maximum_fusion), channel_id=1, source_target_pairs={{0,1},{1,0},{2,3},{3,2},{4,5},{5,4},{6,7},{7,6},{8,9},{9,8},{10,11... | collective-permute-start | bytes 1572872 | tf_op jit(solution)/shard_map/ppermute | solution.py:25
  10.2 1.3 %collective-permute-start.3 = (bf16[256,1024]{1,0:T(8,128)(2,1)S(1)}, bf16[256,1024]{1,0:T(8,128)(2,1)S(1)}, u32[]{:S(2)}, u32[]{:S(2)}) collective-permute-start(bf16[256,1024]{1,0:T(8,128)(2,1)S(1)} %pad_maximum_fusion.1), channel_id=1, source_target_pairs={{0,2},{1,3},{2,0},{3,1},{4,6},{5,7},{6,4},{7,5},{8,10},{9,11},{10,... | collective-permute-start | bytes 1572872 | tf_op jit(solution)/shard_map/ppermute | solution.py:25
  11.5 1.0 fusion.1
  12.5 2.3 %collective-permute-start = (bf16[384,1024]{1,0:T(8,128)(2,1)S(1)}, bf16[384,1024]{1,0:T(8,128)(2,1)S(1)}, u32[]{:S(2)}, u32[]{:S(2)}) collective-permute-start(bf16[384,1024]{1,0:T(8,128)(2,1)S(1)} %get-tuple-element.28), channel_id=1, source_target_pairs={{0,1},{1,2},{2,3},{3,4},{4,5},{5,6},{6,7},{7,8},{8,9},{9,10},{10,1... | collective-permute-start | bytes 2359304 | tf_op jit(solution)/shard_map/ppermute | solution.py:19
  14.8 1.0 fusion
  15.8 12.2 %collective-permute-done.10.rest_8_.rest_9_ = bf16[256,1024]{1,0:T(8,128)(2,1)S(1)} collective-permute-done((bf16[256,1024]{1,0:T(8,128)(2,1)S(1)}, bf16[256,1024]{1,0:T(8,128)(2,1)S(1)}, u32[]{:S(2)}, u32[]{:S(2)}) %collective-permute-start.10) | collective-permute-done | bytes 524320 | tf_op jit(solution)/shard_map/ppermute | solution.py:25
  28.0 4.6 %collective-permute-start.1 = (bf16[384,1024]{1,0:T(8,128)(2,1)S(1)}, bf16[384,1024]{1,0:T(8,128)(2,1)S(1)}, u32[]{:S(2)}, u32[]{:S(2)}) collective-permute-start(bf16[384,1024]{1,0:T(8,128)(2,1)S(1)} %get-tuple-element.26), channel_id=1, source_target_pairs={{0,1},{1,2},{2,3},{3,4},{4,5},{5,6},{6,7},{7,8},{8,9},{9,10},{10,1... | collective-permute-start | bytes 2359304 | tf_op jit(solution)/shard_map/ppermute | solution.py:19
  32.6 2.3 %collective-permute-start.4 = (bf16[256,1024]{1,0:T(8,128)(2,1)S(1)}, bf16[256,1024]{1,0:T(8,128)(2,1)S(1)}, u32[]{:S(2)}, u32[]{:S(2)}) collective-permute-start(bf16[256,1024]{1,0:T(8,128)(2,1)S(1)} %pad_maximum_fusion.2), channel_id=1, source_target_pairs={{0,4},{1,5},{2,6},{3,7},{4,0},{5,1},{6,2},{7,3},{8,12},{9,13},{10,... | collective-permute-start | bytes 1572872 | tf_op jit(solution)/shard_map/ppermute | solution.py:25
  34.9 2.7 %collective-permute-start.6 = (bf16[384,1024]{1,0:T(8,128)(2,1)}, bf16[384,1024]{1,0:T(8,128)(2,1)S(1)}, u32[]{:S(2)}, u32[]{:S(2)}) collective-permute-start(bf16[384,1024]{1,0:T(8,128)(2,1)} %get-tuple-element.27), channel_id=1, source_target_pairs={{0,1},{1,2},{2,3},{3,4},{4,5},{5,6},{6,7},{7,8},{8,9},{9,10},{10,1... | collective-permute-start | bytes 2359304 | tf_op jit(solution)/shard_map/ppermute | solution.py:19
  37.6 1.9 %collective-permute-start.7 = (bf16[384,1024]{1,0:T(8,128)(2,1)}, bf16[384,1024]{1,0:T(8,128)(2,1)}, u32[]{:S(2)}, u32[]{:S(2)}) collective-permute-start(bf16[384,1024]{1,0:T(8,128)(2,1)} %get-tuple-element.25), channel_id=1, source_target_pairs={{0,1},{1,2},{2,3},{3,4},{4,5},{5,6},{6,7},{7,8},{8,9},{9,10},{10,1... | collective-permute-start | bytes 2359304 | tf_op jit(solution)/shard_map/ppermute | solution.py:19
  39.6 0.0 copy-start.13
  39.6 0.9 pad_maximum_fusion.4
  40.5 6.8 %collective-permute-done.4.rest_8_.rest_9_ = bf16[256,1024]{1,0:T(8,128)(2,1)S(1)} collective-permute-done((bf16[256,1024]{1,0:T(8,128)(2,1)S(1)}, bf16[256,1024]{1,0:T(8,128)(2,1)S(1)}, u32[]{:S(2)}, u32[]{:S(2)}) %collective-permute-start.4) | collective-permute-done | bytes 524320 | tf_op jit(solution)/shard_map/ppermute | solution.py:25
  47.3 0.3 collective-permute-start.8
  47.6 13.1 %collective-permute-start.9 = (bf16[256,1024]{1,0:T(8,128)(2,1)S(1)}, bf16[256,1024]{1,0:T(8,128)(2,1)S(1)}, u32[]{:S(2)}, u32[]{:S(2)}) collective-permute-start(bf16[256,1024]{1,0:T(8,128)(2,1)S(1)} %pad_maximum_fusion.5), channel_id=1, source_target_pairs={{0,2},{1,3},{2,0},{3,1},{4,6},{5,7},{6,4},{7,5},{8,10},{9,11},{10,... | collective-permute-start | bytes 1572872 | tf_op jit(solution)/shard_map/ppermute | solution.py:25
  60.7 0.8 pad_maximum_fusion.3
  61.6 2.6 %collective-permute-start.5 = (bf16[256,1024]{1,0:T(8,128)(2,1)}, bf16[256,1024]{1,0:T(8,128)(2,1)S(1)}, u32[]{:S(2)}, u32[]{:S(2)}) collective-permute-start(bf16[256,1024]{1,0:T(8,128)(2,1)} %pad_maximum_fusion.3), channel_id=1, source_target_pairs={{0,8},{1,9},{2,10},{3,11},{4,12},{5,13},{6,14},{7,15},{8,0},{9,1},... | collective-permute-start | bytes 1572872 | tf_op jit(solution)/shard_map/ppermute | solution.py:25
  64.2 0.6 pad_add_fusion.meta
  64.8 13.2 %shard_map.55 = (f32[384,1024]{1,0:T(8,128)}, f32[384,1024]{1,0:T(8,128)}) custom-call(s32[4]{0:T(128)} %pad_add_fusion.meta, bf16[384,2048]{1,0:T(8,128)(2,1)} %q_ref.5, bf16[384,2048]{1,0:T(8,128)(2,1)} %rest_0_.3, bf16[384,2048]{1,0:T(8,128)(2,1)} %rest_1_.3, bf16[384,1024]{1,0:T(8,128)(2,1)} %copy-done.10, bf16[384,1024]{1,0:T(8,128)(2,1)} %copy-done.12, ...), custom_call_target="tpu_custom_call" | custom-call | flops 1811939328 | bytes 15728640 | tf_op jit(solution)/shard_map/pallas_call | solution.py:148
  78.0 10.5 %collective-permute-done.9.rest_6_.rest_7_ = bf16[256,1024]{1,0:T(8,128)(2,1)S(1)} collective-permute-done((bf16[256,1024]{1,0:T(8,128)(2,1)S(1)}, bf16[256,1024]{1,0:T(8,128)(2,1)S(1)}, u32[]{:S(2)}, u32[]{:S(2)}) %collective-permute-start.9) | collective-permute-done | bytes 524320 | tf_op jit(solution)/shard_map/ppermute | solution.py:25
  88.5 0.8 copy-done.8
  89.3 0.2 copy-done.11
  89.6 14.3 %shard_map.56.rest_4_ = bf16[384,2048]{1,0:T(8,128)(2,1)} custom-call(s32[4]{0:T(128)} %pad_add_fusion.meta, bf16[384,2048]{1,0:T(8,128)(2,1)} %q_ref.5, bf16[384,2048]{1,0:T(8,128)(2,1)} %rest_0_.3, bf16[384,2048]{1,0:T(8,128)(2,1)} %rest_1_.3, bf16[384,1024]{1,0:T(8,128)(2,1)} %copy-done.11, bf16[384,1024]{1,0:T(8,128)(2,1)} %collective-permute-done.7.rest_3_, ...), custom_call_target="tpu_custom_call" | custom-call | flops 2013265920 | bytes 16252928 | tf_op jit(solution)/shard_map/pallas_call | solution.py:148
  103.9 0.8 copy-done.9
  104.7 12.4 %shard_map.57 = bf16[384,2048]{1,0:T(8,128)(2,1)} custom-call(s32[4]{0:T(128)} %pad_add_fusion.meta, bf16[384,2048]{1,0:T(8,128)(2,1)} %q_ref.5, f32[384,1024]{1,0:T(8,128)} %get-tuple-element.7.rest_0_, f32[384,1024]{1,0:T(8,128)} %get-tuple-element.8.rest_1_, bf16[256,1024]{1,0:T(8,128)(2,1)} %copy-done.9, ...), custom_call_target="tpu_custom_call", output_to_operand_aliasing={{}: (6, {})} | custom-call | flops 201326592 | bytes 11534336 | tf_op jit(solution)/shard_map/pallas_call | solution.py:148
  (37 shorter events, 0.3 us)
Async XLA Ops:
  3.8 2.0 %copy-start.1 = (bf16[384,2048]{1,0:T(8,128)(2,1)S(1)}, bf16[384,2048]{1,0:T(8,128)(2,1)}, u32[]{:S(2)}) copy-start(bf16[384,2048]{1,0:T(8,128)(2,1)} %rest_1_.3) | copy-start | bytes 4718596
  6.1 21.9 %collective-permute-start.10 = (bf16[256,1024]{1,0:T(8,128)(2,1)S(1)}, bf16[256,1024]{1,0:T(8,128)(2,1)S(1)}, u32[]{:S(2)}, u32[]{:S(2)}) collective-permute-start(bf16[256,1024]{1,0:T(8,128)(2,1)S(1)} %pad_maximum_fusion.6), channel_id=1, source_target_pairs={{0,4},{1,5},{2,6},{3,7},{4,0},{5,1},{6,2},{7,3},{8,12},{9,13},{10,... | collective-permute-start | bytes 1572872 | tf_op jit(solution)/shard_map/ppermute | solution.py:25
  6.4 5.1 %copy-start = (bf16[384,2048]{1,0:T(8,128)(2,1)S(1)}, bf16[384,2048]{1,0:T(8,128)(2,1)}, u32[]{:S(2)}) copy-start(bf16[384,2048]{1,0:T(8,128)(2,1)} %rest_0_.3) | copy-start | bytes 4718596
  6.4 26.2 %collective-permute-start.11 = (bf16[256,1024]{1,0:T(8,128)(2,1)S(1)}, bf16[256,1024]{1,0:T(8,128)(2,1)S(1)}, u32[]{:S(2)}, u32[]{:S(2)}) collective-permute-start(bf16[256,1024]{1,0:T(8,128)(2,1)S(1)} %pad_maximum_fusion.7), channel_id=1, source_target_pairs={{0,8},{1,9},{2,10},{3,11},{4,12},{5,13},{6,14},{7,15},{8,0},{9,1},... | collective-permute-start | bytes 1572872 | tf_op jit(solution)/shard_map/ppermute | solution.py:25
  8.8 26.1 %collective-permute-start.2 = (bf16[256,1024]{1,0:T(8,128)(2,1)S(1)}, bf16[256,1024]{1,0:T(8,128)(2,1)S(1)}, u32[]{:S(2)}, u32[]{:S(2)}) collective-permute-start(bf16[256,1024]{1,0:T(8,128)(2,1)S(1)} %pad_maximum_fusion), channel_id=1, source_target_pairs={{0,1},{1,0},{2,3},{3,2},{4,5},{5,4},{6,7},{7,6},{8,9},{9,8},{10,11... | collective-permute-start | bytes 1572872 | tf_op jit(solution)/shard_map/ppermute | solution.py:25
  10.2 27.4 %collective-permute-start.3 = (bf16[256,1024]{1,0:T(8,128)(2,1)S(1)}, bf16[256,1024]{1,0:T(8,128)(2,1)S(1)}, u32[]{:S(2)}, u32[]{:S(2)}) collective-permute-start(bf16[256,1024]{1,0:T(8,128)(2,1)S(1)} %pad_maximum_fusion.1), channel_id=1, source_target_pairs={{0,2},{1,3},{2,0},{3,1},{4,6},{5,7},{6,4},{7,5},{8,10},{9,11},{10,... | collective-permute-start | bytes 1572872 | tf_op jit(solution)/shard_map/ppermute | solution.py:25
  12.5 35.1 %collective-permute-start = (bf16[384,1024]{1,0:T(8,128)(2,1)S(1)}, bf16[384,1024]{1,0:T(8,128)(2,1)S(1)}, u32[]{:S(2)}, u32[]{:S(2)}) collective-permute-start(bf16[384,1024]{1,0:T(8,128)(2,1)S(1)} %get-tuple-element.28), channel_id=1, source_target_pairs={{0,1},{1,2},{2,3},{3,4},{4,5},{5,6},{6,7},{7,8},{8,9},{9,10},{10,1... | collective-permute-start | bytes 2359304 | tf_op jit(solution)/shard_map/ppermute | solution.py:19
  28.0 12.5 %copy-start.2 = (bf16[256,1024]{1,0:T(8,128)(2,1)}, bf16[256,1024]{1,0:T(8,128)(2,1)S(1)}, u32[]{:S(2)}) copy-start(bf16[256,1024]{1,0:T(8,128)(2,1)S(1)} %collective-permute-done.10.rest_8_.rest_9_) | copy-start | bytes 1572868
  28.0 33.6 %collective-permute-start.1 = (bf16[384,1024]{1,0:T(8,128)(2,1)S(1)}, bf16[384,1024]{1,0:T(8,128)(2,1)S(1)}, u32[]{:S(2)}, u32[]{:S(2)}) collective-permute-start(bf16[384,1024]{1,0:T(8,128)(2,1)S(1)} %get-tuple-element.26), channel_id=1, source_target_pairs={{0,1},{1,2},{2,3},{3,4},{4,5},{5,6},{6,7},{7,8},{8,9},{9,10},{10,1... | collective-permute-start | bytes 2359304 | tf_op jit(solution)/shard_map/ppermute | solution.py:19
  32.6 29.0 %copy-start.3 = (bf16[256,1024]{1,0:T(8,128)(2,1)}, bf16[256,1024]{1,0:T(8,128)(2,1)S(1)}, u32[]{:S(2)}) copy-start(bf16[256,1024]{1,0:T(8,128)(2,1)S(1)} %collective-permute-done.11.rest_10_.rest_11_) | copy-start | bytes 1572868
  32.6 14.7 %collective-permute-start.4 = (bf16[256,1024]{1,0:T(8,128)(2,1)S(1)}, bf16[256,1024]{1,0:T(8,128)(2,1)S(1)}, u32[]{:S(2)}, u32[]{:S(2)}) collective-permute-start(bf16[256,1024]{1,0:T(8,128)(2,1)S(1)} %pad_maximum_fusion.2), channel_id=1, source_target_pairs={{0,4},{1,5},{2,6},{3,7},{4,0},{5,1},{6,2},{7,3},{8,12},{9,13},{10,... | collective-permute-start | bytes 1572872 | tf_op jit(solution)/shard_map/ppermute | solution.py:25
  34.9 26.7 %copy-start.4 = (bf16[256,1024]{1,0:T(8,128)(2,1)}, bf16[256,1024]{1,0:T(8,128)(2,1)S(1)}, u32[]{:S(2)}) copy-start(bf16[256,1024]{1,0:T(8,128)(2,1)S(1)} %collective-permute-done.2.rest_4_.rest_5_) | copy-start | bytes 1572868
  34.9 53.6 %collective-permute-start.6 = (bf16[384,1024]{1,0:T(8,128)(2,1)}, bf16[384,1024]{1,0:T(8,128)(2,1)S(1)}, u32[]{:S(2)}, u32[]{:S(2)}) collective-permute-start(bf16[384,1024]{1,0:T(8,128)(2,1)} %get-tuple-element.27), channel_id=1, source_target_pairs={{0,1},{1,2},{2,3},{3,4},{4,5},{5,6},{6,7},{7,8},{8,9},{9,10},{10,1... | collective-permute-start | bytes 2359304 | tf_op jit(solution)/shard_map/ppermute | solution.py:19
  37.6 23.9 %copy-start.5 = (bf16[256,1024]{1,0:T(8,128)(2,1)}, bf16[256,1024]{1,0:T(8,128)(2,1)S(1)}, u32[]{:S(2)}) copy-start(bf16[256,1024]{1,0:T(8,128)(2,1)S(1)} %collective-permute-done.3.rest_6_.rest_7_) | copy-start | bytes 1572868
  37.6 50.9 %collective-permute-start.7 = (bf16[384,1024]{1,0:T(8,128)(2,1)}, bf16[384,1024]{1,0:T(8,128)(2,1)}, u32[]{:S(2)}, u32[]{:S(2)}) collective-permute-start(bf16[384,1024]{1,0:T(8,128)(2,1)} %get-tuple-element.25), channel_id=1, source_target_pairs={{0,1},{1,2},{2,3},{3,4},{4,5},{5,6},{6,7},{7,8},{8,9},{9,10},{10,1... | collective-permute-start | bytes 2359304 | tf_op jit(solution)/shard_map/ppermute | solution.py:19
  39.6 24.6 %copy-start.13 = (s32[3]{0:T(128)S(1)}, s32[3]{0:T(128)}, u32[]{:S(2)}) copy-start(s32[3]{0:T(128)} %param.8) | copy-start | bytes 40
  47.3 17.5 %copy-start.6 = (bf16[256,1024]{1,0:T(8,128)(2,1)}, bf16[256,1024]{1,0:T(8,128)(2,1)S(1)}, u32[]{:S(2)}) copy-start(bf16[256,1024]{1,0:T(8,128)(2,1)S(1)} %collective-permute-done.4.rest_8_.rest_9_) | copy-start | bytes 1572868
  47.3 30.7 %collective-permute-start.8 = (bf16[256,1024]{1,0:T(8,128)(2,1)}, bf16[256,1024]{1,0:T(8,128)(2,1)S(1)}, u32[]{:S(2)}, u32[]{:S(2)}) collective-permute-start(bf16[256,1024]{1,0:T(8,128)(2,1)} %pad_maximum_fusion.4), channel_id=1, source_target_pairs={{0,1},{1,0},{2,3},{3,2},{4,5},{5,4},{6,7},{7,6},{8,9},{9,8},{10,11... | collective-permute-start | bytes 1572872 | tf_op jit(solution)/shard_map/ppermute | solution.py:25
  47.6 14.0 %copy-start.10 = (bf16[384,1024]{1,0:T(8,128)(2,1)}, bf16[384,1024]{1,0:T(8,128)(2,1)S(1)}, u32[]{:S(2)}) copy-start(bf16[384,1024]{1,0:T(8,128)(2,1)S(1)} %collective-permute-done.rest_2_) | copy-start | bytes 2359300
  47.6 40.9 %collective-permute-start.9 = (bf16[256,1024]{1,0:T(8,128)(2,1)S(1)}, bf16[256,1024]{1,0:T(8,128)(2,1)S(1)}, u32[]{:S(2)}, u32[]{:S(2)}) collective-permute-start(bf16[256,1024]{1,0:T(8,128)(2,1)S(1)} %pad_maximum_fusion.5), channel_id=1, source_target_pairs={{0,2},{1,3},{2,0},{3,1},{4,6},{5,7},{6,4},{7,5},{8,10},{9,11},{10,... | collective-permute-start | bytes 1572872 | tf_op jit(solution)/shard_map/ppermute | solution.py:25
  61.6 2.6 %copy-start.12 = (bf16[384,1024]{1,0:T(8,128)(2,1)}, bf16[384,1024]{1,0:T(8,128)(2,1)S(1)}, u32[]{:S(2)}) copy-start(bf16[384,1024]{1,0:T(8,128)(2,1)S(1)} %collective-permute-done.1.rest_3_) | copy-start | bytes 2359300
  61.6 42.3 %collective-permute-start.5 = (bf16[256,1024]{1,0:T(8,128)(2,1)}, bf16[256,1024]{1,0:T(8,128)(2,1)S(1)}, u32[]{:S(2)}, u32[]{:S(2)}) collective-permute-start(bf16[256,1024]{1,0:T(8,128)(2,1)} %pad_maximum_fusion.3), channel_id=1, source_target_pairs={{0,8},{1,9},{2,10},{3,11},{4,12},{5,13},{6,14},{7,15},{8,0},{9,1},... | collective-permute-start | bytes 1572872 | tf_op jit(solution)/shard_map/ppermute | solution.py:25
  78.0 10.5 %copy-start.7 = (bf16[256,1024]{1,0:T(8,128)(2,1)}, bf16[256,1024]{1,0:T(8,128)(2,1)S(1)}, u32[]{:S(2)}) copy-start(bf16[256,1024]{1,0:T(8,128)(2,1)S(1)} %collective-permute-done.8.rest_4_.rest_5_) | copy-start | bytes 1572868
  88.5 0.8 copy-start.8
  88.5 1.1 copy-start.11
  103.9 0.8 copy-start.9

commit v14 on v6

--- a/solution.py
+++ b/solution.py
@@ -10,6 +10,8 @@
 HEADS = 16
 BLK = 128
 WIN = 4
+HDIM = 128
+HEADS_PER_STEP = 2
 CHUNKS = 2
 
 
@@ -40,7 +42,8 @@
 def attend_kernel(level_count, meta, q_ref, ok_ref, ov_ref, pk_ref, pv_ref, *rest):
     far_refs = rest[: 2 * level_count]
     out_ref, bias_ref = rest[-2:]
-    rows, head_dim = q_ref.shape
+    rows = q_ref.shape[0]
+    head_dim = HDIM
     panel_len = rows // BLK
     scale = head_dim ** (-0.5)
 
@@ -61,51 +64,55 @@
         bias_ref[:, :rows] = jnp.where(prev_vis, 0.0, -jnp.inf)
         bias_ref[:, rows:] = jnp.where(own_vis, 0.0, -jnp.inf)
 
-    q = q_ref[...]
-    s_prev = _nt(q, pk_ref[...]) * scale + bias_ref[:, :rows]
-    s_own = _nt(q, ok_ref[...]) * scale + bias_ref[:, rows:]
-    m_w = jnp.maximum(s_own.max(-1, keepdims=True), s_prev.max(-1, keepdims=True))
-    e_own = jnp.exp(s_own - m_w)
-    e_prev = jnp.exp(s_prev - m_w)
-    l_w = e_own.sum(-1, keepdims=True) + e_prev.sum(-1, keepdims=True)
-    o_w = _nn(e_own.astype(jnp.bfloat16), ov_ref[...]) + _nn(e_prev.astype(jnp.bfloat16), pv_ref[...])
+    for sub in range(q_ref.shape[1] // head_dim):
+        cols = slice(sub * head_dim, (sub + 1) * head_dim)
+        q = q_ref[:, cols]
+        s_prev = _nt(q, pk_ref[:, cols]) * scale + bias_ref[:, :rows]
+        s_own = _nt(q, ok_ref[:, cols]) * scale + bias_ref[:, rows:]
+        m_w = jnp.maximum(s_own.max(-1, keepdims=True), s_prev.max(-1, keepdims=True))
+        e_own = jnp.exp(s_own - m_w)
+        e_prev = jnp.exp(s_prev - m_w)
+        l_w = e_own.sum(-1, keepdims=True) + e_prev.sum(-1, keepdims=True)
+        o_w = _nn(e_own.astype(jnp.bfloat16), ov_ref[:, cols]) + _nn(e_prev.astype(jnp.bfloat16), pv_ref[:, cols])
 
-    maxes, totals, sums = [m_w], [l_w], [o_w]
-    for b in range(level_count):
-        s = _nt(q, far_refs[2 * b][...]) * scale
-        m = s.max(-1, keepdims=True)
-        e = jnp.exp(s - m)
-        maxes.append(m)
-        totals.append(e.sum(-1, keepdims=True))
-        sums.append(_nn(e.astype(jnp.bfloat16), far_refs[2 * b + 1][...]))
+        maxes, totals, sums = [m_w], [l_w], [o_w]
+        for b in range(level_count):
+            s = _nt(q, far_refs[2 * b][:, cols]) * scale
+            m = s.max(-1, keepdims=True)
+            e = jnp.exp(s - m)
+            maxes.append(m)
+            totals.append(e.sum(-1, keepdims=True))
+            sums.append(_nn(e.astype(jnp.bfloat16), far_refs[2 * b + 1][:, cols]))
 
-    top = maxes[0]
-    for m in maxes[1:]:
-        top = jnp.maximum(top, m)
-    total = jnp.zeros_like(l_w)
-    output = jnp.zeros_like(o_w)
-    for m, l, o in zip(maxes, totals, sums):
-        factor = jnp.exp(m - top)
-        total = total + l * factor
-        output = output + o * factor
-    out_ref[...] = (output / total).astype(out_ref.dtype)
+        top = maxes[0]
+        for m in maxes[1:]:
+            top = jnp.maximum(top, m)
+        total = jnp.zeros_like(l_w)
+        output = jnp.zeros_like(o_w)
+        for m, l, o in zip(maxes, totals, sums):
+            factor = jnp.exp(m - top)
+            total = total + l * factor
+            output = output + o * factor
+        out_ref[:, cols] = (output / total).astype(out_ref.dtype)
 
 
 def attend(meta, queries, own_k, own_v, prev_k, prev_v, far, first_head, prior=None):
     rows, features = queries.shape
     head_dim = features // HEADS
-    heads = prev_k.shape[1] // head_dim
+    block = head_dim * HEADS_PER_STEP
+    heads = prev_k.shape[1] // block
+    first_head = first_head // HEADS_PER_STEP
     level_count = len(far)
     far_rows = far[0].shape[0] // 2
-    whole = pl.BlockSpec((rows, head_dim), lambda h, meta: (0, h + first_head))
-    part = pl.BlockSpec((rows, head_dim), lambda h, meta: (0, h))
+    whole = pl.BlockSpec((rows, block), lambda h, meta: (0, h + first_head))
+    part = pl.BlockSpec((rows, block), lambda h, meta: (0, h))
     far_specs = []
     for _ in range(level_count):
-        far_specs.append(pl.BlockSpec((far_rows, head_dim), lambda h, meta: (0, h)))
-        far_specs.append(pl.BlockSpec((far_rows, head_dim), lambda h, meta: (1, h)))
+        far_specs.append(pl.BlockSpec((far_rows, block), lambda h, meta: (0, h)))
+        far_specs.append(pl.BlockSpec((far_rows, block), lambda h, meta: (1, h)))
     far_args = []
-    for block in far:
-        far_args += [block, block]
+    for arrived in far:
+        far_args += [arrived, arrived]
     keys = 2 * rows + level_count * far_rows
     args = [meta, queries, own_k, own_v, prev_k, prev_v, *far_args]
     in_specs = [whole] * 3 + [part] * 2 + far_specs
@@ -127,9 +134,9 @@
         input_output_aliases=aliases,
         compiler_params=pltpu.CompilerParams(dimension_semantics=("arbitrary",)),
         cost_estimate=pl.CostEstimate(
-            flops=4 * rows * keys * head_dim * heads,
-            transcendentals=rows * keys * heads,
-            bytes_accessed=2 * head_dim * heads * (6 * rows + 2 * level_count * far_rows),
+            flops=4 * rows * keys * head_dim * HEADS_PER_STEP * heads,
+            transcendentals=rows * keys * heads * HEADS_PER_STEP,
+            bytes_accessed=2 * head_dim * HEADS_PER_STEP * heads * (6 * rows + 2 * level_count * far_rows),
         ),
     )(*args)
 

time: 108 us -> 107 us (level)
  Pallas kernels: 28.6 us -> 26.4 us
  waiting for transfers between devices: 55.4 us -> 56.5 us
    pallas_call x2, Pallas kernels: 28.6 us -> 26.4 us  [attend(): pl.pallas_call(functools.partial(attend_kernel, level_count), out_shape=j...]
  transfers between devices with their start and end apart: 12 -> 12, of which waited for: 5 -> 5; matrix products, arithmetic and copies ran while one was open for 4% -> 4% of each run, Pallas kernels for 13% -> 12%
where the time goes in v14:
time: 107 us
  waiting for transfers between devices  56.5 us (53%)
  Pallas kernels  26.4 us (25%)
  starting transfers between devices  11.8 us (11%)
  local copies, waits for them, and re-layouts  6.91 us (6%)
  between operations  2.7 us (3%)
  other arithmetic  2.44 us (2%)
    ppermute x8, waiting for transfers between devices, from_partner(): return lax.ppermute(value, axis, pairs)  56.5 us
    pallas_call x2, Pallas kernels, attend(): pl.pallas_call(functools.partial(attend_kernel, level_count), out_shape=j...  26.4 us
    ppermute x8, starting transfers between devices, from_partner(): return lax.ppermute(value, axis, pairs)  6.68 us
    ppermute x4, starting transfers between devices, passed_along(): return lax.ppermute(block, axis, route)  5.13 us
    slice x1, local copies, waits for them, and re-layouts, on_device(): key_rows[:, cols]  2.77 us
  transfers between devices with their start and end apart: 12, of which 5 were waited for; matrix products, arithmetic and copies ran while one was open for 4% of the time, Pallas kernels for 12%

profile of v14, /device:TPU:29, one launch (start us, length us, event | category | flops | bytes accessed | tf_op | source)
XLA Modules:
  0.0 106.8 jit_solution(10189367551162485163)
XLA Ops:
  0.0 2.8 %fusion.1 = (bf16[384,1024]{1,0:T(8,128)(2,1)}, bf16[384,1024]{1,0:T(8,128)(2,1)}) fusion(bf16[384,2048]{1,0:T(8,128)(2,1)} %ok_ref.3), kind=kLoop, calls=%fused_computation.22 | loop fusion | bytes 3145728 | tf_op jit(solution)/shard_map/slice | solution.py:155
  2.8 1.3 %collective-permute-start.6 = (bf16[384,1024]{1,0:T(8,128)(2,1)}, bf16[384,1024]{1,0:T(8,128)(2,1)}, u32[]{:S(2)}, u32[]{:S(2)}) collective-permute-start(bf16[384,1024]{1,0:T(8,128)(2,1)} %get-tuple-element.23), channel_id=1, source_target_pairs={{0,1},{1,2},{2,3},{3,4},{4,5},{5,6},{6,7},{7,8},{8,9},{9,10},{10,1... | collective-permute-start | bytes 2359304 | tf_op jit(solution)/shard_map/ppermute | solution.py:21
  4.1 0.7 constant_dynamic-slice_fusion.2
  7.3 0.0 copy-start.1
  7.3 0.2 constant_dynamic-slice_fusion.1
  7.5 1.2 %copy-done.1 = bf16[384,2048]{1,0:T(8,128)(2,1)S(1)} copy-done((bf16[384,2048]{1,0:T(8,128)(2,1)S(1)}, bf16[384,2048]{1,0:T(8,128)(2,1)}, u32[]{:S(2)}) %copy-start.1) | copy-done | bytes 1572888
  8.7 0.2 constant_dynamic-slice_fusion
  9.0 1.4 %collective-permute-start.8 = (bf16[256,1024]{1,0:T(8,128)(2,1)S(1)}, bf16[256,1024]{1,0:T(8,128)(2,1)S(1)}, u32[]{:S(2)}, u32[]{:S(2)}) collective-permute-start(bf16[256,1024]{1,0:T(8,128)(2,1)S(1)} %pad_maximum_fusion.4), channel_id=1, source_target_pairs={{0,1},{1,0},{2,3},{3,2},{4,5},{5,4},{6,7},{7,6},{8,9},{9,8},{10,11... | collective-permute-start | bytes 1572872 | tf_op jit(solution)/shard_map/ppermute | solution.py:27
  10.4 1.4 %collective-permute-start.9 = (bf16[256,1024]{1,0:T(8,128)(2,1)S(1)}, bf16[256,1024]{1,0:T(8,128)(2,1)S(1)}, u32[]{:S(2)}, u32[]{:S(2)}) collective-permute-start(bf16[256,1024]{1,0:T(8,128)(2,1)S(1)} %pad_maximum_fusion.5), channel_id=1, source_target_pairs={{0,2},{1,3},{2,0},{3,1},{4,6},{5,7},{6,4},{7,5},{8,10},{9,11},{10,... | collective-permute-start | bytes 1572872 | tf_op jit(solution)/shard_map/ppermute | solution.py:27
  11.8 0.2 collective-permute-start.10
  12.1 1.1 %collective-permute-start.2 = (bf16[256,1024]{1,0:T(8,128)(2,1)S(1)}, bf16[256,1024]{1,0:T(8,128)(2,1)S(1)}, u32[]{:S(2)}, u32[]{:S(2)}) collective-permute-start(bf16[256,1024]{1,0:T(8,128)(2,1)S(1)} %pad_maximum_fusion), channel_id=1, source_target_pairs={{0,1},{1,0},{2,3},{3,2},{4,5},{5,4},{6,7},{7,6},{8,9},{9,8},{10,11... | collective-permute-start | bytes 1572872 | tf_op jit(solution)/shard_map/ppermute | solution.py:27
  13.2 1.0 fusion
  14.3 1.3 %collective-permute-start.7 = (bf16[384,1024]{1,0:T(8,128)(2,1)S(1)}, bf16[384,1024]{1,0:T(8,128)(2,1)S(1)}, u32[]{:S(2)}, u32[]{:S(2)}) collective-permute-start(bf16[384,1024]{1,0:T(8,128)(2,1)S(1)} %get-tuple-element.21), channel_id=1, source_target_pairs={{0,1},{1,2},{2,3},{3,4},{4,5},{5,6},{6,7},{7,8},{8,9},{9,10},{10,1... | collective-permute-start | bytes 2359304 | tf_op jit(solution)/shard_map/ppermute | solution.py:21
  15.6 11.9 %collective-permute-done.9.rest_2_.rest_3_ = bf16[256,1024]{1,0:T(8,128)(2,1)S(1)} collective-permute-done((bf16[256,1024]{1,0:T(8,128)(2,1)S(1)}, bf16[256,1024]{1,0:T(8,128)(2,1)S(1)}, u32[]{:S(2)}, u32[]{:S(2)}) %collective-permute-start.9) | collective-permute-done | bytes 524320 | tf_op jit(solution)/shard_map/ppermute | solution.py:27
  27.5 0.1 collective-permute-start.11
  27.6 1.3 %collective-permute-start = (bf16[384,1024]{1,0:T(8,128)(2,1)}, bf16[384,1024]{1,0:T(8,128)(2,1)}, u32[]{:S(2)}, u32[]{:S(2)}) collective-permute-start(bf16[384,1024]{1,0:T(8,128)(2,1)} %get-tuple-element.24), channel_id=1, source_target_pairs={{0,1},{1,2},{2,3},{3,4},{4,5},{5,6},{6,7},{7,8},{8,9},{9,10},{10,1... | collective-permute-start | bytes 2359304 | tf_op jit(solution)/shard_map/ppermute | solution.py:21
  28.9 0.0 collective-permute-done.2.rest_0_.rest_1_
  28.9 1.3 %collective-permute-start.1 = (bf16[384,1024]{1,0:T(8,128)(2,1)}, bf16[384,1024]{1,0:T(8,128)(2,1)}, u32[]{:S(2)}, u32[]{:S(2)}) collective-permute-start(bf16[384,1024]{1,0:T(8,128)(2,1)} %get-tuple-element.22), channel_id=1, source_target_pairs={{0,1},{1,2},{2,3},{3,4},{4,5},{5,6},{6,7},{7,8},{8,9},{9,10},{10,1... | collective-permute-start | bytes 2359304 | tf_op jit(solution)/shard_map/ppermute | solution.py:21
  30.2 0.0 copy-start.12
  30.2 0.8 pad_maximum_fusion.2
  31.1 0.8 pad_maximum_fusion.1
  31.9 21.7 %collective-permute-done.11.rest_6_.rest_7_ = bf16[256,1024]{1,0:T(8,128)(2,1)S(1)} collective-permute-done((bf16[256,1024]{1,0:T(8,128)(2,1)S(1)}, bf16[256,1024]{1,0:T(8,128)(2,1)S(1)}, u32[]{:S(2)}, u32[]{:S(2)}) %collective-permute-start.11) | collective-permute-done | bytes 524320 | tf_op jit(solution)/shard_map/ppermute | solution.py:27
  53.6 0.5 collective-permute-start.3
  54.1 0.0 collective-permute-done.6.pk_ref
  54.1 2.0 %collective-permute-start.5 = (bf16[256,1024]{1,0:T(8,128)(2,1)S(1)}, bf16[256,1024]{1,0:T(8,128)(2,1)S(1)}, u32[]{:S(2)}, u32[]{:S(2)}) collective-permute-start(bf16[256,1024]{1,0:T(8,128)(2,1)S(1)} %pad_maximum_fusion.3), channel_id=1, source_target_pairs={{0,8},{1,9},{2,10},{3,11},{4,12},{5,13},{6,14},{7,15},{8,0},{9,1},... | collective-permute-start | bytes 1572872 | tf_op jit(solution)/shard_map/ppermute | solution.py:27
  56.1 0.6 pad_add_fusion.meta
  56.7 13.2 %shard_map.55.rest_8_ = bf16[384,2048]{1,0:T(8,128)(2,1)} custom-call(s32[4]{0:T(128)} %pad_add_fusion.meta, bf16[384,2048]{1,0:T(8,128)(2,1)} %q_ref.3, bf16[384,2048]{1,0:T(8,128)(2,1)} %ok_ref.3, bf16[384,2048]{1,0:T(8,128)(2,1)} %ov_ref.3, bf16[384,1024]{1,0:T(8,128)(2,1)} %collective-permute-done.6.pk_ref, bf16[384,1024]{1,0:T(8,128)(2,1)} %copy-done.10, ...), custom_call_target="tpu_custom_call" | custom-call | flops 2013265920 | bytes 6815744 | tf_op jit(solution)/shard_map/pallas_call | solution.py:124
  69.8 4.3 %collective-permute-done.3.rest_2_.rest_3_ = bf16[256,1024]{1,0:T(8,128)(2,1)S(1)} collective-permute-done((bf16[256,1024]{1,0:T(8,128)(2,1)}, bf16[256,1024]{1,0:T(8,128)(2,1)S(1)}, u32[]{:S(2)}, u32[]{:S(2)}) %collective-permute-start.3) | collective-permute-done | bytes 524320 | tf_op jit(solution)/shard_map/ppermute | solution.py:27
  74.1 6.8 %collective-permute-done.4.rest_4_.rest_5_ = bf16[256,1024]{1,0:T(8,128)(2,1)S(1)} collective-permute-done((bf16[256,1024]{1,0:T(8,128)(2,1)}, bf16[256,1024]{1,0:T(8,128)(2,1)S(1)}, u32[]{:S(2)}, u32[]{:S(2)}) %collective-permute-start.4) | collective-permute-done | bytes 524320 | tf_op jit(solution)/shard_map/ppermute | solution.py:27
  80.9 11.8 %collective-permute-done.5.rest_6_.rest_7_ = bf16[256,1024]{1,0:T(8,128)(2,1)S(1)} collective-permute-done((bf16[256,1024]{1,0:T(8,128)(2,1)S(1)}, bf16[256,1024]{1,0:T(8,128)(2,1)S(1)}, u32[]{:S(2)}, u32[]{:S(2)}) %collective-permute-start.5) | collective-permute-done | bytes 524320 | tf_op jit(solution)/shard_map/ppermute | solution.py:27
  92.8 0.8 copy-done.9
  93.5 13.2 %shard_map.56 = bf16[384,2048]{1,0:T(8,128)(2,1)} custom-call(s32[4]{0:T(128)} %pad_add_fusion.meta, bf16[384,2048]{1,0:T(8,128)(2,1)} %q_ref.3, bf16[384,2048]{1,0:T(8,128)(2,1)} %ok_ref.3, bf16[384,2048]{1,0:T(8,128)(2,1)} %ov_ref.3, bf16[384,1024]{1,0:T(8,128)(2,1)} %collective-permute-done.pk_ref, ...), custom_call_target="tpu_custom_call", output_to_operand_aliasing={{}: (14, {})} | custom-call | flops 2013265920 | bytes 6815744 | tf_op jit(solution)/shard_map/pallas_call | solution.py:124
  (34 shorter events, 0.3 us)
Async XLA Ops:
  0.0 7.3 %copy-start = (bf16[384,2048]{1,0:T(8,128)(2,1)S(1)}, bf16[384,2048]{1,0:T(8,128)(2,1)}, u32[]{:S(2)}) copy-start(bf16[384,2048]{1,0:T(8,128)(2,1)} %ok_ref.3) | copy-start | bytes 4718596
  0.0 4.1 %copy-start.11 = (s32[16,4,1]{0,2,1:T(1,128)S(1)}, s32[16,4,1]{0,2,1:T(1,128)}, u32[]{:S(2)}) copy-start(s32[16,4,1]{0,2,1:T(1,128)} %param.9) | copy-start | bytes 772
  2.8 51.3 %collective-permute-start.6 = (bf16[384,1024]{1,0:T(8,128)(2,1)}, bf16[384,1024]{1,0:T(8,128)(2,1)}, u32[]{:S(2)}, u32[]{:S(2)}) collective-permute-start(bf16[384,1024]{1,0:T(8,128)(2,1)} %get-tuple-element.23), channel_id=1, source_target_pairs={{0,1},{1,2},{2,3},{3,4},{4,5},{5,6},{6,7},{7,8},{8,9},{9,10},{10,1... | collective-permute-start | bytes 2359304 | tf_op jit(solution)/shard_map/ppermute | solution.py:21
  7.3 1.4 %copy-start.1 = (bf16[384,2048]{1,0:T(8,128)(2,1)S(1)}, bf16[384,2048]{1,0:T(8,128)(2,1)}, u32[]{:S(2)}) copy-start(bf16[384,2048]{1,0:T(8,128)(2,1)} %ov_ref.3) | copy-start | bytes 4718596
  9.0 5.3 %collective-permute-start.8 = (bf16[256,1024]{1,0:T(8,128)(2,1)S(1)}, bf16[256,1024]{1,0:T(8,128)(2,1)S(1)}, u32[]{:S(2)}, u32[]{:S(2)}) collective-permute-start(bf16[256,1024]{1,0:T(8,128)(2,1)S(1)} %pad_maximum_fusion.4), channel_id=1, source_target_pairs={{0,1},{1,0},{2,3},{3,2},{4,5},{5,4},{6,7},{7,6},{8,9},{9,8},{10,11... | collective-permute-start | bytes 1572872 | tf_op jit(solution)/shard_map/ppermute | solution.py:27
  10.4 17.1 %collective-permute-start.9 = (bf16[256,1024]{1,0:T(8,128)(2,1)S(1)}, bf16[256,1024]{1,0:T(8,128)(2,1)S(1)}, u32[]{:S(2)}, u32[]{:S(2)}) collective-permute-start(bf16[256,1024]{1,0:T(8,128)(2,1)S(1)} %pad_maximum_fusion.5), channel_id=1, source_target_pairs={{0,2},{1,3},{2,0},{3,1},{4,6},{5,7},{6,4},{7,5},{8,10},{9,11},{10,... | collective-permute-start | bytes 1572872 | tf_op jit(solution)/shard_map/ppermute | solution.py:27
  11.8 15.7 %collective-permute-start.10 = (bf16[256,1024]{1,0:T(8,128)(2,1)S(1)}, bf16[256,1024]{1,0:T(8,128)(2,1)S(1)}, u32[]{:S(2)}, u32[]{:S(2)}) collective-permute-start(bf16[256,1024]{1,0:T(8,128)(2,1)S(1)} %pad_maximum_fusion.6), channel_id=1, source_target_pairs={{0,4},{1,5},{2,6},{3,7},{4,0},{5,1},{6,2},{7,3},{8,12},{9,13},{10,... | collective-permute-start | bytes 1572872 | tf_op jit(solution)/shard_map/ppermute | solution.py:27
  12.1 16.8 %collective-permute-start.2 = (bf16[256,1024]{1,0:T(8,128)(2,1)S(1)}, bf16[256,1024]{1,0:T(8,128)(2,1)S(1)}, u32[]{:S(2)}, u32[]{:S(2)}) collective-permute-start(bf16[256,1024]{1,0:T(8,128)(2,1)S(1)} %pad_maximum_fusion), channel_id=1, source_target_pairs={{0,1},{1,0},{2,3},{3,2},{4,5},{5,4},{6,7},{7,6},{8,9},{9,8},{10,11... | collective-permute-start | bytes 1572872 | tf_op jit(solution)/shard_map/ppermute | solution.py:27
  14.3 16.8 %copy-start.2 = (bf16[256,1024]{1,0:T(8,128)(2,1)}, bf16[256,1024]{1,0:T(8,128)(2,1)S(1)}, u32[]{:S(2)}) copy-start(bf16[256,1024]{1,0:T(8,128)(2,1)S(1)} %collective-permute-done.8.rest_0_.rest_1_) | copy-start | bytes 1572868
  14.3 39.8 %collective-permute-start.7 = (bf16[384,1024]{1,0:T(8,128)(2,1)S(1)}, bf16[384,1024]{1,0:T(8,128)(2,1)S(1)}, u32[]{:S(2)}, u32[]{:S(2)}) collective-permute-start(bf16[384,1024]{1,0:T(8,128)(2,1)S(1)} %get-tuple-element.21), channel_id=1, source_target_pairs={{0,1},{1,2},{2,3},{3,4},{4,5},{5,6},{6,7},{7,8},{8,9},{9,10},{10,1... | collective-permute-start | bytes 2359304 | tf_op jit(solution)/shard_map/ppermute | solution.py:21
  27.5 4.4 %copy-start.3 = (bf16[256,1024]{1,0:T(8,128)(2,1)}, bf16[256,1024]{1,0:T(8,128)(2,1)S(1)}, u32[]{:S(2)}) copy-start(bf16[256,1024]{1,0:T(8,128)(2,1)S(1)} %collective-permute-done.9.rest_2_.rest_3_) | copy-start | bytes 1572868
  27.5 26.1 %collective-permute-start.11 = (bf16[256,1024]{1,0:T(8,128)(2,1)S(1)}, bf16[256,1024]{1,0:T(8,128)(2,1)S(1)}, u32[]{:S(2)}, u32[]{:S(2)}) collective-permute-start(bf16[256,1024]{1,0:T(8,128)(2,1)S(1)} %pad_maximum_fusion.7), channel_id=1, source_target_pairs={{0,8},{1,9},{2,10},{3,11},{4,12},{5,13},{6,14},{7,15},{8,0},{9,1},... | collective-permute-start | bytes 1572872 | tf_op jit(solution)/shard_map/ppermute | solution.py:27
  27.6 4.4 %copy-start.4 = (bf16[256,1024]{1,0:T(8,128)(2,1)}, bf16[256,1024]{1,0:T(8,128)(2,1)S(1)}, u32[]{:S(2)}) copy-start(bf16[256,1024]{1,0:T(8,128)(2,1)S(1)} %collective-permute-done.10.rest_4_.rest_5_) | copy-start | bytes 1572868
  27.6 65.2 %collective-permute-start = (bf16[384,1024]{1,0:T(8,128)(2,1)}, bf16[384,1024]{1,0:T(8,128)(2,1)}, u32[]{:S(2)}, u32[]{:S(2)}) collective-permute-start(bf16[384,1024]{1,0:T(8,128)(2,1)} %get-tuple-element.24), channel_id=1, source_target_pairs={{0,1},{1,2},{2,3},{3,4},{4,5},{5,6},{6,7},{7,8},{8,9},{9,10},{10,1... | collective-permute-start | bytes 2359304 | tf_op jit(solution)/shard_map/ppermute | solution.py:21
  28.9 3.1 %copy-start.6 = (bf16[256,1024]{1,0:T(8,128)(2,1)}, bf16[256,1024]{1,0:T(8,128)(2,1)S(1)}, u32[]{:S(2)}) copy-start(bf16[256,1024]{1,0:T(8,128)(2,1)S(1)} %collective-permute-done.2.rest_0_.rest_1_) | copy-start | bytes 1572868
  28.9 63.9 %collective-permute-start.1 = (bf16[384,1024]{1,0:T(8,128)(2,1)}, bf16[384,1024]{1,0:T(8,128)(2,1)}, u32[]{:S(2)}, u32[]{:S(2)}) collective-permute-start(bf16[384,1024]{1,0:T(8,128)(2,1)} %get-tuple-element.22), channel_id=1, source_target_pairs={{0,1},{1,2},{2,3},{3,4},{4,5},{5,6},{6,7},{7,8},{8,9},{9,10},{10,1... | collective-permute-start | bytes 2359304 | tf_op jit(solution)/shard_map/ppermute | solution.py:21
  30.2 25.9 %copy-start.12 = (s32[3]{0:T(128)S(1)}, s32[3]{0:T(128)}, u32[]{:S(2)}) copy-start(s32[3]{0:T(128)} %param.8) | copy-start | bytes 40
  53.6 3.1 %copy-start.5 = (bf16[256,1024]{1,0:T(8,128)(2,1)}, bf16[256,1024]{1,0:T(8,128)(2,1)S(1)}, u32[]{:S(2)}) copy-start(bf16[256,1024]{1,0:T(8,128)(2,1)S(1)} %collective-permute-done.11.rest_6_.rest_7_) | copy-start | bytes 1572868
  53.6 20.5 %collective-permute-start.3 = (bf16[256,1024]{1,0:T(8,128)(2,1)}, bf16[256,1024]{1,0:T(8,128)(2,1)S(1)}, u32[]{:S(2)}, u32[]{:S(2)}) collective-permute-start(bf16[256,1024]{1,0:T(8,128)(2,1)} %pad_maximum_fusion.1), channel_id=1, source_target_pairs={{0,2},{1,3},{2,0},{3,1},{4,6},{5,7},{6,4},{7,5},{8,10},{9,11},{10,... | collective-permute-start | bytes 1572872 | tf_op jit(solution)/shard_map/ppermute | solution.py:27
  54.1 26.8 %collective-permute-start.4 = (bf16[256,1024]{1,0:T(8,128)(2,1)}, bf16[256,1024]{1,0:T(8,128)(2,1)S(1)}, u32[]{:S(2)}, u32[]{:S(2)}) collective-permute-start(bf16[256,1024]{1,0:T(8,128)(2,1)} %pad_maximum_fusion.2), channel_id=1, source_target_pairs={{0,4},{1,5},{2,6},{3,7},{4,0},{5,1},{6,2},{7,3},{8,12},{9,13},{10,... | collective-permute-start | bytes 1572872 | tf_op jit(solution)/shard_map/ppermute | solution.py:27
  54.1 2.6 %copy-start.10 = (bf16[384,1024]{1,0:T(8,128)(2,1)}, bf16[384,1024]{1,0:T(8,128)(2,1)S(1)}, u32[]{:S(2)}) copy-start(bf16[384,1024]{1,0:T(8,128)(2,1)S(1)} %collective-permute-done.7.pv_ref) | copy-start | bytes 2359300
  54.1 38.7 %collective-permute-start.5 = (bf16[256,1024]{1,0:T(8,128)(2,1)S(1)}, bf16[256,1024]{1,0:T(8,128)(2,1)S(1)}, u32[]{:S(2)}, u32[]{:S(2)}) collective-permute-start(bf16[256,1024]{1,0:T(8,128)(2,1)S(1)} %pad_maximum_fusion.3), channel_id=1, source_target_pairs={{0,8},{1,9},{2,10},{3,11},{4,12},{5,13},{6,14},{7,15},{8,0},{9,1},... | collective-permute-start | bytes 1572872 | tf_op jit(solution)/shard_map/ppermute | solution.py:27
  74.1 18.6 %copy-start.7 = (bf16[256,1024]{1,0:T(8,128)(2,1)}, bf16[256,1024]{1,0:T(8,128)(2,1)S(1)}, u32[]{:S(2)}) copy-start(bf16[256,1024]{1,0:T(8,128)(2,1)S(1)} %collective-permute-done.3.rest_2_.rest_3_) | copy-start | bytes 1572868
  80.9 11.9 %copy-start.8 = (bf16[256,1024]{1,0:T(8,128)(2,1)}, bf16[256,1024]{1,0:T(8,128)(2,1)S(1)}, u32[]{:S(2)}) copy-start(bf16[256,1024]{1,0:T(8,128)(2,1)S(1)} %collective-permute-done.4.rest_4_.rest_5_) | copy-start | bytes 1572868
  92.7 0.8 copy-start.9

commit v15 on v14

--- a/solution.py
+++ b/solution.py
@@ -11,7 +11,7 @@
 BLK = 128
 WIN = 4
 HDIM = 128
-HEADS_PER_STEP = 2
+HEADS_PER_STEP = 4
 CHUNKS = 2
 
 

time: 107 us -> 107 us (level)
  no operation moved by 1% of the time
where the time goes in v15:
time: 107 us; the launch traced here: 106 us
  waiting for transfers between devices  57 us (53%)
  Pallas kernels  25.5 us (24%)
  starting transfers between devices  11.8 us (11%)
  local copies, waits for them, and re-layouts  6.91 us (6%)
  between operations  2.7 us (3%)
  other arithmetic  2.44 us (2%)
    ppermute x8, waiting for transfers between devices, from_partner(): return lax.ppermute(value, axis, pairs)  57 us
    pallas_call x2, Pallas kernels, attend(): pl.pallas_call(functools.partial(attend_kernel, level_count), out_shape=j...  25.5 us
    ppermute x8, starting transfers between devices, from_partner(): return lax.ppermute(value, axis, pairs)  6.68 us
    ppermute x4, starting transfers between devices, passed_along(): return lax.ppermute(block, axis, route)  5.13 us
    slice x1, local copies, waits for them, and re-layouts, on_device(): key_rows[:, cols]  2.77 us
  transfers between devices with their start and end apart: 12, of which 5 were waited for; matrix products, arithmetic and copies ran while one was open for 4% of the time, Pallas kernels for 12%

profile of v15, /device:TPU:29, one launch (start us, length us, event | category | flops | bytes accessed | tf_op | source)
XLA Modules:
  0.0 106.3 jit_solution(3851457778187704735)
XLA Ops:
  0.0 2.8 %fusion.1 = (bf16[384,1024]{1,0:T(8,128)(2,1)}, bf16[384,1024]{1,0:T(8,128)(2,1)}) fusion(bf16[384,2048]{1,0:T(8,128)(2,1)} %ok_ref.3), kind=kLoop, calls=%fused_computation.22 | loop fusion | bytes 3145728 | tf_op jit(solution)/shard_map/slice | solution.py:155
  2.8 1.3 %collective-permute-start.6 = (bf16[384,1024]{1,0:T(8,128)(2,1)}, bf16[384,1024]{1,0:T(8,128)(2,1)}, u32[]{:S(2)}, u32[]{:S(2)}) collective-permute-start(bf16[384,1024]{1,0:T(8,128)(2,1)} %get-tuple-element.23), channel_id=1, source_target_pairs={{0,1},{1,2},{2,3},{3,4},{4,5},{5,6},{6,7},{7,8},{8,9},{9,10},{10,1... | collective-permute-start | bytes 2359304 | tf_op jit(solution)/shard_map/ppermute | solution.py:21
  4.1 0.7 constant_dynamic-slice_fusion.2
  7.3 0.0 copy-start.1
  7.3 0.2 constant_dynamic-slice_fusion.1
  7.5 1.2 %copy-done.1 = bf16[384,2048]{1,0:T(8,128)(2,1)S(1)} copy-done((bf16[384,2048]{1,0:T(8,128)(2,1)S(1)}, bf16[384,2048]{1,0:T(8,128)(2,1)}, u32[]{:S(2)}) %copy-start.1) | copy-done | bytes 1572888
  8.7 0.2 constant_dynamic-slice_fusion
  9.0 1.4 %collective-permute-start.8 = (bf16[256,1024]{1,0:T(8,128)(2,1)S(1)}, bf16[256,1024]{1,0:T(8,128)(2,1)S(1)}, u32[]{:S(2)}, u32[]{:S(2)}) collective-permute-start(bf16[256,1024]{1,0:T(8,128)(2,1)S(1)} %pad_maximum_fusion.4), channel_id=1, source_target_pairs={{0,1},{1,0},{2,3},{3,2},{4,5},{5,4},{6,7},{7,6},{8,9},{9,8},{10,11... | collective-permute-start | bytes 1572872 | tf_op jit(solution)/shard_map/ppermute | solution.py:27
  10.4 1.4 %collective-permute-start.9 = (bf16[256,1024]{1,0:T(8,128)(2,1)S(1)}, bf16[256,1024]{1,0:T(8,128)(2,1)S(1)}, u32[]{:S(2)}, u32[]{:S(2)}) collective-permute-start(bf16[256,1024]{1,0:T(8,128)(2,1)S(1)} %pad_maximum_fusion.5), channel_id=1, source_target_pairs={{0,2},{1,3},{2,0},{3,1},{4,6},{5,7},{6,4},{7,5},{8,10},{9,11},{10,... | collective-permute-start | bytes 1572872 | tf_op jit(solution)/shard_map/ppermute | solution.py:27
  11.8 0.2 collective-permute-start.10
  12.1 1.1 %collective-permute-start.2 = (bf16[256,1024]{1,0:T(8,128)(2,1)S(1)}, bf16[256,1024]{1,0:T(8,128)(2,1)S(1)}, u32[]{:S(2)}, u32[]{:S(2)}) collective-permute-start(bf16[256,1024]{1,0:T(8,128)(2,1)S(1)} %pad_maximum_fusion), channel_id=1, source_target_pairs={{0,1},{1,0},{2,3},{3,2},{4,5},{5,4},{6,7},{7,6},{8,9},{9,8},{10,11... | collective-permute-start | bytes 1572872 | tf_op jit(solution)/shard_map/ppermute | solution.py:27
  13.2 1.0 fusion
  14.3 1.3 %collective-permute-start.7 = (bf16[384,1024]{1,0:T(8,128)(2,1)S(1)}, bf16[384,1024]{1,0:T(8,128)(2,1)S(1)}, u32[]{:S(2)}, u32[]{:S(2)}) collective-permute-start(bf16[384,1024]{1,0:T(8,128)(2,1)S(1)} %get-tuple-element.21), channel_id=1, source_target_pairs={{0,1},{1,2},{2,3},{3,4},{4,5},{5,6},{6,7},{7,8},{8,9},{9,10},{10,1... | collective-permute-start | bytes 2359304 | tf_op jit(solution)/shard_map/ppermute | solution.py:21
  15.6 11.9 %collective-permute-done.9.rest_2_.rest_3_ = bf16[256,1024]{1,0:T(8,128)(2,1)S(1)} collective-permute-done((bf16[256,1024]{1,0:T(8,128)(2,1)S(1)}, bf16[256,1024]{1,0:T(8,128)(2,1)S(1)}, u32[]{:S(2)}, u32[]{:S(2)}) %collective-permute-start.9) | collective-permute-done | bytes 524320 | tf_op jit(solution)/shard_map/ppermute | solution.py:27
  27.5 0.1 collective-permute-start.11
  27.6 1.3 %collective-permute-start = (bf16[384,1024]{1,0:T(8,128)(2,1)}, bf16[384,1024]{1,0:T(8,128)(2,1)}, u32[]{:S(2)}, u32[]{:S(2)}) collective-permute-start(bf16[384,1024]{1,0:T(8,128)(2,1)} %get-tuple-element.24), channel_id=1, source_target_pairs={{0,1},{1,2},{2,3},{3,4},{4,5},{5,6},{6,7},{7,8},{8,9},{9,10},{10,1... | collective-permute-start | bytes 2359304 | tf_op jit(solution)/shard_map/ppermute | solution.py:21
  28.9 0.0 collective-permute-done.2.rest_0_.rest_1_
  28.9 1.3 %collective-permute-start.1 = (bf16[384,1024]{1,0:T(8,128)(2,1)}, bf16[384,1024]{1,0:T(8,128)(2,1)}, u32[]{:S(2)}, u32[]{:S(2)}) collective-permute-start(bf16[384,1024]{1,0:T(8,128)(2,1)} %get-tuple-element.22), channel_id=1, source_target_pairs={{0,1},{1,2},{2,3},{3,4},{4,5},{5,6},{6,7},{7,8},{8,9},{9,10},{10,1... | collective-permute-start | bytes 2359304 | tf_op jit(solution)/shard_map/ppermute | solution.py:21
  30.2 0.0 copy-start.12
  30.2 0.8 pad_maximum_fusion.2
  31.1 0.8 pad_maximum_fusion.1
  31.9 21.7 %collective-permute-done.11.rest_6_.rest_7_ = bf16[256,1024]{1,0:T(8,128)(2,1)S(1)} collective-permute-done((bf16[256,1024]{1,0:T(8,128)(2,1)S(1)}, bf16[256,1024]{1,0:T(8,128)(2,1)S(1)}, u32[]{:S(2)}, u32[]{:S(2)}) %collective-permute-start.11) | collective-permute-done | bytes 524320 | tf_op jit(solution)/shard_map/ppermute | solution.py:27
  53.6 0.5 collective-permute-start.3
  54.1 0.0 collective-permute-done.6.pk_ref
  54.1 2.0 %collective-permute-start.5 = (bf16[256,1024]{1,0:T(8,128)(2,1)S(1)}, bf16[256,1024]{1,0:T(8,128)(2,1)S(1)}, u32[]{:S(2)}, u32[]{:S(2)}) collective-permute-start(bf16[256,1024]{1,0:T(8,128)(2,1)S(1)} %pad_maximum_fusion.3), channel_id=1, source_target_pairs={{0,8},{1,9},{2,10},{3,11},{4,12},{5,13},{6,14},{7,15},{8,0},{9,1},... | collective-permute-start | bytes 1572872 | tf_op jit(solution)/shard_map/ppermute | solution.py:27
  56.1 0.6 pad_add_fusion.meta
  56.7 12.7 %shard_map.55.rest_8_ = bf16[384,2048]{1,0:T(8,128)(2,1)} custom-call(s32[4]{0:T(128)} %pad_add_fusion.meta, bf16[384,2048]{1,0:T(8,128)(2,1)} %q_ref.3, bf16[384,2048]{1,0:T(8,128)(2,1)} %ok_ref.3, bf16[384,2048]{1,0:T(8,128)(2,1)} %ov_ref.3, bf16[384,1024]{1,0:T(8,128)(2,1)} %collective-permute-done.6.pk_ref, bf16[384,1024]{1,0:T(8,128)(2,1)} %copy-done.10, ...), custom_call_target="tpu_custom_call" | custom-call | flops 2013265920 | bytes 6815744 | tf_op jit(solution)/shard_map/pallas_call | solution.py:124
  69.4 4.8 %collective-permute-done.3.rest_2_.rest_3_ = bf16[256,1024]{1,0:T(8,128)(2,1)S(1)} collective-permute-done((bf16[256,1024]{1,0:T(8,128)(2,1)}, bf16[256,1024]{1,0:T(8,128)(2,1)S(1)}, u32[]{:S(2)}, u32[]{:S(2)}) %collective-permute-start.3) | collective-permute-done | bytes 524320 | tf_op jit(solution)/shard_map/ppermute | solution.py:27
  74.1 6.8 %collective-permute-done.4.rest_4_.rest_5_ = bf16[256,1024]{1,0:T(8,128)(2,1)S(1)} collective-permute-done((bf16[256,1024]{1,0:T(8,128)(2,1)}, bf16[256,1024]{1,0:T(8,128)(2,1)S(1)}, u32[]{:S(2)}, u32[]{:S(2)}) %collective-permute-start.4) | collective-permute-done | bytes 524320 | tf_op jit(solution)/shard_map/ppermute | solution.py:27
  80.9 11.8 %collective-permute-done.5.rest_6_.rest_7_ = bf16[256,1024]{1,0:T(8,128)(2,1)S(1)} collective-permute-done((bf16[256,1024]{1,0:T(8,128)(2,1)S(1)}, bf16[256,1024]{1,0:T(8,128)(2,1)S(1)}, u32[]{:S(2)}, u32[]{:S(2)}) %collective-permute-start.5) | collective-permute-done | bytes 524320 | tf_op jit(solution)/shard_map/ppermute | solution.py:27
  92.8 0.8 copy-done.9
  93.5 12.8 %shard_map.56 = bf16[384,2048]{1,0:T(8,128)(2,1)} custom-call(s32[4]{0:T(128)} %pad_add_fusion.meta, bf16[384,2048]{1,0:T(8,128)(2,1)} %q_ref.3, bf16[384,2048]{1,0:T(8,128)(2,1)} %ok_ref.3, bf16[384,2048]{1,0:T(8,128)(2,1)} %ov_ref.3, bf16[384,1024]{1,0:T(8,128)(2,1)} %collective-permute-done.pk_ref, ...), custom_call_target="tpu_custom_call", output_to_operand_aliasing={{}: (14, {})} | custom-call | flops 2013265920 | bytes 6815744 | tf_op jit(solution)/shard_map/pallas_call | solution.py:124
  (34 shorter events, 0.3 us)
Async XLA Ops:
  0.0 7.3 %copy-start = (bf16[384,2048]{1,0:T(8,128)(2,1)S(1)}, bf16[384,2048]{1,0:T(8,128)(2,1)}, u32[]{:S(2)}) copy-start(bf16[384,2048]{1,0:T(8,128)(2,1)} %ok_ref.3) | copy-start | bytes 4718596
  0.0 4.1 %copy-start.11 = (s32[16,4,1]{0,2,1:T(1,128)S(1)}, s32[16,4,1]{0,2,1:T(1,128)}, u32[]{:S(2)}) copy-start(s32[16,4,1]{0,2,1:T(1,128)} %param.9) | copy-start | bytes 772
  2.8 51.3 %collective-permute-start.6 = (bf16[384,1024]{1,0:T(8,128)(2,1)}, bf16[384,1024]{1,0:T(8,128)(2,1)}, u32[]{:S(2)}, u32[]{:S(2)}) collective-permute-start(bf16[384,1024]{1,0:T(8,128)(2,1)} %get-tuple-element.23), channel_id=1, source_target_pairs={{0,1},{1,2},{2,3},{3,4},{4,5},{5,6},{6,7},{7,8},{8,9},{9,10},{10,1... | collective-permute-start | bytes 2359304 | tf_op jit(solution)/shard_map/ppermute | solution.py:21
  7.3 1.4 %copy-start.1 = (bf16[384,2048]{1,0:T(8,128)(2,1)S(1)}, bf16[384,2048]{1,0:T(8,128)(2,1)}, u32[]{:S(2)}) copy-start(bf16[384,2048]{1,0:T(8,128)(2,1)} %ov_ref.3) | copy-start | bytes 4718596
  9.0 5.3 %collective-permute-start.8 = (bf16[256,1024]{1,0:T(8,128)(2,1)S(1)}, bf16[256,1024]{1,0:T(8,128)(2,1)S(1)}, u32[]{:S(2)}, u32[]{:S(2)}) collective-permute-start(bf16[256,1024]{1,0:T(8,128)(2,1)S(1)} %pad_maximum_fusion.4), channel_id=1, source_target_pairs={{0,1},{1,0},{2,3},{3,2},{4,5},{5,4},{6,7},{7,6},{8,9},{9,8},{10,11... | collective-permute-start | bytes 1572872 | tf_op jit(solution)/shard_map/ppermute | solution.py:27
  10.4 17.1 %collective-permute-start.9 = (bf16[256,1024]{1,0:T(8,128)(2,1)S(1)}, bf16[256,1024]{1,0:T(8,128)(2,1)S(1)}, u32[]{:S(2)}, u32[]{:S(2)}) collective-permute-start(bf16[256,1024]{1,0:T(8,128)(2,1)S(1)} %pad_maximum_fusion.5), channel_id=1, source_target_pairs={{0,2},{1,3},{2,0},{3,1},{4,6},{5,7},{6,4},{7,5},{8,10},{9,11},{10,... | collective-permute-start | bytes 1572872 | tf_op jit(solution)/shard_map/ppermute | solution.py:27
  11.8 15.7 %collective-permute-start.10 = (bf16[256,1024]{1,0:T(8,128)(2,1)S(1)}, bf16[256,1024]{1,0:T(8,128)(2,1)S(1)}, u32[]{:S(2)}, u32[]{:S(2)}) collective-permute-start(bf16[256,1024]{1,0:T(8,128)(2,1)S(1)} %pad_maximum_fusion.6), channel_id=1, source_target_pairs={{0,4},{1,5},{2,6},{3,7},{4,0},{5,1},{6,2},{7,3},{8,12},{9,13},{10,... | collective-permute-start | bytes 1572872 | tf_op jit(solution)/shard_map/ppermute | solution.py:27
  12.1 16.8 %collective-permute-start.2 = (bf16[256,1024]{1,0:T(8,128)(2,1)S(1)}, bf16[256,1024]{1,0:T(8,128)(2,1)S(1)}, u32[]{:S(2)}, u32[]{:S(2)}) collective-permute-start(bf16[256,1024]{1,0:T(8,128)(2,1)S(1)} %pad_maximum_fusion), channel_id=1, source_target_pairs={{0,1},{1,0},{2,3},{3,2},{4,5},{5,4},{6,7},{7,6},{8,9},{9,8},{10,11... | collective-permute-start | bytes 1572872 | tf_op jit(solution)/shard_map/ppermute | solution.py:27
  14.3 16.8 %copy-start.2 = (bf16[256,1024]{1,0:T(8,128)(2,1)}, bf16[256,1024]{1,0:T(8,128)(2,1)S(1)}, u32[]{:S(2)}) copy-start(bf16[256,1024]{1,0:T(8,128)(2,1)S(1)} %collective-permute-done.8.rest_0_.rest_1_) | copy-start | bytes 1572868
  14.3 39.8 %collective-permute-start.7 = (bf16[384,1024]{1,0:T(8,128)(2,1)S(1)}, bf16[384,1024]{1,0:T(8,128)(2,1)S(1)}, u32[]{:S(2)}, u32[]{:S(2)}) collective-permute-start(bf16[384,1024]{1,0:T(8,128)(2,1)S(1)} %get-tuple-element.21), channel_id=1, source_target_pairs={{0,1},{1,2},{2,3},{3,4},{4,5},{5,6},{6,7},{7,8},{8,9},{9,10},{10,1... | collective-permute-start | bytes 2359304 | tf_op jit(solution)/shard_map/ppermute | solution.py:21
  27.5 4.4 %copy-start.3 = (bf16[256,1024]{1,0:T(8,128)(2,1)}, bf16[256,1024]{1,0:T(8,128)(2,1)S(1)}, u32[]{:S(2)}) copy-start(bf16[256,1024]{1,0:T(8,128)(2,1)S(1)} %collective-permute-done.9.rest_2_.rest_3_) | copy-start | bytes 1572868
  27.5 26.1 %collective-permute-start.11 = (bf16[256,1024]{1,0:T(8,128)(2,1)S(1)}, bf16[256,1024]{1,0:T(8,128)(2,1)S(1)}, u32[]{:S(2)}, u32[]{:S(2)}) collective-permute-start(bf16[256,1024]{1,0:T(8,128)(2,1)S(1)} %pad_maximum_fusion.7), channel_id=1, source_target_pairs={{0,8},{1,9},{2,10},{3,11},{4,12},{5,13},{6,14},{7,15},{8,0},{9,1},... | collective-permute-start | bytes 1572872 | tf_op jit(solution)/shard_map/ppermute | solution.py:27
  27.6 4.4 %copy-start.4 = (bf16[256,1024]{1,0:T(8,128)(2,1)}, bf16[256,1024]{1,0:T(8,128)(2,1)S(1)}, u32[]{:S(2)}) copy-start(bf16[256,1024]{1,0:T(8,128)(2,1)S(1)} %collective-permute-done.10.rest_4_.rest_5_) | copy-start | bytes 1572868
  27.6 65.2 %collective-permute-start = (bf16[384,1024]{1,0:T(8,128)(2,1)}, bf16[384,1024]{1,0:T(8,128)(2,1)}, u32[]{:S(2)}, u32[]{:S(2)}) collective-permute-start(bf16[384,1024]{1,0:T(8,128)(2,1)} %get-tuple-element.24), channel_id=1, source_target_pairs={{0,1},{1,2},{2,3},{3,4},{4,5},{5,6},{6,7},{7,8},{8,9},{9,10},{10,1... | collective-permute-start | bytes 2359304 | tf_op jit(solution)/shard_map/ppermute | solution.py:21
  28.9 3.1 %copy-start.6 = (bf16[256,1024]{1,0:T(8,128)(2,1)}, bf16[256,1024]{1,0:T(8,128)(2,1)S(1)}, u32[]{:S(2)}) copy-start(bf16[256,1024]{1,0:T(8,128)(2,1)S(1)} %collective-permute-done.2.rest_0_.rest_1_) | copy-start | bytes 1572868
  28.9 63.9 %collective-permute-start.1 = (bf16[384,1024]{1,0:T(8,128)(2,1)}, bf16[384,1024]{1,0:T(8,128)(2,1)}, u32[]{:S(2)}, u32[]{:S(2)}) collective-permute-start(bf16[384,1024]{1,0:T(8,128)(2,1)} %get-tuple-element.22), channel_id=1, source_target_pairs={{0,1},{1,2},{2,3},{3,4},{4,5},{5,6},{6,7},{7,8},{8,9},{9,10},{10,1... | collective-permute-start | bytes 2359304 | tf_op jit(solution)/shard_map/ppermute | solution.py:21
  30.2 25.9 %copy-start.12 = (s32[3]{0:T(128)S(1)}, s32[3]{0:T(128)}, u32[]{:S(2)}) copy-start(s32[3]{0:T(128)} %param.8) | copy-start | bytes 40
  53.6 3.1 %copy-start.5 = (bf16[256,1024]{1,0:T(8,128)(2,1)}, bf16[256,1024]{1,0:T(8,128)(2,1)S(1)}, u32[]{:S(2)}) copy-start(bf16[256,1024]{1,0:T(8,128)(2,1)S(1)} %collective-permute-done.11.rest_6_.rest_7_) | copy-start | bytes 1572868
  53.6 20.5 %collective-permute-start.3 = (bf16[256,1024]{1,0:T(8,128)(2,1)}, bf16[256,1024]{1,0:T(8,128)(2,1)S(1)}, u32[]{:S(2)}, u32[]{:S(2)}) collective-permute-start(bf16[256,1024]{1,0:T(8,128)(2,1)} %pad_maximum_fusion.1), channel_id=1, source_target_pairs={{0,2},{1,3},{2,0},{3,1},{4,6},{5,7},{6,4},{7,5},{8,10},{9,11},{10,... | collective-permute-start | bytes 1572872 | tf_op jit(solution)/shard_map/ppermute | solution.py:27
  54.1 26.8 %collective-permute-start.4 = (bf16[256,1024]{1,0:T(8,128)(2,1)}, bf16[256,1024]{1,0:T(8,128)(2,1)S(1)}, u32[]{:S(2)}, u32[]{:S(2)}) collective-permute-start(bf16[256,1024]{1,0:T(8,128)(2,1)} %pad_maximum_fusion.2), channel_id=1, source_target_pairs={{0,4},{1,5},{2,6},{3,7},{4,0},{5,1},{6,2},{7,3},{8,12},{9,13},{10,... | collective-permute-start | bytes 1572872 | tf_op jit(solution)/shard_map/ppermute | solution.py:27
  54.1 2.6 %copy-start.10 = (bf16[384,1024]{1,0:T(8,128)(2,1)}, bf16[384,1024]{1,0:T(8,128)(2,1)S(1)}, u32[]{:S(2)}) copy-start(bf16[384,1024]{1,0:T(8,128)(2,1)S(1)} %collective-permute-done.7.pv_ref) | copy-start | bytes 2359300
  54.1 38.7 %collective-permute-start.5 = (bf16[256,1024]{1,0:T(8,128)(2,1)S(1)}, bf16[256,1024]{1,0:T(8,128)(2,1)S(1)}, u32[]{:S(2)}, u32[]{:S(2)}) collective-permute-start(bf16[256,1024]{1,0:T(8,128)(2,1)S(1)} %pad_maximum_fusion.3), channel_id=1, source_target_pairs={{0,8},{1,9},{2,10},{3,11},{4,12},{5,13},{6,14},{7,15},{8,0},{9,1},... | collective-permute-start | bytes 1572872 | tf_op jit(solution)/shard_map/ppermute | solution.py:27
  74.1 18.6 %copy-start.7 = (bf16[256,1024]{1,0:T(8,128)(2,1)}, bf16[256,1024]{1,0:T(8,128)(2,1)S(1)}, u32[]{:S(2)}) copy-start(bf16[256,1024]{1,0:T(8,128)(2,1)S(1)} %collective-permute-done.3.rest_2_.rest_3_) | copy-start | bytes 1572868
  80.9 11.9 %copy-start.8 = (bf16[256,1024]{1,0:T(8,128)(2,1)}, bf16[256,1024]{1,0:T(8,128)(2,1)S(1)}, u32[]{:S(2)}) copy-start(bf16[256,1024]{1,0:T(8,128)(2,1)S(1)} %collective-permute-done.4.rest_4_.rest_5_) | copy-start | bytes 1572868
  92.7 0.8 copy-start.9

commit v16 on v15

--- a/solution.py
+++ b/solution.py
@@ -11,6 +11,7 @@
 BLK = 128
 WIN = 4
 HDIM = 128
+LOG2E = 1.4426950408889634
 HEADS_PER_STEP = 4
 CHUNKS = 2
 
@@ -45,7 +46,7 @@
     rows = q_ref.shape[0]
     head_dim = HDIM
     panel_len = rows // BLK
-    scale = head_dim ** (-0.5)
+    scale = head_dim ** (-0.5) * LOG2E
 
     @pl.when(pl.program_id(0) == 0)
     def _():
@@ -70,8 +71,8 @@
         s_prev = _nt(q, pk_ref[:, cols]) * scale + bias_ref[:, :rows]
         s_own = _nt(q, ok_ref[:, cols]) * scale + bias_ref[:, rows:]
         m_w = jnp.maximum(s_own.max(-1, keepdims=True), s_prev.max(-1, keepdims=True))
-        e_own = jnp.exp(s_own - m_w)
-        e_prev = jnp.exp(s_prev - m_w)
+        e_own = jnp.exp2(s_own - m_w)
+        e_prev = jnp.exp2(s_prev - m_w)
         l_w = e_own.sum(-1, keepdims=True) + e_prev.sum(-1, keepdims=True)
         o_w = _nn(e_own.astype(jnp.bfloat16), ov_ref[:, cols]) + _nn(e_prev.astype(jnp.bfloat16), pv_ref[:, cols])
 
@@ -79,7 +80,7 @@
         for b in range(level_count):
             s = _nt(q, far_refs[2 * b][:, cols]) * scale
             m = s.max(-1, keepdims=True)
-            e = jnp.exp(s - m)
+            e = jnp.exp2(s - m)
             maxes.append(m)
             totals.append(e.sum(-1, keepdims=True))
             sums.append(_nn(e.astype(jnp.bfloat16), far_refs[2 * b + 1][:, cols]))
@@ -90,7 +91,7 @@
         total = jnp.zeros_like(l_w)
         output = jnp.zeros_like(o_w)
         for m, l, o in zip(maxes, totals, sums):
-            factor = jnp.exp(m - top)
+            factor = jnp.exp2(m - top)
             total = total + l * factor
             output = output + o * factor
         out_ref[:, cols] = (output / total).astype(out_ref.dtype)

time: 107 us -> 106 us (level)
  no operation moved by 1% of the time
where the time goes in v16:
time: 106 us
  waiting for transfers between devices  57.3 us (54%)
  Pallas kernels  24.9 us (23%)
  starting transfers between devices  11.8 us (11%)
  local copies, waits for them, and re-layouts  6.91 us (7%)
  between operations  2.7 us (3%)
  other arithmetic  2.44 us (2%)
    ppermute x8, waiting for transfers between devices, from_partner(): return lax.ppermute(value, axis, pairs)  57.3 us
    pallas_call x2, Pallas kernels, attend(): pl.pallas_call(functools.partial(attend_kernel, level_count), out_shape=j...  24.9 us
    ppermute x8, starting transfers between devices, from_partner(): return lax.ppermute(value, axis, pairs)  6.68 us
    ppermute x4, starting transfers between devices, passed_along(): return lax.ppermute(block, axis, route)  5.13 us
    slice x1, local copies, waits for them, and re-layouts, on_device(): key_rows[:, cols]  2.77 us
  transfers between devices with their start and end apart: 12, of which 5 were waited for; matrix products, arithmetic and copies ran while one was open for 4% of the time, Pallas kernels for 12%

profile of v16, /device:TPU:29, one launch (start us, length us, event | category | flops | bytes accessed | tf_op | source)
XLA Modules:
  0.0 106.0 jit_solution(3609976717260878451)
XLA Ops:
  0.0 2.8 %fusion.1 = (bf16[384,1024]{1,0:T(8,128)(2,1)}, bf16[384,1024]{1,0:T(8,128)(2,1)}) fusion(bf16[384,2048]{1,0:T(8,128)(2,1)} %ok_ref.3), kind=kLoop, calls=%fused_computation.22 | loop fusion | bytes 3145728 | tf_op jit(solution)/shard_map/slice | solution.py:156
  2.8 1.3 %collective-permute-start.6 = (bf16[384,1024]{1,0:T(8,128)(2,1)}, bf16[384,1024]{1,0:T(8,128)(2,1)}, u32[]{:S(2)}, u32[]{:S(2)}) collective-permute-start(bf16[384,1024]{1,0:T(8,128)(2,1)} %get-tuple-element.23), channel_id=1, source_target_pairs={{0,1},{1,2},{2,3},{3,4},{4,5},{5,6},{6,7},{7,8},{8,9},{9,10},{10,1... | collective-permute-start | bytes 2359304 | tf_op jit(solution)/shard_map/ppermute | solution.py:22
  4.1 0.7 constant_dynamic-slice_fusion.2
  7.3 0.0 copy-start.1
  7.3 0.2 constant_dynamic-slice_fusion.1
  7.5 1.2 %copy-done.1 = bf16[384,2048]{1,0:T(8,128)(2,1)S(1)} copy-done((bf16[384,2048]{1,0:T(8,128)(2,1)S(1)}, bf16[384,2048]{1,0:T(8,128)(2,1)}, u32[]{:S(2)}) %copy-start.1) | copy-done | bytes 1572888
  8.7 0.2 constant_dynamic-slice_fusion
  9.0 1.4 %collective-permute-start.8 = (bf16[256,1024]{1,0:T(8,128)(2,1)S(1)}, bf16[256,1024]{1,0:T(8,128)(2,1)S(1)}, u32[]{:S(2)}, u32[]{:S(2)}) collective-permute-start(bf16[256,1024]{1,0:T(8,128)(2,1)S(1)} %pad_maximum_fusion.4), channel_id=1, source_target_pairs={{0,1},{1,0},{2,3},{3,2},{4,5},{5,4},{6,7},{7,6},{8,9},{9,8},{10,11... | collective-permute-start | bytes 1572872 | tf_op jit(solution)/shard_map/ppermute | solution.py:28
  10.4 1.4 %collective-permute-start.9 = (bf16[256,1024]{1,0:T(8,128)(2,1)S(1)}, bf16[256,1024]{1,0:T(8,128)(2,1)S(1)}, u32[]{:S(2)}, u32[]{:S(2)}) collective-permute-start(bf16[256,1024]{1,0:T(8,128)(2,1)S(1)} %pad_maximum_fusion.5), channel_id=1, source_target_pairs={{0,2},{1,3},{2,0},{3,1},{4,6},{5,7},{6,4},{7,5},{8,10},{9,11},{10,... | collective-permute-start | bytes 1572872 | tf_op jit(solution)/shard_map/ppermute | solution.py:28
  11.8 0.2 collective-permute-start.10
  12.1 1.1 %collective-permute-start.2 = (bf16[256,1024]{1,0:T(8,128)(2,1)S(1)}, bf16[256,1024]{1,0:T(8,128)(2,1)S(1)}, u32[]{:S(2)}, u32[]{:S(2)}) collective-permute-start(bf16[256,1024]{1,0:T(8,128)(2,1)S(1)} %pad_maximum_fusion), channel_id=1, source_target_pairs={{0,1},{1,0},{2,3},{3,2},{4,5},{5,4},{6,7},{7,6},{8,9},{9,8},{10,11... | collective-permute-start | bytes 1572872 | tf_op jit(solution)/shard_map/ppermute | solution.py:28
  13.2 1.0 fusion
  14.3 1.3 %collective-permute-start.7 = (bf16[384,1024]{1,0:T(8,128)(2,1)S(1)}, bf16[384,1024]{1,0:T(8,128)(2,1)S(1)}, u32[]{:S(2)}, u32[]{:S(2)}) collective-permute-start(bf16[384,1024]{1,0:T(8,128)(2,1)S(1)} %get-tuple-element.21), channel_id=1, source_target_pairs={{0,1},{1,2},{2,3},{3,4},{4,5},{5,6},{6,7},{7,8},{8,9},{9,10},{10,1... | collective-permute-start | bytes 2359304 | tf_op jit(solution)/shard_map/ppermute | solution.py:22
  15.6 11.9 %collective-permute-done.9.rest_2_.rest_3_ = bf16[256,1024]{1,0:T(8,128)(2,1)S(1)} collective-permute-done((bf16[256,1024]{1,0:T(8,128)(2,1)S(1)}, bf16[256,1024]{1,0:T(8,128)(2,1)S(1)}, u32[]{:S(2)}, u32[]{:S(2)}) %collective-permute-start.9) | collective-permute-done | bytes 524320 | tf_op jit(solution)/shard_map/ppermute | solution.py:28
  27.5 0.1 collective-permute-start.11
  27.6 1.3 %collective-permute-start = (bf16[384,1024]{1,0:T(8,128)(2,1)}, bf16[384,1024]{1,0:T(8,128)(2,1)}, u32[]{:S(2)}, u32[]{:S(2)}) collective-permute-start(bf16[384,1024]{1,0:T(8,128)(2,1)} %get-tuple-element.24), channel_id=1, source_target_pairs={{0,1},{1,2},{2,3},{3,4},{4,5},{5,6},{6,7},{7,8},{8,9},{9,10},{10,1... | collective-permute-start | bytes 2359304 | tf_op jit(solution)/shard_map/ppermute | solution.py:22
  28.9 0.0 collective-permute-done.2.rest_0_.rest_1_
  28.9 1.3 %collective-permute-start.1 = (bf16[384,1024]{1,0:T(8,128)(2,1)}, bf16[384,1024]{1,0:T(8,128)(2,1)}, u32[]{:S(2)}, u32[]{:S(2)}) collective-permute-start(bf16[384,1024]{1,0:T(8,128)(2,1)} %get-tuple-element.22), channel_id=1, source_target_pairs={{0,1},{1,2},{2,3},{3,4},{4,5},{5,6},{6,7},{7,8},{8,9},{9,10},{10,1... | collective-permute-start | bytes 2359304 | tf_op jit(solution)/shard_map/ppermute | solution.py:22
  30.2 0.0 copy-start.12
  30.2 0.8 pad_maximum_fusion.2
  31.1 0.8 pad_maximum_fusion.1
  31.9 21.7 %collective-permute-done.11.rest_6_.rest_7_ = bf16[256,1024]{1,0:T(8,128)(2,1)S(1)} collective-permute-done((bf16[256,1024]{1,0:T(8,128)(2,1)S(1)}, bf16[256,1024]{1,0:T(8,128)(2,1)S(1)}, u32[]{:S(2)}, u32[]{:S(2)}) %collective-permute-start.11) | collective-permute-done | bytes 524320 | tf_op jit(solution)/shard_map/ppermute | solution.py:28
  53.6 0.5 collective-permute-start.3
  54.1 0.0 collective-permute-done.6.pk_ref
  54.1 2.0 %collective-permute-start.5 = (bf16[256,1024]{1,0:T(8,128)(2,1)S(1)}, bf16[256,1024]{1,0:T(8,128)(2,1)S(1)}, u32[]{:S(2)}, u32[]{:S(2)}) collective-permute-start(bf16[256,1024]{1,0:T(8,128)(2,1)S(1)} %pad_maximum_fusion.3), channel_id=1, source_target_pairs={{0,8},{1,9},{2,10},{3,11},{4,12},{5,13},{6,14},{7,15},{8,0},{9,1},... | collective-permute-start | bytes 1572872 | tf_op jit(solution)/shard_map/ppermute | solution.py:28
  56.1 0.6 pad_add_fusion.meta
  56.7 12.4 %shard_map.55.rest_8_ = bf16[384,2048]{1,0:T(8,128)(2,1)} custom-call(s32[4]{0:T(128)} %pad_add_fusion.meta, bf16[384,2048]{1,0:T(8,128)(2,1)} %q_ref.3, bf16[384,2048]{1,0:T(8,128)(2,1)} %ok_ref.3, bf16[384,2048]{1,0:T(8,128)(2,1)} %ov_ref.3, bf16[384,1024]{1,0:T(8,128)(2,1)} %collective-permute-done.6.pk_ref, bf16[384,1024]{1,0:T(8,128)(2,1)} %copy-done.10, ...), custom_call_target="tpu_custom_call" | custom-call | flops 2013265920 | bytes 6815744 | tf_op jit(solution)/shard_map/pallas_call | solution.py:125
  69.1 5.1 %collective-permute-done.3.rest_2_.rest_3_ = bf16[256,1024]{1,0:T(8,128)(2,1)S(1)} collective-permute-done((bf16[256,1024]{1,0:T(8,128)(2,1)}, bf16[256,1024]{1,0:T(8,128)(2,1)S(1)}, u32[]{:S(2)}, u32[]{:S(2)}) %collective-permute-start.3) | collective-permute-done | bytes 524320 | tf_op jit(solution)/shard_map/ppermute | solution.py:28
  74.1 6.8 %collective-permute-done.4.rest_4_.rest_5_ = bf16[256,1024]{1,0:T(8,128)(2,1)S(1)} collective-permute-done((bf16[256,1024]{1,0:T(8,128)(2,1)}, bf16[256,1024]{1,0:T(8,128)(2,1)S(1)}, u32[]{:S(2)}, u32[]{:S(2)}) %collective-permute-start.4) | collective-permute-done | bytes 524320 | tf_op jit(solution)/shard_map/ppermute | solution.py:28
  80.9 11.8 %collective-permute-done.5.rest_6_.rest_7_ = bf16[256,1024]{1,0:T(8,128)(2,1)S(1)} collective-permute-done((bf16[256,1024]{1,0:T(8,128)(2,1)S(1)}, bf16[256,1024]{1,0:T(8,128)(2,1)S(1)}, u32[]{:S(2)}, u32[]{:S(2)}) %collective-permute-start.5) | collective-permute-done | bytes 524320 | tf_op jit(solution)/shard_map/ppermute | solution.py:28
  92.8 0.8 copy-done.9
  93.5 12.5 %shard_map.56 = bf16[384,2048]{1,0:T(8,128)(2,1)} custom-call(s32[4]{0:T(128)} %pad_add_fusion.meta, bf16[384,2048]{1,0:T(8,128)(2,1)} %q_ref.3, bf16[384,2048]{1,0:T(8,128)(2,1)} %ok_ref.3, bf16[384,2048]{1,0:T(8,128)(2,1)} %ov_ref.3, bf16[384,1024]{1,0:T(8,128)(2,1)} %collective-permute-done.pk_ref, ...), custom_call_target="tpu_custom_call", output_to_operand_aliasing={{}: (14, {})} | custom-call | flops 2013265920 | bytes 6815744 | tf_op jit(solution)/shard_map/pallas_call | solution.py:125
  (34 shorter events, 0.3 us)
Async XLA Ops:
  0.0 7.3 %copy-start = (bf16[384,2048]{1,0:T(8,128)(2,1)S(1)}, bf16[384,2048]{1,0:T(8,128)(2,1)}, u32[]{:S(2)}) copy-start(bf16[384,2048]{1,0:T(8,128)(2,1)} %ok_ref.3) | copy-start | bytes 4718596
  0.0 4.1 %copy-start.11 = (s32[16,4,1]{0,2,1:T(1,128)S(1)}, s32[16,4,1]{0,2,1:T(1,128)}, u32[]{:S(2)}) copy-start(s32[16,4,1]{0,2,1:T(1,128)} %param.9) | copy-start | bytes 772
  2.8 51.3 %collective-permute-start.6 = (bf16[384,1024]{1,0:T(8,128)(2,1)}, bf16[384,1024]{1,0:T(8,128)(2,1)}, u32[]{:S(2)}, u32[]{:S(2)}) collective-permute-start(bf16[384,1024]{1,0:T(8,128)(2,1)} %get-tuple-element.23), channel_id=1, source_target_pairs={{0,1},{1,2},{2,3},{3,4},{4,5},{5,6},{6,7},{7,8},{8,9},{9,10},{10,1... | collective-permute-start | bytes 2359304 | tf_op jit(solution)/shard_map/ppermute | solution.py:22
  7.3 1.4 %copy-start.1 = (bf16[384,2048]{1,0:T(8,128)(2,1)S(1)}, bf16[384,2048]{1,0:T(8,128)(2,1)}, u32[]{:S(2)}) copy-start(bf16[384,2048]{1,0:T(8,128)(2,1)} %ov_ref.3) | copy-start | bytes 4718596
  9.0 5.3 %collective-permute-start.8 = (bf16[256,1024]{1,0:T(8,128)(2,1)S(1)}, bf16[256,1024]{1,0:T(8,128)(2,1)S(1)}, u32[]{:S(2)}, u32[]{:S(2)}) collective-permute-start(bf16[256,1024]{1,0:T(8,128)(2,1)S(1)} %pad_maximum_fusion.4), channel_id=1, source_target_pairs={{0,1},{1,0},{2,3},{3,2},{4,5},{5,4},{6,7},{7,6},{8,9},{9,8},{10,11... | collective-permute-start | bytes 1572872 | tf_op jit(solution)/shard_map/ppermute | solution.py:28
  10.4 17.1 %collective-permute-start.9 = (bf16[256,1024]{1,0:T(8,128)(2,1)S(1)}, bf16[256,1024]{1,0:T(8,128)(2,1)S(1)}, u32[]{:S(2)}, u32[]{:S(2)}) collective-permute-start(bf16[256,1024]{1,0:T(8,128)(2,1)S(1)} %pad_maximum_fusion.5), channel_id=1, source_target_pairs={{0,2},{1,3},{2,0},{3,1},{4,6},{5,7},{6,4},{7,5},{8,10},{9,11},{10,... | collective-permute-start | bytes 1572872 | tf_op jit(solution)/shard_map/ppermute | solution.py:28
  11.8 15.7 %collective-permute-start.10 = (bf16[256,1024]{1,0:T(8,128)(2,1)S(1)}, bf16[256,1024]{1,0:T(8,128)(2,1)S(1)}, u32[]{:S(2)}, u32[]{:S(2)}) collective-permute-start(bf16[256,1024]{1,0:T(8,128)(2,1)S(1)} %pad_maximum_fusion.6), channel_id=1, source_target_pairs={{0,4},{1,5},{2,6},{3,7},{4,0},{5,1},{6,2},{7,3},{8,12},{9,13},{10,... | collective-permute-start | bytes 1572872 | tf_op jit(solution)/shard_map/ppermute | solution.py:28
  12.1 16.8 %collective-permute-start.2 = (bf16[256,1024]{1,0:T(8,128)(2,1)S(1)}, bf16[256,1024]{1,0:T(8,128)(2,1)S(1)}, u32[]{:S(2)}, u32[]{:S(2)}) collective-permute-start(bf16[256,1024]{1,0:T(8,128)(2,1)S(1)} %pad_maximum_fusion), channel_id=1, source_target_pairs={{0,1},{1,0},{2,3},{3,2},{4,5},{5,4},{6,7},{7,6},{8,9},{9,8},{10,11... | collective-permute-start | bytes 1572872 | tf_op jit(solution)/shard_map/ppermute | solution.py:28
  14.3 16.8 %copy-start.2 = (bf16[256,1024]{1,0:T(8,128)(2,1)}, bf16[256,1024]{1,0:T(8,128)(2,1)S(1)}, u32[]{:S(2)}) copy-start(bf16[256,1024]{1,0:T(8,128)(2,1)S(1)} %collective-permute-done.8.rest_0_.rest_1_) | copy-start | bytes 1572868
  14.3 39.8 %collective-permute-start.7 = (bf16[384,1024]{1,0:T(8,128)(2,1)S(1)}, bf16[384,1024]{1,0:T(8,128)(2,1)S(1)}, u32[]{:S(2)}, u32[]{:S(2)}) collective-permute-start(bf16[384,1024]{1,0:T(8,128)(2,1)S(1)} %get-tuple-element.21), channel_id=1, source_target_pairs={{0,1},{1,2},{2,3},{3,4},{4,5},{5,6},{6,7},{7,8},{8,9},{9,10},{10,1... | collective-permute-start | bytes 2359304 | tf_op jit(solution)/shard_map/ppermute | solution.py:22
  27.5 4.4 %copy-start.3 = (bf16[256,1024]{1,0:T(8,128)(2,1)}, bf16[256,1024]{1,0:T(8,128)(2,1)S(1)}, u32[]{:S(2)}) copy-start(bf16[256,1024]{1,0:T(8,128)(2,1)S(1)} %collective-permute-done.9.rest_2_.rest_3_) | copy-start | bytes 1572868
  27.5 26.1 %collective-permute-start.11 = (bf16[256,1024]{1,0:T(8,128)(2,1)S(1)}, bf16[256,1024]{1,0:T(8,128)(2,1)S(1)}, u32[]{:S(2)}, u32[]{:S(2)}) collective-permute-start(bf16[256,1024]{1,0:T(8,128)(2,1)S(1)} %pad_maximum_fusion.7), channel_id=1, source_target_pairs={{0,8},{1,9},{2,10},{3,11},{4,12},{5,13},{6,14},{7,15},{8,0},{9,1},... | collective-permute-start | bytes 1572872 | tf_op jit(solution)/shard_map/ppermute | solution.py:28
  27.6 4.4 %copy-start.4 = (bf16[256,1024]{1,0:T(8,128)(2,1)}, bf16[256,1024]{1,0:T(8,128)(2,1)S(1)}, u32[]{:S(2)}) copy-start(bf16[256,1024]{1,0:T(8,128)(2,1)S(1)} %collective-permute-done.10.rest_4_.rest_5_) | copy-start | bytes 1572868
  27.6 65.2 %collective-permute-start = (bf16[384,1024]{1,0:T(8,128)(2,1)}, bf16[384,1024]{1,0:T(8,128)(2,1)}, u32[]{:S(2)}, u32[]{:S(2)}) collective-permute-start(bf16[384,1024]{1,0:T(8,128)(2,1)} %get-tuple-element.24), channel_id=1, source_target_pairs={{0,1},{1,2},{2,3},{3,4},{4,5},{5,6},{6,7},{7,8},{8,9},{9,10},{10,1... | collective-permute-start | bytes 2359304 | tf_op jit(solution)/shard_map/ppermute | solution.py:22
  28.9 3.1 %copy-start.6 = (bf16[256,1024]{1,0:T(8,128)(2,1)}, bf16[256,1024]{1,0:T(8,128)(2,1)S(1)}, u32[]{:S(2)}) copy-start(bf16[256,1024]{1,0:T(8,128)(2,1)S(1)} %collective-permute-done.2.rest_0_.rest_1_) | copy-start | bytes 1572868
  28.9 63.9 %collective-permute-start.1 = (bf16[384,1024]{1,0:T(8,128)(2,1)}, bf16[384,1024]{1,0:T(8,128)(2,1)}, u32[]{:S(2)}, u32[]{:S(2)}) collective-permute-start(bf16[384,1024]{1,0:T(8,128)(2,1)} %get-tuple-element.22), channel_id=1, source_target_pairs={{0,1},{1,2},{2,3},{3,4},{4,5},{5,6},{6,7},{7,8},{8,9},{9,10},{10,1... | collective-permute-start | bytes 2359304 | tf_op jit(solution)/shard_map/ppermute | solution.py:22
  30.2 25.9 %copy-start.12 = (s32[3]{0:T(128)S(1)}, s32[3]{0:T(128)}, u32[]{:S(2)}) copy-start(s32[3]{0:T(128)} %param.8) | copy-start | bytes 40
  53.6 3.1 %copy-start.5 = (bf16[256,1024]{1,0:T(8,128)(2,1)}, bf16[256,1024]{1,0:T(8,128)(2,1)S(1)}, u32[]{:S(2)}) copy-start(bf16[256,1024]{1,0:T(8,128)(2,1)S(1)} %collective-permute-done.11.rest_6_.rest_7_) | copy-start | bytes 1572868
  53.6 20.5 %collective-permute-start.3 = (bf16[256,1024]{1,0:T(8,128)(2,1)}, bf16[256,1024]{1,0:T(8,128)(2,1)S(1)}, u32[]{:S(2)}, u32[]{:S(2)}) collective-permute-start(bf16[256,1024]{1,0:T(8,128)(2,1)} %pad_maximum_fusion.1), channel_id=1, source_target_pairs={{0,2},{1,3},{2,0},{3,1},{4,6},{5,7},{6,4},{7,5},{8,10},{9,11},{10,... | collective-permute-start | bytes 1572872 | tf_op jit(solution)/shard_map/ppermute | solution.py:28
  54.1 26.8 %collective-permute-start.4 = (bf16[256,1024]{1,0:T(8,128)(2,1)}, bf16[256,1024]{1,0:T(8,128)(2,1)S(1)}, u32[]{:S(2)}, u32[]{:S(2)}) collective-permute-start(bf16[256,1024]{1,0:T(8,128)(2,1)} %pad_maximum_fusion.2), channel_id=1, source_target_pairs={{0,4},{1,5},{2,6},{3,7},{4,0},{5,1},{6,2},{7,3},{8,12},{9,13},{10,... | collective-permute-start | bytes 1572872 | tf_op jit(solution)/shard_map/ppermute | solution.py:28
  54.1 2.6 %copy-start.10 = (bf16[384,1024]{1,0:T(8,128)(2,1)}, bf16[384,1024]{1,0:T(8,128)(2,1)S(1)}, u32[]{:S(2)}) copy-start(bf16[384,1024]{1,0:T(8,128)(2,1)S(1)} %collective-permute-done.7.pv_ref) | copy-start | bytes 2359300
  54.1 38.7 %collective-permute-start.5 = (bf16[256,1024]{1,0:T(8,128)(2,1)S(1)}, bf16[256,1024]{1,0:T(8,128)(2,1)S(1)}, u32[]{:S(2)}, u32[]{:S(2)}) collective-permute-start(bf16[256,1024]{1,0:T(8,128)(2,1)S(1)} %pad_maximum_fusion.3), channel_id=1, source_target_pairs={{0,8},{1,9},{2,10},{3,11},{4,12},{5,13},{6,14},{7,15},{8,0},{9,1},... | collective-permute-start | bytes 1572872 | tf_op jit(solution)/shard_map/ppermute | solution.py:28
  74.1 18.6 %copy-start.7 = (bf16[256,1024]{1,0:T(8,128)(2,1)}, bf16[256,1024]{1,0:T(8,128)(2,1)S(1)}, u32[]{:S(2)}) copy-start(bf16[256,1024]{1,0:T(8,128)(2,1)S(1)} %collective-permute-done.3.rest_2_.rest_3_) | copy-start | bytes 1572868
  80.9 11.9 %copy-start.8 = (bf16[256,1024]{1,0:T(8,128)(2,1)}, bf16[256,1024]{1,0:T(8,128)(2,1)S(1)}, u32[]{:S(2)}) copy-start(bf16[256,1024]{1,0:T(8,128)(2,1)S(1)} %collective-permute-done.4.rest_4_.rest_5_) | copy-start | bytes 1572868
  92.7 0.8 copy-start.9

commit v17 on v16

--- a/solution.py
+++ b/solution.py
@@ -108,9 +108,10 @@
     whole = pl.BlockSpec((rows, block), lambda h, meta: (0, h + first_head))
     part = pl.BlockSpec((rows, block), lambda h, meta: (0, h))
     far_specs = []
-    for _ in range(level_count):
-        far_specs.append(pl.BlockSpec((far_rows, block), lambda h, meta: (0, h)))
-        far_specs.append(pl.BlockSpec((far_rows, block), lambda h, meta: (1, h)))
+    for arrived in far:
+        shift = first_head if arrived.shape[1] == features else 0
+        far_specs.append(pl.BlockSpec((far_rows, block), lambda h, meta, shift=shift: (0, h + shift)))
+        far_specs.append(pl.BlockSpec((far_rows, block), lambda h, meta, shift=shift: (1, h + shift)))
     far_args = []
     for arrived in far:
         far_args += [arrived, arrived]
@@ -154,13 +155,18 @@
     for c in range(CHUNKS):
         cols = slice(c * width, (c + 1) * width)
         prev_keys, prev_values = passed_along((key_rows[:, cols], value_rows[:, cols]), "outer", 1)
-        far = []
+        far = [] if c == 0 else [level0]
         for level_bit in range(level_count):
+            if level_bit == 0 and c > 0:
+                continue
+            cols_b = slice(0, features) if level_bit == 0 else cols
             outgoing = jnp.concatenate(
-                [pick_blocks(key_rows, wanted[level_bit])[:, cols], pick_blocks(value_rows, wanted[level_bit])[:, cols]],
+                [pick_blocks(key_rows, wanted[level_bit])[:, cols_b], pick_blocks(value_rows, wanted[level_bit])[:, cols_b]],
                 axis=0,
             )
             far.append(from_partner(outgoing, "outer", level_bit))
+            if level_bit == 0:
+                level0 = far[0]
         context = attend(
             meta, queries, key_rows, value_rows, prev_keys, prev_values, far, c * (HEADS // CHUNKS), context
         )

time: 106 us -> 107 us (level)
  waiting for transfers between devices: 57.3 us -> 40.4 us
  starting transfers between devices: 11.8 us -> 25.3 us
  local copies, waits for them, and re-layouts: 6.91 us -> 9.17 us
  other arithmetic: 2.44 us -> 4.27 us
    ppermute x8 -> x7, waiting for transfers between devices: 57.3 us -> 40.4 us  [from_partner(): return lax.ppermute(value, axis, pairs)]
    ppermute x8 -> x7, starting transfers between devices: 6.68 us -> 20.2 us  [from_partner(): return lax.ppermute(value, axis, pairs)]
    dynamic_slice x0 -> x2, local copies, waits for them, and re-layouts: none -> 2.29 us  [pick_blocks(): return lax.dynamic_slice_in_dim(source, block_index[0] * BLK, BLK, 0)]
    concatenate x8 -> x7, other arithmetic: 1.89 us -> 3.68 us  [on_device(): jnp.concatenate([pick_blocks(key_rows, wanted[level_bit])[:, cols_b], pic...]
    slice x1, local copies, waits for them, and re-layouts: 2.77 us -> 1.02 us  [on_device(): key_rows[:, cols]]
    unnamed x26 -> x24, local copies, waits for them, and re-layouts: 2 us -> 3.18 us
  transfers between devices with their start and end apart: 12 -> 11, of which waited for: 5 -> 5; matrix products, arithmetic and copies ran while one was open for 4% -> 5% of each run, Pallas kernels for 12% -> 12%
where the time goes in v17:
time: 107 us
  waiting for transfers between devices  40.4 us (38%)
  starting transfers between devices  25.3 us (24%)
  Pallas kernels  24.8 us (23%)
  local copies, waits for them, and re-layouts  9.17 us (9%)
  other arithmetic  4.27 us (4%)
  between operations  2.69 us (3%)
    ppermute x7, waiting for transfers between devices, from_partner(): return lax.ppermute(value, axis, pairs)  40.4 us
    pallas_call x2, Pallas kernels, attend(): pl.pallas_call(functools.partial(attend_kernel, level_count), out_shape=j...  24.8 us
    ppermute x7, starting transfers between devices, from_partner(): return lax.ppermute(value, axis, pairs)  20.2 us
    ppermute x4, starting transfers between devices, passed_along(): return lax.ppermute(block, axis, route)  5.12 us
    concatenate x7, other arithmetic, on_device(): jnp.concatenate([pick_blocks(key_rows, wanted[level_bit])[:, cols_b], pic...  3.68 us
    unnamed x24, local copies, waits for them, and re-layouts  3.18 us
    dynamic_slice x2, local copies, waits for them, and re-layouts, pick_blocks(): return lax.dynamic_slice_in_dim(source, block_index[0] * BLK, BLK, 0)  2.29 us
  transfers between devices with their start and end apart: 11, of which 5 were waited for; matrix products, arithmetic and copies ran while one was open for 5% of the time, Pallas kernels for 12%

profile of v17, /device:TPU:29, one launch (start us, length us, event | category | flops | bytes accessed | tf_op | source)
XLA Modules:
  0.0 106.7 jit_solution(12216473551151696116)
XLA Ops:
  0.0 1.4 %constant_dynamic-slice_fusion.2 = (s32[1,1,1]{0,2,1:T(1,128)}, s32[1,1,1]{0,2,1:T(1,128)}, s32[1,1,1]{0,2,1:T(1,128)}, s32[1,1,1]{0,2,1:T(1,128)}) fusion(s32[16,4,1]{0,2,1:T(1,128)} %param.9, s32[]{:T(128)S(6)} %select_n.40, s32[]{:T(128)S(6)} %select_n.36, s32[]{:T(128)S(6)} %select_n.16, s32[]{:T(128)S(6)} %select_n.38), kind=kLoop, calls=%fused_computation.9 | loop fusion | bytes 48 | tf_op jit(solution)/shard_map/dynamic_slice | solution.py:152
  2.0 1.1 %constant_dynamic-slice_fusion.9 = bf16[128,2048]{1,0:T(8,128)(2,1)S(1)} fusion(bf16[384,2048]{1,0:T(8,128)(2,1)} %ov_ref.3, s32[]{:T(128)S(6)} %select_n.17), kind=kLoop, calls=%fused_computation.16 | loop fusion | bytes 1048580 | tf_op jit(solution)/shard_map/dynamic_slice | solution.py:32
  3.1 1.2 %constant_dynamic-slice_fusion.10 = bf16[128,2048]{1,0:T(8,128)(2,1)S(1)} fusion(bf16[384,2048]{1,0:T(8,128)(2,1)} %ok_ref.3, s32[]{:T(128)S(6)} %select_n.17), kind=kLoop, calls=%fused_computation.17 | loop fusion | bytes 1048580 | tf_op jit(solution)/shard_map/dynamic_slice | solution.py:32
  4.3 1.1 %pad_maximum_fusion = bf16[256,2048]{1,0:T(8,128)(2,1)} fusion(bf16[128,2048]{1,0:T(8,128)(2,1)S(1)} %constant_dynamic-slice_fusion.9, bf16[128,2048]{1,0:T(8,128)(2,1)S(1)} %constant_dynamic-slice_fusion.10), kind=kLoop, calls=%fused_computation | loop fusion | flops 2097152 | bytes 2097152 | tf_op jit(solution)/shard_map/concatenate | solution.py:163
  5.4 0.7 collective-permute-start.2
  8.0 0.2 constant_dynamic-slice_fusion
  8.1 1.2 %copy-done = bf16[384,2048]{1,0:T(8,128)(2,1)S(1)} copy-done((bf16[384,2048]{1,0:T(8,128)(2,1)S(1)}, bf16[384,2048]{1,0:T(8,128)(2,1)}, u32[]{:S(2)}) %copy-start) | copy-done | bytes 1572888
  9.3 0.1 constant_dynamic-slice_fusion.1
  9.5 0.3 collective-permute-start.8
  9.9 0.2 collective-permute-start.9
  10.2 1.0 fusion.1
  11.2 1.3 %collective-permute-start.6 = (bf16[384,1024]{1,0:T(8,128)(2,1)S(1)}, bf16[384,1024]{1,0:T(8,128)(2,1)S(1)}, u32[]{:S(2)}, u32[]{:S(2)}) collective-permute-start(bf16[384,1024]{1,0:T(8,128)(2,1)S(1)} %get-tuple-element.19), channel_id=1, source_target_pairs={{0,1},{1,2},{2,3},{3,4},{4,5},{5,6},{6,7},{7,8},{8,9},{9,10},{10,1... | collective-permute-start | bytes 2359304 | tf_op jit(solution)/shard_map/ppermute | solution.py:22
  12.5 1.0 fusion
  13.6 9.5 %collective-permute-done.8.rest_2_.rest_3_ = bf16[256,1024]{1,0:T(8,128)(2,1)S(1)} collective-permute-done((bf16[256,1024]{1,0:T(8,128)(2,1)S(1)}, bf16[256,1024]{1,0:T(8,128)(2,1)S(1)}, u32[]{:S(2)}, u32[]{:S(2)}) %collective-permute-start.8) | collective-permute-done | bytes 524320 | tf_op jit(solution)/shard_map/ppermute | solution.py:28
  23.1 1.3 %collective-permute-start.7 = (bf16[384,1024]{1,0:T(8,128)(2,1)S(1)}, bf16[384,1024]{1,0:T(8,128)(2,1)}, u32[]{:S(2)}, u32[]{:S(2)}) collective-permute-start(bf16[384,1024]{1,0:T(8,128)(2,1)S(1)} %get-tuple-element.17), channel_id=1, source_target_pairs={{0,1},{1,2},{2,3},{3,4},{4,5},{5,6},{6,7},{7,8},{8,9},{9,10},{10,1... | collective-permute-start | bytes 2359304 | tf_op jit(solution)/shard_map/ppermute | solution.py:22
  24.4 8.8 %collective-permute-done.9.rest_4_.rest_5_ = bf16[256,1024]{1,0:T(8,128)(2,1)S(1)} collective-permute-done((bf16[256,1024]{1,0:T(8,128)(2,1)S(1)}, bf16[256,1024]{1,0:T(8,128)(2,1)S(1)}, u32[]{:S(2)}, u32[]{:S(2)}) %collective-permute-start.9) | collective-permute-done | bytes 524320 | tf_op jit(solution)/shard_map/ppermute | solution.py:28
  33.1 1.3 %collective-permute-start = (bf16[384,1024]{1,0:T(8,128)(2,1)}, bf16[384,1024]{1,0:T(8,128)(2,1)S(1)}, u32[]{:S(2)}, u32[]{:S(2)}) collective-permute-start(bf16[384,1024]{1,0:T(8,128)(2,1)} %get-tuple-element.20), channel_id=1, source_target_pairs={{0,1},{1,2},{2,3},{3,4},{4,5},{5,6},{6,7},{7,8},{8,9},{9,10},{10,1... | collective-permute-start | bytes 2359304 | tf_op jit(solution)/shard_map/ppermute | solution.py:22
  34.4 0.6 collective-permute-done.10.rest_6_.rest_7_
  35.0 1.3 %collective-permute-start.1 = (bf16[384,1024]{1,0:T(8,128)(2,1)}, bf16[384,1024]{1,0:T(8,128)(2,1)S(1)}, u32[]{:S(2)}, u32[]{:S(2)}) collective-permute-start(bf16[384,1024]{1,0:T(8,128)(2,1)} %get-tuple-element.18), channel_id=1, source_target_pairs={{0,1},{1,2},{2,3},{3,4},{4,5},{5,6},{6,7},{7,8},{8,9},{9,10},{10,1... | collective-permute-start | bytes 2359304 | tf_op jit(solution)/shard_map/ppermute | solution.py:22
  36.3 0.8 pad_maximum_fusion.3
  37.2 0.8 pad_maximum_fusion.2
  38.0 0.8 pad_maximum_fusion.1
  38.8 4.7 %collective-permute-start.3 = (bf16[256,1024]{1,0:T(8,128)(2,1)}, bf16[256,1024]{1,0:T(8,128)(2,1)S(1)}, u32[]{:S(2)}, u32[]{:S(2)}) collective-permute-start(bf16[256,1024]{1,0:T(8,128)(2,1)} %pad_maximum_fusion.1), channel_id=1, source_target_pairs={{0,2},{1,3},{2,0},{3,1},{4,6},{5,7},{6,4},{7,5},{8,10},{9,11},{10,... | collective-permute-start | bytes 1572872 | tf_op jit(solution)/shard_map/ppermute | solution.py:28
  43.6 14.2 %collective-permute-start.4 = (bf16[256,1024]{1,0:T(8,128)(2,1)}, bf16[256,1024]{1,0:T(8,128)(2,1)S(1)}, u32[]{:S(2)}, u32[]{:S(2)}) collective-permute-start(bf16[256,1024]{1,0:T(8,128)(2,1)} %pad_maximum_fusion.2), channel_id=1, source_target_pairs={{0,4},{1,5},{2,6},{3,7},{4,0},{5,1},{6,2},{7,3},{8,12},{9,13},{10,... | collective-permute-start | bytes 1572872 | tf_op jit(solution)/shard_map/ppermute | solution.py:28
  57.8 0.6 pad_add_fusion.meta
  58.4 12.4 %shard_map.55.rest_8_ = bf16[384,2048]{1,0:T(8,128)(2,1)} custom-call(s32[4]{0:T(128)} %pad_add_fusion.meta, bf16[384,2048]{1,0:T(8,128)(2,1)} %q_ref.3, bf16[384,2048]{1,0:T(8,128)(2,1)} %ok_ref.3, bf16[384,2048]{1,0:T(8,128)(2,1)} %ov_ref.3, bf16[384,1024]{1,0:T(8,128)(2,1)} %copy-done.10, bf16[384,1024]{1,0:T(8,128)(2,1)} %collective-permute-done.7.pv_ref, ...), custom_call_target="tpu_custom_call" | custom-call | flops 2013265920 | bytes 6815744 | tf_op jit(solution)/shard_map/pallas_call | solution.py:126
  70.8 18.9 %collective-permute-done.4.rest_4_.rest_5_ = bf16[256,1024]{1,0:T(8,128)(2,1)S(1)} collective-permute-done((bf16[256,1024]{1,0:T(8,128)(2,1)}, bf16[256,1024]{1,0:T(8,128)(2,1)S(1)}, u32[]{:S(2)}, u32[]{:S(2)}) %collective-permute-start.4) | collective-permute-done | bytes 524320 | tf_op jit(solution)/shard_map/ppermute | solution.py:28
  89.7 2.6 %collective-permute-done.5.rest_6_.rest_7_ = bf16[256,1024]{1,0:T(8,128)(2,1)S(1)} collective-permute-done((bf16[256,1024]{1,0:T(8,128)(2,1)}, bf16[256,1024]{1,0:T(8,128)(2,1)S(1)}, u32[]{:S(2)}, u32[]{:S(2)}) %collective-permute-start.5) | collective-permute-done | bytes 524320 | tf_op jit(solution)/shard_map/ppermute | solution.py:28
  92.3 0.8 copy-done.7
  93.1 0.3 copy-done.8
  93.4 0.9 copy-done.9
  94.2 12.4 %shard_map.56 = bf16[384,2048]{1,0:T(8,128)(2,1)} custom-call(s32[4]{0:T(128)} %pad_add_fusion.meta, bf16[384,2048]{1,0:T(8,128)(2,1)} %q_ref.3, bf16[384,2048]{1,0:T(8,128)(2,1)} %ok_ref.3, bf16[384,2048]{1,0:T(8,128)(2,1)} %ov_ref.3, bf16[384,1024]{1,0:T(8,128)(2,1)} %copy-done.8, bf16[384,1024]{1,0:T(8,128)(2,1)} %copy-done.9, ...), custom_call_target="tpu_custom_call", output_to_operand_aliasing={{}: (14, {})} | custom-call | flops 2013265920 | bytes 6815744 | tf_op jit(solution)/shard_map/pallas_call | solution.py:126
  (31 shorter events, 0.2 us)
Async XLA Ops:
  3.1 4.8 %copy-start.1 = (bf16[384,2048]{1,0:T(8,128)(2,1)S(1)}, bf16[384,2048]{1,0:T(8,128)(2,1)}, u32[]{:S(2)}) copy-start(bf16[384,2048]{1,0:T(8,128)(2,1)} %ov_ref.3) | copy-start | bytes 4718596
  5.4 52.4 %collective-permute-start.2 = (bf16[256,2048]{1,0:T(8,128)(2,1)}, bf16[256,2048]{1,0:T(8,128)(2,1)}, u32[]{:S(2)}, u32[]{:S(2)}) collective-permute-start(bf16[256,2048]{1,0:T(8,128)(2,1)} %pad_maximum_fusion), channel_id=1, source_target_pairs={{0,1},{1,0},{2,3},{3,2},{4,5},{5,4},{6,7},{7,6},{8,9},{9,8},{10,11... | collective-permute-start | bytes 3145736 | tf_op jit(solution)/shard_map/ppermute | solution.py:28
  7.9 1.4 %copy-start = (bf16[384,2048]{1,0:T(8,128)(2,1)S(1)}, bf16[384,2048]{1,0:T(8,128)(2,1)}, u32[]{:S(2)}) copy-start(bf16[384,2048]{1,0:T(8,128)(2,1)} %ok_ref.3) | copy-start | bytes 4718596
  9.5 13.5 %collective-permute-start.8 = (bf16[256,1024]{1,0:T(8,128)(2,1)S(1)}, bf16[256,1024]{1,0:T(8,128)(2,1)S(1)}, u32[]{:S(2)}, u32[]{:S(2)}) collective-permute-start(bf16[256,1024]{1,0:T(8,128)(2,1)S(1)} %pad_maximum_fusion.4), channel_id=1, source_target_pairs={{0,2},{1,3},{2,0},{3,1},{4,6},{5,7},{6,4},{7,5},{8,10},{9,11},{10,... | collective-permute-start | bytes 1572872 | tf_op jit(solution)/shard_map/ppermute | solution.py:28
  9.9 23.3 %collective-permute-start.9 = (bf16[256,1024]{1,0:T(8,128)(2,1)S(1)}, bf16[256,1024]{1,0:T(8,128)(2,1)S(1)}, u32[]{:S(2)}, u32[]{:S(2)}) collective-permute-start(bf16[256,1024]{1,0:T(8,128)(2,1)S(1)} %pad_maximum_fusion.5), channel_id=1, source_target_pairs={{0,4},{1,5},{2,6},{3,7},{4,0},{5,1},{6,2},{7,3},{8,12},{9,13},{10,... | collective-permute-start | bytes 1572872 | tf_op jit(solution)/shard_map/ppermute | solution.py:28
  10.1 24.9 %collective-permute-start.10 = (bf16[256,1024]{1,0:T(8,128)(2,1)S(1)}, bf16[256,1024]{1,0:T(8,128)(2,1)S(1)}, u32[]{:S(2)}, u32[]{:S(2)}) collective-permute-start(bf16[256,1024]{1,0:T(8,128)(2,1)S(1)} %pad_maximum_fusion.6), channel_id=1, source_target_pairs={{0,8},{1,9},{2,10},{3,11},{4,12},{5,13},{6,14},{7,15},{8,0},{9,1},... | collective-permute-start | bytes 1572872 | tf_op jit(solution)/shard_map/ppermute | solution.py:28
  11.2 27.6 %collective-permute-start.6 = (bf16[384,1024]{1,0:T(8,128)(2,1)S(1)}, bf16[384,1024]{1,0:T(8,128)(2,1)S(1)}, u32[]{:S(2)}, u32[]{:S(2)}) collective-permute-start(bf16[384,1024]{1,0:T(8,128)(2,1)S(1)} %get-tuple-element.19), channel_id=1, source_target_pairs={{0,1},{1,2},{2,3},{3,4},{4,5},{5,6},{6,7},{7,8},{8,9},{9,10},{10,1... | collective-permute-start | bytes 2359304 | tf_op jit(solution)/shard_map/ppermute | solution.py:22
  23.1 15.7 %copy-start.2 = (bf16[256,1024]{1,0:T(8,128)(2,1)}, bf16[256,1024]{1,0:T(8,128)(2,1)S(1)}, u32[]{:S(2)}) copy-start(bf16[256,1024]{1,0:T(8,128)(2,1)S(1)} %collective-permute-done.8.rest_2_.rest_3_) | copy-start | bytes 1572868
  23.1 20.5 %collective-permute-start.7 = (bf16[384,1024]{1,0:T(8,128)(2,1)S(1)}, bf16[384,1024]{1,0:T(8,128)(2,1)}, u32[]{:S(2)}, u32[]{:S(2)}) collective-permute-start(bf16[384,1024]{1,0:T(8,128)(2,1)S(1)} %get-tuple-element.17), channel_id=1, source_target_pairs={{0,1},{1,2},{2,3},{3,4},{4,5},{5,6},{6,7},{7,8},{8,9},{9,10},{10,1... | collective-permute-start | bytes 2359304 | tf_op jit(solution)/shard_map/ppermute | solution.py:22
  33.1 5.7 %copy-start.3 = (bf16[256,1024]{1,0:T(8,128)(2,1)}, bf16[256,1024]{1,0:T(8,128)(2,1)S(1)}, u32[]{:S(2)}) copy-start(bf16[256,1024]{1,0:T(8,128)(2,1)S(1)} %collective-permute-done.9.rest_4_.rest_5_) | copy-start | bytes 1572868
  33.1 59.2 %collective-permute-start = (bf16[384,1024]{1,0:T(8,128)(2,1)}, bf16[384,1024]{1,0:T(8,128)(2,1)S(1)}, u32[]{:S(2)}, u32[]{:S(2)}) collective-permute-start(bf16[384,1024]{1,0:T(8,128)(2,1)} %get-tuple-element.20), channel_id=1, source_target_pairs={{0,1},{1,2},{2,3},{3,4},{4,5},{5,6},{6,7},{7,8},{8,9},{9,10},{10,1... | collective-permute-start | bytes 2359304 | tf_op jit(solution)/shard_map/ppermute | solution.py:22
  35.0 3.8 %copy-start.4 = (bf16[256,1024]{1,0:T(8,128)(2,1)}, bf16[256,1024]{1,0:T(8,128)(2,1)S(1)}, u32[]{:S(2)}) copy-start(bf16[256,1024]{1,0:T(8,128)(2,1)S(1)} %collective-permute-done.10.rest_6_.rest_7_) | copy-start | bytes 1572868
  35.0 57.3 %collective-permute-start.1 = (bf16[384,1024]{1,0:T(8,128)(2,1)}, bf16[384,1024]{1,0:T(8,128)(2,1)S(1)}, u32[]{:S(2)}, u32[]{:S(2)}) collective-permute-start(bf16[384,1024]{1,0:T(8,128)(2,1)} %get-tuple-element.18), channel_id=1, source_target_pairs={{0,1},{1,2},{2,3},{3,4},{4,5},{5,6},{6,7},{7,8},{8,9},{9,10},{10,1... | collective-permute-start | bytes 2359304 | tf_op jit(solution)/shard_map/ppermute | solution.py:22
  36.3 21.5 %copy-start.11 = (s32[3]{0:T(128)S(1)}, s32[3]{0:T(128)}, u32[]{:S(2)}) copy-start(s32[3]{0:T(128)} %param.8) | copy-start | bytes 40
  38.8 18.9 %copy-start.10 = (bf16[384,1024]{1,0:T(8,128)(2,1)}, bf16[384,1024]{1,0:T(8,128)(2,1)S(1)}, u32[]{:S(2)}) copy-start(bf16[384,1024]{1,0:T(8,128)(2,1)S(1)} %collective-permute-done.6.pk_ref) | copy-start | bytes 2359300
  38.8 32.0 %collective-permute-start.3 = (bf16[256,1024]{1,0:T(8,128)(2,1)}, bf16[256,1024]{1,0:T(8,128)(2,1)S(1)}, u32[]{:S(2)}, u32[]{:S(2)}) collective-permute-start(bf16[256,1024]{1,0:T(8,128)(2,1)} %pad_maximum_fusion.1), channel_id=1, source_target_pairs={{0,2},{1,3},{2,0},{3,1},{4,6},{5,7},{6,4},{7,5},{8,10},{9,11},{10,... | collective-permute-start | bytes 1572872 | tf_op jit(solution)/shard_map/ppermute | solution.py:28
  43.6 46.1 %collective-permute-start.4 = (bf16[256,1024]{1,0:T(8,128)(2,1)}, bf16[256,1024]{1,0:T(8,128)(2,1)S(1)}, u32[]{:S(2)}, u32[]{:S(2)}) collective-permute-start(bf16[256,1024]{1,0:T(8,128)(2,1)} %pad_maximum_fusion.2), channel_id=1, source_target_pairs={{0,4},{1,5},{2,6},{3,7},{4,0},{5,1},{6,2},{7,3},{8,12},{9,13},{10,... | collective-permute-start | bytes 1572872 | tf_op jit(solution)/shard_map/ppermute | solution.py:28
  57.8 34.5 %collective-permute-start.5 = (bf16[256,1024]{1,0:T(8,128)(2,1)}, bf16[256,1024]{1,0:T(8,128)(2,1)S(1)}, u32[]{:S(2)}, u32[]{:S(2)}) collective-permute-start(bf16[256,1024]{1,0:T(8,128)(2,1)} %pad_maximum_fusion.3), channel_id=1, source_target_pairs={{0,8},{1,9},{2,10},{3,11},{4,12},{5,13},{6,14},{7,15},{8,0},{9,1},... | collective-permute-start | bytes 1572872 | tf_op jit(solution)/shard_map/ppermute | solution.py:28
  70.8 21.5 %copy-start.5 = (bf16[256,1024]{1,0:T(8,128)(2,1)}, bf16[256,1024]{1,0:T(8,128)(2,1)S(1)}, u32[]{:S(2)}) copy-start(bf16[256,1024]{1,0:T(8,128)(2,1)S(1)} %collective-permute-done.3.rest_2_.rest_3_) | copy-start | bytes 1572868
  89.7 2.6 %copy-start.6 = (bf16[256,1024]{1,0:T(8,128)(2,1)}, bf16[256,1024]{1,0:T(8,128)(2,1)S(1)}, u32[]{:S(2)}) copy-start(bf16[256,1024]{1,0:T(8,128)(2,1)S(1)} %collective-permute-done.4.rest_4_.rest_5_) | copy-start | bytes 1572868
  92.3 0.8 copy-start.7
  92.3 1.0 copy-start.8
  93.4 0.9 copy-start.9

commit v18 on v16

--- a/solution.py
+++ b/solution.py
@@ -151,9 +151,11 @@
     wanted = [columns[jnp.bitwise_xor(device, 1 << b), b] - device * panel_len for b in range(level_count)]
     width = features // CHUNKS
     context = None
+    held = ()
     for c in range(CHUNKS):
         cols = slice(c * width, (c + 1) * width)
-        prev_keys, prev_values = passed_along((key_rows[:, cols], value_rows[:, cols]), "outer", 1)
+        rim_keys, rim_values, *_ = lax.optimization_barrier((key_rows, value_rows, *held))
+        prev_keys, prev_values = passed_along((rim_keys[:, cols], rim_values[:, cols]), "outer", 1)
         far = []
         for level_bit in range(level_count):
             outgoing = jnp.concatenate(
@@ -164,6 +166,7 @@
         context = attend(
             meta, queries, key_rows, value_rows, prev_keys, prev_values, far, c * (HEADS // CHUNKS), context
         )
+        held = (far[-1],)
     return context
 
 

time: 106 us -> 119 us (1.12); the launches traced: 106 us -> 117 us
  waiting for transfers between devices: 57.3 us -> 66.2 us
  local copies, waits for them, and re-layouts: 6.91 us -> 11.1 us
  starting transfers between devices: 11.8 us -> 9.12 us
    ppermute x8, waiting for transfers between devices: 57.3 us -> 66.2 us  [from_partner(): return lax.ppermute(value, axis, pairs)]
    slice x1, local copies, waits for them, and re-layouts: 0.21 us -> 3.05 us  [on_device(): pick_blocks(value_rows, wanted[level_bit])[:, cols]]
    ppermute x8, starting transfers between devices: 6.68 us -> 3.97 us  [from_partner(): return lax.ppermute(value, axis, pairs)]
    unnamed x26 -> x30, local copies, waits for them, and re-layouts: 2 us -> 4.52 us
    slice x3 -> x4, local copies, waits for them, and re-layouts: 4.01 us -> 2.15 us  [the longest x2 1.09 us: on_device(): rim_keys[:, cols]]
  transfers between devices with their start and end apart: 12 -> 12, of which waited for: 5 -> 5; matrix products, arithmetic and copies ran while one was open for 4% -> 5% of each run, Pallas kernels for 12% -> 11%
where the time goes in v18:
time: 119 us; the launch traced here: 117 us
  waiting for transfers between devices  66.2 us (56%)
  Pallas kernels  24.8 us (21%)
  local copies, waits for them, and re-layouts  11.1 us (9%)
  starting transfers between devices  9.12 us (8%)
  other arithmetic  3.29 us (3%)
  between operations  2.83 us (2%)
    ppermute x8, waiting for transfers between devices, from_partner(): return lax.ppermute(value, axis, pairs)  66.2 us
    pallas_call x2, Pallas kernels, attend(): pl.pallas_call(functools.partial(attend_kernel, level_count), out_shape=j...  24.8 us
    ppermute x4, starting transfers between devices, passed_along(): return lax.ppermute(block, axis, route)  5.15 us
    unnamed x30, local copies, waits for them, and re-layouts  4.52 us
    ppermute x8, starting transfers between devices, from_partner(): return lax.ppermute(value, axis, pairs)  3.97 us
    slice x1, local copies, waits for them, and re-layouts, on_device(): pick_blocks(value_rows, wanted[level_bit])[:, cols]  3.05 us
    concatenate x8, other arithmetic, on_device(): jnp.concatenate([pick_blocks(key_rows, wanted[level_bit])[:, cols], pick_...  2.7 us
  transfers between devices with their start and end apart: 12, of which 5 were waited for; matrix products, arithmetic and copies ran while one was open for 5% of the time, Pallas kernels for 11%

profile of v18, /device:TPU:29, one launch (start us, length us, event | category | flops | bytes accessed | tf_op | source)
XLA Modules:
  0.0 117.3 jit_solution(6122195236671966648)
XLA Ops:
  0.0 1.4 %constant_dynamic-slice_fusion.3 = (s32[1,1,1]{0,2,1:T(1,128)}, s32[1,1,1]{0,2,1:T(1,128)}, s32[1,1,1]{0,2,1:T(1,128)}, s32[1,1,1]{0,2,1:T(1,128)}) fusion(s32[16,4,1]{0,2,1:T(1,128)} %param.9, s32[]{:T(128)S(6)} %select_n.42, s32[]{:T(128)S(6)} %select_n.18, s32[]{:T(128)S(6)} %select_n.16, s32[]{:T(128)S(6)} %select_n.40), kind=kLoop, calls=%fused_computation.11 | loop fusion | bytes 48 | tf_op jit(solution)/shard_map/dynamic_slice | solution.py:151
  4.0 3.1 %constant_dynamic-slice_fusion.1 = (bf16[128,1024]{1,0:T(8,128)(2,1)S(1)}, bf16[128,1024]{1,0:T(8,128)(2,1)S(1)}, bf16[128,1024]{1,0:T(8,128)(2,1)S(1)}, bf16[12...) fusion(bf16[384,2048]{1,0:T(8,128)(2,1)} %ov_ref.3, ...), kind=kLoop, calls=%fused_computation.9 | loop fusion | bytes 8388628 | tf_op jit(solution)/shard_map/slice | solution.py:162
  7.1 0.1 collective-permute-start.6
  7.3 2.4 %collective-permute-start = (bf16[256,1024]{1,0:T(8,128)(2,1)S(1)}, bf16[256,1024]{1,0:T(8,128)(2,1)S(1)}, u32[]{:S(2)}, u32[]{:S(2)}) collective-permute-start(bf16[256,1024]{1,0:T(8,128)(2,1)S(1)} %pad_maximum_fusion), channel_id=1, source_target_pairs={{0,8},{1,9},{2,10},{3,11},{4,12},{5,13},{6,14},{7,15},{8,0},{9,1},... | collective-permute-start | bytes 1572872 | tf_op jit(solution)/shard_map/ppermute | solution.py:28
  9.7 1.1 collective-permute-start.9
  10.9 0.3 collective-permute-start.10
  11.2 1.3 %collective-permute-start.8 = (bf16[384,1024]{1,0:T(8,128)(2,1)S(1)}, bf16[384,1024]{1,0:T(8,128)(2,1)S(1)}, u32[]{:S(2)}, u32[]{:S(2)}) collective-permute-start(bf16[384,1024]{1,0:T(8,128)(2,1)S(1)} %slice.73), channel_id=1, source_target_pairs={{0,1},{1,2},{2,3},{3,4},{4,5},{5,6},{6,7},{7,8},{8,9},{9,10},{10,1... | collective-permute-start | bytes 2359304 | tf_op jit(solution)/shard_map/ppermute | solution.py:22
  12.5 0.1 slice.72
  12.6 31.5 %collective-permute-done.6.rest_6_.rest_7_ = bf16[256,1024]{1,0:T(8,128)(2,1)S(1)} collective-permute-done((bf16[256,1024]{1,0:T(8,128)(2,1)S(1)}, bf16[256,1024]{1,0:T(8,128)(2,1)S(1)}, u32[]{:S(2)}, u32[]{:S(2)}) %collective-permute-start.6) | collective-permute-done | bytes 524320 | tf_op jit(solution)/shard_map/ppermute | solution.py:28
  44.1 1.3 %collective-permute-start.7 = (bf16[384,1024]{1,0:T(8,128)(2,1)S(1)}, bf16[384,1024]{1,0:T(8,128)(2,1)S(1)}, u32[]{:S(2)}, u32[]{:S(2)}) collective-permute-start(bf16[384,1024]{1,0:T(8,128)(2,1)S(1)} %slice.72), channel_id=1, source_target_pairs={{0,1},{1,2},{2,3},{3,4},{4,5},{5,6},{6,7},{7,8},{8,9},{9,10},{10,1... | collective-permute-start | bytes 2359304 | tf_op jit(solution)/shard_map/ppermute | solution.py:22
  45.4 9.9 %collective-permute-done.rest_6_.rest_7_ = bf16[256,1024]{1,0:T(8,128)(2,1)S(1)} collective-permute-done((bf16[256,1024]{1,0:T(8,128)(2,1)S(1)}, bf16[256,1024]{1,0:T(8,128)(2,1)S(1)}, u32[]{:S(2)}, u32[]{:S(2)}) %collective-permute-start) | collective-permute-done | bytes 524320 | tf_op jit(solution)/shard_map/ppermute | solution.py:28
  55.4 1.0 slice.62
  56.4 1.0 slice.63
  57.4 1.3 %collective-permute-start.2 = (bf16[384,1024]{1,0:T(8,128)(2,1)}, bf16[384,1024]{1,0:T(8,128)(2,1)S(1)}, u32[]{:S(2)}, u32[]{:S(2)}) collective-permute-start(bf16[384,1024]{1,0:T(8,128)(2,1)} %slice.63), channel_id=1, source_target_pairs={{0,1},{1,2},{2,3},{3,4},{4,5},{5,6},{6,7},{7,8},{8,9},{9,10},{10,1... | collective-permute-start | bytes 2359304 | tf_op jit(solution)/shard_map/ppermute | solution.py:22
  58.7 1.3 %collective-permute-start.1 = (bf16[384,1024]{1,0:T(8,128)(2,1)}, bf16[384,1024]{1,0:T(8,128)(2,1)S(1)}, u32[]{:S(2)}, u32[]{:S(2)}) collective-permute-start(bf16[384,1024]{1,0:T(8,128)(2,1)} %slice.62), channel_id=1, source_target_pairs={{0,1},{1,2},{2,3},{3,4},{4,5},{5,6},{6,7},{7,8},{8,9},{9,10},{10,1... | collective-permute-start | bytes 2359304 | tf_op jit(solution)/shard_map/ppermute | solution.py:22
  60.0 0.8 pad_maximum_fusion.3
  60.9 0.8 pad_maximum_fusion.2
  61.7 0.9 pad_maximum_fusion.1
  62.6 12.5 %collective-permute-done.11.rest_4_.rest_5_ = bf16[256,1024]{1,0:T(8,128)(2,1)S(1)} collective-permute-done((bf16[256,1024]{1,0:T(8,128)(2,1)S(1)}, bf16[256,1024]{1,0:T(8,128)(2,1)S(1)}, u32[]{:S(2)}, u32[]{:S(2)}) %collective-permute-start.11) | collective-permute-done | bytes 524320 | tf_op jit(solution)/shard_map/ppermute | solution.py:28
  75.1 0.8 copy-done.5
  75.9 0.1 collective-permute-start.4
  76.0 0.8 copy-done.10
  76.8 0.9 copy-done.11
  77.7 0.6 pad_add_fusion.meta
  78.3 12.4 %shard_map.55.rest_8_ = bf16[384,2048]{1,0:T(8,128)(2,1)} custom-call(s32[4]{0:T(128)} %pad_add_fusion.meta, bf16[384,2048]{1,0:T(8,128)(2,1)} %q_ref.3, bf16[384,2048]{1,0:T(8,128)(2,1)} %ok_ref.3, bf16[384,2048]{1,0:T(8,128)(2,1)} %ov_ref.3, bf16[384,1024]{1,0:T(8,128)(2,1)} %copy-done.11, bf16[384,1024]{1,0:T(8,128)(2,1)} %copy-done.10, ...), custom_call_target="tpu_custom_call" | custom-call | flops 2013265920 | bytes 6815744 | tf_op jit(solution)/shard_map/pallas_call | solution.py:125
  90.7 11.5 %collective-permute-done.4.rest_2_.rest_3_ = bf16[256,1024]{1,0:T(8,128)(2,1)S(1)} collective-permute-done((bf16[256,1024]{1,0:T(8,128)(2,1)}, bf16[256,1024]{1,0:T(8,128)(2,1)S(1)}, u32[]{:S(2)}, u32[]{:S(2)}) %collective-permute-start.4) | collective-permute-done | bytes 524320 | tf_op jit(solution)/shard_map/ppermute | solution.py:28
  102.2 0.7 collective-permute-done.5.rest_4_.rest_5_
  103.0 0.1 copy-done.8
  103.0 0.7 copy-done.9
  103.7 0.3 copy-done.12
  104.0 0.9 copy-done.13
  104.9 12.4 %shard_map.56 = bf16[384,2048]{1,0:T(8,128)(2,1)} custom-call(s32[4]{0:T(128)} %pad_add_fusion.meta, bf16[384,2048]{1,0:T(8,128)(2,1)} %q_ref.3, bf16[384,2048]{1,0:T(8,128)(2,1)} %ok_ref.3, bf16[384,2048]{1,0:T(8,128)(2,1)} %ov_ref.3, bf16[384,1024]{1,0:T(8,128)(2,1)} %copy-done.13, bf16[384,1024]{1,0:T(8,128)(2,1)} %copy-done.12, ...), custom_call_target="tpu_custom_call", output_to_operand_aliasing={{}: (14, {})} | custom-call | flops 2013265920 | bytes 6815744 | tf_op jit(solution)/shard_map/pallas_call | solution.py:125
  (39 shorter events, 0.3 us)
Async XLA Ops:
  7.1 37.0 %collective-permute-start.6 = (bf16[256,1024]{1,0:T(8,128)(2,1)S(1)}, bf16[256,1024]{1,0:T(8,128)(2,1)S(1)}, u32[]{:S(2)}, u32[]{:S(2)}) collective-permute-start(bf16[256,1024]{1,0:T(8,128)(2,1)S(1)} %pad_maximum_fusion.4), channel_id=1, source_target_pairs={{0,8},{1,9},{2,10},{3,11},{4,12},{5,13},{6,14},{7,15},{8,0},{9,1},... | collective-permute-start | bytes 1572872 | tf_op jit(solution)/shard_map/ppermute | solution.py:28
  7.3 3.9 %copy-start.1 = (bf16[384,2048]{1,0:T(8,128)(2,1)S(1)}, bf16[384,2048]{1,0:T(8,128)(2,1)}, u32[]{:S(2)}) copy-start(bf16[384,2048]{1,0:T(8,128)(2,1)} %ov_ref.3) | copy-start | bytes 4718596
  7.3 48.1 %collective-permute-start = (bf16[256,1024]{1,0:T(8,128)(2,1)S(1)}, bf16[256,1024]{1,0:T(8,128)(2,1)S(1)}, u32[]{:S(2)}, u32[]{:S(2)}) collective-permute-start(bf16[256,1024]{1,0:T(8,128)(2,1)S(1)} %pad_maximum_fusion), channel_id=1, source_target_pairs={{0,8},{1,9},{2,10},{3,11},{4,12},{5,13},{6,14},{7,15},{8,0},{9,1},... | collective-permute-start | bytes 1572872 | tf_op jit(solution)/shard_map/ppermute | solution.py:28
  9.7 2.8 %copy-start = (bf16[384,2048]{1,0:T(8,128)(2,1)S(1)}, bf16[384,2048]{1,0:T(8,128)(2,1)}, u32[]{:S(2)}) copy-start(bf16[384,2048]{1,0:T(8,128)(2,1)} %ok_ref.3) | copy-start | bytes 4718596
  9.7 47.7 %collective-permute-start.9 = (bf16[256,1024]{1,0:T(8,128)(2,1)S(1)}, bf16[256,1024]{1,0:T(8,128)(2,1)S(1)}, u32[]{:S(2)}, u32[]{:S(2)}) collective-permute-start(bf16[256,1024]{1,0:T(8,128)(2,1)S(1)} %pad_maximum_fusion.5), channel_id=1, source_target_pairs={{0,1},{1,0},{2,3},{3,2},{4,5},{5,4},{6,7},{7,6},{8,9},{9,8},{10,11... | collective-permute-start | bytes 1572872 | tf_op jit(solution)/shard_map/ppermute | solution.py:28
  10.9 47.9 %collective-permute-start.10 = (bf16[256,1024]{1,0:T(8,128)(2,1)S(1)}, bf16[256,1024]{1,0:T(8,128)(2,1)S(1)}, u32[]{:S(2)}, u32[]{:S(2)}) collective-permute-start(bf16[256,1024]{1,0:T(8,128)(2,1)S(1)} %pad_maximum_fusion.6), channel_id=1, source_target_pairs={{0,2},{1,3},{2,0},{3,1},{4,6},{5,7},{6,4},{7,5},{8,10},{9,11},{10,... | collective-permute-start | bytes 1572872 | tf_op jit(solution)/shard_map/ppermute | solution.py:28
  11.2 64.7 %collective-permute-start.8 = (bf16[384,1024]{1,0:T(8,128)(2,1)S(1)}, bf16[384,1024]{1,0:T(8,128)(2,1)S(1)}, u32[]{:S(2)}, u32[]{:S(2)}) collective-permute-start(bf16[384,1024]{1,0:T(8,128)(2,1)S(1)} %slice.73), channel_id=1, source_target_pairs={{0,1},{1,2},{2,3},{3,4},{4,5},{5,6},{6,7},{7,8},{8,9},{9,10},{10,1... | collective-permute-start | bytes 2359304 | tf_op jit(solution)/shard_map/ppermute | solution.py:22
  44.1 1.3 %copy-start.6 = (bf16[256,1024]{1,0:T(8,128)(2,1)}, bf16[256,1024]{1,0:T(8,128)(2,1)S(1)}, u32[]{:S(2)}) copy-start(bf16[256,1024]{1,0:T(8,128)(2,1)S(1)} %collective-permute-done.6.rest_6_.rest_7_) | copy-start | bytes 1572868
  44.1 32.7 %collective-permute-start.7 = (bf16[384,1024]{1,0:T(8,128)(2,1)S(1)}, bf16[384,1024]{1,0:T(8,128)(2,1)S(1)}, u32[]{:S(2)}, u32[]{:S(2)}) collective-permute-start(bf16[384,1024]{1,0:T(8,128)(2,1)S(1)} %slice.72), channel_id=1, source_target_pairs={{0,1},{1,2},{2,3},{3,4},{4,5},{5,6},{6,7},{7,8},{8,9},{9,10},{10,1... | collective-permute-start | bytes 2359304 | tf_op jit(solution)/shard_map/ppermute | solution.py:22
  55.4 2.0 %copy-start.2 = (bf16[256,1024]{1,0:T(8,128)(2,1)}, bf16[256,1024]{1,0:T(8,128)(2,1)S(1)}, u32[]{:S(2)}) copy-start(bf16[256,1024]{1,0:T(8,128)(2,1)S(1)} %collective-permute-done.rest_6_.rest_7_) | copy-start | bytes 1572868
  55.4 19.7 %collective-permute-start.11 = (bf16[256,1024]{1,0:T(8,128)(2,1)S(1)}, bf16[256,1024]{1,0:T(8,128)(2,1)S(1)}, u32[]{:S(2)}, u32[]{:S(2)}) collective-permute-start(bf16[256,1024]{1,0:T(8,128)(2,1)S(1)} %pad_maximum_fusion.7), channel_id=1, source_target_pairs={{0,4},{1,5},{2,6},{3,7},{4,0},{5,1},{6,2},{7,3},{8,12},{9,13},{10,... | collective-permute-start | bytes 1572872 | tf_op jit(solution)/shard_map/ppermute | solution.py:28
  57.4 5.2 %copy-start.3 = (bf16[256,1024]{1,0:T(8,128)(2,1)}, bf16[256,1024]{1,0:T(8,128)(2,1)S(1)}, u32[]{:S(2)}) copy-start(bf16[256,1024]{1,0:T(8,128)(2,1)S(1)} %collective-permute-done.9.rest_0_.rest_1_) | copy-start | bytes 1572868
  57.4 45.5 %collective-permute-start.2 = (bf16[384,1024]{1,0:T(8,128)(2,1)}, bf16[384,1024]{1,0:T(8,128)(2,1)S(1)}, u32[]{:S(2)}, u32[]{:S(2)}) collective-permute-start(bf16[384,1024]{1,0:T(8,128)(2,1)} %slice.63), channel_id=1, source_target_pairs={{0,1},{1,2},{2,3},{3,4},{4,5},{5,6},{6,7},{7,8},{8,9},{9,10},{10,1... | collective-permute-start | bytes 2359304 | tf_op jit(solution)/shard_map/ppermute | solution.py:22
  58.7 3.8 %copy-start.4 = (bf16[256,1024]{1,0:T(8,128)(2,1)}, bf16[256,1024]{1,0:T(8,128)(2,1)S(1)}, u32[]{:S(2)}) copy-start(bf16[256,1024]{1,0:T(8,128)(2,1)S(1)} %collective-permute-done.10.rest_2_.rest_3_) | copy-start | bytes 1572868
  58.7 44.2 %collective-permute-start.1 = (bf16[384,1024]{1,0:T(8,128)(2,1)}, bf16[384,1024]{1,0:T(8,128)(2,1)S(1)}, u32[]{:S(2)}, u32[]{:S(2)}) collective-permute-start(bf16[384,1024]{1,0:T(8,128)(2,1)} %slice.62), channel_id=1, source_target_pairs={{0,1},{1,2},{2,3},{3,4},{4,5},{5,6},{6,7},{7,8},{8,9},{9,10},{10,1... | collective-permute-start | bytes 2359304 | tf_op jit(solution)/shard_map/ppermute | solution.py:22
  60.0 17.7 %copy-start.14 = (s32[3]{0:T(128)S(1)}, s32[3]{0:T(128)}, u32[]{:S(2)}) copy-start(s32[3]{0:T(128)} %param.8) | copy-start | bytes 40
  75.1 0.8 copy-start.5
  75.9 14.8 %collective-permute-start.3 = (bf16[256,1024]{1,0:T(8,128)(2,1)}, bf16[256,1024]{1,0:T(8,128)(2,1)S(1)}, u32[]{:S(2)}, u32[]{:S(2)}) collective-permute-start(bf16[256,1024]{1,0:T(8,128)(2,1)} %pad_maximum_fusion.1), channel_id=1, source_target_pairs={{0,1},{1,0},{2,3},{3,2},{4,5},{5,4},{6,7},{7,6},{8,9},{9,8},{10,11... | collective-permute-start | bytes 1572872 | tf_op jit(solution)/shard_map/ppermute | solution.py:28
  75.9 0.9 copy-start.10
  75.9 26.3 %collective-permute-start.4 = (bf16[256,1024]{1,0:T(8,128)(2,1)}, bf16[256,1024]{1,0:T(8,128)(2,1)S(1)}, u32[]{:S(2)}, u32[]{:S(2)}) collective-permute-start(bf16[256,1024]{1,0:T(8,128)(2,1)} %pad_maximum_fusion.2), channel_id=1, source_target_pairs={{0,2},{1,3},{2,0},{3,1},{4,6},{5,7},{6,4},{7,5},{8,10},{9,11},{10,... | collective-permute-start | bytes 1572872 | tf_op jit(solution)/shard_map/ppermute | solution.py:28
  76.8 0.9 copy-start.11
  77.7 25.2 %collective-permute-start.5 = (bf16[256,1024]{1,0:T(8,128)(2,1)}, bf16[256,1024]{1,0:T(8,128)(2,1)S(1)}, u32[]{:S(2)}, u32[]{:S(2)}) collective-permute-start(bf16[256,1024]{1,0:T(8,128)(2,1)} %pad_maximum_fusion.3), channel_id=1, source_target_pairs={{0,4},{1,5},{2,6},{3,7},{4,0},{5,1},{6,2},{7,3},{8,12},{9,13},{10,... | collective-permute-start | bytes 1572872 | tf_op jit(solution)/shard_map/ppermute | solution.py:28
  90.7 12.2 %copy-start.7 = (bf16[256,1024]{1,0:T(8,128)(2,1)}, bf16[256,1024]{1,0:T(8,128)(2,1)S(1)}, u32[]{:S(2)}) copy-start(bf16[256,1024]{1,0:T(8,128)(2,1)S(1)} %collective-permute-done.3.rest_0_.rest_1_) | copy-start | bytes 1572868
  102.2 0.8 copy-start.8
  102.9 0.8 copy-start.9
  102.9 1.1 copy-start.12
  104.0 0.9 copy-start.13

commit v19 on v16

--- a/solution.py
+++ b/solution.py
@@ -12,7 +12,7 @@
 WIN = 4
 HDIM = 128
 LOG2E = 1.4426950408889634
-HEADS_PER_STEP = 4
+HEADS_PER_STEP = 8
 CHUNKS = 2
 
 

time: 106 us -> 107 us (level)
  Pallas kernels: 24.9 us -> 26.4 us
    pallas_call x2, Pallas kernels: 24.9 us -> 26.4 us  [attend(): pl.pallas_call(functools.partial(attend_kernel, level_count), out_shape=j...]
where the time goes in v19:
time: 107 us
  waiting for transfers between devices  56.6 us (53%)
  Pallas kernels  26.4 us (25%)
  starting transfers between devices  11.8 us (11%)
  local copies, waits for them, and re-layouts  6.91 us (6%)
  between operations  2.7 us (3%)
  other arithmetic  2.44 us (2%)
    ppermute x8, waiting for transfers between devices, from_partner(): return lax.ppermute(value, axis, pairs)  56.6 us
    pallas_call x2, Pallas kernels, attend(): pl.pallas_call(functools.partial(attend_kernel, level_count), out_shape=j...  26.4 us
    ppermute x8, starting transfers between devices, from_partner(): return lax.ppermute(value, axis, pairs)  6.68 us
    ppermute x4, starting transfers between devices, passed_along(): return lax.ppermute(block, axis, route)  5.13 us
    slice x1, local copies, waits for them, and re-layouts, on_device(): key_rows[:, cols]  2.77 us
  transfers between devices with their start and end apart: 12, of which 5 were waited for; matrix products, arithmetic and copies ran while one was open for 4% of the time, Pallas kernels for 12%

profile of v19, /device:TPU:29, one launch (start us, length us, event | category | flops | bytes accessed | tf_op | source)
XLA Modules:
  0.0 106.8 jit_solution(3226746826455613255)
XLA Ops:
  0.0 2.8 %fusion.1 = (bf16[384,1024]{1,0:T(8,128)(2,1)}, bf16[384,1024]{1,0:T(8,128)(2,1)}) fusion(bf16[384,2048]{1,0:T(8,128)(2,1)} %ok_ref.3), kind=kLoop, calls=%fused_computation.22 | loop fusion | bytes 3145728 | tf_op jit(solution)/shard_map/slice | solution.py:156
  2.8 1.3 %collective-permute-start.6 = (bf16[384,1024]{1,0:T(8,128)(2,1)}, bf16[384,1024]{1,0:T(8,128)(2,1)}, u32[]{:S(2)}, u32[]{:S(2)}) collective-permute-start(bf16[384,1024]{1,0:T(8,128)(2,1)} %get-tuple-element.23), channel_id=1, source_target_pairs={{0,1},{1,2},{2,3},{3,4},{4,5},{5,6},{6,7},{7,8},{8,9},{9,10},{10,1... | collective-permute-start | bytes 2359304 | tf_op jit(solution)/shard_map/ppermute | solution.py:22
  4.1 0.7 constant_dynamic-slice_fusion.2
  7.3 0.0 copy-start.1
  7.3 0.2 constant_dynamic-slice_fusion.1
  7.5 1.2 %copy-done.1 = bf16[384,2048]{1,0:T(8,128)(2,1)S(1)} copy-done((bf16[384,2048]{1,0:T(8,128)(2,1)S(1)}, bf16[384,2048]{1,0:T(8,128)(2,1)}, u32[]{:S(2)}) %copy-start.1) | copy-done | bytes 1572888
  8.7 0.2 constant_dynamic-slice_fusion
  9.0 1.4 %collective-permute-start.8 = (bf16[256,1024]{1,0:T(8,128)(2,1)S(1)}, bf16[256,1024]{1,0:T(8,128)(2,1)S(1)}, u32[]{:S(2)}, u32[]{:S(2)}) collective-permute-start(bf16[256,1024]{1,0:T(8,128)(2,1)S(1)} %pad_maximum_fusion.4), channel_id=1, source_target_pairs={{0,1},{1,0},{2,3},{3,2},{4,5},{5,4},{6,7},{7,6},{8,9},{9,8},{10,11... | collective-permute-start | bytes 1572872 | tf_op jit(solution)/shard_map/ppermute | solution.py:28
  10.4 1.4 %collective-permute-start.9 = (bf16[256,1024]{1,0:T(8,128)(2,1)S(1)}, bf16[256,1024]{1,0:T(8,128)(2,1)S(1)}, u32[]{:S(2)}, u32[]{:S(2)}) collective-permute-start(bf16[256,1024]{1,0:T(8,128)(2,1)S(1)} %pad_maximum_fusion.5), channel_id=1, source_target_pairs={{0,2},{1,3},{2,0},{3,1},{4,6},{5,7},{6,4},{7,5},{8,10},{9,11},{10,... | collective-permute-start | bytes 1572872 | tf_op jit(solution)/shard_map/ppermute | solution.py:28
  11.8 0.2 collective-permute-start.10
  12.1 1.1 %collective-permute-start.2 = (bf16[256,1024]{1,0:T(8,128)(2,1)S(1)}, bf16[256,1024]{1,0:T(8,128)(2,1)S(1)}, u32[]{:S(2)}, u32[]{:S(2)}) collective-permute-start(bf16[256,1024]{1,0:T(8,128)(2,1)S(1)} %pad_maximum_fusion), channel_id=1, source_target_pairs={{0,1},{1,0},{2,3},{3,2},{4,5},{5,4},{6,7},{7,6},{8,9},{9,8},{10,11... | collective-permute-start | bytes 1572872 | tf_op jit(solution)/shard_map/ppermute | solution.py:28
  13.2 1.0 fusion
  14.3 0.0 collective-permute-done.8.rest_0_.rest_1_
  14.3 1.3 %collective-permute-start.7 = (bf16[384,1024]{1,0:T(8,128)(2,1)S(1)}, bf16[384,1024]{1,0:T(8,128)(2,1)S(1)}, u32[]{:S(2)}, u32[]{:S(2)}) collective-permute-start(bf16[384,1024]{1,0:T(8,128)(2,1)S(1)} %get-tuple-element.21), channel_id=1, source_target_pairs={{0,1},{1,2},{2,3},{3,4},{4,5},{5,6},{6,7},{7,8},{8,9},{9,10},{10,1... | collective-permute-start | bytes 2359304 | tf_op jit(solution)/shard_map/ppermute | solution.py:22
  15.6 11.9 %collective-permute-done.9.rest_2_.rest_3_ = bf16[256,1024]{1,0:T(8,128)(2,1)S(1)} collective-permute-done((bf16[256,1024]{1,0:T(8,128)(2,1)S(1)}, bf16[256,1024]{1,0:T(8,128)(2,1)S(1)}, u32[]{:S(2)}, u32[]{:S(2)}) %collective-permute-start.9) | collective-permute-done | bytes 524320 | tf_op jit(solution)/shard_map/ppermute | solution.py:28
  27.5 0.1 collective-permute-start.11
  27.6 1.3 %collective-permute-start = (bf16[384,1024]{1,0:T(8,128)(2,1)}, bf16[384,1024]{1,0:T(8,128)(2,1)}, u32[]{:S(2)}, u32[]{:S(2)}) collective-permute-start(bf16[384,1024]{1,0:T(8,128)(2,1)} %get-tuple-element.24), channel_id=1, source_target_pairs={{0,1},{1,2},{2,3},{3,4},{4,5},{5,6},{6,7},{7,8},{8,9},{9,10},{10,1... | collective-permute-start | bytes 2359304 | tf_op jit(solution)/shard_map/ppermute | solution.py:22
  28.9 0.0 collective-permute-done.2.rest_0_.rest_1_
  28.9 1.3 %collective-permute-start.1 = (bf16[384,1024]{1,0:T(8,128)(2,1)}, bf16[384,1024]{1,0:T(8,128)(2,1)}, u32[]{:S(2)}, u32[]{:S(2)}) collective-permute-start(bf16[384,1024]{1,0:T(8,128)(2,1)} %get-tuple-element.22), channel_id=1, source_target_pairs={{0,1},{1,2},{2,3},{3,4},{4,5},{5,6},{6,7},{7,8},{8,9},{9,10},{10,1... | collective-permute-start | bytes 2359304 | tf_op jit(solution)/shard_map/ppermute | solution.py:22
  30.2 0.0 copy-start.12
  30.2 0.8 pad_maximum_fusion.2
  31.1 0.8 pad_maximum_fusion.1
  31.9 21.7 %collective-permute-done.11.rest_6_.rest_7_ = bf16[256,1024]{1,0:T(8,128)(2,1)S(1)} collective-permute-done((bf16[256,1024]{1,0:T(8,128)(2,1)S(1)}, bf16[256,1024]{1,0:T(8,128)(2,1)S(1)}, u32[]{:S(2)}, u32[]{:S(2)}) %collective-permute-start.11) | collective-permute-done | bytes 524320 | tf_op jit(solution)/shard_map/ppermute | solution.py:28
  53.6 0.5 collective-permute-start.3
  54.1 2.0 %collective-permute-start.5 = (bf16[256,1024]{1,0:T(8,128)(2,1)S(1)}, bf16[256,1024]{1,0:T(8,128)(2,1)S(1)}, u32[]{:S(2)}, u32[]{:S(2)}) collective-permute-start(bf16[256,1024]{1,0:T(8,128)(2,1)S(1)} %pad_maximum_fusion.3), channel_id=1, source_target_pairs={{0,8},{1,9},{2,10},{3,11},{4,12},{5,13},{6,14},{7,15},{8,0},{9,1},... | collective-permute-start | bytes 1572872 | tf_op jit(solution)/shard_map/ppermute | solution.py:28
  56.1 0.6 pad_add_fusion.meta
  56.7 13.1 %shard_map.55.rest_8_ = bf16[384,2048]{1,0:T(8,128)(2,1)} custom-call(s32[4]{0:T(128)} %pad_add_fusion.meta, bf16[384,2048]{1,0:T(8,128)(2,1)} %q_ref.3, bf16[384,2048]{1,0:T(8,128)(2,1)} %ok_ref.3, bf16[384,2048]{1,0:T(8,128)(2,1)} %ov_ref.3, bf16[384,1024]{1,0:T(8,128)(2,1)} %collective-permute-done.6.pk_ref, bf16[384,1024]{1,0:T(8,128)(2,1)} %copy-done.10, ...), custom_call_target="tpu_custom_call" | custom-call | flops 2013265920 | bytes 6815744 | tf_op jit(solution)/shard_map/pallas_call | solution.py:125
  69.8 4.4 %collective-permute-done.3.rest_2_.rest_3_ = bf16[256,1024]{1,0:T(8,128)(2,1)S(1)} collective-permute-done((bf16[256,1024]{1,0:T(8,128)(2,1)}, bf16[256,1024]{1,0:T(8,128)(2,1)S(1)}, u32[]{:S(2)}, u32[]{:S(2)}) %collective-permute-start.3) | collective-permute-done | bytes 524320 | tf_op jit(solution)/shard_map/ppermute | solution.py:28
  74.1 6.8 %collective-permute-done.4.rest_4_.rest_5_ = bf16[256,1024]{1,0:T(8,128)(2,1)S(1)} collective-permute-done((bf16[256,1024]{1,0:T(8,128)(2,1)}, bf16[256,1024]{1,0:T(8,128)(2,1)S(1)}, u32[]{:S(2)}, u32[]{:S(2)}) %collective-permute-start.4) | collective-permute-done | bytes 524320 | tf_op jit(solution)/shard_map/ppermute | solution.py:28
  80.9 11.8 %collective-permute-done.5.rest_6_.rest_7_ = bf16[256,1024]{1,0:T(8,128)(2,1)S(1)} collective-permute-done((bf16[256,1024]{1,0:T(8,128)(2,1)S(1)}, bf16[256,1024]{1,0:T(8,128)(2,1)S(1)}, u32[]{:S(2)}, u32[]{:S(2)}) %collective-permute-start.5) | collective-permute-done | bytes 524320 | tf_op jit(solution)/shard_map/ppermute | solution.py:28
  92.8 0.8 copy-done.9
  93.5 13.3 %shard_map.56 = bf16[384,2048]{1,0:T(8,128)(2,1)} custom-call(s32[4]{0:T(128)} %pad_add_fusion.meta, bf16[384,2048]{1,0:T(8,128)(2,1)} %q_ref.3, bf16[384,2048]{1,0:T(8,128)(2,1)} %ok_ref.3, bf16[384,2048]{1,0:T(8,128)(2,1)} %ov_ref.3, bf16[384,1024]{1,0:T(8,128)(2,1)} %collective-permute-done.pk_ref, ...), custom_call_target="tpu_custom_call", output_to_operand_aliasing={{}: (14, {})} | custom-call | flops 2013265920 | bytes 6815744 | tf_op jit(solution)/shard_map/pallas_call | solution.py:125
  (34 shorter events, 0.3 us)
Async XLA Ops:
  0.0 7.3 %copy-start = (bf16[384,2048]{1,0:T(8,128)(2,1)S(1)}, bf16[384,2048]{1,0:T(8,128)(2,1)}, u32[]{:S(2)}) copy-start(bf16[384,2048]{1,0:T(8,128)(2,1)} %ok_ref.3) | copy-start | bytes 4718596
  0.0 4.1 %copy-start.11 = (s32[16,4,1]{0,2,1:T(1,128)S(1)}, s32[16,4,1]{0,2,1:T(1,128)}, u32[]{:S(2)}) copy-start(s32[16,4,1]{0,2,1:T(1,128)} %param.9) | copy-start | bytes 772
  2.8 51.3 %collective-permute-start.6 = (bf16[384,1024]{1,0:T(8,128)(2,1)}, bf16[384,1024]{1,0:T(8,128)(2,1)}, u32[]{:S(2)}, u32[]{:S(2)}) collective-permute-start(bf16[384,1024]{1,0:T(8,128)(2,1)} %get-tuple-element.23), channel_id=1, source_target_pairs={{0,1},{1,2},{2,3},{3,4},{4,5},{5,6},{6,7},{7,8},{8,9},{9,10},{10,1... | collective-permute-start | bytes 2359304 | tf_op jit(solution)/shard_map/ppermute | solution.py:22
  7.3 1.4 %copy-start.1 = (bf16[384,2048]{1,0:T(8,128)(2,1)S(1)}, bf16[384,2048]{1,0:T(8,128)(2,1)}, u32[]{:S(2)}) copy-start(bf16[384,2048]{1,0:T(8,128)(2,1)} %ov_ref.3) | copy-start | bytes 4718596
  9.0 5.3 %collective-permute-start.8 = (bf16[256,1024]{1,0:T(8,128)(2,1)S(1)}, bf16[256,1024]{1,0:T(8,128)(2,1)S(1)}, u32[]{:S(2)}, u32[]{:S(2)}) collective-permute-start(bf16[256,1024]{1,0:T(8,128)(2,1)S(1)} %pad_maximum_fusion.4), channel_id=1, source_target_pairs={{0,1},{1,0},{2,3},{3,2},{4,5},{5,4},{6,7},{7,6},{8,9},{9,8},{10,11... | collective-permute-start | bytes 1572872 | tf_op jit(solution)/shard_map/ppermute | solution.py:28
  10.4 17.1 %collective-permute-start.9 = (bf16[256,1024]{1,0:T(8,128)(2,1)S(1)}, bf16[256,1024]{1,0:T(8,128)(2,1)S(1)}, u32[]{:S(2)}, u32[]{:S(2)}) collective-permute-start(bf16[256,1024]{1,0:T(8,128)(2,1)S(1)} %pad_maximum_fusion.5), channel_id=1, source_target_pairs={{0,2},{1,3},{2,0},{3,1},{4,6},{5,7},{6,4},{7,5},{8,10},{9,11},{10,... | collective-permute-start | bytes 1572872 | tf_op jit(solution)/shard_map/ppermute | solution.py:28
  11.8 15.7 %collective-permute-start.10 = (bf16[256,1024]{1,0:T(8,128)(2,1)S(1)}, bf16[256,1024]{1,0:T(8,128)(2,1)S(1)}, u32[]{:S(2)}, u32[]{:S(2)}) collective-permute-start(bf16[256,1024]{1,0:T(8,128)(2,1)S(1)} %pad_maximum_fusion.6), channel_id=1, source_target_pairs={{0,4},{1,5},{2,6},{3,7},{4,0},{5,1},{6,2},{7,3},{8,12},{9,13},{10,... | collective-permute-start | bytes 1572872 | tf_op jit(solution)/shard_map/ppermute | solution.py:28
  12.1 16.8 %collective-permute-start.2 = (bf16[256,1024]{1,0:T(8,128)(2,1)S(1)}, bf16[256,1024]{1,0:T(8,128)(2,1)S(1)}, u32[]{:S(2)}, u32[]{:S(2)}) collective-permute-start(bf16[256,1024]{1,0:T(8,128)(2,1)S(1)} %pad_maximum_fusion), channel_id=1, source_target_pairs={{0,1},{1,0},{2,3},{3,2},{4,5},{5,4},{6,7},{7,6},{8,9},{9,8},{10,11... | collective-permute-start | bytes 1572872 | tf_op jit(solution)/shard_map/ppermute | solution.py:28
  14.3 16.8 %copy-start.2 = (bf16[256,1024]{1,0:T(8,128)(2,1)}, bf16[256,1024]{1,0:T(8,128)(2,1)S(1)}, u32[]{:S(2)}) copy-start(bf16[256,1024]{1,0:T(8,128)(2,1)S(1)} %collective-permute-done.8.rest_0_.rest_1_) | copy-start | bytes 1572868
  14.3 39.8 %collective-permute-start.7 = (bf16[384,1024]{1,0:T(8,128)(2,1)S(1)}, bf16[384,1024]{1,0:T(8,128)(2,1)S(1)}, u32[]{:S(2)}, u32[]{:S(2)}) collective-permute-start(bf16[384,1024]{1,0:T(8,128)(2,1)S(1)} %get-tuple-element.21), channel_id=1, source_target_pairs={{0,1},{1,2},{2,3},{3,4},{4,5},{5,6},{6,7},{7,8},{8,9},{9,10},{10,1... | collective-permute-start | bytes 2359304 | tf_op jit(solution)/shard_map/ppermute | solution.py:22
  27.5 4.4 %copy-start.3 = (bf16[256,1024]{1,0:T(8,128)(2,1)}, bf16[256,1024]{1,0:T(8,128)(2,1)S(1)}, u32[]{:S(2)}) copy-start(bf16[256,1024]{1,0:T(8,128)(2,1)S(1)} %collective-permute-done.9.rest_2_.rest_3_) | copy-start | bytes 1572868
  27.5 26.1 %collective-permute-start.11 = (bf16[256,1024]{1,0:T(8,128)(2,1)S(1)}, bf16[256,1024]{1,0:T(8,128)(2,1)S(1)}, u32[]{:S(2)}, u32[]{:S(2)}) collective-permute-start(bf16[256,1024]{1,0:T(8,128)(2,1)S(1)} %pad_maximum_fusion.7), channel_id=1, source_target_pairs={{0,8},{1,9},{2,10},{3,11},{4,12},{5,13},{6,14},{7,15},{8,0},{9,1},... | collective-permute-start | bytes 1572872 | tf_op jit(solution)/shard_map/ppermute | solution.py:28
  27.6 4.4 %copy-start.4 = (bf16[256,1024]{1,0:T(8,128)(2,1)}, bf16[256,1024]{1,0:T(8,128)(2,1)S(1)}, u32[]{:S(2)}) copy-start(bf16[256,1024]{1,0:T(8,128)(2,1)S(1)} %collective-permute-done.10.rest_4_.rest_5_) | copy-start | bytes 1572868
  27.6 65.2 %collective-permute-start = (bf16[384,1024]{1,0:T(8,128)(2,1)}, bf16[384,1024]{1,0:T(8,128)(2,1)}, u32[]{:S(2)}, u32[]{:S(2)}) collective-permute-start(bf16[384,1024]{1,0:T(8,128)(2,1)} %get-tuple-element.24), channel_id=1, source_target_pairs={{0,1},{1,2},{2,3},{3,4},{4,5},{5,6},{6,7},{7,8},{8,9},{9,10},{10,1... | collective-permute-start | bytes 2359304 | tf_op jit(solution)/shard_map/ppermute | solution.py:22
  28.9 3.1 %copy-start.6 = (bf16[256,1024]{1,0:T(8,128)(2,1)}, bf16[256,1024]{1,0:T(8,128)(2,1)S(1)}, u32[]{:S(2)}) copy-start(bf16[256,1024]{1,0:T(8,128)(2,1)S(1)} %collective-permute-done.2.rest_0_.rest_1_) | copy-start | bytes 1572868
  28.9 63.9 %collective-permute-start.1 = (bf16[384,1024]{1,0:T(8,128)(2,1)}, bf16[384,1024]{1,0:T(8,128)(2,1)}, u32[]{:S(2)}, u32[]{:S(2)}) collective-permute-start(bf16[384,1024]{1,0:T(8,128)(2,1)} %get-tuple-element.22), channel_id=1, source_target_pairs={{0,1},{1,2},{2,3},{3,4},{4,5},{5,6},{6,7},{7,8},{8,9},{9,10},{10,1... | collective-permute-start | bytes 2359304 | tf_op jit(solution)/shard_map/ppermute | solution.py:22
  30.2 25.9 %copy-start.12 = (s32[3]{0:T(128)S(1)}, s32[3]{0:T(128)}, u32[]{:S(2)}) copy-start(s32[3]{0:T(128)} %param.8) | copy-start | bytes 40
  53.6 3.1 %copy-start.5 = (bf16[256,1024]{1,0:T(8,128)(2,1)}, bf16[256,1024]{1,0:T(8,128)(2,1)S(1)}, u32[]{:S(2)}) copy-start(bf16[256,1024]{1,0:T(8,128)(2,1)S(1)} %collective-permute-done.11.rest_6_.rest_7_) | copy-start | bytes 1572868
  53.6 20.5 %collective-permute-start.3 = (bf16[256,1024]{1,0:T(8,128)(2,1)}, bf16[256,1024]{1,0:T(8,128)(2,1)S(1)}, u32[]{:S(2)}, u32[]{:S(2)}) collective-permute-start(bf16[256,1024]{1,0:T(8,128)(2,1)} %pad_maximum_fusion.1), channel_id=1, source_target_pairs={{0,2},{1,3},{2,0},{3,1},{4,6},{5,7},{6,4},{7,5},{8,10},{9,11},{10,... | collective-permute-start | bytes 1572872 | tf_op jit(solution)/shard_map/ppermute | solution.py:28
  54.1 26.8 %collective-permute-start.4 = (bf16[256,1024]{1,0:T(8,128)(2,1)}, bf16[256,1024]{1,0:T(8,128)(2,1)S(1)}, u32[]{:S(2)}, u32[]{:S(2)}) collective-permute-start(bf16[256,1024]{1,0:T(8,128)(2,1)} %pad_maximum_fusion.2), channel_id=1, source_target_pairs={{0,4},{1,5},{2,6},{3,7},{4,0},{5,1},{6,2},{7,3},{8,12},{9,13},{10,... | collective-permute-start | bytes 1572872 | tf_op jit(solution)/shard_map/ppermute | solution.py:28
  54.1 2.6 %copy-start.10 = (bf16[384,1024]{1,0:T(8,128)(2,1)}, bf16[384,1024]{1,0:T(8,128)(2,1)S(1)}, u32[]{:S(2)}) copy-start(bf16[384,1024]{1,0:T(8,128)(2,1)S(1)} %collective-permute-done.7.pv_ref) | copy-start | bytes 2359300
  54.1 38.7 %collective-permute-start.5 = (bf16[256,1024]{1,0:T(8,128)(2,1)S(1)}, bf16[256,1024]{1,0:T(8,128)(2,1)S(1)}, u32[]{:S(2)}, u32[]{:S(2)}) collective-permute-start(bf16[256,1024]{1,0:T(8,128)(2,1)S(1)} %pad_maximum_fusion.3), channel_id=1, source_target_pairs={{0,8},{1,9},{2,10},{3,11},{4,12},{5,13},{6,14},{7,15},{8,0},{9,1},... | collective-permute-start | bytes 1572872 | tf_op jit(solution)/shard_map/ppermute | solution.py:28
  74.1 18.6 %copy-start.7 = (bf16[256,1024]{1,0:T(8,128)(2,1)}, bf16[256,1024]{1,0:T(8,128)(2,1)S(1)}, u32[]{:S(2)}) copy-start(bf16[256,1024]{1,0:T(8,128)(2,1)S(1)} %collective-permute-done.3.rest_2_.rest_3_) | copy-start | bytes 1572868
  80.9 11.9 %copy-start.8 = (bf16[256,1024]{1,0:T(8,128)(2,1)}, bf16[256,1024]{1,0:T(8,128)(2,1)S(1)}, u32[]{:S(2)}) copy-start(bf16[256,1024]{1,0:T(8,128)(2,1)S(1)} %collective-permute-done.4.rest_4_.rest_5_) | copy-start | bytes 1572868
  92.7 0.8 copy-start.9
